TPU v7x, 128 devices: a whole 4x4x4 slice. The times are simulated.
128 devices in a mesh: dom: 8 (over x, core), band: 16 (over z, y).
Axes of the slice: x: 4, y: 4, z: 4, core: 2. Of those that a mesh axis runs over, the one named last changes fastest.
Arguments:
- psi: float32 [192, 32, 32, 128], P('band', 'dom'), may hold values from -6 to 6
- potential: float32 [32, 32, 128], P('dom'), may hold values from -3 to 0
Outputs:
- basis: float32 [192, 32, 32, 128], P('band', 'dom')
- projected: float32 [192, 192], P('band')
All inputs are finite; a program needn't handle non-finite values.
Results may differ from a plain program's by a relative error of at most 0.000092.
Values sent between devices are 32-bit elements; how exact they have to be, the bound alone decides.
No kernel may reach another device: no remote copies, remote signals or barrier semaphores. Data moves between devices by JAX's collectives and lax.ppermute only.
A program may use at most 128 MiB of HBM per device.

v0:
```python
import jax
import jax.numpy as jnp
from jax import lax
from jax.sharding import PartitionSpec as P

DEGREE = 4


stencil_coef = (-205.0 / 72.0, 8.0 / 5.0, -1.0 / 5.0, 8.0 / 315.0, -1.0 / 560.0)
stencil_reach = 4
center = 5.25
half = 4.75


def extended(array, sides, width):
    for axis, dim in sides:
        count, length = (lax.axis_size(axis), array.shape[dim])
        up = [(i, (i + 1) % count) for i in range(count)]
        down = [(j, i) for i, j in up]
        last = lax.slice_in_dim(array, length - width, length, axis=dim)
        initial = lax.slice_in_dim(array, 0, width, axis=dim)
        before = lax.ppermute(last, axis, up)
        after = lax.ppermute(initial, axis, down)
        array = jnp.concatenate([before, array, after], axis=dim)
    return array


def inner(left, right):
    return lax.dot_general(
        left,
        right,
        (((1,), (1,)), ((), ())),
        precision=lax.Precision.HIGHEST,
        preferred_element_type=jnp.float32,
    )


def hamiltonian(field, padded, potential):
    depth = field.shape[1]
    laplace = 3.0 * stencil_coef[0] * field
    for reach in range(1, 5):
        near = (
            padded[:, stencil_reach + reach : stencil_reach + reach + depth]
            + padded[:, stencil_reach - reach : stencil_reach - reach + depth]
        )
        near = near + jnp.roll(field, reach, 2) + jnp.roll(field, -reach, 2)
        near = near + jnp.roll(field, reach, 3) + jnp.roll(field, -reach, 3)
        laplace = laplace + stencil_coef[reach] * near
    return potential[None] * field - 0.5 * laplace


def local(psi, potential):
    bdev = psi.shape[0]
    depth, rows_y, rows_x = (psi.shape[1], psi.shape[2], psi.shape[3])
    nbands = bdev * lax.axis_size("band")
    ncells = depth * lax.axis_size("dom") * rows_y * rows_x
    own_start = lax.axis_index("band") * bdev

    def apply(field):
        padded = extended(field, (("dom", 1),), stencil_reach)
        return hamiltonian(field, padded, potential)

    previous = psi
    current = (apply(psi) - center * psi) / half
    for order in range(1, DEGREE):
        following = 2.0 / half * (apply(current) - center * current) - previous
        previous, current = (current, following)
    flat = current.reshape(bdev, -1)
    square = jnp.zeros((nbands, nbands), jnp.float32)
    over_part = lax.dynamic_update_slice(
        square,
        inner(flat, lax.all_gather(flat, "band", axis=0, tiled=True)),
        (own_start, jnp.int32(0)),
    )
    correlation = lax.psum(over_part, ("dom", "band"))
    lower = jnp.linalg.cholesky(correlation / ncells)
    inverse = jax.scipy.linalg.solve_triangular(
        lower, jnp.eye(nbands, dtype=jnp.float32), lower=True
    )
    own_rows = lax.dynamic_slice_in_dim(inverse, own_start, bdev, 0)
    basis_flat = jnp.dot(
        own_rows,
        lax.all_gather(flat, "band", axis=0, tiled=True),
        precision=lax.Precision.HIGHEST,
        preferred_element_type=jnp.float32,
    )
    basis = basis_flat.reshape(psi.shape)
    applied = apply(basis).reshape(bdev, -1)
    rows_part = inner(basis_flat, lax.all_gather(applied, "band", axis=0, tiled=True))
    projected = lax.psum(rows_part, "dom") / ncells
    return (basis, projected)


def solution(mesh):
    in_specs = (P("band", "dom", None, None), P("dom", None, None))
    out_specs = (P("band", "dom", None, None), P("band", None))
    return jax.shard_map(local, mesh=mesh, in_specs=in_specs, out_specs=out_specs, check_vma=False)
```

profile of v0, /device:TPU:0, one launch (start us, length us, event | category | flops | bytes accessed | tf_op | source)
XLA Modules:
  0.0 610.4 jit_solution(2942308282543192776)
XLA Ops:
  7.2 2.9 collective-permute-start
  11.3 1.1 fusion.239
  12.3 1.1 fusion.243
  18.1 2.0 collective-permute-done.1
  20.4 4.3 broadcast_multiply_fusion
  25.1 2.7 collective-permute-start.2
  30.9 6.6 %collective-permute-done.3 = f32[12,4,32,128]{3,2,1,0:T(8,128)S(1)} collective-permute-done((f32[12,4,32,128]{3,2,1,0:T(8,128)S(1)}, f32[12,4,32,128]{3,2,1,0:T(8,128)S(1)}, u32[]{:S(2)}, u32[]{:S(2)}) %collective-permute-start.3) | collective-permute-done | bytes 786464 | tf_op jit(solution)/shard_map/ppermute | solution.py:22
  37.5 3.8 fusion.64
  41.4 3.0 collective-permute-start.4
  47.5 6.5 %collective-permute-done.5 = f32[12,4,32,128]{3,2,1,0:T(8,128)S(1)} collective-permute-done((f32[12,4,32,128]{3,2,1,0:T(8,128)S(1)}, f32[12,4,32,128]{3,2,1,0:T(8,128)S(1)}, u32[]{:S(2)}, u32[]{:S(2)}) %collective-permute-start.5) | collective-permute-done | bytes 786464 | tf_op jit(solution)/shard_map/ppermute | solution.py:22
  54.1 4.0 fusion.39
  58.2 3.0 collective-permute-start.6
  64.3 6.5 %collective-permute-done.7 = f32[12,4,32,128]{3,2,1,0:T(8,128)S(1)} collective-permute-done((f32[12,4,32,128]{3,2,1,0:T(8,128)S(1)}, f32[12,4,32,128]{3,2,1,0:T(8,128)S(1)}, u32[]{:S(2)}, u32[]{:S(2)}) %collective-permute-start.7) | collective-permute-done | bytes 786464 | tf_op jit(solution)/shard_map/ppermute | solution.py:22
  70.8 3.8 fusion.14
  74.6 1.1 reshape.69
  76.6 113.2 %all-gather.5.cloned.1.call-done = f32[16,12,16384]{2,1,0:T(8,128)} async-done(((f32[1,12,16384]{2,1,0:T(8,128)}), f32[16,12,16384]{2,1,0:T(8,128)}) %all-gather.5.cloned.1.call-update) | async-done | bytes 12582928 | tf_op jit(solution)/shard_map/all_gather | solution.py:72
  189.7 12.6 %reshape.70 = f32[192,16384]{1,0:T(8,128)} reshape(f32[16,12,16384]{2,1,0:T(8,128)} %all-gather.5.cloned.1.call-done) | data formatting | bytes 25165824
  202.3 12.7 %fusion.251 = f32[12,192]{1,0:T(8,128)S(1)} fusion(f32[12,16384]{1,0:T(8,128)S(1)} %bitcast.66, f32[192,16384]{1,0:T(8,128)} %reshape.70), kind=kOutput, calls=%fused_computation.328 | convolution fusion | flops 452984832 | bytes 13378560 | tf_op jit(solution)/shard_map/dot_general | solution.py:29
  216.3 144.1 %all-reduce.5.cloned.1.call-done = f32[192,192]{1,0:T(8,128)} async-done(((f32[192,192]{1,0:T(8,128)}), f32[192,192]{1,0:T(8,128)}) %all-reduce.5.cloned.1.call-update) | async-done | bytes 147472 | tf_op jit(solution)/shard_map/psum | solution.py:75
  362.4 11.7 %cholesky.50 = f32[128,128]{1,0:T(8,128)S(1)} custom-call(f32[128,128]{1,0:T(8,128)S(1)} %cholesky.121), custom_call_target="Cholesky" | custom-call | tf_op jit(solution)/shard_map/jit(cholesky)/cholesky | solution.py:76
  374.8 9.8 %custom-call.15 = f32[1,128,128]{1,2,0:T(8,128)S(1)} custom-call(f32[1,128,128]{2,1,0:T(8,128)S(1)} %get-tuple-element.189), custom_call_target="InvertDiagBlocksLowerTriangular" | custom-call | tf_op jit(solution)/shard_map/jit(cholesky)/cholesky | solution.py:76
  385.0 5.8 cholesky.108
  393.0 19.9 %custom-call.16 = f32[2,128,128]{1,2,0:T(8,128)S(1)} custom-call(f32[2,128,128]{2,1,0:T(8,128)S(1)} %pad_maximum_fusion.6), custom_call_target="InvertDiagBlocksLowerTriangular" | custom-call | tf_op jit(solution)/shard_map/jit(_solve_triangular)/triangular_solve | solution.py:77
  413.9 9.1 %fusion.160 = f32[12,16384]{1,0:T(8,128)S(1)} fusion(f32[192,16384]{1,0:T(8,128)} %reshape.70, s32[]{:T(128)S(6)} %select_n.8, f32[128,192]{0,1:T(8,128)S(1)} %fusion.157, f32[64,192]{0,1:T(8,128)S(1)} %fusion.166), kind=kOutput, calls=%fused_computation.211 | convolution fusion | flops 452987136 | bytes 13516804 | tf_op jit(solution)/shard_map/dot_general | solution.py:81
  423.4 2.9 collective-permute-start.8
  429.5 6.6 %collective-permute-done.9 = f32[12,4,32,128]{3,2,1,0:T(8,128)S(1)} collective-permute-done((f32[12,4,32,128]{3,2,1,0:T(8,128)S(1)}, f32[12,4,32,128]{3,2,1,0:T(8,128)S(1)}, u32[]{:S(2)}, u32[]{:S(2)}) %collective-permute-start.9) | collective-permute-done | bytes 786464 | tf_op jit(solution)/shard_map/ppermute | solution.py:22
  436.4 3.8 fusion.83
  440.2 1.1 reshape.71
  441.4 110.5 %all-gather.7.cloned.1.call-done = f32[16,12,16384]{2,1,0:T(8,128)} async-done(((f32[1,12,16384]{2,1,0:T(8,128)}), f32[16,12,16384]{2,1,0:T(8,128)}) %all-gather.7.cloned.1.call-update) | async-done | bytes 12582928 | tf_op jit(solution)/shard_map/all_gather | solution.py:89
  551.9 12.6 %reshape.72 = f32[192,16384]{1,0:T(8,128)} reshape(f32[16,12,16384]{2,1,0:T(8,128)} %all-gather.7.cloned.1.call-done) | data formatting | bytes 25165824
  564.4 13.0 %fusion.252 = f32[12,192]{1,0:T(8,128)S(1)} fusion(f32[12,16384]{1,0:T(8,128)S(1)} %fusion.160, f32[192,16384]{1,0:T(8,128)} %reshape.72), kind=kOutput, calls=%fused_computation.329 | convolution fusion | flops 452984832 | bytes 13378560 | tf_op jit(solution)/shard_map/dot_general | solution.py:29
  577.4 25.4 %psum.15 = f32[12,192]{1,0:T(8,128)S(1)} all-reduce(f32[12,192]{1,0:T(8,128)S(1)} %fusion.252), channel_id=1, replica_groups=mesh['dom'=8,'band'=16] {'dom'}, use_global_device_ids=true, to_apply=%region_5.6 | all-reduce | flops 2304 | bytes 18432 | tf_op jit(solution)/shard_map/psum | solution.py:90
  (137 shorter events, 26.9 us)
Async XLA Ops:
  7.2 7.3 %copy-start = (f32[12,4,32,128]{3,2,1,0:T(8,128)S(1)}, f32[12,4,32,128]{3,2,1,0:T(8,128)}, u32[]{:S(2)}) copy-start(f32[12,4,32,128]{3,2,1,0:T(8,128)} %param.2) | copy-start | bytes 2359300
  7.2 182.6 %all-gather.5.cloned.1.call-start = ((), (), s32[]{:S(2)}) async-start(), calls=%async_computation.1 | async-start | bytes 17825792 | tf_op jit(solution)/shard_map/all_gather | solution.py:72
  7.2 12.8 %collective-permute-start.1 = (f32[12,4,32,128]{3,2,1,0:T(8,128)}, f32[12,4,32,128]{3,2,1,0:T(8,128)S(1)}, u32[]{:S(2)}, u32[]{:S(2)}) collective-permute-start(f32[12,4,32,128]{3,2,1,0:T(8,128)} %param.2), channel_id=1, source_target_pairs={{0,16},{16,32},{32,48},{48,64},{64,80},{80,96},{96,112},{112,0},{1... | collective-permute-start | bytes 2359304 | tf_op jit(solution)/shard_map/ppermute | solution.py:22
  7.2 13.1 %collective-permute-start = (f32[12,4,32,128]{3,2,1,0:T(8,128)}, f32[12,4,32,128]{3,2,1,0:T(8,128)S(1)}, u32[]{:S(2)}, u32[]{:S(2)}) collective-permute-start(f32[12,4,32,128]{3,2,1,0:T(8,128)} %param.2), channel_id=1, source_target_pairs={{16,0},{32,16},{48,32},{64,48},{80,64},{96,80},{112,96},{0,112},{1... | collective-permute-start | bytes 2359304 | tf_op jit(solution)/shard_map/ppermute | solution.py:23
  17.1 0.8 copy-start.2
  24.9 12.6 %collective-permute-start.3 = (f32[12,4,32,128]{3,2,1,0:T(8,128)S(1)}, f32[12,4,32,128]{3,2,1,0:T(8,128)S(1)}, u32[]{:S(2)}, u32[]{:S(2)}) collective-permute-start(f32[12,4,32,128]{3,2,1,0:T(8,128)S(1)} %get-tuple-element.22), channel_id=1, source_target_pairs={{0,16},{16,32},{32,48},{48,64},{64,80},{80,96},{96,112},{112,0},{1... | collective-permute-start | bytes 2359304 | tf_op jit(solution)/shard_map/ppermute | solution.py:22
  25.1 12.4 %collective-permute-start.2 = (f32[12,4,32,128]{3,2,1,0:T(8,128)S(1)}, f32[12,4,32,128]{3,2,1,0:T(8,128)S(1)}, u32[]{:S(2)}, u32[]{:S(2)}) collective-permute-start(f32[12,4,32,128]{3,2,1,0:T(8,128)S(1)} %get-tuple-element.22), channel_id=1, source_target_pairs={{16,0},{32,16},{48,32},{64,48},{80,64},{96,80},{112,96},{0,112},{1... | collective-permute-start | bytes 2359304 | tf_op jit(solution)/shard_map/ppermute | solution.py:23
  41.4 12.6 %collective-permute-start.5 = (f32[12,4,32,128]{3,2,1,0:T(8,128)S(1)}, f32[12,4,32,128]{3,2,1,0:T(8,128)S(1)}, u32[]{:S(2)}, u32[]{:S(2)}) collective-permute-start(f32[12,4,32,128]{3,2,1,0:T(8,128)S(1)} %fusion.64), channel_id=1, source_target_pairs={{0,16},{16,32},{32,48},{48,64},{64,80},{80,96},{96,112},{112,0},{1... | collective-permute-start | bytes 2359304 | tf_op jit(solution)/shard_map/ppermute | solution.py:22
  41.4 12.6 %collective-permute-start.4 = (f32[12,4,32,128]{3,2,1,0:T(8,128)S(1)}, f32[12,4,32,128]{3,2,1,0:T(8,128)S(1)}, u32[]{:S(2)}, u32[]{:S(2)}) collective-permute-start(f32[12,4,32,128]{3,2,1,0:T(8,128)S(1)} %fusion.64), channel_id=1, source_target_pairs={{16,0},{32,16},{48,32},{64,48},{80,64},{96,80},{112,96},{0,112},{1... | collective-permute-start | bytes 2359304 | tf_op jit(solution)/shard_map/ppermute | solution.py:23
  58.2 12.7 %collective-permute-start.7 = (f32[12,4,32,128]{3,2,1,0:T(8,128)S(1)}, f32[12,4,32,128]{3,2,1,0:T(8,128)S(1)}, u32[]{:S(2)}, u32[]{:S(2)}) collective-permute-start(f32[12,4,32,128]{3,2,1,0:T(8,128)S(1)} %fusion.39), channel_id=1, source_target_pairs={{0,16},{16,32},{32,48},{48,64},{64,80},{80,96},{96,112},{112,0},{1... | collective-permute-start | bytes 2359304 | tf_op jit(solution)/shard_map/ppermute | solution.py:22
  58.2 12.6 %collective-permute-start.6 = (f32[12,4,32,128]{3,2,1,0:T(8,128)S(1)}, f32[12,4,32,128]{3,2,1,0:T(8,128)S(1)}, u32[]{:S(2)}, u32[]{:S(2)}) collective-permute-start(f32[12,4,32,128]{3,2,1,0:T(8,128)S(1)} %fusion.39), channel_id=1, source_target_pairs={{16,0},{32,16},{48,32},{64,48},{80,64},{96,80},{112,96},{0,112},{1... | collective-permute-start | bytes 2359304 | tf_op jit(solution)/shard_map/ppermute | solution.py:23
  75.8 284.6 %all-reduce.5.cloned.1.call-start = ((), (), s32[]{:S(2)}) async-start(), calls=%async_computation | async-start | bytes 393216 | tf_op jit(solution)/shard_map/psum | solution.py:75
  215.3 0.7 copy-start.3
  216.0 335.9 %all-gather.7.cloned.1.call-start = ((), (), s32[]{:S(2)}) async-start(), calls=%async_computation.2 | async-start | bytes 17825792 | tf_op jit(solution)/shard_map/all_gather | solution.py:89
  423.3 13.1 %copy-start.1 = (f32[12,128,128]{2,1,0:T(8,128)}, f32[12,128,128]{2,1,0:T(8,128)S(1)}, u32[]{:S(2)}) copy-start(f32[12,128,128]{2,1,0:T(8,128)S(1)} %slice.1055) | copy-start | bytes 2359300
  423.4 12.6 %collective-permute-start.9 = (f32[12,4,32,128]{3,2,1,0:T(8,128)S(1)}, f32[12,4,32,128]{3,2,1,0:T(8,128)S(1)}, u32[]{:S(2)}, u32[]{:S(2)}) collective-permute-start(f32[12,4,32,128]{3,2,1,0:T(8,128)S(1)} %bitcast.45), channel_id=1, source_target_pairs={{0,16},{16,32},{32,48},{48,64},{64,80},{80,96},{96,112},{112,0},{1... | collective-permute-start | bytes 2359304 | tf_op jit(solution)/shard_map/ppermute | solution.py:22
  423.4 12.9 %collective-permute-start.8 = (f32[12,4,32,128]{3,2,1,0:T(8,128)S(1)}, f32[12,4,32,128]{3,2,1,0:T(8,128)S(1)}, u32[]{:S(2)}, u32[]{:S(2)}) collective-permute-start(f32[12,4,32,128]{3,2,1,0:T(8,128)S(1)} %bitcast.46), channel_id=1, source_target_pairs={{16,0},{32,16},{48,32},{64,48},{80,64},{96,80},{112,96},{0,112},{1... | collective-permute-start | bytes 2359304 | tf_op jit(solution)/shard_map/ppermute | solution.py:23
Sparse Core Ops, SparseCore 0:
  75.9 113.8 all-gather.4
  216.1 144.2 all-reduce.4
  441.5 110.3 all-gather.6
where the time goes:
time: 614 us; the launch traced here: 610 us
  waiting for transfers between devices  396 us (64%)
  other arithmetic  70.9 us (12%)
  local copies, waits for them, and re-layouts  50.3 us (8%)
  matrix products  36.1 us (6%)
  blocking collectives  25.4 us (4%)
  between operations  16.5 us (3%)
  starting transfers between devices  15.2 us (2%)
    psum x1, waiting for transfers between devices, local(): correlation = lax.psum(over_part, ('dom', 'band'))  144 us
    all_gather x1, waiting for transfers between devices, local(): lax.all_gather(flat, 'band', axis=0, tiled=True)  113 us
    all_gather x1, waiting for transfers between devices, local(): lax.all_gather(applied, 'band', axis=0, tiled=True)  111 us
    unnamed x20, local copies, waits for them, and re-layouts  30 us
    another operation x7, other arithmetic, local(): lower = jnp.linalg.cholesky(correlation / ncells)  28.7 us
    ppermute x5, waiting for transfers between devices, extended(): before = lax.ppermute(last, axis, up)  28.2 us
    dot_general x2, matrix products, inner(): lax.dot_general(left, right, (((1,), (1,)), ((), ())), precision=lax.Prec...  25.7 us
    psum x1, blocking collectives, local(): projected = lax.psum(rows_part, 'dom') / ncells  25.4 us
  transfers between devices with their start and end apart: 13, of which 8 were waited for; matrix products, arithmetic and copies ran while one was open for 3% of the time, Pallas kernels for 0%

commit v1 on v0

--- a/solution.py
+++ b/solution.py
@@ -25,11 +25,11 @@
     return array
 
 
-def inner(left, right):
+def hp_dot(left, right, dims):
     return lax.dot_general(
         left,
         right,
-        (((1,), (1,)), ((), ())),
+        (dims, ((), ())),
         precision=lax.Precision.HIGHEST,
         preferred_element_type=jnp.float32,
     )
@@ -49,6 +49,17 @@
     return potential[None] * field - 0.5 * laplace
 
 
+def butterfly_sum(x, axes):
+    for axis in axes:
+        count = lax.axis_size(axis)
+        step = 1
+        while step < count:
+            pairs = [(i, i ^ step) for i in range(count)]
+            x = x + lax.ppermute(x, axis, pairs)
+            step *= 2
+    return x
+
+
 def local(psi, potential):
     bdev = psi.shape[0]
     depth, rows_y, rows_x = (psi.shape[1], psi.shape[2], psi.shape[3])
@@ -65,29 +76,26 @@
     for order in range(1, DEGREE):
         following = 2.0 / half * (apply(current) - center * current) - previous
         previous, current = (current, following)
-    flat = current.reshape(bdev, -1)
-    square = jnp.zeros((nbands, nbands), jnp.float32)
-    over_part = lax.dynamic_update_slice(
-        square,
-        inner(flat, lax.all_gather(flat, "band", axis=0, tiled=True)),
-        (own_start, jnp.int32(0)),
+    image = apply(current)
+    pair = jnp.stack([current.reshape(bdev, -1), image.reshape(bdev, -1)])
+    spread = lax.all_to_all(pair, "band", 2, 1, tiled=True)
+    flat_cd, image_cd = spread[0], spread[1]
+    sums = jnp.stack(
+        [
+            hp_dot(flat_cd, flat_cd, ((1,), (1,))),
+            hp_dot(flat_cd, image_cd, ((1,), (1,))),
+        ]
     )
-    correlation = lax.psum(over_part, ("dom", "band"))
-    lower = jnp.linalg.cholesky(correlation / ncells)
+    sums = butterfly_sum(sums, ("dom", "band")) / ncells
+    correlation, gram = sums[0], sums[1]
+    lower = jnp.linalg.cholesky(correlation)
     inverse = jax.scipy.linalg.solve_triangular(
         lower, jnp.eye(nbands, dtype=jnp.float32), lower=True
     )
+    basis_cd = hp_dot(inverse, flat_cd, ((1,), (0,)))
+    basis = lax.all_to_all(basis_cd, "band", 0, 1, tiled=True).reshape(psi.shape)
     own_rows = lax.dynamic_slice_in_dim(inverse, own_start, bdev, 0)
-    basis_flat = jnp.dot(
-        own_rows,
-        lax.all_gather(flat, "band", axis=0, tiled=True),
-        precision=lax.Precision.HIGHEST,
-        preferred_element_type=jnp.float32,
-    )
-    basis = basis_flat.reshape(psi.shape)
-    applied = apply(basis).reshape(bdev, -1)
-    rows_part = inner(basis_flat, lax.all_gather(applied, "band", axis=0, tiled=True))
-    projected = lax.psum(rows_part, "dom") / ncells
+    projected = hp_dot(hp_dot(own_rows, gram, ((1,), (0,))), inverse, ((1,), (1,)))
     return (basis, projected)
 
 

time: 614 us -> 385 us (0.63)
  waiting for transfers between devices: 396 us -> 126 us
  local copies, waits for them, and re-layouts: 50.3 us -> 128 us
  matrix products: 36.1 us -> 6.12 us
  between operations: 16.5 us -> 3.17 us
  other arithmetic: 70.9 us -> 77.3 us
    all_gather x2 -> x0, waiting for transfers between devices: 224 us -> none  [the longest x1 113 us: local(): lax.all_gather(flat, 'band', axis=0, tiled=True)]
    psum x1 -> x0, waiting for transfers between devices: 144 us -> none  [local(): correlation = lax.psum(over_part, ('dom', 'band'))]
    ppermute x0 -> x7, waiting for transfers between devices: none -> 62.3 us  [butterfly_sum(): x = x + lax.ppermute(x, axis, pairs)]
    ppermute x5, waiting for transfers between devices: 0.01 us -> 33.9 us  [extended(): after = lax.ppermute(initial, axis, down)]
    unnamed x20 -> x28, local copies, waits for them, and re-layouts: 30 us -> 62.8 us
    dot_general x3 -> x5, matrix products: 34.8 us -> 4.81 us  [hp_dot(): lax.dot_general(left, right, (dims, ((), ())), precision=lax.Precision.HI...]
    all_to_all x0 -> x1, blocking collectives: none -> 28.9 us  [local(): spread = lax.all_to_all(pair, 'band', 2, 1, tiled=True)]
    psum x1 -> x0, blocking collectives: 25.4 us -> none  [local(): projected = lax.psum(rows_part, 'dom') / ncells]
  transfers between devices with their start and end apart: 13 -> 18, of which waited for: 8 -> 17; matrix products, arithmetic and copies ran while one was open for 3% -> 2% of each run, Pallas kernels for 0% -> 0%
where the time goes in v1:
time: 385 us; the launch traced here: 381 us
  local copies, waits for them, and re-layouts  128 us (33%)
  waiting for transfers between devices  126 us (33%)
  other arithmetic  77.3 us (20%)
  blocking collectives  28.9 us (8%)
  starting transfers between devices  12.2 us (3%)
  matrix products  6.12 us (2%)
    unnamed x28, local copies, waits for them, and re-layouts  62.8 us
    ppermute x7, waiting for transfers between devices, butterfly_sum(): x = x + lax.ppermute(x, axis, pairs)  62.3 us
    ppermute x5, waiting for transfers between devices, extended(): after = lax.ppermute(initial, axis, down)  33.9 us
    all_to_all x1, blocking collectives, local(): spread = lax.all_to_all(pair, 'band', 2, 1, tiled=True)  28.9 us
    another operation x7, other arithmetic, local(): lower = jnp.linalg.cholesky(correlation)  28.7 us
    another operation x7, other arithmetic, local(): jax.scipy.linalg.solve_triangular(lower, jnp.eye(nbands, dtype=jnp.float3...  19.8 us
    slice x40, local copies, waits for them, and re-layouts, hamiltonian(): near = near + jnp.roll(field, reach, 3) + jnp.roll(field, -reach, 3)  19.8 us
    ppermute x5, waiting for transfers between devices, extended(): before = lax.ppermute(last, axis, up)  17.2 us
  transfers between devices with their start and end apart: 18, of which 17 were waited for; matrix products, arithmetic and copies ran while one was open for 2% of the time, Pallas kernels for 0%

profile of v1, /device:TPU:0, one launch (start us, length us, event | category | flops | bytes accessed | tf_op | source)
XLA Modules:
  0.0 381.3 jit_solution(17342354009668051355)
XLA Ops:
  8.9 4.6 %collective-permute-done.1 = f32[12,4,32,128]{3,2,1,0:T(8,128)S(1)} collective-permute-done((f32[12,4,32,128]{3,2,1,0:T(8,128)}, f32[12,4,32,128]{3,2,1,0:T(8,128)S(1)}, u32[]{:S(2)}, u32[]{:S(2)}) %collective-permute-start.1) | collective-permute-done | bytes 786464 | tf_op jit(solution)/shard_map/ppermute | solution.py:22
  13.8 4.2 %broadcast_multiply_fusion = (f32[12,4,32,128]{3,2,1,0:T(8,128)S(1)}, f32[12,4,32,128]{3,2,1,0:T(8,128)S(1)}) fusion(f32[12,4,32,128]{3,2,1,0:T(8,128)S(1)} %copy-done, f32[12,4,32,4]{3,2,1,0:T(8,128)S(1)} %get-tuple-element.185, f32[12,4,32,124]{3,2,1,0:T(8,128)S(1)} %get-tuple-element.187, f32[12,4,32,124]{3,2,1,0:T(8,128)S(1)} %get-tuple-element.186, ...), kind=kLoop, calls=%fused_computation.218 | loop fusion | flops 10027008 | bytes 21299200 | tf_op jit(solution)/shard_map/div | solution.py:75
  24.0 9.0 %collective-permute-done.2 = f32[12,4,32,128]{3,2,1,0:T(8,128)S(1)} collective-permute-done((f32[12,4,32,128]{3,2,1,0:T(8,128)S(1)}, f32[12,4,32,128]{3,2,1,0:T(8,128)S(1)}, u32[]{:S(2)}, u32[]{:S(2)}) %collective-permute-start.2) | collective-permute-done | bytes 786464 | tf_op jit(solution)/shard_map/ppermute | solution.py:23
  33.0 3.1 collective-permute-done.3
  36.1 3.8 fusion.86
  43.7 8.4 %collective-permute-done.4 = f32[12,4,32,128]{3,2,1,0:T(8,128)S(1)} collective-permute-done((f32[12,4,32,128]{3,2,1,0:T(8,128)S(1)}, f32[12,4,32,128]{3,2,1,0:T(8,128)S(1)}, u32[]{:S(2)}, u32[]{:S(2)}) %collective-permute-start.4) | collective-permute-done | bytes 786464 | tf_op jit(solution)/shard_map/ppermute | solution.py:23
  52.0 3.1 collective-permute-done.5
  55.2 4.0 %fusion.61 = f32[12,4,32,128]{3,2,1,0:T(8,128)S(1)} fusion(f32[12,4,32,128]{3,2,1,0:T(8,128)S(1)} %collective-permute-done.5, f32[12,4,32,128]{3,2,1,0:T(8,128)S(1)} %fusion.86, f32[12,4,32,128]{3,2,1,0:T(8,128)S(1)} %collective-permute-done.4, f32[12,4,31,128]{3,2,1,0:T(8,128)S(1)} %get-tuple-element.119, f32[12,4,1,128]{3,2,1,0:T(1,128)S(1)} %get-tuple-element.121, ...), kind=kLoop, calls=%fused_computation.98 | loop fusion | flops 11599872 | bytes 16580608 | tf_op jit(solution)/shard_map/sub | solution.py:77
  62.9 8.4 %collective-permute-done.6 = f32[12,4,32,128]{3,2,1,0:T(8,128)S(1)} collective-permute-done((f32[12,4,32,128]{3,2,1,0:T(8,128)S(1)}, f32[12,4,32,128]{3,2,1,0:T(8,128)S(1)}, u32[]{:S(2)}, u32[]{:S(2)}) %collective-permute-start.6) | collective-permute-done | bytes 786464 | tf_op jit(solution)/shard_map/ppermute | solution.py:23
  71.3 3.1 collective-permute-done.7
  74.4 3.8 fusion.36
  93.6 8.1 %collective-permute-done.8 = f32[12,4,32,128]{3,2,1,0:T(8,128)S(1)} collective-permute-done((f32[12,4,32,128]{3,2,1,0:T(8,128)S(1)}, f32[12,4,32,128]{3,2,1,0:T(8,128)S(1)}, u32[]{:S(2)}, u32[]{:S(2)}) %collective-permute-start.8) | collective-permute-done | bytes 786464 | tf_op jit(solution)/shard_map/ppermute | solution.py:23
  101.7 3.2 collective-permute-done.9
  105.0 6.8 %fusion.11 = f32[12,4,32,128]{3,2,1,0:T(8,128)S(1)} fusion(f32[12,4,32,128]{3,2,1,0:T(8,128)} %collective-permute-done.9, f32[12,4,32,128]{3,2,1,0:T(8,128)S(1)} %fusion.36, f32[12,4,32,128]{3,2,1,0:T(8,128)} %copy-done.11, f32[12,4,31,128]{3,2,1,0:T(8,128)S(1)} %get-tuple-element.55, f32[12,4,1,128]{3,2,1,0:T(1,128)S(1)} %get-tuple-element.57, ...), kind=kLoop, calls=%fused_computation.48 | loop fusion | flops 10616832 | bytes 15794176 | tf_op jit(solution)/shard_map/sub | solution.py:49
  114.3 15.1 %copy.29 = f32[2,12,16384]{1,0,2:T(2,128)} copy(f32[2,12,16384]{2,1,0:T(8,128)S(1)} %pad_maximum_fusion) | data formatting | bytes 3145728 | tf_op jit(solution)/shard_map/stack | solution.py:80
  129.5 28.6 %reshape.72 = f32[16,1,24576]{2,1,0:T(1,128)S(1)} reshape(f32[16384,2,12]{2,1,0:T(2,128)} %bitcast.51) | data formatting | bytes 3145728
  158.1 28.9 %all_to_all.28 = f32[16,1,24576]{2,1,0:T(1,128)S(1)} all-to-all(f32[16,1,24576]{2,1,0:T(1,128)S(1)} %reshape.72), channel_id=1, replica_groups=mesh['dom'=8,'band'=16] {'band'}, dimensions={0} | all-to-all | bytes 3145728 | tf_op jit(solution)/shard_map/all_to_all | solution.py:81
  187.5 4.4 %reduce.12 = f32[16,24576]{1,0:T(8,128)S(1)} reduce(f32[16,1,24576]{2,1,0:T(1,128)S(1)} %all_to_all.28, f32[]{:T(128)} %broadcast.227), dimensions={1}, to_apply=%all_to_all.21.reduce_sub_computation | reduce | bytes 3145732 | tf_op jit(solution)/shard_map/all_to_all | solution.py:81
  191.9 33.1 %reshape.73 = f32[16384,2,12]{2,1,0:T(2,128)} reshape(f32[16,24576]{1,0:T(8,128)S(1)} %reduce.12) | data formatting | bytes 3145728
  225.0 13.6 %copy.46 = f32[2,12,16,1024]{3,2,0,1:T(8,128)S(1)} copy(f32[2,12,16,1024]{1,0,3,2:T(2,128)} %bitcast.52) | data formatting | bytes 3145728 | tf_op jit(solution)/shard_map/all_to_all | solution.py:81
  246.8 11.1 %collective-permute-done.11 = f32[2,192,192]{1,2,0:T(8,128)S(1)} collective-permute-done((f32[2,192,192]{1,2,0:T(8,128)S(1)}, f32[2,192,192]{1,2,0:T(8,128)S(1)}, u32[]{:S(2)}, u32[]{:S(2)}) %collective-permute-start.11) | collective-permute-done | bytes 294944 | tf_op jit(solution)/shard_map/ppermute | solution.py:58
  258.1 11.8 %collective-permute-done.12 = f32[2,192,192]{1,2,0:T(8,128)S(1)} collective-permute-done((f32[2,192,192]{1,2,0:T(8,128)S(1)}, f32[2,192,192]{1,2,0:T(8,128)S(1)}, u32[]{:S(2)}, u32[]{:S(2)}) %collective-permute-start.12) | collective-permute-done | bytes 294944 | tf_op jit(solution)/shard_map/ppermute | solution.py:58
  270.6 9.4 %collective-permute-done.13 = f32[2,192,192]{1,2,0:T(8,128)S(1)} collective-permute-done((f32[2,192,192]{1,2,0:T(8,128)S(1)}, f32[2,192,192]{1,2,0:T(8,128)S(1)}, u32[]{:S(2)}, u32[]{:S(2)}) %collective-permute-start.13) | collective-permute-done | bytes 294944 | tf_op jit(solution)/shard_map/ppermute | solution.py:58
  280.3 9.4 %collective-permute-done.14 = f32[2,192,192]{1,2,0:T(8,128)S(1)} collective-permute-done((f32[2,192,192]{1,2,0:T(8,128)S(1)}, f32[2,192,192]{1,2,0:T(8,128)S(1)}, u32[]{:S(2)}, u32[]{:S(2)}) %collective-permute-start.14) | collective-permute-done | bytes 294944 | tf_op jit(solution)/shard_map/ppermute | solution.py:58
  289.8 9.8 %collective-permute-done.15 = f32[2,192,192]{1,2,0:T(8,128)S(1)} collective-permute-done((f32[2,192,192]{1,2,0:T(8,128)S(1)}, f32[2,192,192]{1,2,0:T(8,128)S(1)}, u32[]{:S(2)}, u32[]{:S(2)}) %collective-permute-start.15) | collective-permute-done | bytes 294944 | tf_op jit(solution)/shard_map/ppermute | solution.py:58
  299.9 9.1 %collective-permute-done.16 = f32[2,192,192]{1,2,0:T(8,128)S(1)} collective-permute-done((f32[2,192,192]{1,2,0:T(8,128)S(1)}, f32[2,192,192]{1,2,0:T(8,128)S(1)}, u32[]{:S(2)}, u32[]{:S(2)}) %collective-permute-start.16) | collective-permute-done | bytes 294944 | tf_op jit(solution)/shard_map/ppermute | solution.py:58
  309.3 11.7 %cholesky.51 = f32[128,128]{1,0:T(8,128)S(1)} custom-call(f32[128,128]{1,0:T(8,128)S(1)} %cholesky.124), custom_call_target="Cholesky" | custom-call | tf_op jit(solution)/shard_map/jit(cholesky)/cholesky | solution.py:91
  321.1 9.8 %custom-call.15 = f32[1,128,128]{1,2,0:T(8,128)S(1)} custom-call(f32[1,128,128]{2,1,0:T(8,128)S(1)} %get-tuple-element.189), custom_call_target="InvertDiagBlocksLowerTriangular" | custom-call | tf_op jit(solution)/shard_map/jit(cholesky)/cholesky | solution.py:91
  331.3 5.8 %cholesky.110 = f32[64,64]{1,0:T(8,128)S(1)} custom-call(f32[64,64]{1,0:T(8,128)S(1)} %convolution_subtract_fusion.1), custom_call_target="Cholesky" | custom-call | tf_op jit(solution)/shard_map/jit(cholesky)/cholesky | solution.py:91
  339.9 19.7 %custom-call.16 = f32[2,128,128]{1,2,0:T(8,128)S(1)} custom-call(f32[2,128,128]{2,1,0:T(8,128)S(1)} %pad_maximum_fusion.11), custom_call_target="InvertDiagBlocksLowerTriangular" | custom-call | tf_op jit(solution)/shard_map/jit(_solve_triangular)/triangular_solve | solution.py:92
  362.7 3.7 all-to-all-start.1
  367.6 12.1 %all-to-all-done.1 = f32[16,12,1024]{2,1,0:T(8,128)S(1)} async-done(((f32[16,12,1024]{2,1,0:T(8,128)}), f32[16,12,1024]{2,1,0:T(8,128)S(1)}, u32[]{:S(2)}, u32[]{:S(2)}) %all-to-all-start.1) | async-done | bytes 786464 | tf_op jit(solution)/shard_map/all_to_all | solution.py:96
  (176 shorter events, 57.3 us)
Async XLA Ops:
  0.6 4.6 %copy-start = (f32[12,4,32,128]{3,2,1,0:T(8,128)S(1)}, f32[12,4,32,128]{3,2,1,0:T(8,128)}, u32[]{:S(2)}) copy-start(f32[12,4,32,128]{3,2,1,0:T(8,128)} %param.2) | copy-start | bytes 2359300
  0.6 12.8 %collective-permute-start.1 = (f32[12,4,32,128]{3,2,1,0:T(8,128)}, f32[12,4,32,128]{3,2,1,0:T(8,128)S(1)}, u32[]{:S(2)}, u32[]{:S(2)}) collective-permute-start(f32[12,4,32,128]{3,2,1,0:T(8,128)} %param.2), channel_id=1, source_target_pairs={{0,16},{16,32},{32,48},{48,64},{64,80},{80,96},{96,112},{112,0},{1... | collective-permute-start | bytes 2359304 | tf_op jit(solution)/shard_map/ppermute | solution.py:22
  0.7 13.1 %collective-permute-start = (f32[12,4,32,128]{3,2,1,0:T(8,128)}, f32[12,4,32,128]{3,2,1,0:T(8,128)S(1)}, u32[]{:S(2)}, u32[]{:S(2)}) collective-permute-start(f32[12,4,32,128]{3,2,1,0:T(8,128)} %param.2), channel_id=1, source_target_pairs={{16,0},{32,16},{48,32},{64,48},{80,64},{96,80},{112,96},{0,112},{1... | collective-permute-start | bytes 2359304 | tf_op jit(solution)/shard_map/ppermute | solution.py:23
  7.7 0.8 copy-start.10
  20.8 12.2 %collective-permute-start.2 = (f32[12,4,32,128]{3,2,1,0:T(8,128)S(1)}, f32[12,4,32,128]{3,2,1,0:T(8,128)S(1)}, u32[]{:S(2)}, u32[]{:S(2)}) collective-permute-start(f32[12,4,32,128]{3,2,1,0:T(8,128)S(1)} %get-tuple-element.22), channel_id=1, source_target_pairs={{16,0},{32,16},{48,32},{64,48},{80,64},{96,80},{112,96},{0,112},{1... | collective-permute-start | bytes 2359304 | tf_op jit(solution)/shard_map/ppermute | solution.py:23
  23.5 12.6 %collective-permute-start.3 = (f32[12,4,32,128]{3,2,1,0:T(8,128)S(1)}, f32[12,4,32,128]{3,2,1,0:T(8,128)S(1)}, u32[]{:S(2)}, u32[]{:S(2)}) collective-permute-start(f32[12,4,32,128]{3,2,1,0:T(8,128)S(1)} %get-tuple-element.22), channel_id=1, source_target_pairs={{0,16},{16,32},{32,48},{48,64},{64,80},{80,96},{96,112},{112,0},{1... | collective-permute-start | bytes 2359304 | tf_op jit(solution)/shard_map/ppermute | solution.py:22
  42.5 9.5 %collective-permute-start.4 = (f32[12,4,32,128]{3,2,1,0:T(8,128)S(1)}, f32[12,4,32,128]{3,2,1,0:T(8,128)S(1)}, u32[]{:S(2)}, u32[]{:S(2)}) collective-permute-start(f32[12,4,32,128]{3,2,1,0:T(8,128)S(1)} %fusion.86), channel_id=1, source_target_pairs={{16,0},{32,16},{48,32},{64,48},{80,64},{96,80},{112,96},{0,112},{1... | collective-permute-start | bytes 2359304 | tf_op jit(solution)/shard_map/ppermute | solution.py:23
  42.5 12.6 %collective-permute-start.5 = (f32[12,4,32,128]{3,2,1,0:T(8,128)S(1)}, f32[12,4,32,128]{3,2,1,0:T(8,128)S(1)}, u32[]{:S(2)}, u32[]{:S(2)}) collective-permute-start(f32[12,4,32,128]{3,2,1,0:T(8,128)S(1)} %fusion.86), channel_id=1, source_target_pairs={{0,16},{16,32},{32,48},{48,64},{64,80},{80,96},{96,112},{112,0},{1... | collective-permute-start | bytes 2359304 | tf_op jit(solution)/shard_map/ppermute | solution.py:22
  61.8 9.5 %collective-permute-start.6 = (f32[12,4,32,128]{3,2,1,0:T(8,128)S(1)}, f32[12,4,32,128]{3,2,1,0:T(8,128)S(1)}, u32[]{:S(2)}, u32[]{:S(2)}) collective-permute-start(f32[12,4,32,128]{3,2,1,0:T(8,128)S(1)} %fusion.61), channel_id=1, source_target_pairs={{16,0},{32,16},{48,32},{64,48},{80,64},{96,80},{112,96},{0,112},{1... | collective-permute-start | bytes 2359304 | tf_op jit(solution)/shard_map/ppermute | solution.py:23
  61.8 12.6 %collective-permute-start.7 = (f32[12,4,32,128]{3,2,1,0:T(8,128)S(1)}, f32[12,4,32,128]{3,2,1,0:T(8,128)S(1)}, u32[]{:S(2)}, u32[]{:S(2)}) collective-permute-start(f32[12,4,32,128]{3,2,1,0:T(8,128)S(1)} %fusion.61), channel_id=1, source_target_pairs={{0,16},{16,32},{32,48},{48,64},{64,80},{80,96},{96,112},{112,0},{1... | collective-permute-start | bytes 2359304 | tf_op jit(solution)/shard_map/ppermute | solution.py:22
  92.2 9.5 %collective-permute-start.8 = (f32[12,4,32,128]{3,2,1,0:T(8,128)S(1)}, f32[12,4,32,128]{3,2,1,0:T(8,128)S(1)}, u32[]{:S(2)}, u32[]{:S(2)}) collective-permute-start(f32[12,4,32,128]{3,2,1,0:T(8,128)S(1)} %fusion.36), channel_id=1, source_target_pairs={{16,0},{32,16},{48,32},{64,48},{80,64},{96,80},{112,96},{0,112},{1... | collective-permute-start | bytes 2359304 | tf_op jit(solution)/shard_map/ppermute | solution.py:23
  92.2 12.7 %collective-permute-start.9 = (f32[12,4,32,128]{3,2,1,0:T(8,128)S(1)}, f32[12,4,32,128]{3,2,1,0:T(8,128)}, u32[]{:S(2)}, u32[]{:S(2)}) collective-permute-start(f32[12,4,32,128]{3,2,1,0:T(8,128)S(1)} %fusion.36), channel_id=1, source_target_pairs={{0,16},{16,32},{32,48},{48,64},{64,80},{80,96},{96,112},{112,0},{1... | collective-permute-start | bytes 2359304 | tf_op jit(solution)/shard_map/ppermute | solution.py:22
  93.1 11.9 %copy-start.5 = (f32[12,4,28,128]{3,2,1,0:T(8,128)S(1)}, f32[12,4,28,128]{3,2,1,0:T(8,128)}, u32[]{:S(2)}) copy-start(f32[12,4,28,128]{3,2,1,0:T(8,128)} %get-tuple-element.30) | copy-start | bytes 2064388
  93.1 11.9 %copy-start.6 = (f32[12,4,28,128]{3,2,1,0:T(8,128)S(1)}, f32[12,4,28,128]{3,2,1,0:T(8,128)}, u32[]{:S(2)}) copy-start(f32[12,4,28,128]{3,2,1,0:T(8,128)} %get-tuple-element.31) | copy-start | bytes 2064388
  93.1 11.9 %copy-start.7 = (f32[12,4,32,125]{3,2,1,0:T(8,128)S(1)}, f32[12,4,32,125]{3,2,1,0:T(8,128)}, u32[]{:S(2)}) copy-start(f32[12,4,32,125]{3,2,1,0:T(8,128)} %get-tuple-element.34) | copy-start | bytes 2304004
  93.1 11.9 %copy-start.8 = (f32[12,4,32,125]{3,2,1,0:T(8,128)S(1)}, f32[12,4,32,125]{3,2,1,0:T(8,128)}, u32[]{:S(2)}) copy-start(f32[12,4,32,125]{3,2,1,0:T(8,128)} %get-tuple-element.35) | copy-start | bytes 2304004
  93.4 11.6 %copy-start.1 = (f32[12,4,32,124]{3,2,1,0:T(8,128)S(1)}, f32[12,4,32,124]{3,2,1,0:T(8,128)}, u32[]{:S(2)}) copy-start(f32[12,4,32,124]{3,2,1,0:T(8,128)} %get-tuple-element.26) | copy-start | bytes 2285572
  93.4 11.6 %copy-start.2 = (f32[12,4,32,124]{3,2,1,0:T(8,128)S(1)}, f32[12,4,32,124]{3,2,1,0:T(8,128)}, u32[]{:S(2)}) copy-start(f32[12,4,32,124]{3,2,1,0:T(8,128)} %get-tuple-element.27) | copy-start | bytes 2285572
  93.4 11.6 %copy-start.3 = (f32[12,4,32,4]{3,2,1,0:T(8,128)S(1)}, f32[12,4,32,4]{3,2,1,0:T(8,128)}, u32[]{:S(2)}) copy-start(f32[12,4,32,4]{3,2,1,0:T(8,128)} %get-tuple-element.28) | copy-start | bytes 73732
  93.4 11.6 %copy-start.4 = (f32[12,4,32,4]{3,2,1,0:T(8,128)S(1)}, f32[12,4,32,4]{3,2,1,0:T(8,128)}, u32[]{:S(2)}) copy-start(f32[12,4,32,4]{3,2,1,0:T(8,128)} %get-tuple-element.29) | copy-start | bytes 73732
  101.7 3.2 copy-start.11
  242.8 1.1 copy-start.9
  244.8 1.8 collective-permute-start.10
  246.7 11.2 %collective-permute-start.11 = (f32[2,192,192]{1,2,0:T(8,128)S(1)}, f32[2,192,192]{1,2,0:T(8,128)S(1)}, u32[]{:S(2)}, u32[]{:S(2)}) collective-permute-start(f32[2,192,192]{1,2,0:T(8,128)S(1)} %fusion.178), channel_id=1, source_target_pairs={{0,32},{16,48},{32,0},{48,16},{64,96},{80,112},{96,64},{112,80},{1... | collective-permute-start | bytes 884744 | tf_op jit(solution)/shard_map/ppermute | solution.py:58
  258.0 11.9 %collective-permute-start.12 = (f32[2,192,192]{1,2,0:T(8,128)S(1)}, f32[2,192,192]{1,2,0:T(8,128)S(1)}, u32[]{:S(2)}, u32[]{:S(2)}) collective-permute-start(f32[2,192,192]{1,2,0:T(8,128)S(1)} %fusion.273), channel_id=1, source_target_pairs={{0,64},{16,80},{32,96},{48,112},{64,0},{80,16},{96,32},{112,48},{1... | collective-permute-start | bytes 884744 | tf_op jit(solution)/shard_map/ppermute | solution.py:58
  269.9 10.0 %collective-permute-start.13 = (f32[2,192,192]{1,2,0:T(8,128)S(1)}, f32[2,192,192]{1,2,0:T(8,128)S(1)}, u32[]{:S(2)}, u32[]{:S(2)}) collective-permute-start(f32[2,192,192]{1,2,0:T(8,128)S(1)} %add.531), channel_id=1, source_target_pairs={{0,1},{1,0},{2,3},{3,2},{4,5},{5,4},{6,7},{7,6},{8,9},{9,8},{10,11... | collective-permute-start | bytes 884744 | tf_op jit(solution)/shard_map/ppermute | solution.py:58
  280.0 9.7 %collective-permute-start.14 = (f32[2,192,192]{1,2,0:T(8,128)S(1)}, f32[2,192,192]{1,2,0:T(8,128)S(1)}, u32[]{:S(2)}, u32[]{:S(2)}) collective-permute-start(f32[2,192,192]{1,2,0:T(8,128)S(1)} %add.532), channel_id=1, source_target_pairs={{0,2},{1,3},{2,0},{3,1},{4,6},{5,7},{6,4},{7,5},{8,10},{9,11},{10,... | collective-permute-start | bytes 884744 | tf_op jit(solution)/shard_map/ppermute | solution.py:58
  289.7 9.9 %collective-permute-start.15 = (f32[2,192,192]{1,2,0:T(8,128)S(1)}, f32[2,192,192]{1,2,0:T(8,128)S(1)}, u32[]{:S(2)}, u32[]{:S(2)}) collective-permute-start(f32[2,192,192]{1,2,0:T(8,128)S(1)} %add.533), channel_id=1, source_target_pairs={{0,4},{1,5},{2,6},{3,7},{4,0},{5,1},{6,2},{7,3},{8,12},{9,13},{10,... | collective-permute-start | bytes 884744 | tf_op jit(solution)/shard_map/ppermute | solution.py:58
  299.7 9.4 %collective-permute-start.16 = (f32[2,192,192]{1,2,0:T(8,128)S(1)}, f32[2,192,192]{1,2,0:T(8,128)S(1)}, u32[]{:S(2)}, u32[]{:S(2)}) collective-permute-start(f32[2,192,192]{1,2,0:T(8,128)S(1)} %add.534), channel_id=1, source_target_pairs={{0,8},{1,9},{2,10},{3,11},{4,12},{5,13},{6,14},{7,15},{8,0},{9,1},... | collective-permute-start | bytes 884744 | tf_op jit(solution)/shard_map/ppermute | solution.py:58
  362.7 17.0 %all-to-all-start.1 = ((f32[16,12,1024]{2,1,0:T(8,128)}), f32[16,12,1024]{2,1,0:T(8,128)S(1)}, u32[]{:S(2)}, u32[]{:S(2)}) async-start(f32[16,12,1024]{2,1,0:T(8,128)} %fusion.261), calls=%async_computation.1 | async-start | bytes 2097152 | tf_op jit(solution)/shard_map/all_to_all | solution.py:96

commit v2 on v1

--- a/solution.py
+++ b/solution.py
@@ -1,6 +1,8 @@
 import jax
 import jax.numpy as jnp
 from jax import lax
+from jax.experimental import pallas as pl
+from jax.experimental.pallas import tpu as pltpu
 from jax.sharding import PartitionSpec as P
 
 DEGREE = 4
@@ -60,6 +62,49 @@
     return x
 
 
+def gram_kernel(rows, f_ref, h_ref, c_ref, g_ref):
+    nb = c_ref.shape[0]
+    c_ref[...] = jnp.zeros_like(c_ref)
+    g_ref[...] = jnp.zeros_like(g_ref)
+    for r in range(rows):
+        f = f_ref[pl.ds(r, nb, stride=rows), :]
+        h = h_ref[pl.ds(r, nb, stride=rows), :]
+        c_ref[...] += hp_dot(f, f, ((1,), (1,)))
+        g_ref[...] += hp_dot(f, h, ((1,), (1,)))
+
+
+def rotate_kernel(rows, m_ref, f_ref, o_ref):
+    nb = m_ref.shape[0]
+    for r in range(rows):
+        o_ref[pl.ds(r, nb, stride=rows), :] = hp_dot(
+            m_ref[...], f_ref[pl.ds(r, nb, stride=rows), :], ((1,), (0,))
+        )
+
+
+def vspec():
+    return pl.BlockSpec(memory_space=pltpu.VMEM)
+
+
+def grams(rows, f, h):
+    nb = f.shape[0] // rows
+    out = jax.ShapeDtypeStruct((nb, nb), jnp.float32)
+    return pl.pallas_call(
+        lambda *refs: gram_kernel(rows, *refs),
+        out_shape=(out, out),
+        in_specs=[vspec(), vspec()],
+        out_specs=(vspec(), vspec()),
+    )(f, h)
+
+
+def rotate(rows, m, f):
+    return pl.pallas_call(
+        lambda *refs: rotate_kernel(rows, *refs),
+        out_shape=jax.ShapeDtypeStruct(f.shape, jnp.float32),
+        in_specs=[vspec(), vspec()],
+        out_specs=vspec(),
+    )(m, f)
+
+
 def local(psi, potential):
     bdev = psi.shape[0]
     depth, rows_y, rows_x = (psi.shape[1], psi.shape[2], psi.shape[3])
@@ -77,23 +122,29 @@
         following = 2.0 / half * (apply(current) - center * current) - previous
         previous, current = (current, following)
     image = apply(current)
-    pair = jnp.stack([current.reshape(bdev, -1), image.reshape(bdev, -1)])
-    spread = lax.all_to_all(pair, "band", 2, 1, tiled=True)
-    flat_cd, image_cd = spread[0], spread[1]
-    sums = jnp.stack(
-        [
-            hp_dot(flat_cd, flat_cd, ((1,), (1,))),
-            hp_dot(flat_cd, image_cd, ((1,), (1,))),
-        ]
-    )
-    sums = butterfly_sum(sums, ("dom", "band")) / ncells
-    correlation, gram = sums[0], sums[1]
+    groups = lax.axis_size("band")
+    rows = depth * rows_y * rows_x // groups // rows_x
+    lanes = rows_x
+    chunked = jnp.stack([current, image]).reshape(2, bdev, groups, rows, lanes)
+    spread = lax.all_to_all(chunked, "band", 2, 2, tiled=True)
+    flat_cd = spread[0].reshape(bdev * groups * rows, lanes)
+    image_cd = spread[1].reshape(bdev * groups * rows, lanes)
+    c_perm, g_perm = grams(rows, flat_cd, image_cd)
+    sums = butterfly_sum(jnp.stack([c_perm, g_perm]), ("dom", "band")) / ncells
+
+    def to_true(m):
+        return m.reshape(bdev, groups, bdev, groups).transpose(1, 0, 3, 2).reshape(nbands, nbands)
+
+    def to_perm(m):
+        return m.reshape(groups, bdev, groups, bdev).transpose(1, 0, 3, 2).reshape(nbands, nbands)
+
+    correlation, gram = to_true(sums[0]), to_true(sums[1])
     lower = jnp.linalg.cholesky(correlation)
     inverse = jax.scipy.linalg.solve_triangular(
         lower, jnp.eye(nbands, dtype=jnp.float32), lower=True
     )
-    basis_cd = hp_dot(inverse, flat_cd, ((1,), (0,)))
-    basis = lax.all_to_all(basis_cd, "band", 0, 1, tiled=True).reshape(psi.shape)
+    basis_cd = rotate(rows, to_perm(inverse), flat_cd).reshape(bdev, groups, rows, lanes)
+    basis = lax.all_to_all(basis_cd, "band", 1, 1, tiled=True).reshape(psi.shape)
     own_rows = lax.dynamic_slice_in_dim(inverse, own_start, bdev, 0)
     projected = hp_dot(hp_dot(own_rows, gram, ((1,), (0,))), inverse, ((1,), (1,)))
     return (basis, projected)

time: 385 us -> 283 us (0.74)
  local copies, waits for them, and re-layouts: 128 us -> 32.8 us
  Pallas kernels: 0 us -> 8.3 us
  other arithmetic: 77.3 us -> 71.3 us
  waiting for transfers between devices: 126 us -> 120 us
    unnamed x28 -> x12, local copies, waits for them, and re-layouts: 62.8 us -> 0.82 us
    another operation x3, local copies, waits for them, and re-layouts: 16.4 us -> 1.09 us  [the longest x2 0.9 us: to_true(): m.reshape(bdev, groups, bdev, groups).transpose(1, 0, 3, 2)]
    all_to_all x3 -> x1, local copies, waits for them, and re-layouts: 14.6 us -> 2.08 us  [local(): lax.all_to_all(basis_cd, 'band', 1, 1, tiled=True).reshape(psi.shape)]
    pallas_call x0 -> x2, Pallas kernels: none -> 8.3 us  [the longest x1 4.75 us: grams(): pl.pallas_call(lambda *refs: gram_kernel(rows, *refs), out_shape=(out, ou...]
    slice x40, local copies, waits for them, and re-layouts: 19.8 us -> 11.8 us  [hamiltonian(): near = near + jnp.roll(field, reach, 3) + jnp.roll(field, -reach, 3)]
    reshape x1 -> x6, local copies, waits for them, and re-layouts: 1 us -> 5.82 us  [the longest x1 2.09 us: local(): rotate(rows, to_perm(inverse), flat_cd).reshape(bdev, groups, rows, lanes)]
    all_to_all x1 -> x0, other arithmetic: 4.42 us -> none  [local(): spread = lax.all_to_all(pair, 'band', 2, 1, tiled=True)]
    all_to_all x1, waiting for transfers between devices: 12.1 us -> 7.97 us  [local(): lax.all_to_all(basis_cd, 'band', 1, 1, tiled=True).reshape(psi.shape)]
  transfers between devices with their start and end apart: 18 -> 18, of which waited for: 17 -> 17; matrix products, arithmetic and copies ran while one was open for 2% -> 4% of each run, Pallas kernels for 0% -> 0%
where the time goes in v2:
time: 283 us; the launch traced here: 280 us
  waiting for transfers between devices  120 us (42%)
  other arithmetic  71.3 us (25%)
  local copies, waits for them, and re-layouts  32.8 us (12%)
  blocking collectives  27.8 us (10%)
  starting transfers between devices  14.2 us (5%)
  Pallas kernels  8.3 us (3%)
  between operations  3.12 us (1%)
    ppermute x7, waiting for transfers between devices, butterfly_sum(): x = x + lax.ppermute(x, axis, pairs)  60.4 us
    ppermute x5, waiting for transfers between devices, extended(): after = lax.ppermute(initial, axis, down)  34.1 us
    another operation x7, other arithmetic, local(): lower = jnp.linalg.cholesky(correlation)  28.8 us
    all_to_all x1, blocking collectives, local(): spread = lax.all_to_all(chunked, 'band', 2, 2, tiled=True)  27.8 us
    another operation x7, other arithmetic, local(): jax.scipy.linalg.solve_triangular(lower, jnp.eye(nbands, dtype=jnp.float3...  20 us
    ppermute x5, waiting for transfers between devices, extended(): before = lax.ppermute(last, axis, up)  17.1 us
    slice x40, local copies, waits for them, and re-layouts, hamiltonian(): near = near + jnp.roll(field, reach, 3) + jnp.roll(field, -reach, 3)  11.8 us
    sub x3, other arithmetic, local(): following = 2.0 / half * (apply(current) - center * current) - previous  11.6 us
  transfers between devices with their start and end apart: 18, of which 17 were waited for; matrix products, arithmetic and copies ran while one was open for 4% of the time, Pallas kernels for 0%

profile of v2, /device:TPU:0, one launch (start us, length us, event | category | flops | bytes accessed | tf_op | source)
XLA Modules:
  0.0 279.7 jit_solution(5506990399723596586)
XLA Ops:
  0.7 2.9 %collective-permute-start = (f32[12,4,32,128]{3,2,1,0:T(8,128)}, f32[12,4,32,128]{3,2,1,0:T(8,128)S(1)}, u32[]{:S(2)}, u32[]{:S(2)}) collective-permute-start(f32[12,4,32,128]{3,2,1,0:T(8,128)} %param.2), channel_id=1, source_target_pairs={{16,0},{32,16},{48,32},{64,48},{80,64},{96,80},{112,96},{0,112},{1... | collective-permute-start | bytes 2359304 | tf_op jit(solution)/shard_map/ppermute | solution.py:25
  8.9 4.6 %collective-permute-done.1 = f32[12,4,32,128]{3,2,1,0:T(8,128)S(1)} collective-permute-done((f32[12,4,32,128]{3,2,1,0:T(8,128)}, f32[12,4,32,128]{3,2,1,0:T(8,128)S(1)}, u32[]{:S(2)}, u32[]{:S(2)}) %collective-permute-start.1) | collective-permute-done | bytes 786464 | tf_op jit(solution)/shard_map/ppermute | solution.py:24
  13.9 3.9 %broadcast_multiply_fusion = (f32[12,4,32,128]{3,2,1,0:T(8,128)S(1)}, f32[12,4,32,128]{3,2,1,0:T(8,128)S(1)}) fusion(f32[12,4,32,128]{3,2,1,0:T(8,128)S(1)} %copy-done, f32[12,4,32,4]{3,2,1,0:T(8,128)S(1)} %get-tuple-element.189, f32[12,4,32,124]{3,2,1,0:T(8,128)S(1)} %get-tuple-element.191, f32[12,4,32,124]{3,2,1,0:T(8,128)S(1)} %get-tuple-element.190, ...), kind=kLoop, calls=%fused_computation.216 | loop fusion | flops 10027008 | bytes 21299200 | tf_op jit(solution)/shard_map/div | solution.py:120
  20.5 2.7 collective-permute-start.2
  23.7 9.0 %collective-permute-done.2 = f32[12,4,32,128]{3,2,1,0:T(8,128)S(1)} collective-permute-done((f32[12,4,32,128]{3,2,1,0:T(8,128)S(1)}, f32[12,4,32,128]{3,2,1,0:T(8,128)S(1)}, u32[]{:S(2)}, u32[]{:S(2)}) %collective-permute-start.2) | collective-permute-done | bytes 786464 | tf_op jit(solution)/shard_map/ppermute | solution.py:25
  32.7 3.1 %collective-permute-done.3 = f32[12,4,32,128]{3,2,1,0:T(8,128)S(1)} collective-permute-done((f32[12,4,32,128]{3,2,1,0:T(8,128)S(1)}, f32[12,4,32,128]{3,2,1,0:T(8,128)S(1)}, u32[]{:S(2)}, u32[]{:S(2)}) %collective-permute-start.3) | collective-permute-done | bytes 786464 | tf_op jit(solution)/shard_map/ppermute | solution.py:24
  35.8 3.8 %fusion.86 = f32[12,4,32,128]{3,2,1,0:T(8,128)S(1)} fusion(f32[12,4,32,128]{3,2,1,0:T(8,128)S(1)} %copy-done, f32[12,4,32,128]{3,2,1,0:T(8,128)S(1)} %collective-permute-done.3, f32[12,4,32,128]{3,2,1,0:T(8,128)S(1)} %get-tuple-element.26, f32[12,4,32,128]{3,2,1,0:T(8,128)S(1)} %collective-permute-done.2, f32[12,4,31,128]{3,2,1,0:T(8,128)S(1)} %get-tuple-element.155, ...), kind=kLoop, calls=%fused_computation.121 | loop fusion | flops 11403264 | bytes 17367040 | tf_op jit(solution)/shard_map/sub | solution.py:122
  43.4 8.4 %collective-permute-done.4 = f32[12,4,32,128]{3,2,1,0:T(8,128)S(1)} collective-permute-done((f32[12,4,32,128]{3,2,1,0:T(8,128)S(1)}, f32[12,4,32,128]{3,2,1,0:T(8,128)S(1)}, u32[]{:S(2)}, u32[]{:S(2)}) %collective-permute-start.4) | collective-permute-done | bytes 786464 | tf_op jit(solution)/shard_map/ppermute | solution.py:25
  51.7 3.1 %collective-permute-done.5 = f32[12,4,32,128]{3,2,1,0:T(8,128)S(1)} collective-permute-done((f32[12,4,32,128]{3,2,1,0:T(8,128)S(1)}, f32[12,4,32,128]{3,2,1,0:T(8,128)S(1)}, u32[]{:S(2)}, u32[]{:S(2)}) %collective-permute-start.5) | collective-permute-done | bytes 786464 | tf_op jit(solution)/shard_map/ppermute | solution.py:24
  54.9 4.0 %fusion.61 = f32[12,4,32,128]{3,2,1,0:T(8,128)S(1)} fusion(f32[12,4,32,128]{3,2,1,0:T(8,128)S(1)} %collective-permute-done.5, f32[12,4,32,128]{3,2,1,0:T(8,128)S(1)} %fusion.86, f32[12,4,32,128]{3,2,1,0:T(8,128)S(1)} %collective-permute-done.4, f32[12,4,31,128]{3,2,1,0:T(8,128)S(1)} %get-tuple-element.123, f32[12,4,1,128]{3,2,1,0:T(1,128)S(1)} %get-tuple-element.125, ...), kind=kLoop, calls=%fused_computation.96 | loop fusion | flops 11599872 | bytes 16580608 | tf_op jit(solution)/shard_map/sub | solution.py:122
  62.7 8.4 %collective-permute-done.6 = f32[12,4,32,128]{3,2,1,0:T(8,128)S(1)} collective-permute-done((f32[12,4,32,128]{3,2,1,0:T(8,128)S(1)}, f32[12,4,32,128]{3,2,1,0:T(8,128)S(1)}, u32[]{:S(2)}, u32[]{:S(2)}) %collective-permute-start.6) | collective-permute-done | bytes 786464 | tf_op jit(solution)/shard_map/ppermute | solution.py:25
  71.0 3.1 %collective-permute-done.7 = f32[12,4,32,128]{3,2,1,0:T(8,128)S(1)} collective-permute-done((f32[12,4,32,128]{3,2,1,0:T(8,128)S(1)}, f32[12,4,32,128]{3,2,1,0:T(8,128)S(1)}, u32[]{:S(2)}, u32[]{:S(2)}) %collective-permute-start.7) | collective-permute-done | bytes 786464 | tf_op jit(solution)/shard_map/ppermute | solution.py:24
  74.2 3.8 %fusion.36 = f32[12,4,32,128]{3,2,1,0:T(8,128)S(1)} fusion(f32[12,4,32,128]{3,2,1,0:T(8,128)S(1)} %fusion.86, f32[12,4,32,128]{3,2,1,0:T(8,128)S(1)} %collective-permute-done.7, f32[12,4,32,128]{3,2,1,0:T(8,128)S(1)} %fusion.61, f32[12,4,32,128]{3,2,1,0:T(8,128)S(1)} %collective-permute-done.6, f32[12,4,31,128]{3,2,1,0:T(8,128)S(1)} %get-tuple-element.91, ...), kind=kLoop, calls=%fused_computation.71 | loop fusion | flops 11403264 | bytes 16580608 | tf_op jit(solution)/shard_map/sub | solution.py:122
  81.7 8.4 %collective-permute-done.8 = f32[12,4,32,128]{3,2,1,0:T(8,128)S(1)} collective-permute-done((f32[12,4,32,128]{3,2,1,0:T(8,128)S(1)}, f32[12,4,32,128]{3,2,1,0:T(8,128)S(1)}, u32[]{:S(2)}, u32[]{:S(2)}) %collective-permute-start.8) | collective-permute-done | bytes 786464 | tf_op jit(solution)/shard_map/ppermute | solution.py:25
  90.1 3.1 %collective-permute-done.9 = f32[12,4,32,128]{3,2,1,0:T(8,128)S(1)} collective-permute-done((f32[12,4,32,128]{3,2,1,0:T(8,128)S(1)}, f32[12,4,32,128]{3,2,1,0:T(8,128)S(1)}, u32[]{:S(2)}, u32[]{:S(2)}) %collective-permute-start.9) | collective-permute-done | bytes 786464 | tf_op jit(solution)/shard_map/ppermute | solution.py:24
  93.2 3.7 %fusion.11 = f32[12,4,32,128]{3,2,1,0:T(8,128)S(1)} fusion(f32[12,4,32,128]{3,2,1,0:T(8,128)S(1)} %collective-permute-done.9, f32[12,4,32,128]{3,2,1,0:T(8,128)S(1)} %fusion.36, f32[12,4,32,128]{3,2,1,0:T(8,128)S(1)} %collective-permute-done.8, f32[12,4,31,128]{3,2,1,0:T(8,128)S(1)} %get-tuple-element.59, f32[12,4,1,128]{3,2,1,0:T(1,128)S(1)} %get-tuple-element.61, ...), kind=kLoop, calls=%fused_computation.46 | loop fusion | flops 10616832 | bytes 15794176 | tf_op jit(solution)/shard_map/sub | solution.py:51
  97.3 27.8 %all_to_all.10 = f32[2,12,16,8,128]{4,3,1,0,2:T(8,128)S(1)} all-to-all(f32[2,12,16,8,128]{4,3,1,0,2:T(8,128)S(1)} %copy.23), channel_id=1, replica_groups=mesh['dom'=8,'band'=16] {'band'}, dimensions={2} | all-to-all | bytes 3145728 | tf_op jit(solution)/shard_map/all_to_all | solution.py:129
  127.1 4.8 %shard_map.41 = (f32[192,192]{1,0:T(8,128)}, f32[192,192]{1,0:T(8,128)}) custom-call(f32[1536,128]{1,0:T(8,128)} %bitcast.43, f32[1536,128]{1,0:T(8,128)} %bitcast.50), custom_call_target="tpu_custom_call" | custom-call | tf_op jit(solution)/shard_map/pallas_call | solution.py:91
  135.9 11.1 %collective-permute-done.11 = f32[2,192,192]{2,1,0:T(8,128)S(1)} collective-permute-done((f32[2,192,192]{2,1,0:T(8,128)S(1)}, f32[2,192,192]{2,1,0:T(8,128)S(1)}, u32[]{:S(2)}, u32[]{:S(2)}) %collective-permute-start.11) | collective-permute-done | bytes 294944 | tf_op jit(solution)/shard_map/ppermute | solution.py:60
  148.2 10.9 %collective-permute-done.12 = f32[2,192,192]{2,1,0:T(8,128)S(1)} collective-permute-done((f32[2,192,192]{2,1,0:T(8,128)S(1)}, f32[2,192,192]{2,1,0:T(8,128)S(1)}, u32[]{:S(2)}, u32[]{:S(2)}) %collective-permute-start.12) | collective-permute-done | bytes 294944 | tf_op jit(solution)/shard_map/ppermute | solution.py:60
  159.7 9.3 %collective-permute-done.13 = f32[2,192,192]{2,1,0:T(8,128)S(1)} collective-permute-done((f32[2,192,192]{2,1,0:T(8,128)S(1)}, f32[2,192,192]{2,1,0:T(8,128)S(1)}, u32[]{:S(2)}, u32[]{:S(2)}) %collective-permute-start.13) | collective-permute-done | bytes 294944 | tf_op jit(solution)/shard_map/ppermute | solution.py:60
  169.5 9.4 %collective-permute-done.14 = f32[2,192,192]{2,1,0:T(8,128)S(1)} collective-permute-done((f32[2,192,192]{2,1,0:T(8,128)S(1)}, f32[2,192,192]{2,1,0:T(8,128)S(1)}, u32[]{:S(2)}, u32[]{:S(2)}) %collective-permute-start.14) | collective-permute-done | bytes 294944 | tf_op jit(solution)/shard_map/ppermute | solution.py:60
  179.0 9.4 %collective-permute-done.15 = f32[2,192,192]{2,1,0:T(8,128)S(1)} collective-permute-done((f32[2,192,192]{2,1,0:T(8,128)S(1)}, f32[2,192,192]{2,1,0:T(8,128)S(1)}, u32[]{:S(2)}, u32[]{:S(2)}) %collective-permute-start.15) | collective-permute-done | bytes 294944 | tf_op jit(solution)/shard_map/ppermute | solution.py:60
  189.6 8.6 %collective-permute-done.16 = f32[2,192,192]{2,1,0:T(8,128)S(1)} collective-permute-done((f32[2,192,192]{2,1,0:T(8,128)S(1)}, f32[2,192,192]{2,1,0:T(8,128)S(1)}, u32[]{:S(2)}, u32[]{:S(2)}) %collective-permute-start.16) | collective-permute-done | bytes 294944 | tf_op jit(solution)/shard_map/ppermute | solution.py:60
  200.9 11.7 %cholesky.51 = f32[128,128]{1,0:T(8,128)S(1)} custom-call(f32[128,128]{1,0:T(8,128)S(1)} %cholesky.124), custom_call_target="Cholesky" | custom-call | tf_op jit(solution)/shard_map/jit(cholesky)/cholesky | solution.py:142
  212.7 9.8 %custom-call.15 = f32[1,128,128]{1,2,0:T(8,128)S(1)} custom-call(f32[1,128,128]{2,1,0:T(8,128)S(1)} %get-tuple-element.195), custom_call_target="InvertDiagBlocksLowerTriangular" | custom-call | tf_op jit(solution)/shard_map/jit(cholesky)/cholesky | solution.py:142
  222.9 5.8 %cholesky.110 = f32[64,64]{1,0:T(8,128)S(1)} custom-call(f32[64,64]{1,0:T(8,128)S(1)} %convolution_subtract_fusion.1), custom_call_target="Cholesky" | custom-call | tf_op jit(solution)/shard_map/jit(cholesky)/cholesky | solution.py:142
  231.6 19.8 %custom-call.16 = f32[2,128,128]{1,2,0:T(8,128)S(1)} custom-call(f32[2,128,128]{2,1,0:T(8,128)S(1)} %pad_maximum_fusion.11), custom_call_target="InvertDiagBlocksLowerTriangular" | custom-call | tf_op jit(solution)/shard_map/jit(_solve_triangular)/triangular_solve | solution.py:143
  255.9 3.5 %shard_map.42 = f32[1536,128]{1,0:T(8,128)} custom-call(f32[192,192]{1,0:T(8,128)} %reshape.53.refs_0_, f32[1536,128]{1,0:T(8,128)} %bitcast.44), custom_call_target="tpu_custom_call" | custom-call | tf_op jit(solution)/shard_map/pallas_call | solution.py:100
  259.4 2.1 copy.31
  261.5 4.3 %all-to-all-start.1 = ((f32[12,16,8,128]{3,2,0,1:T(8,128)}), f32[12,16,8,128]{3,2,0,1:T(8,128)}, u32[]{:S(2)}, u32[]{:S(2)}) async-start(f32[12,16,8,128]{3,2,0,1:T(8,128)} %copy.31), calls=%async_computation.1 | async-start | bytes 1572864 | tf_op jit(solution)/shard_map/all_to_all | solution.py:147
  269.4 8.0 %all-to-all-done.1 = f32[12,16,8,128]{3,2,0,1:T(8,128)} async-done(((f32[12,16,8,128]{3,2,0,1:T(8,128)}), f32[12,16,8,128]{3,2,0,1:T(8,128)}, u32[]{:S(2)}, u32[]{:S(2)}) %all-to-all-start.1) | async-done | bytes 786464 | tf_op jit(solution)/shard_map/all_to_all | solution.py:147
  (159 shorter events, 44.1 us)
Async XLA Ops:
  0.6 4.6 %copy-start = (f32[12,4,32,128]{3,2,1,0:T(8,128)S(1)}, f32[12,4,32,128]{3,2,1,0:T(8,128)}, u32[]{:S(2)}) copy-start(f32[12,4,32,128]{3,2,1,0:T(8,128)} %param.2) | copy-start | bytes 2359300
  0.6 12.8 %collective-permute-start.1 = (f32[12,4,32,128]{3,2,1,0:T(8,128)}, f32[12,4,32,128]{3,2,1,0:T(8,128)S(1)}, u32[]{:S(2)}, u32[]{:S(2)}) collective-permute-start(f32[12,4,32,128]{3,2,1,0:T(8,128)} %param.2), channel_id=1, source_target_pairs={{0,16},{16,32},{32,48},{48,64},{64,80},{80,96},{96,112},{112,0},{1... | collective-permute-start | bytes 2359304 | tf_op jit(solution)/shard_map/ppermute | solution.py:24
  0.7 13.1 %collective-permute-start = (f32[12,4,32,128]{3,2,1,0:T(8,128)}, f32[12,4,32,128]{3,2,1,0:T(8,128)S(1)}, u32[]{:S(2)}, u32[]{:S(2)}) collective-permute-start(f32[12,4,32,128]{3,2,1,0:T(8,128)} %param.2), channel_id=1, source_target_pairs={{16,0},{32,16},{48,32},{64,48},{80,64},{96,80},{112,96},{0,112},{1... | collective-permute-start | bytes 2359304 | tf_op jit(solution)/shard_map/ppermute | solution.py:25
  7.7 0.8 copy-start.3
  20.5 12.2 %collective-permute-start.2 = (f32[12,4,32,128]{3,2,1,0:T(8,128)S(1)}, f32[12,4,32,128]{3,2,1,0:T(8,128)S(1)}, u32[]{:S(2)}, u32[]{:S(2)}) collective-permute-start(f32[12,4,32,128]{3,2,1,0:T(8,128)S(1)} %get-tuple-element.26), channel_id=1, source_target_pairs={{16,0},{32,16},{48,32},{64,48},{80,64},{96,80},{112,96},{0,112},{1... | collective-permute-start | bytes 2359304 | tf_op jit(solution)/shard_map/ppermute | solution.py:25
  23.2 12.6 %collective-permute-start.3 = (f32[12,4,32,128]{3,2,1,0:T(8,128)S(1)}, f32[12,4,32,128]{3,2,1,0:T(8,128)S(1)}, u32[]{:S(2)}, u32[]{:S(2)}) collective-permute-start(f32[12,4,32,128]{3,2,1,0:T(8,128)S(1)} %get-tuple-element.26), channel_id=1, source_target_pairs={{0,16},{16,32},{32,48},{48,64},{64,80},{80,96},{96,112},{112,0},{1... | collective-permute-start | bytes 2359304 | tf_op jit(solution)/shard_map/ppermute | solution.py:24
  42.2 9.5 %collective-permute-start.4 = (f32[12,4,32,128]{3,2,1,0:T(8,128)S(1)}, f32[12,4,32,128]{3,2,1,0:T(8,128)S(1)}, u32[]{:S(2)}, u32[]{:S(2)}) collective-permute-start(f32[12,4,32,128]{3,2,1,0:T(8,128)S(1)} %fusion.86), channel_id=1, source_target_pairs={{16,0},{32,16},{48,32},{64,48},{80,64},{96,80},{112,96},{0,112},{1... | collective-permute-start | bytes 2359304 | tf_op jit(solution)/shard_map/ppermute | solution.py:25
  42.2 12.6 %collective-permute-start.5 = (f32[12,4,32,128]{3,2,1,0:T(8,128)S(1)}, f32[12,4,32,128]{3,2,1,0:T(8,128)S(1)}, u32[]{:S(2)}, u32[]{:S(2)}) collective-permute-start(f32[12,4,32,128]{3,2,1,0:T(8,128)S(1)} %fusion.86), channel_id=1, source_target_pairs={{0,16},{16,32},{32,48},{48,64},{64,80},{80,96},{96,112},{112,0},{1... | collective-permute-start | bytes 2359304 | tf_op jit(solution)/shard_map/ppermute | solution.py:24
  61.5 9.5 %collective-permute-start.6 = (f32[12,4,32,128]{3,2,1,0:T(8,128)S(1)}, f32[12,4,32,128]{3,2,1,0:T(8,128)S(1)}, u32[]{:S(2)}, u32[]{:S(2)}) collective-permute-start(f32[12,4,32,128]{3,2,1,0:T(8,128)S(1)} %fusion.61), channel_id=1, source_target_pairs={{16,0},{32,16},{48,32},{64,48},{80,64},{96,80},{112,96},{0,112},{1... | collective-permute-start | bytes 2359304 | tf_op jit(solution)/shard_map/ppermute | solution.py:25
  61.5 12.6 %collective-permute-start.7 = (f32[12,4,32,128]{3,2,1,0:T(8,128)S(1)}, f32[12,4,32,128]{3,2,1,0:T(8,128)S(1)}, u32[]{:S(2)}, u32[]{:S(2)}) collective-permute-start(f32[12,4,32,128]{3,2,1,0:T(8,128)S(1)} %fusion.61), channel_id=1, source_target_pairs={{0,16},{16,32},{32,48},{48,64},{64,80},{80,96},{96,112},{112,0},{1... | collective-permute-start | bytes 2359304 | tf_op jit(solution)/shard_map/ppermute | solution.py:24
  80.6 9.5 %collective-permute-start.8 = (f32[12,4,32,128]{3,2,1,0:T(8,128)S(1)}, f32[12,4,32,128]{3,2,1,0:T(8,128)S(1)}, u32[]{:S(2)}, u32[]{:S(2)}) collective-permute-start(f32[12,4,32,128]{3,2,1,0:T(8,128)S(1)} %fusion.36), channel_id=1, source_target_pairs={{16,0},{32,16},{48,32},{64,48},{80,64},{96,80},{112,96},{0,112},{1... | collective-permute-start | bytes 2359304 | tf_op jit(solution)/shard_map/ppermute | solution.py:25
  80.6 12.6 %collective-permute-start.9 = (f32[12,4,32,128]{3,2,1,0:T(8,128)S(1)}, f32[12,4,32,128]{3,2,1,0:T(8,128)S(1)}, u32[]{:S(2)}, u32[]{:S(2)}) collective-permute-start(f32[12,4,32,128]{3,2,1,0:T(8,128)S(1)} %fusion.36), channel_id=1, source_target_pairs={{0,16},{16,32},{32,48},{48,64},{64,80},{80,96},{96,112},{112,0},{1... | collective-permute-start | bytes 2359304 | tf_op jit(solution)/shard_map/ppermute | solution.py:24
  131.9 15.2 %copy-start.1 = (f32[192,192]{1,0:T(8,128)S(1)}, f32[192,192]{1,0:T(8,128)}, u32[]{:S(2)}) copy-start(f32[192,192]{1,0:T(8,128)} %get-tuple-element.4) | copy-start | bytes 442372
  131.9 15.2 %copy-start.2 = (f32[192,192]{1,0:T(8,128)S(1)}, f32[192,192]{1,0:T(8,128)}, u32[]{:S(2)}) copy-start(f32[192,192]{1,0:T(8,128)} %get-tuple-element.5) | copy-start | bytes 442372
  133.0 1.8 collective-permute-start.10
  135.8 11.2 %collective-permute-start.11 = (f32[2,192,192]{2,1,0:T(8,128)S(1)}, f32[2,192,192]{2,1,0:T(8,128)S(1)}, u32[]{:S(2)}, u32[]{:S(2)}) collective-permute-start(f32[2,192,192]{2,1,0:T(8,128)S(1)} %fusion.178), channel_id=1, source_target_pairs={{0,32},{16,48},{32,0},{48,16},{64,96},{80,112},{96,64},{112,80},{1... | collective-permute-start | bytes 884744 | tf_op jit(solution)/shard_map/ppermute | solution.py:60
  147.2 11.9 %collective-permute-start.12 = (f32[2,192,192]{2,1,0:T(8,128)S(1)}, f32[2,192,192]{2,1,0:T(8,128)S(1)}, u32[]{:S(2)}, u32[]{:S(2)}) collective-permute-start(f32[2,192,192]{2,1,0:T(8,128)S(1)} %fusion.268), channel_id=1, source_target_pairs={{0,64},{16,80},{32,96},{48,112},{64,0},{80,16},{96,32},{112,48},{1... | collective-permute-start | bytes 884744 | tf_op jit(solution)/shard_map/ppermute | solution.py:60
  159.1 10.0 %collective-permute-start.13 = (f32[2,192,192]{2,1,0:T(8,128)S(1)}, f32[2,192,192]{2,1,0:T(8,128)S(1)}, u32[]{:S(2)}, u32[]{:S(2)}) collective-permute-start(f32[2,192,192]{2,1,0:T(8,128)S(1)} %add.531), channel_id=1, source_target_pairs={{0,1},{1,0},{2,3},{3,2},{4,5},{5,4},{6,7},{7,6},{8,9},{9,8},{10,11... | collective-permute-start | bytes 884744 | tf_op jit(solution)/shard_map/ppermute | solution.py:60
  169.1 9.7 %collective-permute-start.14 = (f32[2,192,192]{2,1,0:T(8,128)S(1)}, f32[2,192,192]{2,1,0:T(8,128)S(1)}, u32[]{:S(2)}, u32[]{:S(2)}) collective-permute-start(f32[2,192,192]{2,1,0:T(8,128)S(1)} %add.532), channel_id=1, source_target_pairs={{0,2},{1,3},{2,0},{3,1},{4,6},{5,7},{6,4},{7,5},{8,10},{9,11},{10,... | collective-permute-start | bytes 884744 | tf_op jit(solution)/shard_map/ppermute | solution.py:60
  178.9 9.5 %collective-permute-start.15 = (f32[2,192,192]{2,1,0:T(8,128)S(1)}, f32[2,192,192]{2,1,0:T(8,128)S(1)}, u32[]{:S(2)}, u32[]{:S(2)}) collective-permute-start(f32[2,192,192]{2,1,0:T(8,128)S(1)} %add.533), channel_id=1, source_target_pairs={{0,4},{1,5},{2,6},{3,7},{4,0},{5,1},{6,2},{7,3},{8,12},{9,13},{10,... | collective-permute-start | bytes 884744 | tf_op jit(solution)/shard_map/ppermute | solution.py:60
  188.4 9.8 %collective-permute-start.16 = (f32[2,192,192]{2,1,0:T(8,128)S(1)}, f32[2,192,192]{2,1,0:T(8,128)S(1)}, u32[]{:S(2)}, u32[]{:S(2)}) collective-permute-start(f32[2,192,192]{2,1,0:T(8,128)S(1)} %add.534), channel_id=1, source_target_pairs={{0,8},{1,9},{2,10},{3,11},{4,12},{5,13},{6,14},{7,15},{8,0},{9,1},... | collective-permute-start | bytes 884744 | tf_op jit(solution)/shard_map/ppermute | solution.py:60
  200.7 50.7 %copy-start.4 = (pred[192,192]{1,0:T(32,128)(4,1)S(1)}, pred[192,192]{1,0:T(32,128)(4,1)}, u32[]{:S(2)}) copy-start(pred[192,192]{1,0:T(32,128)(4,1)} %iota_compare_fusion) | copy-start | bytes 110596
  261.5 15.9 %all-to-all-start.1 = ((f32[12,16,8,128]{3,2,0,1:T(8,128)}), f32[12,16,8,128]{3,2,0,1:T(8,128)}, u32[]{:S(2)}, u32[]{:S(2)}) async-start(f32[12,16,8,128]{3,2,0,1:T(8,128)} %copy.31), calls=%async_computation.1 | async-start | bytes 1572864 | tf_op jit(solution)/shard_map/all_to_all | solution.py:147

commit v3 on v2

--- a/solution.py
+++ b/solution.py
@@ -51,15 +51,32 @@
     return potential[None] * field - 0.5 * laplace
 
 
-def butterfly_sum(x, axes):
-    for axis in axes:
-        count = lax.axis_size(axis)
-        step = 1
-        while step < count:
-            pairs = [(i, i ^ step) for i in range(count)]
-            x = x + lax.ppermute(x, axis, pairs)
-            step *= 2
-    return x
+def group_sum(x, axis, stride, size):
+    count = lax.axis_size(axis)
+    pos = (lax.axis_index(axis) // stride) % size
+    received = [x]
+    for shift in range(1, size):
+        pairs = []
+        for i in range(count):
+            p = (i // stride) % size
+            pairs.append((i, i + (((p + shift) % size) - p) * stride))
+        received.append(lax.ppermute(x, axis, pairs))
+    def at(p):
+        value = received[0]
+        for shift in range(1, size):
+            value = jnp.where((pos - p) % size == shift, received[shift], value)
+        return value
+    values = [at(p) for p in range(size)]
+    while len(values) > 1:
+        values = [values[i] + values[i + 1] for i in range(0, len(values), 2)]
+    return values[0]
+
+
+def mesh_sum(x):
+    x = group_sum(x, "dom", 1, 2)
+    x = group_sum(x, "dom", 2, lax.axis_size("dom") // 2)
+    x = group_sum(x, "band", 1, 4)
+    return group_sum(x, "band", 4, lax.axis_size("band") // 4)
 
 
 def gram_kernel(rows, f_ref, h_ref, c_ref, g_ref):
@@ -130,7 +147,17 @@
     flat_cd = spread[0].reshape(bdev * groups * rows, lanes)
     image_cd = spread[1].reshape(bdev * groups * rows, lanes)
     c_perm, g_perm = grams(rows, flat_cd, image_cd)
-    sums = butterfly_sum(jnp.stack([c_perm, g_perm]), ("dom", "band")) / ncells
+    below = lax.broadcasted_iota(jnp.int32, (nbands, nbands), 0) >= lax.broadcasted_iota(
+        jnp.int32, (nbands, nbands), 1
+    )
+    packed = jnp.concatenate(
+        [jnp.where(below, c_perm, g_perm), jnp.diagonal(g_perm)[None], jnp.zeros((7, nbands), jnp.float32)]
+    )
+    packed = mesh_sum(packed) / ncells
+    tri, g_diag = packed[:nbands], packed[nbands]
+    c_sum = jnp.where(below, tri, tri.T)
+    g_sum = jnp.where(below, tri.T, tri)
+    g_sum = jnp.where(jnp.eye(nbands, dtype=bool), g_diag[None, :], g_sum)
 
     def to_true(m):
         return m.reshape(bdev, groups, bdev, groups).transpose(1, 0, 3, 2).reshape(nbands, nbands)
@@ -138,7 +165,7 @@
     def to_perm(m):
         return m.reshape(groups, bdev, groups, bdev).transpose(1, 0, 3, 2).reshape(nbands, nbands)
 
-    correlation, gram = to_true(sums[0]), to_true(sums[1])
+    correlation, gram = to_true(c_sum), to_true(g_sum)
     lower = jnp.linalg.cholesky(correlation)
     inverse = jax.scipy.linalg.solve_triangular(
         lower, jnp.eye(nbands, dtype=jnp.float32), lower=True

time: 283 us -> 269 us (0.951)
  blocking collectives: 27.8 us -> 0 us
  starting transfers between devices: 14.2 us -> 28 us
  local copies, waits for them, and re-layouts: 32.8 us -> 37.3 us
  waiting for transfers between devices: 120 us -> 116 us
    all_to_all x1 -> x0, blocking collectives: 27.8 us -> none  [local(): spread = lax.all_to_all(chunked, 'band', 2, 2, tiled=True)]
    ppermute x7 -> x10, waiting for transfers between devices: 60.4 us -> 32.7 us  [group_sum(): received.append(lax.ppermute(x, axis, pairs))]
    all_to_all x0 -> x1, waiting for transfers between devices: none -> 20.9 us  [local(): spread = lax.all_to_all(chunked, 'band', 2, 2, tiled=True)]
    all_to_all x0 -> x1, starting transfers between devices: none -> 8.63 us  [local(): spread = lax.all_to_all(chunked, 'band', 2, 2, tiled=True)]
    ppermute x7 -> x10, starting transfers between devices: 2.77 us -> 7.89 us  [group_sum(): received.append(lax.ppermute(x, axis, pairs))]
    gather x0 -> x1, local copies, waits for them, and re-layouts: none -> 3.23 us  [local(): jnp.diagonal(g_perm)[None]]
    all_to_all x1, waiting for transfers between devices: 7.97 us -> 11.2 us  [local(): lax.all_to_all(basis_cd, 'band', 1, 1, tiled=True).reshape(psi.shape)]
  transfers between devices with their start and end apart: 18 -> 22, of which waited for: 17 -> 21; matrix products, arithmetic and copies ran while one was open for 4% -> 4% of each run, Pallas kernels for 0% -> 0%
where the time goes in v3:
time: 269 us; the launch traced here: 266 us
  waiting for transfers between devices  116 us (43%)
  other arithmetic  70.5 us (26%)
  local copies, waits for them, and re-layouts  37.3 us (14%)
  starting transfers between devices  28 us (10%)
  Pallas kernels  8.29 us (3%)
  between operations  3.3 us (1%)
    ppermute x5, waiting for transfers between devices, extended(): after = lax.ppermute(initial, axis, down)  34.1 us
    ppermute x10, waiting for transfers between devices, group_sum(): received.append(lax.ppermute(x, axis, pairs))  32.7 us
    another operation x7, other arithmetic, local(): lower = jnp.linalg.cholesky(correlation)  28.7 us
    all_to_all x1, waiting for transfers between devices, local(): spread = lax.all_to_all(chunked, 'band', 2, 2, tiled=True)  20.9 us
    another operation x7, other arithmetic, local(): jax.scipy.linalg.solve_triangular(lower, jnp.eye(nbands, dtype=jnp.float3...  20 us
    ppermute x5, waiting for transfers between devices, extended(): before = lax.ppermute(last, axis, up)  17.1 us
    slice x40, local copies, waits for them, and re-layouts, hamiltonian(): near = near + jnp.roll(field, reach, 3) + jnp.roll(field, -reach, 3)  11.8 us
    sub x3, other arithmetic, local(): following = 2.0 / half * (apply(current) - center * current) - previous  11.6 us
  transfers between devices with their start and end apart: 22, of which 21 were waited for; matrix products, arithmetic and copies ran while one was open for 4% of the time, Pallas kernels for 0%

profile of v3, /device:TPU:0, one launch (start us, length us, event | category | flops | bytes accessed | tf_op | source)
XLA Modules:
  0.0 265.9 jit_solution(16980128024012099981)
XLA Ops:
  0.7 2.9 %collective-permute-start = (f32[12,4,32,128]{3,2,1,0:T(8,128)}, f32[12,4,32,128]{3,2,1,0:T(8,128)S(1)}, u32[]{:S(2)}, u32[]{:S(2)}) collective-permute-start(f32[12,4,32,128]{3,2,1,0:T(8,128)} %param.2), channel_id=1, source_target_pairs={{16,0},{32,16},{48,32},{64,48},{80,64},{96,80},{112,96},{0,112},{1... | collective-permute-start | bytes 2359304 | tf_op jit(solution)/shard_map/ppermute | solution.py:25
  8.9 4.6 %collective-permute-done.1 = f32[12,4,32,128]{3,2,1,0:T(8,128)S(1)} collective-permute-done((f32[12,4,32,128]{3,2,1,0:T(8,128)}, f32[12,4,32,128]{3,2,1,0:T(8,128)S(1)}, u32[]{:S(2)}, u32[]{:S(2)}) %collective-permute-start.1) | collective-permute-done | bytes 786464 | tf_op jit(solution)/shard_map/ppermute | solution.py:24
  13.9 4.0 %broadcast_multiply_fusion = (f32[12,4,32,128]{3,2,1,0:T(8,128)S(1)}, f32[12,4,32,128]{3,2,1,0:T(8,128)S(1)}) fusion(f32[12,4,32,128]{3,2,1,0:T(8,128)S(1)} %copy-done, f32[12,4,32,4]{3,2,1,0:T(8,128)S(1)} %get-tuple-element.189, f32[12,4,32,124]{3,2,1,0:T(8,128)S(1)} %get-tuple-element.191, f32[12,4,32,124]{3,2,1,0:T(8,128)S(1)} %get-tuple-element.190, ...), kind=kLoop, calls=%fused_computation.215 | loop fusion | flops 10027008 | bytes 21299200 | tf_op jit(solution)/shard_map/div | solution.py:137
  23.8 9.0 %collective-permute-done.2 = f32[12,4,32,128]{3,2,1,0:T(8,128)S(1)} collective-permute-done((f32[12,4,32,128]{3,2,1,0:T(8,128)S(1)}, f32[12,4,32,128]{3,2,1,0:T(8,128)S(1)}, u32[]{:S(2)}, u32[]{:S(2)}) %collective-permute-start.2) | collective-permute-done | bytes 786464 | tf_op jit(solution)/shard_map/ppermute | solution.py:25
  32.8 3.1 %collective-permute-done.3 = f32[12,4,32,128]{3,2,1,0:T(8,128)S(1)} collective-permute-done((f32[12,4,32,128]{3,2,1,0:T(8,128)S(1)}, f32[12,4,32,128]{3,2,1,0:T(8,128)S(1)}, u32[]{:S(2)}, u32[]{:S(2)}) %collective-permute-start.3) | collective-permute-done | bytes 786464 | tf_op jit(solution)/shard_map/ppermute | solution.py:24
  35.9 3.8 %fusion.86 = f32[12,4,32,128]{3,2,1,0:T(8,128)S(1)} fusion(f32[12,4,32,128]{3,2,1,0:T(8,128)S(1)} %copy-done, f32[12,4,32,128]{3,2,1,0:T(8,128)S(1)} %collective-permute-done.3, f32[12,4,32,128]{3,2,1,0:T(8,128)S(1)} %get-tuple-element.26, f32[12,4,32,128]{3,2,1,0:T(8,128)S(1)} %collective-permute-done.2, f32[12,4,31,128]{3,2,1,0:T(8,128)S(1)} %get-tuple-element.155, ...), kind=kLoop, calls=%fused_computation.122 | loop fusion | flops 11403264 | bytes 17367040 | tf_op jit(solution)/shard_map/sub | solution.py:139
  43.4 8.4 %collective-permute-done.4 = f32[12,4,32,128]{3,2,1,0:T(8,128)S(1)} collective-permute-done((f32[12,4,32,128]{3,2,1,0:T(8,128)S(1)}, f32[12,4,32,128]{3,2,1,0:T(8,128)S(1)}, u32[]{:S(2)}, u32[]{:S(2)}) %collective-permute-start.4) | collective-permute-done | bytes 786464 | tf_op jit(solution)/shard_map/ppermute | solution.py:25
  51.8 3.1 %collective-permute-done.5 = f32[12,4,32,128]{3,2,1,0:T(8,128)S(1)} collective-permute-done((f32[12,4,32,128]{3,2,1,0:T(8,128)S(1)}, f32[12,4,32,128]{3,2,1,0:T(8,128)S(1)}, u32[]{:S(2)}, u32[]{:S(2)}) %collective-permute-start.5) | collective-permute-done | bytes 786464 | tf_op jit(solution)/shard_map/ppermute | solution.py:24
  54.9 4.1 %fusion.61 = f32[12,4,32,128]{3,2,1,0:T(8,128)S(1)} fusion(f32[12,4,32,128]{3,2,1,0:T(8,128)S(1)} %collective-permute-done.5, f32[12,4,32,128]{3,2,1,0:T(8,128)S(1)} %fusion.86, f32[12,4,32,128]{3,2,1,0:T(8,128)S(1)} %collective-permute-done.4, f32[12,4,31,128]{3,2,1,0:T(8,128)S(1)} %get-tuple-element.123, f32[12,4,1,128]{3,2,1,0:T(1,128)S(1)} %get-tuple-element.125, ...), kind=kLoop, calls=%fused_computation.97 | loop fusion | flops 11599872 | bytes 16580608 | tf_op jit(solution)/shard_map/sub | solution.py:139
  62.7 8.4 %collective-permute-done.6 = f32[12,4,32,128]{3,2,1,0:T(8,128)S(1)} collective-permute-done((f32[12,4,32,128]{3,2,1,0:T(8,128)S(1)}, f32[12,4,32,128]{3,2,1,0:T(8,128)S(1)}, u32[]{:S(2)}, u32[]{:S(2)}) %collective-permute-start.6) | collective-permute-done | bytes 786464 | tf_op jit(solution)/shard_map/ppermute | solution.py:25
  71.1 3.1 %collective-permute-done.7 = f32[12,4,32,128]{3,2,1,0:T(8,128)S(1)} collective-permute-done((f32[12,4,32,128]{3,2,1,0:T(8,128)S(1)}, f32[12,4,32,128]{3,2,1,0:T(8,128)S(1)}, u32[]{:S(2)}, u32[]{:S(2)}) %collective-permute-start.7) | collective-permute-done | bytes 786464 | tf_op jit(solution)/shard_map/ppermute | solution.py:24
  74.3 3.8 %fusion.36 = f32[12,4,32,128]{3,2,1,0:T(8,128)S(1)} fusion(f32[12,4,32,128]{3,2,1,0:T(8,128)S(1)} %fusion.86, f32[12,4,32,128]{3,2,1,0:T(8,128)S(1)} %collective-permute-done.7, f32[12,4,32,128]{3,2,1,0:T(8,128)S(1)} %fusion.61, f32[12,4,32,128]{3,2,1,0:T(8,128)S(1)} %collective-permute-done.6, f32[12,4,31,128]{3,2,1,0:T(8,128)S(1)} %get-tuple-element.91, ...), kind=kLoop, calls=%fused_computation.72 | loop fusion | flops 11403264 | bytes 16580608 | tf_op jit(solution)/shard_map/sub | solution.py:139
  81.8 8.4 %collective-permute-done.8 = f32[12,4,32,128]{3,2,1,0:T(8,128)S(1)} collective-permute-done((f32[12,4,32,128]{3,2,1,0:T(8,128)S(1)}, f32[12,4,32,128]{3,2,1,0:T(8,128)S(1)}, u32[]{:S(2)}, u32[]{:S(2)}) %collective-permute-start.8) | collective-permute-done | bytes 786464 | tf_op jit(solution)/shard_map/ppermute | solution.py:25
  90.2 3.1 %collective-permute-done.9 = f32[12,4,32,128]{3,2,1,0:T(8,128)S(1)} collective-permute-done((f32[12,4,32,128]{3,2,1,0:T(8,128)S(1)}, f32[12,4,32,128]{3,2,1,0:T(8,128)S(1)}, u32[]{:S(2)}, u32[]{:S(2)}) %collective-permute-start.9) | collective-permute-done | bytes 786464 | tf_op jit(solution)/shard_map/ppermute | solution.py:24
  93.3 3.7 %fusion.11 = f32[12,4,32,128]{3,2,1,0:T(8,128)S(1)} fusion(f32[12,4,32,128]{3,2,1,0:T(8,128)S(1)} %collective-permute-done.9, f32[12,4,32,128]{3,2,1,0:T(8,128)S(1)} %fusion.36, f32[12,4,32,128]{3,2,1,0:T(8,128)S(1)} %collective-permute-done.8, f32[12,4,31,128]{3,2,1,0:T(8,128)S(1)} %get-tuple-element.59, f32[12,4,1,128]{3,2,1,0:T(1,128)S(1)} %get-tuple-element.61, ...), kind=kLoop, calls=%fused_computation.47 | loop fusion | flops 10616832 | bytes 15794176 | tf_op jit(solution)/shard_map/sub | solution.py:51
  98.5 8.6 %all-to-all-start = ((f32[2,12,16,8,128]{4,3,1,0,2:T(8,128)}), f32[2,12,16,8,128]{4,3,1,0,2:T(8,128)S(1)}, u32[]{:S(2)}, u32[]{:S(2)}) async-start(f32[2,12,16,8,128]{4,3,1,0,2:T(8,128)} %copy.26), calls=%async_computation | async-start | bytes 3145728 | tf_op jit(solution)/shard_map/all_to_all | solution.py:146
  107.2 20.9 %all-to-all-done = f32[2,12,16,8,128]{4,3,1,0,2:T(8,128)S(1)} async-done(((f32[2,12,16,8,128]{4,3,1,0,2:T(8,128)}), f32[2,12,16,8,128]{4,3,1,0,2:T(8,128)S(1)}, u32[]{:S(2)}, u32[]{:S(2)}) %all-to-all-start) | async-done | bytes 1572896 | tf_op jit(solution)/shard_map/all_to_all | solution.py:146
  130.1 4.8 %shard_map.41 = (f32[192,192]{1,0:T(8,128)}, f32[192,192]{1,0:T(8,128)}) custom-call(f32[1536,128]{1,0:T(8,128)} %bitcast.50, f32[1536,128]{1,0:T(8,128)} %bitcast.57), custom_call_target="tpu_custom_call" | custom-call | tf_op jit(solution)/shard_map/pallas_call | solution.py:108
  135.9 3.2 %gather_fusion = f32[192]{0:T(256)S(1)} fusion(f32[192,192]{1,0:T(8,128)} %get-tuple-element.5, s32[192]{0:T(256)S(1)} %bitcast.49), kind=kCustom, calls=%fused_computation | custom fusion | bytes 3072 | tf_op jit(solution)/shard_map/jit(diagonal)/cond/branch_0_fun/gather | solution.py:154
  143.0 5.9 %collective-permute-done.11 = f32[200,192]{1,0:T(8,128)S(1)} collective-permute-done((f32[200,192]{1,0:T(8,128)S(1)}, f32[200,192]{1,0:T(8,128)S(1)}, u32[]{:S(2)}, u32[]{:S(2)}) %collective-permute-start.11) | collective-permute-done | bytes 153632 | tf_op jit(solution)/shard_map/ppermute | solution.py:63
  150.6 3.5 %collective-permute-done.13 = f32[200,192]{1,0:T(8,128)S(1)} collective-permute-done((f32[200,192]{1,0:T(8,128)S(1)}, f32[200,192]{1,0:T(8,128)S(1)}, u32[]{:S(2)}, u32[]{:S(2)}) %collective-permute-start.13) | collective-permute-done | bytes 153632 | tf_op jit(solution)/shard_map/ppermute | solution.py:63
  157.4 4.8 %collective-permute-done.14 = f32[200,192]{1,0:T(8,128)S(1)} collective-permute-done((f32[200,192]{1,0:T(8,128)S(1)}, f32[200,192]{1,0:T(8,128)S(1)}, u32[]{:S(2)}, u32[]{:S(2)}) %collective-permute-start.14) | collective-permute-done | bytes 153632 | tf_op jit(solution)/shard_map/ppermute | solution.py:63
  163.9 3.4 %collective-permute-done.16 = f32[200,192]{1,0:T(8,128)S(1)} collective-permute-done((f32[200,192]{1,0:T(8,128)S(1)}, f32[200,192]{1,0:T(8,128)S(1)}, u32[]{:S(2)}, u32[]{:S(2)}) %collective-permute-start.16) | collective-permute-done | bytes 153632 | tf_op jit(solution)/shard_map/ppermute | solution.py:63
  170.7 4.7 %collective-permute-done.17 = f32[200,192]{1,0:T(8,128)S(1)} collective-permute-done((f32[200,192]{1,0:T(8,128)S(1)}, f32[200,192]{1,0:T(8,128)S(1)}, u32[]{:S(2)}, u32[]{:S(2)}) %collective-permute-start.17) | collective-permute-done | bytes 153632 | tf_op jit(solution)/shard_map/ppermute | solution.py:63
  177.9 3.1 %collective-permute-done.19 = f32[200,192]{1,0:T(8,128)S(1)} collective-permute-done((f32[200,192]{1,0:T(8,128)S(1)}, f32[200,192]{1,0:T(8,128)S(1)}, u32[]{:S(2)}, u32[]{:S(2)}) %collective-permute-start.19) | collective-permute-done | bytes 153632 | tf_op jit(solution)/shard_map/ppermute | solution.py:63
  184.0 11.7 %cholesky.51 = f32[128,128]{1,0:T(8,128)S(1)} custom-call(f32[128,128]{1,0:T(8,128)S(1)} %cholesky.124), custom_call_target="Cholesky" | custom-call | tf_op jit(solution)/shard_map/jit(cholesky)/cholesky | solution.py:169
  195.7 9.8 %custom-call.15 = f32[1,128,128]{1,2,0:T(8,128)S(1)} custom-call(f32[1,128,128]{2,1,0:T(8,128)S(1)} %get-tuple-element.195), custom_call_target="InvertDiagBlocksLowerTriangular" | custom-call | tf_op jit(solution)/shard_map/jit(cholesky)/cholesky | solution.py:169
  205.9 5.8 %cholesky.110 = f32[64,64]{1,0:T(8,128)S(1)} custom-call(f32[64,64]{1,0:T(8,128)S(1)} %convolution_subtract_fusion.1), custom_call_target="Cholesky" | custom-call | tf_op jit(solution)/shard_map/jit(cholesky)/cholesky | solution.py:169
  214.6 19.9 %custom-call.16 = f32[2,128,128]{1,2,0:T(8,128)S(1)} custom-call(f32[2,128,128]{2,1,0:T(8,128)S(1)} %pad_maximum_fusion.10), custom_call_target="InvertDiagBlocksLowerTriangular" | custom-call | tf_op jit(solution)/shard_map/jit(_solve_triangular)/triangular_solve | solution.py:170
  238.9 3.5 %shard_map.42 = f32[1536,128]{1,0:T(8,128)} custom-call(f32[192,192]{1,0:T(8,128)} %reshape.60.refs_0_, f32[1536,128]{1,0:T(8,128)} %bitcast.51), custom_call_target="tpu_custom_call" | custom-call | tf_op jit(solution)/shard_map/pallas_call | solution.py:117
  244.5 4.3 %all-to-all-start.1 = ((f32[12,16,8,128]{3,2,0,1:T(8,128)}), f32[12,16,8,128]{3,2,0,1:T(8,128)}, u32[]{:S(2)}, u32[]{:S(2)}) async-start(f32[12,16,8,128]{3,2,0,1:T(8,128)} %copy.35), calls=%async_computation.1 | async-start | bytes 1572864 | tf_op jit(solution)/shard_map/all_to_all | solution.py:174
  252.4 11.2 %all-to-all-done.1 = f32[12,16,8,128]{3,2,0,1:T(8,128)} async-done(((f32[12,16,8,128]{3,2,0,1:T(8,128)}), f32[12,16,8,128]{3,2,0,1:T(8,128)}, u32[]{:S(2)}, u32[]{:S(2)}) %all-to-all-start.1) | async-done | bytes 786464 | tf_op jit(solution)/shard_map/all_to_all | solution.py:174
  (167 shorter events, 59.9 us)
Async XLA Ops:
  0.6 4.6 %copy-start = (f32[12,4,32,128]{3,2,1,0:T(8,128)S(1)}, f32[12,4,32,128]{3,2,1,0:T(8,128)}, u32[]{:S(2)}) copy-start(f32[12,4,32,128]{3,2,1,0:T(8,128)} %param.2) | copy-start | bytes 2359300
  0.6 12.8 %collective-permute-start.1 = (f32[12,4,32,128]{3,2,1,0:T(8,128)}, f32[12,4,32,128]{3,2,1,0:T(8,128)S(1)}, u32[]{:S(2)}, u32[]{:S(2)}) collective-permute-start(f32[12,4,32,128]{3,2,1,0:T(8,128)} %param.2), channel_id=1, source_target_pairs={{0,16},{16,32},{32,48},{48,64},{64,80},{80,96},{96,112},{112,0},{1... | collective-permute-start | bytes 2359304 | tf_op jit(solution)/shard_map/ppermute | solution.py:24
  0.7 13.1 %collective-permute-start = (f32[12,4,32,128]{3,2,1,0:T(8,128)}, f32[12,4,32,128]{3,2,1,0:T(8,128)S(1)}, u32[]{:S(2)}, u32[]{:S(2)}) collective-permute-start(f32[12,4,32,128]{3,2,1,0:T(8,128)} %param.2), channel_id=1, source_target_pairs={{16,0},{32,16},{48,32},{64,48},{80,64},{96,80},{112,96},{0,112},{1... | collective-permute-start | bytes 2359304 | tf_op jit(solution)/shard_map/ppermute | solution.py:25
  7.7 0.8 copy-start.1
  20.6 12.2 %collective-permute-start.2 = (f32[12,4,32,128]{3,2,1,0:T(8,128)S(1)}, f32[12,4,32,128]{3,2,1,0:T(8,128)S(1)}, u32[]{:S(2)}, u32[]{:S(2)}) collective-permute-start(f32[12,4,32,128]{3,2,1,0:T(8,128)S(1)} %get-tuple-element.26), channel_id=1, source_target_pairs={{16,0},{32,16},{48,32},{64,48},{80,64},{96,80},{112,96},{0,112},{1... | collective-permute-start | bytes 2359304 | tf_op jit(solution)/shard_map/ppermute | solution.py:25
  23.2 12.6 %collective-permute-start.3 = (f32[12,4,32,128]{3,2,1,0:T(8,128)S(1)}, f32[12,4,32,128]{3,2,1,0:T(8,128)S(1)}, u32[]{:S(2)}, u32[]{:S(2)}) collective-permute-start(f32[12,4,32,128]{3,2,1,0:T(8,128)S(1)} %get-tuple-element.26), channel_id=1, source_target_pairs={{0,16},{16,32},{32,48},{48,64},{64,80},{80,96},{96,112},{112,0},{1... | collective-permute-start | bytes 2359304 | tf_op jit(solution)/shard_map/ppermute | solution.py:24
  42.3 9.5 %collective-permute-start.4 = (f32[12,4,32,128]{3,2,1,0:T(8,128)S(1)}, f32[12,4,32,128]{3,2,1,0:T(8,128)S(1)}, u32[]{:S(2)}, u32[]{:S(2)}) collective-permute-start(f32[12,4,32,128]{3,2,1,0:T(8,128)S(1)} %fusion.86), channel_id=1, source_target_pairs={{16,0},{32,16},{48,32},{64,48},{80,64},{96,80},{112,96},{0,112},{1... | collective-permute-start | bytes 2359304 | tf_op jit(solution)/shard_map/ppermute | solution.py:25
  42.3 12.6 %collective-permute-start.5 = (f32[12,4,32,128]{3,2,1,0:T(8,128)S(1)}, f32[12,4,32,128]{3,2,1,0:T(8,128)S(1)}, u32[]{:S(2)}, u32[]{:S(2)}) collective-permute-start(f32[12,4,32,128]{3,2,1,0:T(8,128)S(1)} %fusion.86), channel_id=1, source_target_pairs={{0,16},{16,32},{32,48},{48,64},{64,80},{80,96},{96,112},{112,0},{1... | collective-permute-start | bytes 2359304 | tf_op jit(solution)/shard_map/ppermute | solution.py:24
  61.6 9.5 %collective-permute-start.6 = (f32[12,4,32,128]{3,2,1,0:T(8,128)S(1)}, f32[12,4,32,128]{3,2,1,0:T(8,128)S(1)}, u32[]{:S(2)}, u32[]{:S(2)}) collective-permute-start(f32[12,4,32,128]{3,2,1,0:T(8,128)S(1)} %fusion.61), channel_id=1, source_target_pairs={{16,0},{32,16},{48,32},{64,48},{80,64},{96,80},{112,96},{0,112},{1... | collective-permute-start | bytes 2359304 | tf_op jit(solution)/shard_map/ppermute | solution.py:25
  61.6 12.6 %collective-permute-start.7 = (f32[12,4,32,128]{3,2,1,0:T(8,128)S(1)}, f32[12,4,32,128]{3,2,1,0:T(8,128)S(1)}, u32[]{:S(2)}, u32[]{:S(2)}) collective-permute-start(f32[12,4,32,128]{3,2,1,0:T(8,128)S(1)} %fusion.61), channel_id=1, source_target_pairs={{0,16},{16,32},{32,48},{48,64},{64,80},{80,96},{96,112},{112,0},{1... | collective-permute-start | bytes 2359304 | tf_op jit(solution)/shard_map/ppermute | solution.py:24
  80.6 9.5 %collective-permute-start.8 = (f32[12,4,32,128]{3,2,1,0:T(8,128)S(1)}, f32[12,4,32,128]{3,2,1,0:T(8,128)S(1)}, u32[]{:S(2)}, u32[]{:S(2)}) collective-permute-start(f32[12,4,32,128]{3,2,1,0:T(8,128)S(1)} %fusion.36), channel_id=1, source_target_pairs={{16,0},{32,16},{48,32},{64,48},{80,64},{96,80},{112,96},{0,112},{1... | collective-permute-start | bytes 2359304 | tf_op jit(solution)/shard_map/ppermute | solution.py:25
  80.7 12.6 %collective-permute-start.9 = (f32[12,4,32,128]{3,2,1,0:T(8,128)S(1)}, f32[12,4,32,128]{3,2,1,0:T(8,128)S(1)}, u32[]{:S(2)}, u32[]{:S(2)}) collective-permute-start(f32[12,4,32,128]{3,2,1,0:T(8,128)S(1)} %fusion.36), channel_id=1, source_target_pairs={{0,16},{16,32},{32,48},{48,64},{64,80},{80,96},{96,112},{112,0},{1... | collective-permute-start | bytes 2359304 | tf_op jit(solution)/shard_map/ppermute | solution.py:24
  98.5 29.6 %all-to-all-start = ((f32[2,12,16,8,128]{4,3,1,0,2:T(8,128)}), f32[2,12,16,8,128]{4,3,1,0,2:T(8,128)S(1)}, u32[]{:S(2)}, u32[]{:S(2)}) async-start(f32[2,12,16,8,128]{4,3,1,0,2:T(8,128)} %copy.26), calls=%async_computation | async-start | bytes 3145728 | tf_op jit(solution)/shard_map/all_to_all | solution.py:146
  139.3 1.5 collective-permute-start.10
  140.9 8.0 %collective-permute-start.11 = (f32[200,192]{1,0:T(8,128)S(1)}, f32[200,192]{1,0:T(8,128)S(1)}, u32[]{:S(2)}, u32[]{:S(2)}) collective-permute-start(f32[200,192]{1,0:T(8,128)S(1)} %select_add_fusion), channel_id=1, source_target_pairs={{0,96},{16,112},{32,0},{48,16},{64,32},{80,48},{96,64},{112,80},{1... | collective-permute-start | bytes 460808 | tf_op jit(solution)/shard_map/ppermute | solution.py:63
  141.0 9.6 %collective-permute-start.12 = (f32[200,192]{1,0:T(8,128)S(1)}, f32[200,192]{1,0:T(8,128)S(1)}, u32[]{:S(2)}, u32[]{:S(2)}) collective-permute-start(f32[200,192]{1,0:T(8,128)S(1)} %select_add_fusion), channel_id=1, source_target_pairs={{0,64},{16,80},{32,96},{48,112},{64,0},{80,16},{96,32},{112,48},{1... | collective-permute-start | bytes 460808 | tf_op jit(solution)/shard_map/ppermute | solution.py:63
  142.2 11.9 %collective-permute-start.13 = (f32[200,192]{1,0:T(8,128)S(1)}, f32[200,192]{1,0:T(8,128)S(1)}, u32[]{:S(2)}, u32[]{:S(2)}) collective-permute-start(f32[200,192]{1,0:T(8,128)S(1)} %select_add_fusion), channel_id=1, source_target_pairs={{0,32},{16,48},{32,64},{48,80},{64,96},{80,112},{96,0},{112,16},{1... | collective-permute-start | bytes 460808 | tf_op jit(solution)/shard_map/ppermute | solution.py:63
  154.2 8.0 %collective-permute-start.14 = (f32[200,192]{1,0:T(8,128)S(1)}, f32[200,192]{1,0:T(8,128)S(1)}, u32[]{:S(2)}, u32[]{:S(2)}) collective-permute-start(f32[200,192]{1,0:T(8,128)S(1)} %add_add_fusion.1), channel_id=1, source_target_pairs={{0,3},{1,0},{2,1},{3,2},{4,7},{5,4},{6,5},{7,6},{8,11},{9,8},{10,9... | collective-permute-start | bytes 460808 | tf_op jit(solution)/shard_map/ppermute | solution.py:63
  154.3 9.6 %collective-permute-start.15 = (f32[200,192]{1,0:T(8,128)S(1)}, f32[200,192]{1,0:T(8,128)S(1)}, u32[]{:S(2)}, u32[]{:S(2)}) collective-permute-start(f32[200,192]{1,0:T(8,128)S(1)} %add_add_fusion.1), channel_id=1, source_target_pairs={{0,2},{1,3},{2,0},{3,1},{4,6},{5,7},{6,4},{7,5},{8,10},{9,11},{10,... | collective-permute-start | bytes 460808 | tf_op jit(solution)/shard_map/ppermute | solution.py:63
  156.8 10.5 %collective-permute-start.16 = (f32[200,192]{1,0:T(8,128)S(1)}, f32[200,192]{1,0:T(8,128)S(1)}, u32[]{:S(2)}, u32[]{:S(2)}) collective-permute-start(f32[200,192]{1,0:T(8,128)S(1)} %add_add_fusion.1), channel_id=1, source_target_pairs={{0,1},{1,2},{2,3},{3,0},{4,5},{5,6},{6,7},{7,4},{8,9},{9,10},{10,1... | collective-permute-start | bytes 460808 | tf_op jit(solution)/shard_map/ppermute | solution.py:63
  167.4 8.0 %collective-permute-start.17 = (f32[200,192]{1,0:T(8,128)S(1)}, f32[200,192]{1,0:T(8,128)S(1)}, u32[]{:S(2)}, u32[]{:S(2)}) collective-permute-start(f32[200,192]{1,0:T(8,128)S(1)} %add_add_fusion), channel_id=1, source_target_pairs={{0,12},{1,13},{2,14},{3,15},{4,0},{5,1},{6,2},{7,3},{8,4},{9,5},{1... | collective-permute-start | bytes 460808 | tf_op jit(solution)/shard_map/ppermute | solution.py:63
  168.4 9.5 %collective-permute-start.18 = (f32[200,192]{1,0:T(8,128)S(1)}, f32[200,192]{1,0:T(8,128)S(1)}, u32[]{:S(2)}, u32[]{:S(2)}) collective-permute-start(f32[200,192]{1,0:T(8,128)S(1)} %add_add_fusion), channel_id=1, source_target_pairs={{0,8},{1,9},{2,10},{3,11},{4,12},{5,13},{6,14},{7,15},{8,0},{9,1},... | collective-permute-start | bytes 460808 | tf_op jit(solution)/shard_map/ppermute | solution.py:63
  169.9 11.1 %collective-permute-start.19 = (f32[200,192]{1,0:T(8,128)S(1)}, f32[200,192]{1,0:T(8,128)S(1)}, u32[]{:S(2)}, u32[]{:S(2)}) collective-permute-start(f32[200,192]{1,0:T(8,128)S(1)} %add_add_fusion), channel_id=1, source_target_pairs={{0,4},{1,5},{2,6},{3,7},{4,8},{5,9},{6,10},{7,11},{8,12},{9,13},{1... | collective-permute-start | bytes 460808 | tf_op jit(solution)/shard_map/ppermute | solution.py:63
  183.8 50.7 %copy-start.2 = (pred[192,192]{1,0:T(32,128)(4,1)S(1)}, pred[192,192]{1,0:T(32,128)(4,1)}, u32[]{:S(2)}) copy-start(pred[192,192]{1,0:T(32,128)(4,1)} %iota_compare_fusion) | copy-start | bytes 110596
  244.5 19.1 %all-to-all-start.1 = ((f32[12,16,8,128]{3,2,0,1:T(8,128)}), f32[12,16,8,128]{3,2,0,1:T(8,128)}, u32[]{:S(2)}, u32[]{:S(2)}) async-start(f32[12,16,8,128]{3,2,0,1:T(8,128)} %copy.35), calls=%async_computation.1 | async-start | bytes 1572864 | tf_op jit(solution)/shard_map/all_to_all | solution.py:174

commit v4 on v3

--- a/solution.py
+++ b/solution.py
@@ -96,6 +96,44 @@
         o_ref[pl.ds(r, nb, stride=rows), :] = hp_dot(
             m_ref[...], f_ref[pl.ds(r, nb, stride=rows), :], ((1,), (0,))
         )
+
+
+def inverse_kernel(c_ref, o_ref, a_ref, b_ref):
+    n = c_ref.shape[0]
+    a_ref[...] = jnp.zeros_like(a_ref)
+    a_ref[:, :n] = c_ref[...]
+    shape = a_ref.shape
+    sub = lax.broadcasted_iota(jnp.int32, shape, 0)
+    lane = lax.broadcasted_iota(jnp.int32, shape, 1)
+    b_ref[...] = jnp.where(sub == lane, 1.0, 0.0).astype(jnp.float32)
+
+    def step(k, carry):
+        row_a = a_ref[pl.ds(k, 1), :]
+        row_b = b_ref[pl.ds(k, 1), :]
+        a = a_ref[...]
+        pivot = jnp.sum(jnp.where(lane[:1] == k, row_a, 0.0), axis=1, keepdims=True)
+        col = jnp.sum(jnp.where(lane == k, a, 0.0), axis=1, keepdims=True)
+        factor = jnp.where(sub[:, :1] > k, col, 0.0) / pivot
+        a_ref[...] = a - factor * row_a
+        b_ref[...] = b_ref[...] - factor * row_b
+        return carry
+
+    lax.fori_loop(0, n, step, 0)
+    a = a_ref[...]
+    diag = jnp.sum(jnp.where(sub == lane, a, 0.0), axis=1, keepdims=True)
+    o_ref[...] = (b_ref[...] / jnp.sqrt(diag))[:, :n]
+
+
+def lower_inverse(c):
+    n = c.shape[0]
+    wide = ((n + 127) // 128) * 128
+    return pl.pallas_call(
+        inverse_kernel,
+        out_shape=jax.ShapeDtypeStruct((n, n), jnp.float32),
+        in_specs=[vspec()],
+        out_specs=vspec(),
+        scratch_shapes=[pltpu.VMEM((n, wide), jnp.float32), pltpu.VMEM((n, wide), jnp.float32)],
+    )(c)
 
 
 def vspec():
@@ -166,10 +204,7 @@
         return m.reshape(groups, bdev, groups, bdev).transpose(1, 0, 3, 2).reshape(nbands, nbands)
 
     correlation, gram = to_true(c_sum), to_true(g_sum)
-    lower = jnp.linalg.cholesky(correlation)
-    inverse = jax.scipy.linalg.solve_triangular(
-        lower, jnp.eye(nbands, dtype=jnp.float32), lower=True
-    )
+    inverse = lower_inverse(correlation)
     basis_cd = rotate(rows, to_perm(inverse), flat_cd).reshape(bdev, groups, rows, lanes)
     basis = lax.all_to_all(basis_cd, "band", 1, 1, tiled=True).reshape(psi.shape)
     own_rows = lax.dynamic_slice_in_dim(inverse, own_start, bdev, 0)

time: 269 us -> 246 us (0.914)
  other arithmetic: 70.5 us -> 21.3 us
  Pallas kernels: 8.29 us -> 35.3 us
    another operation x14 -> x0, other arithmetic: 48.8 us -> none  [the longest x7 28.7 us: local(): lower = jnp.linalg.cholesky(correlation)]
    pallas_call x0 -> x1, Pallas kernels: none -> 27 us  [lower_inverse(): pl.pallas_call(inverse_kernel, out_shape=jax.ShapeDtypeStruct((n, n), jnp...]
where the time goes in v4:
time: 246 us; the launch traced here: 243 us
  waiting for transfers between devices  117 us (48%)
  local copies, waits for them, and re-layouts  38.8 us (16%)
  Pallas kernels  35.3 us (14%)
  starting transfers between devices  27.6 us (11%)
  other arithmetic  21.3 us (9%)
    ppermute x5, waiting for transfers between devices, extended(): after = lax.ppermute(initial, axis, down)  34.1 us
    ppermute x10, waiting for transfers between devices, group_sum(): received.append(lax.ppermute(x, axis, pairs))  33.6 us
    pallas_call x1, Pallas kernels, lower_inverse(): pl.pallas_call(inverse_kernel, out_shape=jax.ShapeDtypeStruct((n, n), jnp...  27 us
    all_to_all x1, waiting for transfers between devices, local(): spread = lax.all_to_all(chunked, 'band', 2, 2, tiled=True)  20.9 us
    ppermute x5, waiting for transfers between devices, extended(): before = lax.ppermute(last, axis, up)  17.1 us
    slice x40, local copies, waits for them, and re-layouts, hamiltonian(): near = near + jnp.roll(field, reach, 3) + jnp.roll(field, -reach, 3)  11.8 us
    sub x3, other arithmetic, local(): following = 2.0 / half * (apply(current) - center * current) - previous  11.5 us
    all_to_all x1, waiting for transfers between devices, local(): lax.all_to_all(basis_cd, 'band', 1, 1, tiled=True).reshape(psi.shape)  11.2 us
  transfers between devices with their start and end apart: 22, of which 21 were waited for; matrix products, arithmetic and copies ran while one was open for 4% of the time, Pallas kernels for 0%

profile of v4, /device:TPU:0, one launch (start us, length us, event | category | flops | bytes accessed | tf_op | source)
XLA Modules:
  0.0 242.7 jit_solution(16782594136600820517)
XLA Ops:
  0.7 2.9 %collective-permute-start = (f32[12,4,32,128]{3,2,1,0:T(8,128)}, f32[12,4,32,128]{3,2,1,0:T(8,128)S(1)}, u32[]{:S(2)}, u32[]{:S(2)}) collective-permute-start(f32[12,4,32,128]{3,2,1,0:T(8,128)} %param.2), channel_id=1, source_target_pairs={{16,0},{32,16},{48,32},{64,48},{80,64},{96,80},{112,96},{0,112},{1... | collective-permute-start | bytes 2359304 | tf_op jit(solution)/shard_map/ppermute | solution.py:25
  8.9 4.6 %collective-permute-done.1 = f32[12,4,32,128]{3,2,1,0:T(8,128)S(1)} collective-permute-done((f32[12,4,32,128]{3,2,1,0:T(8,128)}, f32[12,4,32,128]{3,2,1,0:T(8,128)S(1)}, u32[]{:S(2)}, u32[]{:S(2)}) %collective-permute-start.1) | collective-permute-done | bytes 786464 | tf_op jit(solution)/shard_map/ppermute | solution.py:24
  13.9 4.3 %broadcast_multiply_fusion = (f32[12,4,32,128]{3,2,1,0:T(8,128)S(1)}, f32[12,4,32,128]{3,2,1,0:T(8,128)S(1)}) fusion(f32[12,4,32,128]{3,2,1,0:T(8,128)S(1)} %copy-done, f32[12,4,32,4]{3,2,1,0:T(8,128)S(1)} %get-tuple-element.169, f32[12,4,32,124]{3,2,1,0:T(8,128)S(1)} %get-tuple-element.171, f32[12,4,32,124]{3,2,1,0:T(8,128)S(1)} %get-tuple-element.170, ...), kind=kLoop, calls=%fused_computation.213 | loop fusion | flops 10027008 | bytes 21299200 | tf_op jit(solution)/shard_map/div | solution.py:175
  20.9 2.7 %collective-permute-start.2 = (f32[12,4,32,128]{3,2,1,0:T(8,128)S(1)}, f32[12,4,32,128]{3,2,1,0:T(8,128)S(1)}, u32[]{:S(2)}, u32[]{:S(2)}) collective-permute-start(f32[12,4,32,128]{3,2,1,0:T(8,128)S(1)} %get-tuple-element.6), channel_id=1, source_target_pairs={{16,0},{32,16},{48,32},{64,48},{80,64},{96,80},{112,96},{0,112},{1... | collective-permute-start | bytes 2359304 | tf_op jit(solution)/shard_map/ppermute | solution.py:25
  24.1 9.0 %collective-permute-done.2 = f32[12,4,32,128]{3,2,1,0:T(8,128)S(1)} collective-permute-done((f32[12,4,32,128]{3,2,1,0:T(8,128)S(1)}, f32[12,4,32,128]{3,2,1,0:T(8,128)S(1)}, u32[]{:S(2)}, u32[]{:S(2)}) %collective-permute-start.2) | collective-permute-done | bytes 786464 | tf_op jit(solution)/shard_map/ppermute | solution.py:25
  33.1 3.1 %collective-permute-done.3 = f32[12,4,32,128]{3,2,1,0:T(8,128)S(1)} collective-permute-done((f32[12,4,32,128]{3,2,1,0:T(8,128)S(1)}, f32[12,4,32,128]{3,2,1,0:T(8,128)S(1)}, u32[]{:S(2)}, u32[]{:S(2)}) %collective-permute-start.3) | collective-permute-done | bytes 786464 | tf_op jit(solution)/shard_map/ppermute | solution.py:24
  36.2 3.8 %fusion.86 = f32[12,4,32,128]{3,2,1,0:T(8,128)S(1)} fusion(f32[12,4,32,128]{3,2,1,0:T(8,128)S(1)} %copy-done, f32[12,4,32,128]{3,2,1,0:T(8,128)S(1)} %collective-permute-done.3, f32[12,4,32,128]{3,2,1,0:T(8,128)S(1)} %get-tuple-element.6, f32[12,4,32,128]{3,2,1,0:T(8,128)S(1)} %collective-permute-done.2, f32[12,4,31,128]{3,2,1,0:T(8,128)S(1)} %get-tuple-element.135, ...), kind=kLoop, calls=%fused_computation.120 | loop fusion | flops 11403264 | bytes 17367040 | tf_op jit(solution)/shard_map/sub | solution.py:177
  43.7 8.4 %collective-permute-done.4 = f32[12,4,32,128]{3,2,1,0:T(8,128)S(1)} collective-permute-done((f32[12,4,32,128]{3,2,1,0:T(8,128)S(1)}, f32[12,4,32,128]{3,2,1,0:T(8,128)S(1)}, u32[]{:S(2)}, u32[]{:S(2)}) %collective-permute-start.4) | collective-permute-done | bytes 786464 | tf_op jit(solution)/shard_map/ppermute | solution.py:25
  52.1 3.1 %collective-permute-done.5 = f32[12,4,32,128]{3,2,1,0:T(8,128)S(1)} collective-permute-done((f32[12,4,32,128]{3,2,1,0:T(8,128)S(1)}, f32[12,4,32,128]{3,2,1,0:T(8,128)S(1)}, u32[]{:S(2)}, u32[]{:S(2)}) %collective-permute-start.5) | collective-permute-done | bytes 786464 | tf_op jit(solution)/shard_map/ppermute | solution.py:24
  55.2 4.0 %fusion.61 = f32[12,4,32,128]{3,2,1,0:T(8,128)S(1)} fusion(f32[12,4,32,128]{3,2,1,0:T(8,128)S(1)} %collective-permute-done.5, f32[12,4,32,128]{3,2,1,0:T(8,128)S(1)} %fusion.86, f32[12,4,32,128]{3,2,1,0:T(8,128)S(1)} %collective-permute-done.4, f32[12,4,31,128]{3,2,1,0:T(8,128)S(1)} %get-tuple-element.103, f32[12,4,1,128]{3,2,1,0:T(1,128)S(1)} %get-tuple-element.105, ...), kind=kLoop, calls=%fused_computation.95 | loop fusion | flops 11599872 | bytes 16580608 | tf_op jit(solution)/shard_map/sub | solution.py:177
  63.0 8.4 %collective-permute-done.6 = f32[12,4,32,128]{3,2,1,0:T(8,128)S(1)} collective-permute-done((f32[12,4,32,128]{3,2,1,0:T(8,128)S(1)}, f32[12,4,32,128]{3,2,1,0:T(8,128)S(1)}, u32[]{:S(2)}, u32[]{:S(2)}) %collective-permute-start.6) | collective-permute-done | bytes 786464 | tf_op jit(solution)/shard_map/ppermute | solution.py:25
  71.4 3.1 %collective-permute-done.7 = f32[12,4,32,128]{3,2,1,0:T(8,128)S(1)} collective-permute-done((f32[12,4,32,128]{3,2,1,0:T(8,128)S(1)}, f32[12,4,32,128]{3,2,1,0:T(8,128)S(1)}, u32[]{:S(2)}, u32[]{:S(2)}) %collective-permute-start.7) | collective-permute-done | bytes 786464 | tf_op jit(solution)/shard_map/ppermute | solution.py:24
  74.5 3.8 %fusion.36 = f32[12,4,32,128]{3,2,1,0:T(8,128)S(1)} fusion(f32[12,4,32,128]{3,2,1,0:T(8,128)S(1)} %fusion.86, f32[12,4,32,128]{3,2,1,0:T(8,128)S(1)} %collective-permute-done.7, f32[12,4,32,128]{3,2,1,0:T(8,128)S(1)} %fusion.61, f32[12,4,32,128]{3,2,1,0:T(8,128)S(1)} %collective-permute-done.6, f32[12,4,31,128]{3,2,1,0:T(8,128)S(1)} %get-tuple-element.71, ...), kind=kLoop, calls=%fused_computation.70 | loop fusion | flops 11403264 | bytes 16580608 | tf_op jit(solution)/shard_map/sub | solution.py:177
  82.0 8.4 %collective-permute-done.8 = f32[12,4,32,128]{3,2,1,0:T(8,128)S(1)} collective-permute-done((f32[12,4,32,128]{3,2,1,0:T(8,128)S(1)}, f32[12,4,32,128]{3,2,1,0:T(8,128)S(1)}, u32[]{:S(2)}, u32[]{:S(2)}) %collective-permute-start.8) | collective-permute-done | bytes 786464 | tf_op jit(solution)/shard_map/ppermute | solution.py:25
  90.4 3.1 %collective-permute-done.9 = f32[12,4,32,128]{3,2,1,0:T(8,128)S(1)} collective-permute-done((f32[12,4,32,128]{3,2,1,0:T(8,128)S(1)}, f32[12,4,32,128]{3,2,1,0:T(8,128)S(1)}, u32[]{:S(2)}, u32[]{:S(2)}) %collective-permute-start.9) | collective-permute-done | bytes 786464 | tf_op jit(solution)/shard_map/ppermute | solution.py:24
  93.5 3.7 %fusion.11 = f32[12,4,32,128]{3,2,1,0:T(8,128)S(1)} fusion(f32[12,4,32,128]{3,2,1,0:T(8,128)S(1)} %collective-permute-done.9, f32[12,4,32,128]{3,2,1,0:T(8,128)S(1)} %fusion.36, f32[12,4,32,128]{3,2,1,0:T(8,128)S(1)} %collective-permute-done.8, f32[12,4,31,128]{3,2,1,0:T(8,128)S(1)} %get-tuple-element.39, f32[12,4,1,128]{3,2,1,0:T(1,128)S(1)} %get-tuple-element.41, ...), kind=kLoop, calls=%fused_computation.45 | loop fusion | flops 10616832 | bytes 15794176 | tf_op jit(solution)/shard_map/sub | solution.py:51
  98.7 8.4 %all-to-all-start = ((f32[2,12,16,8,128]{4,3,1,0,2:T(8,128)}), f32[2,12,16,8,128]{4,3,1,0,2:T(8,128)S(1)}, u32[]{:S(2)}, u32[]{:S(2)}) async-start(f32[2,12,16,8,128]{4,3,1,0,2:T(8,128)} %copy.18), calls=%async_computation | async-start | bytes 3145728 | tf_op jit(solution)/shard_map/all_to_all | solution.py:184
  107.2 20.9 %all-to-all-done = f32[2,12,16,8,128]{4,3,1,0,2:T(8,128)S(1)} async-done(((f32[2,12,16,8,128]{4,3,1,0,2:T(8,128)}), f32[2,12,16,8,128]{4,3,1,0,2:T(8,128)S(1)}, u32[]{:S(2)}, u32[]{:S(2)}) %all-to-all-start) | async-done | bytes 1572896 | tf_op jit(solution)/shard_map/all_to_all | solution.py:184
  130.1 4.7 %shard_map.41 = (f32[192,192]{1,0:T(8,128)}, f32[192,192]{1,0:T(8,128)}) custom-call(f32[1536,128]{1,0:T(8,128)} %bitcast.26, f32[1536,128]{1,0:T(8,128)} %bitcast.33), custom_call_target="tpu_custom_call" | custom-call | tf_op jit(solution)/shard_map/pallas_call | solution.py:146
  135.9 3.2 %gather_fusion = f32[192]{0:T(256)S(1)} fusion(f32[192,192]{1,0:T(8,128)} %get-tuple-element.5, s32[192]{0:T(256)S(1)} %bitcast.25), kind=kCustom, calls=%fused_computation | custom fusion | bytes 3072 | tf_op jit(solution)/shard_map/jit(diagonal)/cond/branch_0_fun/gather | solution.py:192
  143.0 5.9 %collective-permute-done.11 = f32[200,192]{1,0:T(8,128)S(1)} collective-permute-done((f32[200,192]{1,0:T(8,128)S(1)}, f32[200,192]{1,0:T(8,128)S(1)}, u32[]{:S(2)}, u32[]{:S(2)}) %collective-permute-start.11) | collective-permute-done | bytes 153632 | tf_op jit(solution)/shard_map/ppermute | solution.py:63
  150.5 3.5 %collective-permute-done.13 = f32[200,192]{1,0:T(8,128)S(1)} collective-permute-done((f32[200,192]{1,0:T(8,128)S(1)}, f32[200,192]{1,0:T(8,128)S(1)}, u32[]{:S(2)}, u32[]{:S(2)}) %collective-permute-start.13) | collective-permute-done | bytes 153632 | tf_op jit(solution)/shard_map/ppermute | solution.py:63
  154.3 2.5 %collective-permute-start.15 = (f32[200,192]{1,0:T(8,128)S(1)}, f32[200,192]{1,0:T(8,128)S(1)}, u32[]{:S(2)}, u32[]{:S(2)}) collective-permute-start(f32[200,192]{1,0:T(8,128)S(1)} %add_add_fusion.1), channel_id=1, source_target_pairs={{0,2},{1,3},{2,0},{3,1},{4,6},{5,7},{6,4},{7,5},{8,10},{9,11},{10,... | collective-permute-start | bytes 460808 | tf_op jit(solution)/shard_map/ppermute | solution.py:63
  156.8 5.4 %collective-permute-done.14 = f32[200,192]{1,0:T(8,128)S(1)} collective-permute-done((f32[200,192]{1,0:T(8,128)S(1)}, f32[200,192]{1,0:T(8,128)S(1)}, u32[]{:S(2)}, u32[]{:S(2)}) %collective-permute-start.14) | collective-permute-done | bytes 153632 | tf_op jit(solution)/shard_map/ppermute | solution.py:63
  163.8 3.4 %collective-permute-done.16 = f32[200,192]{1,0:T(8,128)S(1)} collective-permute-done((f32[200,192]{1,0:T(8,128)S(1)}, f32[200,192]{1,0:T(8,128)S(1)}, u32[]{:S(2)}, u32[]{:S(2)}) %collective-permute-start.16) | collective-permute-done | bytes 153632 | tf_op jit(solution)/shard_map/ppermute | solution.py:63
  170.3 5.0 %collective-permute-done.17 = f32[200,192]{1,0:T(8,128)S(1)} collective-permute-done((f32[200,192]{1,0:T(8,128)S(1)}, f32[200,192]{1,0:T(8,128)S(1)}, u32[]{:S(2)}, u32[]{:S(2)}) %collective-permute-start.17) | collective-permute-done | bytes 153632 | tf_op jit(solution)/shard_map/ppermute | solution.py:63
  175.4 2.5 %collective-permute-done.18 = f32[200,192]{1,0:T(8,128)S(1)} collective-permute-done((f32[200,192]{1,0:T(8,128)S(1)}, f32[200,192]{1,0:T(8,128)S(1)}, u32[]{:S(2)}, u32[]{:S(2)}) %collective-permute-start.18) | collective-permute-done | bytes 153632 | tf_op jit(solution)/shard_map/ppermute | solution.py:63
  177.9 3.1 %collective-permute-done.19 = f32[200,192]{1,0:T(8,128)S(1)} collective-permute-done((f32[200,192]{1,0:T(8,128)S(1)}, f32[200,192]{1,0:T(8,128)S(1)}, u32[]{:S(2)}, u32[]{:S(2)}) %collective-permute-start.19) | collective-permute-done | bytes 153632 | tf_op jit(solution)/shard_map/ppermute | solution.py:63
  184.4 27.0 %shard_map.42 = f32[192,192]{1,0:T(8,128)} custom-call(f32[192,192]{1,0:T(8,128)} %reshape.35.c_ref), custom_call_target="tpu_custom_call" | custom-call | tf_op jit(solution)/shard_map/pallas_call | solution.py:130
  215.6 3.5 %shard_map.43 = f32[1536,128]{1,0:T(8,128)} custom-call(f32[192,192]{1,0:T(8,128)} %reshape.37.refs_0_, f32[1536,128]{1,0:T(8,128)} %bitcast.27), custom_call_target="tpu_custom_call" | custom-call | tf_op jit(solution)/shard_map/pallas_call | solution.py:155
  221.2 4.3 %all-to-all-start.1 = ((f32[12,16,8,128]{3,2,0,1:T(8,128)}), f32[12,16,8,128]{3,2,0,1:T(8,128)}, u32[]{:S(2)}, u32[]{:S(2)}) async-start(f32[12,16,8,128]{3,2,0,1:T(8,128)} %copy.24), calls=%async_computation.1 | async-start | bytes 1572864 | tf_op jit(solution)/shard_map/all_to_all | solution.py:209
  229.2 11.2 %all-to-all-done.1 = f32[12,16,8,128]{3,2,0,1:T(8,128)} async-done(((f32[12,16,8,128]{3,2,0,1:T(8,128)}), f32[12,16,8,128]{3,2,0,1:T(8,128)}, u32[]{:S(2)}, u32[]{:S(2)}) %all-to-all-start.1) | async-done | bytes 786464 | tf_op jit(solution)/shard_map/all_to_all | solution.py:209
  (142 shorter events, 50.0 us)
Async XLA Ops:
  0.6 4.6 %copy-start = (f32[12,4,32,128]{3,2,1,0:T(8,128)S(1)}, f32[12,4,32,128]{3,2,1,0:T(8,128)}, u32[]{:S(2)}) copy-start(f32[12,4,32,128]{3,2,1,0:T(8,128)} %param.2) | copy-start | bytes 2359300
  0.6 12.8 %collective-permute-start.1 = (f32[12,4,32,128]{3,2,1,0:T(8,128)}, f32[12,4,32,128]{3,2,1,0:T(8,128)S(1)}, u32[]{:S(2)}, u32[]{:S(2)}) collective-permute-start(f32[12,4,32,128]{3,2,1,0:T(8,128)} %param.2), channel_id=1, source_target_pairs={{0,16},{16,32},{32,48},{48,64},{64,80},{80,96},{96,112},{112,0},{1... | collective-permute-start | bytes 2359304 | tf_op jit(solution)/shard_map/ppermute | solution.py:24
  0.7 13.1 %collective-permute-start = (f32[12,4,32,128]{3,2,1,0:T(8,128)}, f32[12,4,32,128]{3,2,1,0:T(8,128)S(1)}, u32[]{:S(2)}, u32[]{:S(2)}) collective-permute-start(f32[12,4,32,128]{3,2,1,0:T(8,128)} %param.2), channel_id=1, source_target_pairs={{16,0},{32,16},{48,32},{64,48},{80,64},{96,80},{112,96},{0,112},{1... | collective-permute-start | bytes 2359304 | tf_op jit(solution)/shard_map/ppermute | solution.py:25
  7.8 0.8 copy-start.2
  20.9 12.2 %collective-permute-start.2 = (f32[12,4,32,128]{3,2,1,0:T(8,128)S(1)}, f32[12,4,32,128]{3,2,1,0:T(8,128)S(1)}, u32[]{:S(2)}, u32[]{:S(2)}) collective-permute-start(f32[12,4,32,128]{3,2,1,0:T(8,128)S(1)} %get-tuple-element.6), channel_id=1, source_target_pairs={{16,0},{32,16},{48,32},{64,48},{80,64},{96,80},{112,96},{0,112},{1... | collective-permute-start | bytes 2359304 | tf_op jit(solution)/shard_map/ppermute | solution.py:25
  23.6 12.6 %collective-permute-start.3 = (f32[12,4,32,128]{3,2,1,0:T(8,128)S(1)}, f32[12,4,32,128]{3,2,1,0:T(8,128)S(1)}, u32[]{:S(2)}, u32[]{:S(2)}) collective-permute-start(f32[12,4,32,128]{3,2,1,0:T(8,128)S(1)} %get-tuple-element.6), channel_id=1, source_target_pairs={{0,16},{16,32},{32,48},{48,64},{64,80},{80,96},{96,112},{112,0},{1... | collective-permute-start | bytes 2359304 | tf_op jit(solution)/shard_map/ppermute | solution.py:24
  42.6 9.5 %collective-permute-start.4 = (f32[12,4,32,128]{3,2,1,0:T(8,128)S(1)}, f32[12,4,32,128]{3,2,1,0:T(8,128)S(1)}, u32[]{:S(2)}, u32[]{:S(2)}) collective-permute-start(f32[12,4,32,128]{3,2,1,0:T(8,128)S(1)} %fusion.86), channel_id=1, source_target_pairs={{16,0},{32,16},{48,32},{64,48},{80,64},{96,80},{112,96},{0,112},{1... | collective-permute-start | bytes 2359304 | tf_op jit(solution)/shard_map/ppermute | solution.py:25
  42.6 12.6 %collective-permute-start.5 = (f32[12,4,32,128]{3,2,1,0:T(8,128)S(1)}, f32[12,4,32,128]{3,2,1,0:T(8,128)S(1)}, u32[]{:S(2)}, u32[]{:S(2)}) collective-permute-start(f32[12,4,32,128]{3,2,1,0:T(8,128)S(1)} %fusion.86), channel_id=1, source_target_pairs={{0,16},{16,32},{32,48},{48,64},{64,80},{80,96},{96,112},{112,0},{1... | collective-permute-start | bytes 2359304 | tf_op jit(solution)/shard_map/ppermute | solution.py:24
  61.8 9.5 %collective-permute-start.6 = (f32[12,4,32,128]{3,2,1,0:T(8,128)S(1)}, f32[12,4,32,128]{3,2,1,0:T(8,128)S(1)}, u32[]{:S(2)}, u32[]{:S(2)}) collective-permute-start(f32[12,4,32,128]{3,2,1,0:T(8,128)S(1)} %fusion.61), channel_id=1, source_target_pairs={{16,0},{32,16},{48,32},{64,48},{80,64},{96,80},{112,96},{0,112},{1... | collective-permute-start | bytes 2359304 | tf_op jit(solution)/shard_map/ppermute | solution.py:25
  61.9 12.6 %collective-permute-start.7 = (f32[12,4,32,128]{3,2,1,0:T(8,128)S(1)}, f32[12,4,32,128]{3,2,1,0:T(8,128)S(1)}, u32[]{:S(2)}, u32[]{:S(2)}) collective-permute-start(f32[12,4,32,128]{3,2,1,0:T(8,128)S(1)} %fusion.61), channel_id=1, source_target_pairs={{0,16},{16,32},{32,48},{48,64},{64,80},{80,96},{96,112},{112,0},{1... | collective-permute-start | bytes 2359304 | tf_op jit(solution)/shard_map/ppermute | solution.py:24
  80.9 9.5 %collective-permute-start.8 = (f32[12,4,32,128]{3,2,1,0:T(8,128)S(1)}, f32[12,4,32,128]{3,2,1,0:T(8,128)S(1)}, u32[]{:S(2)}, u32[]{:S(2)}) collective-permute-start(f32[12,4,32,128]{3,2,1,0:T(8,128)S(1)} %fusion.36), channel_id=1, source_target_pairs={{16,0},{32,16},{48,32},{64,48},{80,64},{96,80},{112,96},{0,112},{1... | collective-permute-start | bytes 2359304 | tf_op jit(solution)/shard_map/ppermute | solution.py:25
  80.9 12.6 %collective-permute-start.9 = (f32[12,4,32,128]{3,2,1,0:T(8,128)S(1)}, f32[12,4,32,128]{3,2,1,0:T(8,128)S(1)}, u32[]{:S(2)}, u32[]{:S(2)}) collective-permute-start(f32[12,4,32,128]{3,2,1,0:T(8,128)S(1)} %fusion.36), channel_id=1, source_target_pairs={{0,16},{16,32},{32,48},{48,64},{64,80},{80,96},{96,112},{112,0},{1... | collective-permute-start | bytes 2359304 | tf_op jit(solution)/shard_map/ppermute | solution.py:24
  98.7 29.4 %all-to-all-start = ((f32[2,12,16,8,128]{4,3,1,0,2:T(8,128)}), f32[2,12,16,8,128]{4,3,1,0,2:T(8,128)S(1)}, u32[]{:S(2)}, u32[]{:S(2)}) async-start(f32[2,12,16,8,128]{4,3,1,0,2:T(8,128)} %copy.18), calls=%async_computation | async-start | bytes 3145728 | tf_op jit(solution)/shard_map/all_to_all | solution.py:184
  139.2 1.5 collective-permute-start.10
  140.9 8.0 %collective-permute-start.11 = (f32[200,192]{1,0:T(8,128)S(1)}, f32[200,192]{1,0:T(8,128)S(1)}, u32[]{:S(2)}, u32[]{:S(2)}) collective-permute-start(f32[200,192]{1,0:T(8,128)S(1)} %select_add_fusion), channel_id=1, source_target_pairs={{0,96},{16,112},{32,0},{48,16},{64,32},{80,48},{96,64},{112,80},{1... | collective-permute-start | bytes 460808 | tf_op jit(solution)/shard_map/ppermute | solution.py:63
  141.0 9.6 %collective-permute-start.12 = (f32[200,192]{1,0:T(8,128)S(1)}, f32[200,192]{1,0:T(8,128)S(1)}, u32[]{:S(2)}, u32[]{:S(2)}) collective-permute-start(f32[200,192]{1,0:T(8,128)S(1)} %select_add_fusion), channel_id=1, source_target_pairs={{0,64},{16,80},{32,96},{48,112},{64,0},{80,16},{96,32},{112,48},{1... | collective-permute-start | bytes 460808 | tf_op jit(solution)/shard_map/ppermute | solution.py:63
  142.2 11.9 %collective-permute-start.13 = (f32[200,192]{1,0:T(8,128)S(1)}, f32[200,192]{1,0:T(8,128)S(1)}, u32[]{:S(2)}, u32[]{:S(2)}) collective-permute-start(f32[200,192]{1,0:T(8,128)S(1)} %select_add_fusion), channel_id=1, source_target_pairs={{0,32},{16,48},{32,64},{48,80},{64,96},{80,112},{96,0},{112,16},{1... | collective-permute-start | bytes 460808 | tf_op jit(solution)/shard_map/ppermute | solution.py:63
  154.2 8.0 %collective-permute-start.14 = (f32[200,192]{1,0:T(8,128)S(1)}, f32[200,192]{1,0:T(8,128)S(1)}, u32[]{:S(2)}, u32[]{:S(2)}) collective-permute-start(f32[200,192]{1,0:T(8,128)S(1)} %add_add_fusion.1), channel_id=1, source_target_pairs={{0,3},{1,0},{2,1},{3,2},{4,7},{5,4},{6,5},{7,6},{8,11},{9,8},{10,9... | collective-permute-start | bytes 460808 | tf_op jit(solution)/shard_map/ppermute | solution.py:63
  154.3 9.6 %collective-permute-start.15 = (f32[200,192]{1,0:T(8,128)S(1)}, f32[200,192]{1,0:T(8,128)S(1)}, u32[]{:S(2)}, u32[]{:S(2)}) collective-permute-start(f32[200,192]{1,0:T(8,128)S(1)} %add_add_fusion.1), channel_id=1, source_target_pairs={{0,2},{1,3},{2,0},{3,1},{4,6},{5,7},{6,4},{7,5},{8,10},{9,11},{10,... | collective-permute-start | bytes 460808 | tf_op jit(solution)/shard_map/ppermute | solution.py:63
  156.7 10.5 %collective-permute-start.16 = (f32[200,192]{1,0:T(8,128)S(1)}, f32[200,192]{1,0:T(8,128)S(1)}, u32[]{:S(2)}, u32[]{:S(2)}) collective-permute-start(f32[200,192]{1,0:T(8,128)S(1)} %add_add_fusion.1), channel_id=1, source_target_pairs={{0,1},{1,2},{2,3},{3,0},{4,5},{5,6},{6,7},{7,4},{8,9},{9,10},{10,1... | collective-permute-start | bytes 460808 | tf_op jit(solution)/shard_map/ppermute | solution.py:63
  167.3 8.0 %collective-permute-start.17 = (f32[200,192]{1,0:T(8,128)S(1)}, f32[200,192]{1,0:T(8,128)S(1)}, u32[]{:S(2)}, u32[]{:S(2)}) collective-permute-start(f32[200,192]{1,0:T(8,128)S(1)} %add_add_fusion), channel_id=1, source_target_pairs={{0,12},{1,13},{2,14},{3,15},{4,0},{5,1},{6,2},{7,3},{8,4},{9,5},{1... | collective-permute-start | bytes 460808 | tf_op jit(solution)/shard_map/ppermute | solution.py:63
  168.4 9.5 %collective-permute-start.18 = (f32[200,192]{1,0:T(8,128)S(1)}, f32[200,192]{1,0:T(8,128)S(1)}, u32[]{:S(2)}, u32[]{:S(2)}) collective-permute-start(f32[200,192]{1,0:T(8,128)S(1)} %add_add_fusion), channel_id=1, source_target_pairs={{0,8},{1,9},{2,10},{3,11},{4,12},{5,13},{6,14},{7,15},{8,0},{9,1},... | collective-permute-start | bytes 460808 | tf_op jit(solution)/shard_map/ppermute | solution.py:63
  169.9 11.1 %collective-permute-start.19 = (f32[200,192]{1,0:T(8,128)S(1)}, f32[200,192]{1,0:T(8,128)S(1)}, u32[]{:S(2)}, u32[]{:S(2)}) collective-permute-start(f32[200,192]{1,0:T(8,128)S(1)} %add_add_fusion), channel_id=1, source_target_pairs={{0,4},{1,5},{2,6},{3,7},{4,8},{5,9},{6,10},{7,11},{8,12},{9,13},{1... | collective-permute-start | bytes 460808 | tf_op jit(solution)/shard_map/ppermute | solution.py:63
  221.2 19.1 %all-to-all-start.1 = ((f32[12,16,8,128]{3,2,0,1:T(8,128)}), f32[12,16,8,128]{3,2,0,1:T(8,128)}, u32[]{:S(2)}, u32[]{:S(2)}) async-start(f32[12,16,8,128]{3,2,0,1:T(8,128)} %copy.24), calls=%async_computation.1 | async-start | bytes 1572864 | tf_op jit(solution)/shard_map/all_to_all | solution.py:209
  227.2 0.9 copy-start.1

commit v5 on v4

--- a/solution.py
+++ b/solution.py
@@ -6,6 +6,7 @@
 from jax.sharding import PartitionSpec as P
 
 DEGREE = 4
+CHUNKS = 2
 
 
 stencil_coef = (-205.0 / 72.0, 8.0 / 5.0, -1.0 / 5.0, 8.0 / 315.0, -1.0 / 560.0)
@@ -171,12 +172,15 @@
         padded = extended(field, (("dom", 1),), stencil_reach)
         return hamiltonian(field, padded, potential)
 
-    previous = psi
-    current = (apply(psi) - center * psi) / half
+    chunks = CHUNKS if bdev % CHUNKS == 0 else 1
+    width = bdev // chunks
+    previous = [psi[i * width : (i + 1) * width] for i in range(chunks)]
+    current = [(apply(p) - center * p) / half for p in previous]
     for order in range(1, DEGREE):
-        following = 2.0 / half * (apply(current) - center * current) - previous
+        following = [2.0 / half * (apply(c) - center * c) - p for c, p in zip(current, previous)]
         previous, current = (current, following)
-    image = apply(current)
+    image = jnp.concatenate([apply(c) for c in current])
+    current = jnp.concatenate(current)
     groups = lax.axis_size("band")
     rows = depth * rows_y * rows_x // groups // rows_x
     lanes = rows_x

time: 246 us -> 224 us (0.911)
  waiting for transfers between devices: 117 us -> 79.9 us
  starting transfers between devices: 27.6 us -> 42.4 us
    ppermute x5 -> x10, waiting for transfers between devices: 34.1 us -> 2.16 us  [extended(): after = lax.ppermute(initial, axis, down)]
    ppermute x5 -> x10, starting transfers between devices: 5.66 us -> 19.5 us  [extended(): after = lax.ppermute(initial, axis, down)]
    ppermute x5 -> x10, waiting for transfers between devices: 17.1 us -> 14.5 us  [extended(): before = lax.ppermute(last, axis, up)]
    slice x40 -> x72, local copies, waits for them, and re-layouts: 11.8 us -> 14.3 us  [hamiltonian(): near = near + jnp.roll(field, reach, 3) + jnp.roll(field, -reach, 3)]
    slice x40 -> x72, local copies, waits for them, and re-layouts: 5.31 us -> 3.54 us  [hamiltonian(): near = near + jnp.roll(field, reach, 2) + jnp.roll(field, -reach, 2)]
    sub x3 -> x6, other arithmetic: 11.5 us -> 11.3 us  [local(): 2.0 / half * (apply(c) - center * c) - p]
  transfers between devices with their start and end apart: 22 -> 32, of which waited for: 21 -> 22; matrix products, arithmetic and copies ran while one was open for 4% -> 17% of each run, Pallas kernels for 0% -> 0%
where the time goes in v5:
time: 224 us; the launch traced here: 221 us
  waiting for transfers between devices  79.9 us (36%)
  starting transfers between devices  42.4 us (19%)
  local copies, waits for them, and re-layouts  40.3 us (18%)
  Pallas kernels  35.2 us (16%)
  other arithmetic  20.3 us (9%)
    ppermute x10, waiting for transfers between devices, group_sum(): received.append(lax.ppermute(x, axis, pairs))  32.3 us
    pallas_call x1, Pallas kernels, lower_inverse(): pl.pallas_call(inverse_kernel, out_shape=jax.ShapeDtypeStruct((n, n), jnp...  26.9 us
    all_to_all x1, waiting for transfers between devices, local(): spread = lax.all_to_all(chunked, 'band', 2, 2, tiled=True)  19.8 us
    ppermute x10, starting transfers between devices, extended(): after = lax.ppermute(initial, axis, down)  19.5 us
    ppermute x10, waiting for transfers between devices, extended(): before = lax.ppermute(last, axis, up)  14.5 us
    slice x72, local copies, waits for them, and re-layouts, hamiltonian(): near = near + jnp.roll(field, reach, 3) + jnp.roll(field, -reach, 3)  14.3 us
    sub x6, other arithmetic, local(): 2.0 / half * (apply(c) - center * c) - p  11.3 us
    all_to_all x1, waiting for transfers between devices, local(): lax.all_to_all(basis_cd, 'band', 1, 1, tiled=True).reshape(psi.shape)  11.1 us
  transfers between devices with their start and end apart: 32, of which 22 were waited for; matrix products, arithmetic and copies ran while one was open for 17% of the time, Pallas kernels for 0%

profile of v5, /device:TPU:0, one launch (start us, length us, event | category | flops | bytes accessed | tf_op | source)
XLA Modules:
  0.0 221.0 jit_solution(13233511829439888195)
XLA Ops:
  1.9 2.3 %collective-permute-start = (f32[6,4,32,128]{3,2,1,0:T(8,128)S(1)}, f32[6,4,32,128]{3,2,1,0:T(8,128)S(1)}, u32[]{:S(2)}, u32[]{:S(2)}) collective-permute-start(f32[6,4,32,128]{3,2,1,0:T(8,128)S(1)} %get-tuple-element.76), channel_id=1, source_target_pairs={{16,0},{32,16},{48,32},{64,48},{80,64},{96,80},{112,96},{0,112},{1... | collective-permute-start | bytes 1179656 | tf_op jit(solution)/shard_map/ppermute | solution.py:26
  4.2 3.0 %collective-permute-start.8 = (f32[6,4,32,128]{3,2,1,0:T(8,128)S(1)}, f32[6,4,32,128]{3,2,1,0:T(8,128)S(1)}, u32[]{:S(2)}, u32[]{:S(2)}) collective-permute-start(f32[6,4,32,128]{3,2,1,0:T(8,128)S(1)} %get-tuple-element.77), channel_id=1, source_target_pairs={{16,0},{32,16},{48,32},{64,48},{80,64},{96,80},{112,96},{0,112},{1... | collective-permute-start | bytes 1179656 | tf_op jit(solution)/shard_map/ppermute | solution.py:26
  10.7 1.9 collective-permute-done.1
  12.6 1.9 broadcast_multiply_fusion.1
  17.7 1.9 broadcast_multiply_fusion
  21.4 3.0 %collective-permute-start.10 = (f32[6,4,32,128]{3,2,1,0:T(8,128)S(1)}, f32[6,4,32,128]{3,2,1,0:T(8,128)S(1)}, u32[]{:S(2)}, u32[]{:S(2)}) collective-permute-start(f32[6,4,32,128]{3,2,1,0:T(8,128)S(1)} %get-tuple-element.8), channel_id=1, source_target_pairs={{16,0},{32,16},{48,32},{64,48},{80,64},{96,80},{112,96},{0,112},{1... | collective-permute-start | bytes 1179656 | tf_op jit(solution)/shard_map/ppermute | solution.py:26
  32.8 1.9 fusion.108
  46.4 2.0 fusion.83
  53.3 1.9 fusion.156
  56.7 1.9 collective-permute-start.16
  68.7 2.1 collective-permute-done.18
  70.8 3.1 %collective-permute-done.19 = f32[6,4,32,128]{3,2,1,0:T(8,128)S(1)} collective-permute-done((f32[6,4,32,128]{3,2,1,0:T(8,128)S(1)}, f32[6,4,32,128]{3,2,1,0:T(8,128)S(1)}, u32[]{:S(2)}, u32[]{:S(2)}) %collective-permute-start.19) | collective-permute-done | bytes 393248 | tf_op jit(solution)/shard_map/ppermute | solution.py:25
  77.2 8.5 %all-to-all-start = ((f32[2,12,16,8,128]{4,3,1,0,2:T(8,128)}), f32[2,12,16,8,128]{4,3,1,0,2:T(8,128)S(1)}, u32[]{:S(2)}, u32[]{:S(2)}) async-start(f32[2,12,16,8,128]{4,3,1,0,2:T(8,128)} %copy.18), calls=%async_computation | async-start | bytes 3145728 | tf_op jit(solution)/shard_map/all_to_all | solution.py:188
  85.7 19.8 %all-to-all-done = f32[2,12,16,8,128]{4,3,1,0,2:T(8,128)S(1)} async-done(((f32[2,12,16,8,128]{4,3,1,0,2:T(8,128)}), f32[2,12,16,8,128]{4,3,1,0,2:T(8,128)S(1)}, u32[]{:S(2)}, u32[]{:S(2)}) %all-to-all-start) | async-done | bytes 1572896 | tf_op jit(solution)/shard_map/all_to_all | solution.py:188
  107.5 4.8 %shard_map.41 = (f32[192,192]{1,0:T(8,128)}, f32[192,192]{1,0:T(8,128)}) custom-call(f32[1536,128]{1,0:T(8,128)} %bitcast.25, f32[1536,128]{1,0:T(8,128)} %bitcast.31), custom_call_target="tpu_custom_call" | custom-call | tf_op jit(solution)/shard_map/pallas_call | solution.py:147
  113.3 3.2 %gather_fusion = f32[192]{0:T(256)S(1)} fusion(f32[192,192]{1,0:T(8,128)} %get-tuple-element.5, s32[192]{0:T(256)S(1)} %bitcast.24), kind=kCustom, calls=%fused_computation | custom fusion | bytes 3072 | tf_op jit(solution)/shard_map/jit(diagonal)/cond/branch_0_fun/gather | solution.py:196
  119.0 2.4 %collective-permute-start.22 = (f32[200,192]{1,0:T(8,128)S(1)}, f32[200,192]{1,0:T(8,128)S(1)}, u32[]{:S(2)}, u32[]{:S(2)}) collective-permute-start(f32[200,192]{1,0:T(8,128)S(1)} %select_add_fusion), channel_id=1, source_target_pairs={{0,64},{16,80},{32,96},{48,112},{64,0},{80,16},{96,32},{112,48},{1... | collective-permute-start | bytes 460808 | tf_op jit(solution)/shard_map/ppermute | solution.py:64
  122.8 3.5 %collective-permute-done.21 = f32[200,192]{1,0:T(8,128)S(1)} collective-permute-done((f32[200,192]{1,0:T(8,128)S(1)}, f32[200,192]{1,0:T(8,128)S(1)}, u32[]{:S(2)}, u32[]{:S(2)}) %collective-permute-start.21) | collective-permute-done | bytes 153632 | tf_op jit(solution)/shard_map/ppermute | solution.py:64
  126.3 2.2 collective-permute-done.22
  128.5 3.5 %collective-permute-done.23 = f32[200,192]{1,0:T(8,128)S(1)} collective-permute-done((f32[200,192]{1,0:T(8,128)S(1)}, f32[200,192]{1,0:T(8,128)S(1)}, u32[]{:S(2)}, u32[]{:S(2)}) %collective-permute-start.23) | collective-permute-done | bytes 153632 | tf_op jit(solution)/shard_map/ppermute | solution.py:64
  132.2 2.0 collective-permute-start.25
  134.2 5.9 %collective-permute-done.24 = f32[200,192]{1,0:T(8,128)S(1)} collective-permute-done((f32[200,192]{1,0:T(8,128)S(1)}, f32[200,192]{1,0:T(8,128)S(1)}, u32[]{:S(2)}, u32[]{:S(2)}) %collective-permute-start.24) | collective-permute-done | bytes 153632 | tf_op jit(solution)/shard_map/ppermute | solution.py:64
  141.8 3.4 %collective-permute-done.26 = f32[200,192]{1,0:T(8,128)S(1)} collective-permute-done((f32[200,192]{1,0:T(8,128)S(1)}, f32[200,192]{1,0:T(8,128)S(1)}, u32[]{:S(2)}, u32[]{:S(2)}) %collective-permute-start.26) | collective-permute-done | bytes 153632 | tf_op jit(solution)/shard_map/ppermute | solution.py:64
  148.7 4.6 %collective-permute-done.27 = f32[200,192]{1,0:T(8,128)S(1)} collective-permute-done((f32[200,192]{1,0:T(8,128)S(1)}, f32[200,192]{1,0:T(8,128)S(1)}, u32[]{:S(2)}, u32[]{:S(2)}) %collective-permute-start.27) | collective-permute-done | bytes 153632 | tf_op jit(solution)/shard_map/ppermute | solution.py:64
  153.3 3.1 %collective-permute-done.28 = f32[200,192]{1,0:T(8,128)S(1)} collective-permute-done((f32[200,192]{1,0:T(8,128)S(1)}, f32[200,192]{1,0:T(8,128)S(1)}, u32[]{:S(2)}, u32[]{:S(2)}) %collective-permute-start.28) | collective-permute-done | bytes 153632 | tf_op jit(solution)/shard_map/ppermute | solution.py:64
  156.4 3.1 %collective-permute-done.29 = f32[200,192]{1,0:T(8,128)S(1)} collective-permute-done((f32[200,192]{1,0:T(8,128)S(1)}, f32[200,192]{1,0:T(8,128)S(1)}, u32[]{:S(2)}, u32[]{:S(2)}) %collective-permute-start.29) | collective-permute-done | bytes 153632 | tf_op jit(solution)/shard_map/ppermute | solution.py:64
  162.9 26.9 %shard_map.42 = f32[192,192]{1,0:T(8,128)} custom-call(f32[192,192]{1,0:T(8,128)} %reshape.35.c_ref), custom_call_target="tpu_custom_call" | custom-call | tf_op jit(solution)/shard_map/pallas_call | solution.py:131
  194.0 3.5 %shard_map.43 = f32[1536,128]{1,0:T(8,128)} custom-call(f32[192,192]{1,0:T(8,128)} %reshape.37.refs_0_, f32[1536,128]{1,0:T(8,128)} %bitcast.26), custom_call_target="tpu_custom_call" | custom-call | tf_op jit(solution)/shard_map/pallas_call | solution.py:156
  197.5 2.1 copy.24
  199.6 4.3 %all-to-all-start.1 = ((f32[12,16,8,128]{3,2,0,1:T(8,128)}), f32[12,16,8,128]{3,2,0,1:T(8,128)}, u32[]{:S(2)}, u32[]{:S(2)}) async-start(f32[12,16,8,128]{3,2,0,1:T(8,128)} %copy.24), calls=%async_computation.1 | async-start | bytes 1572864 | tf_op jit(solution)/shard_map/all_to_all | solution.py:213
  207.6 11.1 %all-to-all-done.1 = f32[12,16,8,128]{3,2,0,1:T(8,128)} async-done(((f32[12,16,8,128]{3,2,0,1:T(8,128)}), f32[12,16,8,128]{3,2,0,1:T(8,128)}, u32[]{:S(2)}, u32[]{:S(2)}) %all-to-all-start.1) | async-done | bytes 786464 | tf_op jit(solution)/shard_map/all_to_all | solution.py:213
  218.7 2.1 copy.25
  (231 shorter events, 72.4 us)
Async XLA Ops:
  1.9 8.8 %collective-permute-start = (f32[6,4,32,128]{3,2,1,0:T(8,128)S(1)}, f32[6,4,32,128]{3,2,1,0:T(8,128)S(1)}, u32[]{:S(2)}, u32[]{:S(2)}) collective-permute-start(f32[6,4,32,128]{3,2,1,0:T(8,128)S(1)} %get-tuple-element.76), channel_id=1, source_target_pairs={{16,0},{32,16},{48,32},{64,48},{80,64},{96,80},{112,96},{0,112},{1... | collective-permute-start | bytes 1179656 | tf_op jit(solution)/shard_map/ppermute | solution.py:26
  4.2 8.4 %collective-permute-start.1 = (f32[6,4,32,128]{3,2,1,0:T(8,128)S(1)}, f32[6,4,32,128]{3,2,1,0:T(8,128)S(1)}, u32[]{:S(2)}, u32[]{:S(2)}) collective-permute-start(f32[6,4,32,128]{3,2,1,0:T(8,128)S(1)} %get-tuple-element.76), channel_id=1, source_target_pairs={{0,16},{16,32},{32,48},{48,64},{64,80},{80,96},{96,112},{112,0},{1... | collective-permute-start | bytes 1179656 | tf_op jit(solution)/shard_map/ppermute | solution.py:25
  4.2 13.4 %collective-permute-start.8 = (f32[6,4,32,128]{3,2,1,0:T(8,128)S(1)}, f32[6,4,32,128]{3,2,1,0:T(8,128)S(1)}, u32[]{:S(2)}, u32[]{:S(2)}) collective-permute-start(f32[6,4,32,128]{3,2,1,0:T(8,128)S(1)} %get-tuple-element.77), channel_id=1, source_target_pairs={{16,0},{32,16},{48,32},{64,48},{80,64},{96,80},{112,96},{0,112},{1... | collective-permute-start | bytes 1179656 | tf_op jit(solution)/shard_map/ppermute | solution.py:26
  7.2 10.5 %collective-permute-start.9 = (f32[6,4,32,128]{3,2,1,0:T(8,128)S(1)}, f32[6,4,32,128]{3,2,1,0:T(8,128)S(1)}, u32[]{:S(2)}, u32[]{:S(2)}) collective-permute-start(f32[6,4,32,128]{3,2,1,0:T(8,128)S(1)} %get-tuple-element.77), channel_id=1, source_target_pairs={{0,16},{16,32},{32,48},{48,64},{64,80},{80,96},{96,112},{112,0},{1... | collective-permute-start | bytes 1179656 | tf_op jit(solution)/shard_map/ppermute | solution.py:25
  16.4 8.0 %collective-permute-start.2 = (f32[6,4,32,128]{3,2,1,0:T(8,128)S(1)}, f32[6,4,32,128]{3,2,1,0:T(8,128)S(1)}, u32[]{:S(2)}, u32[]{:S(2)}) collective-permute-start(f32[6,4,32,128]{3,2,1,0:T(8,128)S(1)} %get-tuple-element.6), channel_id=1, source_target_pairs={{16,0},{32,16},{48,32},{64,48},{80,64},{96,80},{112,96},{0,112},{1... | collective-permute-start | bytes 1179656 | tf_op jit(solution)/shard_map/ppermute | solution.py:26
  17.6 8.4 %collective-permute-start.3 = (f32[6,4,32,128]{3,2,1,0:T(8,128)S(1)}, f32[6,4,32,128]{3,2,1,0:T(8,128)S(1)}, u32[]{:S(2)}, u32[]{:S(2)}) collective-permute-start(f32[6,4,32,128]{3,2,1,0:T(8,128)S(1)} %get-tuple-element.6), channel_id=1, source_target_pairs={{0,16},{16,32},{32,48},{48,64},{64,80},{80,96},{96,112},{112,0},{1... | collective-permute-start | bytes 1179656 | tf_op jit(solution)/shard_map/ppermute | solution.py:25
  21.4 9.9 %collective-permute-start.10 = (f32[6,4,32,128]{3,2,1,0:T(8,128)S(1)}, f32[6,4,32,128]{3,2,1,0:T(8,128)S(1)}, u32[]{:S(2)}, u32[]{:S(2)}) collective-permute-start(f32[6,4,32,128]{3,2,1,0:T(8,128)S(1)} %get-tuple-element.8), channel_id=1, source_target_pairs={{16,0},{32,16},{48,32},{64,48},{80,64},{96,80},{112,96},{0,112},{1... | collective-permute-start | bytes 1179656 | tf_op jit(solution)/shard_map/ppermute | solution.py:26
  24.4 8.4 %collective-permute-start.11 = (f32[6,4,32,128]{3,2,1,0:T(8,128)S(1)}, f32[6,4,32,128]{3,2,1,0:T(8,128)S(1)}, u32[]{:S(2)}, u32[]{:S(2)}) collective-permute-start(f32[6,4,32,128]{3,2,1,0:T(8,128)S(1)} %get-tuple-element.8), channel_id=1, source_target_pairs={{0,16},{16,32},{32,48},{48,64},{64,80},{80,96},{96,112},{112,0},{1... | collective-permute-start | bytes 1179656 | tf_op jit(solution)/shard_map/ppermute | solution.py:25
  29.6 8.6 %collective-permute-start.4 = (f32[6,4,32,128]{3,2,1,0:T(8,128)S(1)}, f32[6,4,32,128]{3,2,1,0:T(8,128)S(1)}, u32[]{:S(2)}, u32[]{:S(2)}) collective-permute-start(f32[6,4,32,128]{3,2,1,0:T(8,128)S(1)} %fusion.206), channel_id=1, source_target_pairs={{16,0},{32,16},{48,32},{64,48},{80,64},{96,80},{112,96},{0,112},{1... | collective-permute-start | bytes 1179656 | tf_op jit(solution)/shard_map/ppermute | solution.py:26
  31.1 8.4 %collective-permute-start.5 = (f32[6,4,32,128]{3,2,1,0:T(8,128)S(1)}, f32[6,4,32,128]{3,2,1,0:T(8,128)S(1)}, u32[]{:S(2)}, u32[]{:S(2)}) collective-permute-start(f32[6,4,32,128]{3,2,1,0:T(8,128)S(1)} %fusion.206), channel_id=1, source_target_pairs={{0,16},{16,32},{32,48},{48,64},{64,80},{80,96},{96,112},{112,0},{1... | collective-permute-start | bytes 1179656 | tf_op jit(solution)/shard_map/ppermute | solution.py:25
  36.4 8.7 %collective-permute-start.12 = (f32[6,4,32,128]{3,2,1,0:T(8,128)S(1)}, f32[6,4,32,128]{3,2,1,0:T(8,128)S(1)}, u32[]{:S(2)}, u32[]{:S(2)}) collective-permute-start(f32[6,4,32,128]{3,2,1,0:T(8,128)S(1)} %fusion.108), channel_id=1, source_target_pairs={{16,0},{32,16},{48,32},{64,48},{80,64},{96,80},{112,96},{0,112},{1... | collective-permute-start | bytes 1179656 | tf_op jit(solution)/shard_map/ppermute | solution.py:26
  38.0 8.4 %collective-permute-start.13 = (f32[6,4,32,128]{3,2,1,0:T(8,128)S(1)}, f32[6,4,32,128]{3,2,1,0:T(8,128)S(1)}, u32[]{:S(2)}, u32[]{:S(2)}) collective-permute-start(f32[6,4,32,128]{3,2,1,0:T(8,128)S(1)} %fusion.108), channel_id=1, source_target_pairs={{0,16},{16,32},{32,48},{48,64},{64,80},{80,96},{96,112},{112,0},{1... | collective-permute-start | bytes 1179656 | tf_op jit(solution)/shard_map/ppermute | solution.py:25
  43.1 8.9 %collective-permute-start.6 = (f32[6,4,32,128]{3,2,1,0:T(8,128)S(1)}, f32[6,4,32,128]{3,2,1,0:T(8,128)S(1)}, u32[]{:S(2)}, u32[]{:S(2)}) collective-permute-start(f32[6,4,32,128]{3,2,1,0:T(8,128)S(1)} %fusion.181), channel_id=1, source_target_pairs={{16,0},{32,16},{48,32},{64,48},{80,64},{96,80},{112,96},{0,112},{1... | collective-permute-start | bytes 1179656 | tf_op jit(solution)/shard_map/ppermute | solution.py:26
  44.8 8.4 %collective-permute-start.7 = (f32[6,4,32,128]{3,2,1,0:T(8,128)S(1)}, f32[6,4,32,128]{3,2,1,0:T(8,128)S(1)}, u32[]{:S(2)}, u32[]{:S(2)}) collective-permute-start(f32[6,4,32,128]{3,2,1,0:T(8,128)S(1)} %fusion.181), channel_id=1, source_target_pairs={{0,16},{16,32},{32,48},{48,64},{64,80},{80,96},{96,112},{112,0},{1... | collective-permute-start | bytes 1179656 | tf_op jit(solution)/shard_map/ppermute | solution.py:25
  50.2 8.7 %collective-permute-start.14 = (f32[6,4,32,128]{3,2,1,0:T(8,128)S(1)}, f32[6,4,32,128]{3,2,1,0:T(8,128)S(1)}, u32[]{:S(2)}, u32[]{:S(2)}) collective-permute-start(f32[6,4,32,128]{3,2,1,0:T(8,128)S(1)} %fusion.83), channel_id=1, source_target_pairs={{16,0},{32,16},{48,32},{64,48},{80,64},{96,80},{112,96},{0,112},{1... | collective-permute-start | bytes 1179656 | tf_op jit(solution)/shard_map/ppermute | solution.py:26
  51.9 8.4 %collective-permute-start.15 = (f32[6,4,32,128]{3,2,1,0:T(8,128)S(1)}, f32[6,4,32,128]{3,2,1,0:T(8,128)S(1)}, u32[]{:S(2)}, u32[]{:S(2)}) collective-permute-start(f32[6,4,32,128]{3,2,1,0:T(8,128)S(1)} %fusion.83), channel_id=1, source_target_pairs={{0,16},{16,32},{32,48},{48,64},{64,80},{80,96},{96,112},{112,0},{1... | collective-permute-start | bytes 1179656 | tf_op jit(solution)/shard_map/ppermute | solution.py:25
  56.7 9.1 %collective-permute-start.16 = (f32[6,4,32,128]{3,2,1,0:T(8,128)S(1)}, f32[6,4,32,128]{3,2,1,0:T(8,128)S(1)}, u32[]{:S(2)}, u32[]{:S(2)}) collective-permute-start(f32[6,4,32,128]{3,2,1,0:T(8,128)S(1)} %fusion.156), channel_id=1, source_target_pairs={{16,0},{32,16},{48,32},{64,48},{80,64},{96,80},{112,96},{0,112},{1... | collective-permute-start | bytes 1179656 | tf_op jit(solution)/shard_map/ppermute | solution.py:26
  58.6 8.4 %collective-permute-start.17 = (f32[6,4,32,128]{3,2,1,0:T(8,128)S(1)}, f32[6,4,32,128]{3,2,1,0:T(8,128)S(1)}, u32[]{:S(2)}, u32[]{:S(2)}) collective-permute-start(f32[6,4,32,128]{3,2,1,0:T(8,128)S(1)} %fusion.156), channel_id=1, source_target_pairs={{0,16},{16,32},{32,48},{48,64},{64,80},{80,96},{96,112},{112,0},{1... | collective-permute-start | bytes 1179656 | tf_op jit(solution)/shard_map/ppermute | solution.py:25
  63.9 7.0 %collective-permute-start.18 = (f32[6,4,32,128]{3,2,1,0:T(8,128)S(1)}, f32[6,4,32,128]{3,2,1,0:T(8,128)S(1)}, u32[]{:S(2)}, u32[]{:S(2)}) collective-permute-start(f32[6,4,32,128]{3,2,1,0:T(8,128)S(1)} %fusion.58), channel_id=1, source_target_pairs={{16,0},{32,16},{48,32},{64,48},{80,64},{96,80},{112,96},{0,112},{1... | collective-permute-start | bytes 1179656 | tf_op jit(solution)/shard_map/ppermute | solution.py:26
  65.6 8.4 %collective-permute-start.19 = (f32[6,4,32,128]{3,2,1,0:T(8,128)S(1)}, f32[6,4,32,128]{3,2,1,0:T(8,128)S(1)}, u32[]{:S(2)}, u32[]{:S(2)}) collective-permute-start(f32[6,4,32,128]{3,2,1,0:T(8,128)S(1)} %fusion.58), channel_id=1, source_target_pairs={{0,16},{16,32},{32,48},{48,64},{64,80},{80,96},{96,112},{112,0},{1... | collective-permute-start | bytes 1179656 | tf_op jit(solution)/shard_map/ppermute | solution.py:25
  77.2 28.3 %all-to-all-start = ((f32[2,12,16,8,128]{4,3,1,0,2:T(8,128)}), f32[2,12,16,8,128]{4,3,1,0,2:T(8,128)S(1)}, u32[]{:S(2)}, u32[]{:S(2)}) async-start(f32[2,12,16,8,128]{4,3,1,0,2:T(8,128)} %copy.18), calls=%async_computation | async-start | bytes 3145728 | tf_op jit(solution)/shard_map/all_to_all | solution.py:188
  116.7 1.5 collective-permute-start.20
  118.3 8.0 %collective-permute-start.21 = (f32[200,192]{1,0:T(8,128)S(1)}, f32[200,192]{1,0:T(8,128)S(1)}, u32[]{:S(2)}, u32[]{:S(2)}) collective-permute-start(f32[200,192]{1,0:T(8,128)S(1)} %select_add_fusion), channel_id=1, source_target_pairs={{0,96},{16,112},{32,0},{48,16},{64,32},{80,48},{96,64},{112,80},{1... | collective-permute-start | bytes 460808 | tf_op jit(solution)/shard_map/ppermute | solution.py:64
  119.0 9.5 %collective-permute-start.22 = (f32[200,192]{1,0:T(8,128)S(1)}, f32[200,192]{1,0:T(8,128)S(1)}, u32[]{:S(2)}, u32[]{:S(2)}) collective-permute-start(f32[200,192]{1,0:T(8,128)S(1)} %select_add_fusion), channel_id=1, source_target_pairs={{0,64},{16,80},{32,96},{48,112},{64,0},{80,16},{96,32},{112,48},{1... | collective-permute-start | bytes 460808 | tf_op jit(solution)/shard_map/ppermute | solution.py:64
  121.5 10.5 %collective-permute-start.23 = (f32[200,192]{1,0:T(8,128)S(1)}, f32[200,192]{1,0:T(8,128)S(1)}, u32[]{:S(2)}, u32[]{:S(2)}) collective-permute-start(f32[200,192]{1,0:T(8,128)S(1)} %select_add_fusion), channel_id=1, source_target_pairs={{0,32},{16,48},{32,64},{48,80},{64,96},{80,112},{96,0},{112,16},{1... | collective-permute-start | bytes 460808 | tf_op jit(solution)/shard_map/ppermute | solution.py:64
  132.1 8.0 %collective-permute-start.24 = (f32[200,192]{1,0:T(8,128)S(1)}, f32[200,192]{1,0:T(8,128)S(1)}, u32[]{:S(2)}, u32[]{:S(2)}) collective-permute-start(f32[200,192]{1,0:T(8,128)S(1)} %add_add_fusion.1), channel_id=1, source_target_pairs={{0,3},{1,0},{2,1},{3,2},{4,7},{5,4},{6,5},{7,6},{8,11},{9,8},{10,9... | collective-permute-start | bytes 460808 | tf_op jit(solution)/shard_map/ppermute | solution.py:64
  132.2 9.6 %collective-permute-start.25 = (f32[200,192]{1,0:T(8,128)S(1)}, f32[200,192]{1,0:T(8,128)S(1)}, u32[]{:S(2)}, u32[]{:S(2)}) collective-permute-start(f32[200,192]{1,0:T(8,128)S(1)} %add_add_fusion.1), channel_id=1, source_target_pairs={{0,2},{1,3},{2,0},{3,1},{4,6},{5,7},{6,4},{7,5},{8,10},{9,11},{10,... | collective-permute-start | bytes 460808 | tf_op jit(solution)/shard_map/ppermute | solution.py:64
  134.2 11.0 %collective-permute-start.26 = (f32[200,192]{1,0:T(8,128)S(1)}, f32[200,192]{1,0:T(8,128)S(1)}, u32[]{:S(2)}, u32[]{:S(2)}) collective-permute-start(f32[200,192]{1,0:T(8,128)S(1)} %add_add_fusion.1), channel_id=1, source_target_pairs={{0,1},{1,2},{2,3},{3,0},{4,5},{5,6},{6,7},{7,4},{8,9},{9,10},{10,1... | collective-permute-start | bytes 460808 | tf_op jit(solution)/shard_map/ppermute | solution.py:64
  145.3 8.0 %collective-permute-start.27 = (f32[200,192]{1,0:T(8,128)S(1)}, f32[200,192]{1,0:T(8,128)S(1)}, u32[]{:S(2)}, u32[]{:S(2)}) collective-permute-start(f32[200,192]{1,0:T(8,128)S(1)} %add_add_fusion), channel_id=1, source_target_pairs={{0,12},{1,13},{2,14},{3,15},{4,0},{5,1},{6,2},{7,3},{8,4},{9,5},{1... | collective-permute-start | bytes 460808 | tf_op jit(solution)/shard_map/ppermute | solution.py:64
  146.9 9.5 %collective-permute-start.28 = (f32[200,192]{1,0:T(8,128)S(1)}, f32[200,192]{1,0:T(8,128)S(1)}, u32[]{:S(2)}, u32[]{:S(2)}) collective-permute-start(f32[200,192]{1,0:T(8,128)S(1)} %add_add_fusion), channel_id=1, source_target_pairs={{0,8},{1,9},{2,10},{3,11},{4,12},{5,13},{6,14},{7,15},{8,0},{9,1},... | collective-permute-start | bytes 460808 | tf_op jit(solution)/shard_map/ppermute | solution.py:64
  147.9 11.6 %collective-permute-start.29 = (f32[200,192]{1,0:T(8,128)S(1)}, f32[200,192]{1,0:T(8,128)S(1)}, u32[]{:S(2)}, u32[]{:S(2)}) collective-permute-start(f32[200,192]{1,0:T(8,128)S(1)} %add_add_fusion), channel_id=1, source_target_pairs={{0,4},{1,5},{2,6},{3,7},{4,8},{5,9},{6,10},{7,11},{8,12},{9,13},{1... | collective-permute-start | bytes 460808 | tf_op jit(solution)/shard_map/ppermute | solution.py:64
  199.6 19.1 %all-to-all-start.1 = ((f32[12,16,8,128]{3,2,0,1:T(8,128)}), f32[12,16,8,128]{3,2,0,1:T(8,128)}, u32[]{:S(2)}, u32[]{:S(2)}) async-start(f32[12,16,8,128]{3,2,0,1:T(8,128)} %copy.24), calls=%async_computation.1 | async-start | bytes 1572864 | tf_op jit(solution)/shard_map/all_to_all | solution.py:213
  (3 other events, 8.3 us)

commit v6 on v5

--- a/solution.py
+++ b/solution.py
@@ -161,6 +161,49 @@
     )(m, f)
 
 
+def stencil_kernel(mode, f_ref, lo_ref, hi_ref, prev_ref, pot_ref, o_ref):
+    depth = f_ref.shape[1]
+    rows, lanes = f_ref.shape[2], f_ref.shape[3]
+
+    def plane(z):
+        if z < 0:
+            return lo_ref[0, depth + z]
+        if z >= depth:
+            return hi_ref[0, z - depth]
+        return f_ref[0, z]
+
+    for z in range(depth):
+        v = f_ref[0, z]
+        laplace = 3.0 * stencil_coef[0] * v
+        for reach in range(1, stencil_reach + 1):
+            near = plane(z + reach) + plane(z - reach)
+            near = near + pltpu.roll(v, reach, 0) + pltpu.roll(v, rows - reach, 0)
+            near = near + pltpu.roll(v, reach, 1) + pltpu.roll(v, lanes - reach, 1)
+            laplace = laplace + stencil_coef[reach] * near
+        h = pot_ref[z] * v - 0.5 * laplace
+        if mode == 0:
+            out = (h - center * v) / half
+        elif mode == 1:
+            out = 2.0 / half * (h - center * v) - prev_ref[0, z]
+        else:
+            out = h
+        o_ref[0, z] = out
+
+
+def stencil(mode, f, lo, hi, prev, pot):
+    band = pl.BlockSpec((1,) + f.shape[1:], lambda b: (b, 0, 0, 0))
+    return pl.pallas_call(
+        lambda *refs: stencil_kernel(mode, *refs),
+        out_shape=jax.ShapeDtypeStruct(f.shape, jnp.float32),
+        grid=(f.shape[0],),
+        in_specs=[band, band, band, band, pl.BlockSpec(pot.shape, lambda b: (0, 0, 0))],
+        out_specs=band,
+        cost_estimate=pl.CostEstimate(
+            flops=60 * f.size, transcendentals=0, bytes_accessed=4 * (5 * f.size + pot.size)
+        ),
+    )(f, lo, hi, prev, pot)
+
+
 def local(psi, potential):
     bdev = psi.shape[0]
     depth, rows_y, rows_x = (psi.shape[1], psi.shape[2], psi.shape[3])
@@ -168,18 +211,26 @@
     ncells = depth * lax.axis_size("dom") * rows_y * rows_x
     own_start = lax.axis_index("band") * bdev
 
-    def apply(field):
-        padded = extended(field, (("dom", 1),), stencil_reach)
-        return hamiltonian(field, padded, potential)
+    def halo(field):
+        count = lax.axis_size("dom")
+        up = [(i, (i + 1) % count) for i in range(count)]
+        down = [(j, i) for i, j in up]
+        lo = lax.ppermute(field[:, depth - stencil_reach :], "dom", up)
+        hi = lax.ppermute(field[:, :stencil_reach], "dom", down)
+        return lo, hi
+
+    def step(mode, field, prev):
+        lo, hi = halo(field)
+        return stencil(mode, field, lo, hi, prev, potential)
 
     chunks = CHUNKS if bdev % CHUNKS == 0 else 1
     width = bdev // chunks
     previous = [psi[i * width : (i + 1) * width] for i in range(chunks)]
-    current = [(apply(p) - center * p) / half for p in previous]
+    current = [step(0, p, p) for p in previous]
     for order in range(1, DEGREE):
-        following = [2.0 / half * (apply(c) - center * c) - p for c, p in zip(current, previous)]
+        following = [step(1, c, p) for c, p in zip(current, previous)]
         previous, current = (current, following)
-    image = jnp.concatenate([apply(c) for c in current])
+    image = jnp.concatenate([step(2, c, c) for c in current])
     current = jnp.concatenate(current)
     groups = lax.axis_size("band")
     rows = depth * rows_y * rows_x // groups // rows_x

time: 224 us -> 250 us (1.12)
  Pallas kernels: 35.2 us -> 83.9 us
  other arithmetic: 20.3 us -> 3.92 us
  waiting for transfers between devices: 79.9 us -> 67.1 us
  starting transfers between devices: 42.4 us -> 54.6 us
  local copies, waits for them, and re-layouts: 40.3 us -> 35.5 us
    pallas_call x0 -> x10, Pallas kernels: none -> 48.8 us  [stencil(): pl.pallas_call(lambda *refs: stencil_kernel(mode, *refs), out_shape=jax.S...]
    slice x144 -> x0, local copies, waits for them, and re-layouts: 17.9 us -> none  [the longest x72 14.3 us: hamiltonian(): near = near + jnp.roll(field, reach, 3) + jnp.roll(field, -reach, 3)]
    sub x8 -> x0, other arithmetic: 14.6 us -> none  [the longest x6 11.3 us: local(): 2.0 / half * (apply(c) - center * c) - p]
    unnamed x6 -> x50, local copies, waits for them, and re-layouts: 0.55 us -> 13.6 us
    ppermute x20, waiting for transfers between devices: 16.7 us -> 6.63 us  [the longest x10 4.27 us: halo(): lo = lax.ppermute(field[:, depth - stencil_reach:], 'dom', up)]
    ppermute x20, starting transfers between devices: 19.6 us -> 26.7 us  [the longest x10 26.7 us: halo(): hi = lax.ppermute(field[:, :stencil_reach], 'dom', down)]
    ppermute x10, waiting for transfers between devices: 32.3 us -> 28.3 us  [group_sum(): received.append(lax.ppermute(x, axis, pairs))]
    div x2 -> x0, other arithmetic: 3.8 us -> none  [local(): current = [(apply(p) - center * p) / half for p in previous]]
  transfers between devices with their start and end apart: 32 -> 32, of which waited for: 22 -> 12; matrix products, arithmetic and copies ran while one was open for 17% -> 2% of each run, Pallas kernels for 0% -> 18%
where the time goes in v6:
time: 250 us; the launch traced here: 247 us
  Pallas kernels  83.9 us (34%)
  waiting for transfers between devices  67.1 us (27%)
  starting transfers between devices  54.6 us (22%)
  local copies, waits for them, and re-layouts  35.5 us (14%)
  other arithmetic  3.92 us (2%)
    pallas_call x10, Pallas kernels, stencil(): pl.pallas_call(lambda *refs: stencil_kernel(mode, *refs), out_shape=jax.S...  48.8 us
    ppermute x10, waiting for transfers between devices, group_sum(): received.append(lax.ppermute(x, axis, pairs))  28.3 us
    pallas_call x1, Pallas kernels, lower_inverse(): pl.pallas_call(inverse_kernel, out_shape=jax.ShapeDtypeStruct((n, n), jnp...  26.7 us
    ppermute x10, starting transfers between devices, halo(): hi = lax.ppermute(field[:, :stencil_reach], 'dom', down)  26.7 us
    all_to_all x1, waiting for transfers between devices, local(): spread = lax.all_to_all(chunked, 'band', 2, 2, tiled=True)  21.2 us
    unnamed x50, local copies, waits for them, and re-layouts  13.6 us
    ppermute x10, starting transfers between devices, group_sum(): received.append(lax.ppermute(x, axis, pairs))  12.9 us
    all_to_all x1, waiting for transfers between devices, local(): lax.all_to_all(basis_cd, 'band', 1, 1, tiled=True).reshape(psi.shape)  11 us
  transfers between devices with their start and end apart: 32, of which 12 were waited for; matrix products, arithmetic and copies ran while one was open for 2% of the time, Pallas kernels for 18%

profile of v6, /device:TPU:0, one launch (start us, length us, event | category | flops | bytes accessed | tf_op | source)
XLA Modules:
  0.0 247.2 jit_solution(6504415740296377786)
XLA Ops:
  4.2 3.0 %collective-permute-start.9 = (f32[6,4,32,128]{3,2,1,0:T(8,128)S(1)}, f32[6,4,32,128]{3,2,1,0:T(8,128)S(1)}, u32[]{:S(2)}, u32[]{:S(2)}) collective-permute-start(f32[6,4,32,128]{3,2,1,0:T(8,128)S(1)} %get-tuple-element.9.refs_0_.refs_3_), channel_id=1, source_target_pairs={{16,0},{32,16},{48,32},{64,48},{80,64},{96,80},{112,96},{0,112},{1... | collective-permute-start | bytes 1179656 | tf_op jit(solution)/shard_map/ppermute | solution.py:219
  9.5 3.1 %collective-permute-done.refs_1_ = f32[6,4,32,128]{3,2,1,0:T(8,128)S(1)} collective-permute-done((f32[6,4,32,128]{3,2,1,0:T(8,128)S(1)}, f32[6,4,32,128]{3,2,1,0:T(8,128)S(1)}, u32[]{:S(2)}, u32[]{:S(2)}) %collective-permute-start) | collective-permute-done | bytes 393248 | tf_op jit(solution)/shard_map/ppermute | solution.py:218
  13.4 4.9 %shard_map.41.refs_0_.refs_3_ = f32[6,4,32,128]{3,2,1,0:T(8,128)} custom-call(f32[6,4,32,128]{3,2,1,0:T(8,128)} %copy-done.1, f32[6,4,32,128]{3,2,1,0:T(8,128)} %copy-done.24, f32[6,4,32,128]{3,2,1,0:T(8,128)} %copy-done.22, f32[6,4,32,128]{3,2,1,0:T(8,128)} %copy-done.1, f32[4,32,128]{2,1,0:T(8,128)} %refs_4_.19), custom_call_target="tpu_custom_call" | custom-call | flops 5898240 | bytes 2031616 | tf_op jit(solution)/shard_map/pallas_call | solution.py:195
  20.5 4.9 %shard_map.45.refs_0_.refs_3_ = f32[6,4,32,128]{3,2,1,0:T(8,128)} custom-call(f32[6,4,32,128]{3,2,1,0:T(8,128)} %copy-done, f32[6,4,32,128]{3,2,1,0:T(8,128)} %copy-done.20, f32[6,4,32,128]{3,2,1,0:T(8,128)} %copy-done.14, f32[6,4,32,128]{3,2,1,0:T(8,128)} %copy-done, f32[4,32,128]{2,1,0:T(8,128)} %refs_4_.19), custom_call_target="tpu_custom_call" | custom-call | flops 5898240 | bytes 2031616 | tf_op jit(solution)/shard_map/pallas_call | solution.py:195
  25.4 3.0 %collective-permute-start.11 = (f32[6,4,32,128]{3,2,1,0:T(8,128)}, f32[6,4,32,128]{3,2,1,0:T(8,128)S(1)}, u32[]{:S(2)}, u32[]{:S(2)}) collective-permute-start(f32[6,4,32,128]{3,2,1,0:T(8,128)} %shard_map.45.refs_0_.refs_3_), channel_id=1, source_target_pairs={{16,0},{32,16},{48,32},{64,48},{80,64},{96,80},{112,96},{0,112},{1... | collective-permute-start | bytes 1179656 | tf_op jit(solution)/shard_map/ppermute | solution.py:219
  29.8 4.9 %shard_map.42.refs_0_.refs_3_ = f32[6,4,32,128]{3,2,1,0:T(8,128)} custom-call(f32[6,4,32,128]{3,2,1,0:T(8,128)} %shard_map.41.refs_0_.refs_3_, f32[6,4,32,128]{3,2,1,0:T(8,128)} %copy-done.19, f32[6,4,32,128]{3,2,1,0:T(8,128)} %copy-done.11, f32[6,4,32,128]{3,2,1,0:T(8,128)} %copy-done.1, f32[4,32,128]{2,1,0:T(8,128)} %refs_4_.19), custom_call_target="tpu_custom_call" | custom-call | flops 5898240 | bytes 2031616 | tf_op jit(solution)/shard_map/pallas_call | solution.py:195
  34.7 3.0 %collective-permute-start.5 = (f32[6,4,32,128]{3,2,1,0:T(8,128)}, f32[6,4,32,128]{3,2,1,0:T(8,128)S(1)}, u32[]{:S(2)}, u32[]{:S(2)}) collective-permute-start(f32[6,4,32,128]{3,2,1,0:T(8,128)} %shard_map.42.refs_0_.refs_3_), channel_id=1, source_target_pairs={{16,0},{32,16},{48,32},{64,48},{80,64},{96,80},{112,96},{0,112},{1... | collective-permute-start | bytes 1179656 | tf_op jit(solution)/shard_map/ppermute | solution.py:219
  39.2 4.9 %shard_map.46.refs_0_.refs_3_ = f32[6,4,32,128]{3,2,1,0:T(8,128)} custom-call(f32[6,4,32,128]{3,2,1,0:T(8,128)} %shard_map.45.refs_0_.refs_3_, f32[6,4,32,128]{3,2,1,0:T(8,128)} %copy-done.16, f32[6,4,32,128]{3,2,1,0:T(8,128)} %copy-done.8, f32[6,4,32,128]{3,2,1,0:T(8,128)} %copy-done, f32[4,32,128]{2,1,0:T(8,128)} %refs_4_.19), custom_call_target="tpu_custom_call" | custom-call | flops 5898240 | bytes 2031616 | tf_op jit(solution)/shard_map/pallas_call | solution.py:195
  44.1 3.0 %collective-permute-start.13 = (f32[6,4,32,128]{3,2,1,0:T(8,128)}, f32[6,4,32,128]{3,2,1,0:T(8,128)S(1)}, u32[]{:S(2)}, u32[]{:S(2)}) collective-permute-start(f32[6,4,32,128]{3,2,1,0:T(8,128)} %shard_map.46.refs_0_.refs_3_), channel_id=1, source_target_pairs={{16,0},{32,16},{48,32},{64,48},{80,64},{96,80},{112,96},{0,112},{1... | collective-permute-start | bytes 1179656 | tf_op jit(solution)/shard_map/ppermute | solution.py:219
  48.5 4.9 %shard_map.43.refs_0_ = f32[6,4,32,128]{3,2,1,0:T(8,128)} custom-call(f32[6,4,32,128]{3,2,1,0:T(8,128)} %shard_map.42.refs_0_.refs_3_, f32[6,4,32,128]{3,2,1,0:T(8,128)} %copy-done.17, f32[6,4,32,128]{3,2,1,0:T(8,128)} %copy-done.9, f32[6,4,32,128]{3,2,1,0:T(8,128)} %shard_map.41.refs_0_.refs_3_, f32[4,32,128]{2,1,0:T(8,128)} %refs_4_.19), custom_call_target="tpu_custom_call" | custom-call | flops 5898240 | bytes 2031616 | tf_op jit(solution)/shard_map/pallas_call | solution.py:195
  53.4 3.0 %collective-permute-start.7 = (f32[6,4,32,128]{3,2,1,0:T(8,128)}, f32[6,4,32,128]{3,2,1,0:T(8,128)S(1)}, u32[]{:S(2)}, u32[]{:S(2)}) collective-permute-start(f32[6,4,32,128]{3,2,1,0:T(8,128)} %shard_map.43.refs_0_), channel_id=1, source_target_pairs={{16,0},{32,16},{48,32},{64,48},{80,64},{96,80},{112,96},{0,112},{1... | collective-permute-start | bytes 1179656 | tf_op jit(solution)/shard_map/ppermute | solution.py:219
  57.9 4.9 %shard_map.47.refs_0_ = f32[6,4,32,128]{3,2,1,0:T(8,128)} custom-call(f32[6,4,32,128]{3,2,1,0:T(8,128)} %shard_map.46.refs_0_.refs_3_, f32[6,4,32,128]{3,2,1,0:T(8,128)} %copy-done.18, f32[6,4,32,128]{3,2,1,0:T(8,128)} %copy-done.10, f32[6,4,32,128]{3,2,1,0:T(8,128)} %shard_map.45.refs_0_.refs_3_, f32[4,32,128]{2,1,0:T(8,128)} %refs_4_.19), custom_call_target="tpu_custom_call" | custom-call | flops 5898240 | bytes 2031616 | tf_op jit(solution)/shard_map/pallas_call | solution.py:195
  62.8 3.0 %collective-permute-start.15 = (f32[6,4,32,128]{3,2,1,0:T(8,128)}, f32[6,4,32,128]{3,2,1,0:T(8,128)S(1)}, u32[]{:S(2)}, u32[]{:S(2)}) collective-permute-start(f32[6,4,32,128]{3,2,1,0:T(8,128)} %shard_map.47.refs_0_), channel_id=1, source_target_pairs={{16,0},{32,16},{48,32},{64,48},{80,64},{96,80},{112,96},{0,112},{1... | collective-permute-start | bytes 1179656 | tf_op jit(solution)/shard_map/ppermute | solution.py:219
  67.2 4.9 %shard_map.44.refs_0_.refs_3_ = f32[6,4,32,128]{3,2,1,0:T(8,128)} custom-call(f32[6,4,32,128]{3,2,1,0:T(8,128)} %shard_map.43.refs_0_, f32[6,4,32,128]{3,2,1,0:T(8,128)} %copy-done.15, f32[6,4,32,128]{3,2,1,0:T(8,128)} %copy-done.7, f32[6,4,32,128]{3,2,1,0:T(8,128)} %shard_map.42.refs_0_.refs_3_, f32[4,32,128]{2,1,0:T(8,128)} %refs_4_.19), custom_call_target="tpu_custom_call" | custom-call | flops 5898240 | bytes 2031616 | tf_op jit(solution)/shard_map/pallas_call | solution.py:195
  72.1 3.0 %collective-permute-start.17 = (f32[6,4,32,128]{3,2,1,0:T(8,128)}, f32[6,4,32,128]{3,2,1,0:T(8,128)S(1)}, u32[]{:S(2)}, u32[]{:S(2)}) collective-permute-start(f32[6,4,32,128]{3,2,1,0:T(8,128)} %shard_map.44.refs_0_.refs_3_), channel_id=1, source_target_pairs={{16,0},{32,16},{48,32},{64,48},{80,64},{96,80},{112,96},{0,112},{1... | collective-permute-start | bytes 1179656 | tf_op jit(solution)/shard_map/ppermute | solution.py:219
  76.6 4.9 %shard_map.48.refs_0_.refs_3_ = f32[6,4,32,128]{3,2,1,0:T(8,128)} custom-call(f32[6,4,32,128]{3,2,1,0:T(8,128)} %shard_map.47.refs_0_, f32[6,4,32,128]{3,2,1,0:T(8,128)} %copy-done.12, f32[6,4,32,128]{3,2,1,0:T(8,128)} %copy-done.5, f32[6,4,32,128]{3,2,1,0:T(8,128)} %shard_map.46.refs_0_.refs_3_, f32[4,32,128]{2,1,0:T(8,128)} %refs_4_.19), custom_call_target="tpu_custom_call" | custom-call | flops 5898240 | bytes 2031616 | tf_op jit(solution)/shard_map/pallas_call | solution.py:195
  81.5 3.0 %collective-permute-start.19 = (f32[6,4,32,128]{3,2,1,0:T(8,128)}, f32[6,4,32,128]{3,2,1,0:T(8,128)S(1)}, u32[]{:S(2)}, u32[]{:S(2)}) collective-permute-start(f32[6,4,32,128]{3,2,1,0:T(8,128)} %shard_map.48.refs_0_.refs_3_), channel_id=1, source_target_pairs={{16,0},{32,16},{48,32},{64,48},{80,64},{96,80},{112,96},{0,112},{1... | collective-permute-start | bytes 1179656 | tf_op jit(solution)/shard_map/ppermute | solution.py:219
  87.0 4.9 %shard_map.49 = f32[6,4,32,128]{3,2,1,0:T(8,128)} custom-call(f32[6,4,32,128]{3,2,1,0:T(8,128)} %shard_map.44.refs_0_.refs_3_, f32[6,4,32,128]{3,2,1,0:T(8,128)} %copy-done.13, f32[6,4,32,128]{3,2,1,0:T(8,128)} %copy-done.6, f32[6,4,32,128]{3,2,1,0:T(8,128)} %shard_map.44.refs_0_.refs_3_, f32[4,32,128]{2,1,0:T(8,128)} %refs_4_.19), custom_call_target="tpu_custom_call" | custom-call | flops 5898240 | bytes 2031616 | tf_op jit(solution)/shard_map/pallas_call | solution.py:195
  93.8 4.9 %shard_map.50 = f32[6,4,32,128]{3,2,1,0:T(8,128)} custom-call(f32[6,4,32,128]{3,2,1,0:T(8,128)} %shard_map.48.refs_0_.refs_3_, f32[6,4,32,128]{3,2,1,0:T(8,128)} %copy-done.23, f32[6,4,32,128]{3,2,1,0:T(8,128)} %copy-done.21, f32[6,4,32,128]{3,2,1,0:T(8,128)} %shard_map.48.refs_0_.refs_3_, f32[4,32,128]{2,1,0:T(8,128)} %refs_4_.19), custom_call_target="tpu_custom_call" | custom-call | flops 5898240 | bytes 2031616 | tf_op jit(solution)/shard_map/pallas_call | solution.py:195
  101.3 8.0 %all-to-all-start = ((f32[2,12,16,8,128]{4,3,1,0,2:T(8,128)}), f32[2,12,16,8,128]{4,3,1,0,2:T(8,128)S(1)}, u32[]{:S(2)}, u32[]{:S(2)}) async-start(f32[2,12,16,8,128]{4,3,1,0,2:T(8,128)} %copy.30), calls=%async_computation | async-start | bytes 3145728 | tf_op jit(solution)/shard_map/all_to_all | solution.py:239
  109.4 21.2 %all-to-all-done = f32[2,12,16,8,128]{4,3,1,0,2:T(8,128)S(1)} async-done(((f32[2,12,16,8,128]{4,3,1,0,2:T(8,128)}), f32[2,12,16,8,128]{4,3,1,0,2:T(8,128)S(1)}, u32[]{:S(2)}, u32[]{:S(2)}) %all-to-all-start) | async-done | bytes 1572896 | tf_op jit(solution)/shard_map/all_to_all | solution.py:239
  132.7 4.8 %shard_map.51 = (f32[192,192]{1,0:T(8,128)}, f32[192,192]{1,0:T(8,128)}) custom-call(f32[1536,128]{1,0:T(8,128)} %bitcast.25, f32[1536,128]{1,0:T(8,128)} %bitcast.31), custom_call_target="tpu_custom_call" | custom-call | tf_op jit(solution)/shard_map/pallas_call | solution.py:147
  138.5 3.2 %gather_fusion = f32[192]{0:T(256)S(1)} fusion(f32[192,192]{1,0:T(8,128)} %get-tuple-element.5, s32[192]{0:T(256)S(1)} %bitcast.24), kind=kCustom, calls=%fused_computation | custom fusion | bytes 3072 | tf_op jit(solution)/shard_map/jit(diagonal)/cond/branch_0_fun/gather | solution.py:247
  143.6 5.3 %collective-permute-start.22 = (f32[200,192]{1,0:T(8,128)S(1)}, f32[200,192]{1,0:T(8,128)S(1)}, u32[]{:S(2)}, u32[]{:S(2)}) collective-permute-start(f32[200,192]{1,0:T(8,128)S(1)} %select_add_fusion), channel_id=1, source_target_pairs={{0,64},{16,80},{32,96},{48,112},{64,0},{80,16},{96,32},{112,48},{1... | collective-permute-start | bytes 460808 | tf_op jit(solution)/shard_map/ppermute | solution.py:64
  148.9 4.1 %collective-permute-done.23 = f32[200,192]{1,0:T(8,128)S(1)} collective-permute-done((f32[200,192]{1,0:T(8,128)S(1)}, f32[200,192]{1,0:T(8,128)S(1)}, u32[]{:S(2)}, u32[]{:S(2)}) %collective-permute-start.23) | collective-permute-done | bytes 153632 | tf_op jit(solution)/shard_map/ppermute | solution.py:64
  153.0 5.6 %collective-permute-done.22 = f32[200,192]{1,0:T(8,128)S(1)} collective-permute-done((f32[200,192]{1,0:T(8,128)S(1)}, f32[200,192]{1,0:T(8,128)S(1)}, u32[]{:S(2)}, u32[]{:S(2)}) %collective-permute-start.22) | collective-permute-done | bytes 153632 | tf_op jit(solution)/shard_map/ppermute | solution.py:64
  162.0 8.9 %collective-permute-done.26 = f32[200,192]{1,0:T(8,128)S(1)} collective-permute-done((f32[200,192]{1,0:T(8,128)S(1)}, f32[200,192]{1,0:T(8,128)S(1)}, u32[]{:S(2)}, u32[]{:S(2)}) %collective-permute-start.26) | collective-permute-done | bytes 153632 | tf_op jit(solution)/shard_map/ppermute | solution.py:64
  175.8 7.1 %collective-permute-done.29 = f32[200,192]{1,0:T(8,128)S(1)} collective-permute-done((f32[200,192]{1,0:T(8,128)S(1)}, f32[200,192]{1,0:T(8,128)S(1)}, u32[]{:S(2)}, u32[]{:S(2)}) %collective-permute-start.29) | collective-permute-done | bytes 153632 | tf_op jit(solution)/shard_map/ppermute | solution.py:64
  186.8 26.7 %shard_map.52 = f32[192,192]{1,0:T(8,128)} custom-call(f32[192,192]{1,0:T(8,128)} %reshape.34.c_ref), custom_call_target="tpu_custom_call" | custom-call | tf_op jit(solution)/shard_map/pallas_call | solution.py:131
  217.8 3.6 %shard_map.53 = f32[1536,128]{1,0:T(8,128)} custom-call(f32[192,192]{1,0:T(8,128)} %reshape.36.refs_0_, f32[1536,128]{1,0:T(8,128)} %bitcast.26), custom_call_target="tpu_custom_call" | custom-call | tf_op jit(solution)/shard_map/pallas_call | solution.py:156
  223.5 7.0 %all-to-all-start.1 = ((f32[12,16,8,128]{3,2,0,1:T(8,128)}), f32[12,16,8,128]{3,2,0,1:T(8,128)}, u32[]{:S(2)}, u32[]{:S(2)}) async-start(f32[12,16,8,128]{3,2,0,1:T(8,128)} %copy.27), calls=%async_computation.1 | async-start | bytes 1572864 | tf_op jit(solution)/shard_map/all_to_all | solution.py:264
  234.1 11.0 %all-to-all-done.1 = f32[12,16,8,128]{3,2,0,1:T(8,128)} async-done(((f32[12,16,8,128]{3,2,0,1:T(8,128)}), f32[12,16,8,128]{3,2,0,1:T(8,128)}, u32[]{:S(2)}, u32[]{:S(2)}) %all-to-all-start.1) | async-done | bytes 786464 | tf_op jit(solution)/shard_map/all_to_all | solution.py:264
  (130 shorter events, 54.2 us)
Async XLA Ops:
  1.8 7.6 %collective-permute-start.1 = (f32[6,4,32,128]{3,2,1,0:T(8,128)S(1)}, f32[6,4,32,128]{3,2,1,0:T(8,128)S(1)}, u32[]{:S(2)}, u32[]{:S(2)}) collective-permute-start(f32[6,4,32,128]{3,2,1,0:T(8,128)S(1)} %get-tuple-element.8.refs_0_.refs_3_), channel_id=1, source_target_pairs={{16,0},{32,16},{48,32},{64,48},{80,64},{96,80},{112,96},{0,112},{1... | collective-permute-start | bytes 1179656 | tf_op jit(solution)/shard_map/ppermute | solution.py:219
  4.2 8.4 %collective-permute-start = (f32[6,4,32,128]{3,2,1,0:T(8,128)S(1)}, f32[6,4,32,128]{3,2,1,0:T(8,128)S(1)}, u32[]{:S(2)}, u32[]{:S(2)}) collective-permute-start(f32[6,4,32,128]{3,2,1,0:T(8,128)S(1)} %get-tuple-element.8.refs_0_.refs_3_), channel_id=1, source_target_pairs={{0,16},{16,32},{32,48},{48,64},{64,80},{80,96},{96,112},{112,0},{1... | collective-permute-start | bytes 1179656 | tf_op jit(solution)/shard_map/ppermute | solution.py:218
  4.2 14.8 %collective-permute-start.9 = (f32[6,4,32,128]{3,2,1,0:T(8,128)S(1)}, f32[6,4,32,128]{3,2,1,0:T(8,128)S(1)}, u32[]{:S(2)}, u32[]{:S(2)}) collective-permute-start(f32[6,4,32,128]{3,2,1,0:T(8,128)S(1)} %get-tuple-element.9.refs_0_.refs_3_), channel_id=1, source_target_pairs={{16,0},{32,16},{48,32},{64,48},{80,64},{96,80},{112,96},{0,112},{1... | collective-permute-start | bytes 1179656 | tf_op jit(solution)/shard_map/ppermute | solution.py:219
  7.1 11.9 %collective-permute-start.8 = (f32[6,4,32,128]{3,2,1,0:T(8,128)S(1)}, f32[6,4,32,128]{3,2,1,0:T(8,128)S(1)}, u32[]{:S(2)}, u32[]{:S(2)}) collective-permute-start(f32[6,4,32,128]{3,2,1,0:T(8,128)S(1)} %get-tuple-element.9.refs_0_.refs_3_), channel_id=1, source_target_pairs={{0,16},{16,32},{32,48},{48,64},{64,80},{80,96},{96,112},{112,0},{1... | collective-permute-start | bytes 1179656 | tf_op jit(solution)/shard_map/ppermute | solution.py:218
  18.2 10.1 %collective-permute-start.3 = (f32[6,4,32,128]{3,2,1,0:T(8,128)}, f32[6,4,32,128]{3,2,1,0:T(8,128)S(1)}, u32[]{:S(2)}, u32[]{:S(2)}) collective-permute-start(f32[6,4,32,128]{3,2,1,0:T(8,128)} %shard_map.41.refs_0_.refs_3_), channel_id=1, source_target_pairs={{16,0},{32,16},{48,32},{64,48},{80,64},{96,80},{112,96},{0,112},{1... | collective-permute-start | bytes 1179656 | tf_op jit(solution)/shard_map/ppermute | solution.py:219
  19.0 9.3 %collective-permute-start.2 = (f32[6,4,32,128]{3,2,1,0:T(8,128)}, f32[6,4,32,128]{3,2,1,0:T(8,128)S(1)}, u32[]{:S(2)}, u32[]{:S(2)}) collective-permute-start(f32[6,4,32,128]{3,2,1,0:T(8,128)} %shard_map.41.refs_0_.refs_3_), channel_id=1, source_target_pairs={{0,16},{16,32},{32,48},{48,64},{64,80},{80,96},{96,112},{112,0},{1... | collective-permute-start | bytes 1179656 | tf_op jit(solution)/shard_map/ppermute | solution.py:218
  25.4 12.3 %collective-permute-start.11 = (f32[6,4,32,128]{3,2,1,0:T(8,128)}, f32[6,4,32,128]{3,2,1,0:T(8,128)S(1)}, u32[]{:S(2)}, u32[]{:S(2)}) collective-permute-start(f32[6,4,32,128]{3,2,1,0:T(8,128)} %shard_map.45.refs_0_.refs_3_), channel_id=1, source_target_pairs={{16,0},{32,16},{48,32},{64,48},{80,64},{96,80},{112,96},{0,112},{1... | collective-permute-start | bytes 1179656 | tf_op jit(solution)/shard_map/ppermute | solution.py:219
  28.3 9.4 %collective-permute-start.10 = (f32[6,4,32,128]{3,2,1,0:T(8,128)}, f32[6,4,32,128]{3,2,1,0:T(8,128)S(1)}, u32[]{:S(2)}, u32[]{:S(2)}) collective-permute-start(f32[6,4,32,128]{3,2,1,0:T(8,128)} %shard_map.45.refs_0_.refs_3_), channel_id=1, source_target_pairs={{0,16},{16,32},{32,48},{48,64},{64,80},{80,96},{96,112},{112,0},{1... | collective-permute-start | bytes 1179656 | tf_op jit(solution)/shard_map/ppermute | solution.py:218
  34.7 12.3 %collective-permute-start.5 = (f32[6,4,32,128]{3,2,1,0:T(8,128)}, f32[6,4,32,128]{3,2,1,0:T(8,128)S(1)}, u32[]{:S(2)}, u32[]{:S(2)}) collective-permute-start(f32[6,4,32,128]{3,2,1,0:T(8,128)} %shard_map.42.refs_0_.refs_3_), channel_id=1, source_target_pairs={{16,0},{32,16},{48,32},{64,48},{80,64},{96,80},{112,96},{0,112},{1... | collective-permute-start | bytes 1179656 | tf_op jit(solution)/shard_map/ppermute | solution.py:219
  37.7 9.4 %collective-permute-start.4 = (f32[6,4,32,128]{3,2,1,0:T(8,128)}, f32[6,4,32,128]{3,2,1,0:T(8,128)S(1)}, u32[]{:S(2)}, u32[]{:S(2)}) collective-permute-start(f32[6,4,32,128]{3,2,1,0:T(8,128)} %shard_map.42.refs_0_.refs_3_), channel_id=1, source_target_pairs={{0,16},{16,32},{32,48},{48,64},{64,80},{80,96},{96,112},{112,0},{1... | collective-permute-start | bytes 1179656 | tf_op jit(solution)/shard_map/ppermute | solution.py:218
  44.1 12.3 %collective-permute-start.13 = (f32[6,4,32,128]{3,2,1,0:T(8,128)}, f32[6,4,32,128]{3,2,1,0:T(8,128)S(1)}, u32[]{:S(2)}, u32[]{:S(2)}) collective-permute-start(f32[6,4,32,128]{3,2,1,0:T(8,128)} %shard_map.46.refs_0_.refs_3_), channel_id=1, source_target_pairs={{16,0},{32,16},{48,32},{64,48},{80,64},{96,80},{112,96},{0,112},{1... | collective-permute-start | bytes 1179656 | tf_op jit(solution)/shard_map/ppermute | solution.py:219
  47.0 9.3 %collective-permute-start.12 = (f32[6,4,32,128]{3,2,1,0:T(8,128)}, f32[6,4,32,128]{3,2,1,0:T(8,128)S(1)}, u32[]{:S(2)}, u32[]{:S(2)}) collective-permute-start(f32[6,4,32,128]{3,2,1,0:T(8,128)} %shard_map.46.refs_0_.refs_3_), channel_id=1, source_target_pairs={{0,16},{16,32},{32,48},{48,64},{64,80},{80,96},{96,112},{112,0},{1... | collective-permute-start | bytes 1179656 | tf_op jit(solution)/shard_map/ppermute | solution.py:218
  53.4 12.3 %collective-permute-start.7 = (f32[6,4,32,128]{3,2,1,0:T(8,128)}, f32[6,4,32,128]{3,2,1,0:T(8,128)S(1)}, u32[]{:S(2)}, u32[]{:S(2)}) collective-permute-start(f32[6,4,32,128]{3,2,1,0:T(8,128)} %shard_map.43.refs_0_), channel_id=1, source_target_pairs={{16,0},{32,16},{48,32},{64,48},{80,64},{96,80},{112,96},{0,112},{1... | collective-permute-start | bytes 1179656 | tf_op jit(solution)/shard_map/ppermute | solution.py:219
  56.4 9.4 %collective-permute-start.6 = (f32[6,4,32,128]{3,2,1,0:T(8,128)}, f32[6,4,32,128]{3,2,1,0:T(8,128)S(1)}, u32[]{:S(2)}, u32[]{:S(2)}) collective-permute-start(f32[6,4,32,128]{3,2,1,0:T(8,128)} %shard_map.43.refs_0_), channel_id=1, source_target_pairs={{0,16},{16,32},{32,48},{48,64},{64,80},{80,96},{96,112},{112,0},{1... | collective-permute-start | bytes 1179656 | tf_op jit(solution)/shard_map/ppermute | solution.py:218
  62.8 12.3 %collective-permute-start.15 = (f32[6,4,32,128]{3,2,1,0:T(8,128)}, f32[6,4,32,128]{3,2,1,0:T(8,128)S(1)}, u32[]{:S(2)}, u32[]{:S(2)}) collective-permute-start(f32[6,4,32,128]{3,2,1,0:T(8,128)} %shard_map.47.refs_0_), channel_id=1, source_target_pairs={{16,0},{32,16},{48,32},{64,48},{80,64},{96,80},{112,96},{0,112},{1... | collective-permute-start | bytes 1179656 | tf_op jit(solution)/shard_map/ppermute | solution.py:219
  65.7 9.4 %collective-permute-start.14 = (f32[6,4,32,128]{3,2,1,0:T(8,128)}, f32[6,4,32,128]{3,2,1,0:T(8,128)S(1)}, u32[]{:S(2)}, u32[]{:S(2)}) collective-permute-start(f32[6,4,32,128]{3,2,1,0:T(8,128)} %shard_map.47.refs_0_), channel_id=1, source_target_pairs={{0,16},{16,32},{32,48},{48,64},{64,80},{80,96},{96,112},{112,0},{1... | collective-permute-start | bytes 1179656 | tf_op jit(solution)/shard_map/ppermute | solution.py:218
  72.1 13.4 %collective-permute-start.17 = (f32[6,4,32,128]{3,2,1,0:T(8,128)}, f32[6,4,32,128]{3,2,1,0:T(8,128)S(1)}, u32[]{:S(2)}, u32[]{:S(2)}) collective-permute-start(f32[6,4,32,128]{3,2,1,0:T(8,128)} %shard_map.44.refs_0_.refs_3_), channel_id=1, source_target_pairs={{16,0},{32,16},{48,32},{64,48},{80,64},{96,80},{112,96},{0,112},{1... | collective-permute-start | bytes 1179656 | tf_op jit(solution)/shard_map/ppermute | solution.py:219
  75.1 10.5 %collective-permute-start.16 = (f32[6,4,32,128]{3,2,1,0:T(8,128)}, f32[6,4,32,128]{3,2,1,0:T(8,128)S(1)}, u32[]{:S(2)}, u32[]{:S(2)}) collective-permute-start(f32[6,4,32,128]{3,2,1,0:T(8,128)} %shard_map.44.refs_0_.refs_3_), channel_id=1, source_target_pairs={{0,16},{16,32},{32,48},{48,64},{64,80},{80,96},{96,112},{112,0},{1... | collective-permute-start | bytes 1179656 | tf_op jit(solution)/shard_map/ppermute | solution.py:218
  81.5 10.4 %collective-permute-start.19 = (f32[6,4,32,128]{3,2,1,0:T(8,128)}, f32[6,4,32,128]{3,2,1,0:T(8,128)S(1)}, u32[]{:S(2)}, u32[]{:S(2)}) collective-permute-start(f32[6,4,32,128]{3,2,1,0:T(8,128)} %shard_map.48.refs_0_.refs_3_), channel_id=1, source_target_pairs={{16,0},{32,16},{48,32},{64,48},{80,64},{96,80},{112,96},{0,112},{1... | collective-permute-start | bytes 1179656 | tf_op jit(solution)/shard_map/ppermute | solution.py:219
  84.4 8.6 %collective-permute-start.18 = (f32[6,4,32,128]{3,2,1,0:T(8,128)}, f32[6,4,32,128]{3,2,1,0:T(8,128)S(1)}, u32[]{:S(2)}, u32[]{:S(2)}) collective-permute-start(f32[6,4,32,128]{3,2,1,0:T(8,128)} %shard_map.48.refs_0_.refs_3_), channel_id=1, source_target_pairs={{0,16},{16,32},{32,48},{48,64},{64,80},{80,96},{96,112},{112,0},{1... | collective-permute-start | bytes 1179656 | tf_op jit(solution)/shard_map/ppermute | solution.py:218
  101.3 29.4 %all-to-all-start = ((f32[2,12,16,8,128]{4,3,1,0,2:T(8,128)}), f32[2,12,16,8,128]{4,3,1,0,2:T(8,128)S(1)}, u32[]{:S(2)}, u32[]{:S(2)}) async-start(f32[2,12,16,8,128]{4,3,1,0,2:T(8,128)} %copy.30), calls=%async_computation | async-start | bytes 3145728 | tf_op jit(solution)/shard_map/all_to_all | solution.py:239
  141.8 1.5 collective-permute-start.20
  143.5 9.5 %collective-permute-start.23 = (f32[200,192]{1,0:T(8,128)S(1)}, f32[200,192]{1,0:T(8,128)S(1)}, u32[]{:S(2)}, u32[]{:S(2)}) collective-permute-start(f32[200,192]{1,0:T(8,128)S(1)} %select_add_fusion), channel_id=1, source_target_pairs={{0,32},{16,48},{32,64},{48,80},{64,96},{80,112},{96,0},{112,16},{1... | collective-permute-start | bytes 460808 | tf_op jit(solution)/shard_map/ppermute | solution.py:64
  143.6 15.0 %collective-permute-start.22 = (f32[200,192]{1,0:T(8,128)S(1)}, f32[200,192]{1,0:T(8,128)S(1)}, u32[]{:S(2)}, u32[]{:S(2)}) collective-permute-start(f32[200,192]{1,0:T(8,128)S(1)} %select_add_fusion), channel_id=1, source_target_pairs={{0,64},{16,80},{32,96},{48,112},{64,0},{80,16},{96,32},{112,48},{1... | collective-permute-start | bytes 460808 | tf_op jit(solution)/shard_map/ppermute | solution.py:64
  148.9 9.7 %collective-permute-start.21 = (f32[200,192]{1,0:T(8,128)S(1)}, f32[200,192]{1,0:T(8,128)S(1)}, u32[]{:S(2)}, u32[]{:S(2)}) collective-permute-start(f32[200,192]{1,0:T(8,128)S(1)} %select_add_fusion), channel_id=1, source_target_pairs={{0,96},{16,112},{32,0},{48,16},{64,32},{80,48},{96,64},{112,80},{1... | collective-permute-start | bytes 460808 | tf_op jit(solution)/shard_map/ppermute | solution.py:64
  158.7 12.2 %collective-permute-start.26 = (f32[200,192]{1,0:T(8,128)S(1)}, f32[200,192]{1,0:T(8,128)S(1)}, u32[]{:S(2)}, u32[]{:S(2)}) collective-permute-start(f32[200,192]{1,0:T(8,128)S(1)} %add_add_fusion.1), channel_id=1, source_target_pairs={{0,1},{1,2},{2,3},{3,0},{4,5},{5,6},{6,7},{7,4},{8,9},{9,10},{10,1... | collective-permute-start | bytes 460808 | tf_op jit(solution)/shard_map/ppermute | solution.py:64
  158.8 12.1 %collective-permute-start.25 = (f32[200,192]{1,0:T(8,128)S(1)}, f32[200,192]{1,0:T(8,128)S(1)}, u32[]{:S(2)}, u32[]{:S(2)}) collective-permute-start(f32[200,192]{1,0:T(8,128)S(1)} %add_add_fusion.1), channel_id=1, source_target_pairs={{0,2},{1,3},{2,0},{3,1},{4,6},{5,7},{6,4},{7,5},{8,10},{9,11},{10,... | collective-permute-start | bytes 460808 | tf_op jit(solution)/shard_map/ppermute | solution.py:64
  159.2 12.3 %collective-permute-start.24 = (f32[200,192]{1,0:T(8,128)S(1)}, f32[200,192]{1,0:T(8,128)S(1)}, u32[]{:S(2)}, u32[]{:S(2)}) collective-permute-start(f32[200,192]{1,0:T(8,128)S(1)} %add_add_fusion.1), channel_id=1, source_target_pairs={{0,3},{1,0},{2,1},{3,2},{4,7},{5,4},{6,5},{7,6},{8,11},{9,8},{10,9... | collective-permute-start | bytes 460808 | tf_op jit(solution)/shard_map/ppermute | solution.py:64
  171.6 11.2 %collective-permute-start.29 = (f32[200,192]{1,0:T(8,128)S(1)}, f32[200,192]{1,0:T(8,128)S(1)}, u32[]{:S(2)}, u32[]{:S(2)}) collective-permute-start(f32[200,192]{1,0:T(8,128)S(1)} %add_add_fusion), channel_id=1, source_target_pairs={{0,4},{1,5},{2,6},{3,7},{4,8},{5,9},{6,10},{7,11},{8,12},{9,13},{1... | collective-permute-start | bytes 460808 | tf_op jit(solution)/shard_map/ppermute | solution.py:64
  171.7 11.2 %collective-permute-start.28 = (f32[200,192]{1,0:T(8,128)S(1)}, f32[200,192]{1,0:T(8,128)S(1)}, u32[]{:S(2)}, u32[]{:S(2)}) collective-permute-start(f32[200,192]{1,0:T(8,128)S(1)} %add_add_fusion), channel_id=1, source_target_pairs={{0,8},{1,9},{2,10},{3,11},{4,12},{5,13},{6,14},{7,15},{8,0},{9,1},... | collective-permute-start | bytes 460808 | tf_op jit(solution)/shard_map/ppermute | solution.py:64
  174.2 9.2 %collective-permute-start.27 = (f32[200,192]{1,0:T(8,128)S(1)}, f32[200,192]{1,0:T(8,128)S(1)}, u32[]{:S(2)}, u32[]{:S(2)}) collective-permute-start(f32[200,192]{1,0:T(8,128)S(1)} %add_add_fusion), channel_id=1, source_target_pairs={{0,12},{1,13},{2,14},{3,15},{4,0},{5,1},{6,2},{7,3},{8,4},{9,5},{1... | collective-permute-start | bytes 460808 | tf_op jit(solution)/shard_map/ppermute | solution.py:64
  223.5 21.7 %all-to-all-start.1 = ((f32[12,16,8,128]{3,2,0,1:T(8,128)}), f32[12,16,8,128]{3,2,0,1:T(8,128)}, u32[]{:S(2)}, u32[]{:S(2)}) async-start(f32[12,16,8,128]{3,2,0,1:T(8,128)} %copy.27), calls=%async_computation.1 | async-start | bytes 1572864 | tf_op jit(solution)/shard_map/all_to_all | solution.py:264
  (25 other events, 65.8 us)

commit v7 on v5

--- a/solution.py
+++ b/solution.py
@@ -107,19 +107,31 @@
     sub = lax.broadcasted_iota(jnp.int32, shape, 0)
     lane = lax.broadcasted_iota(jnp.int32, shape, 1)
     b_ref[...] = jnp.where(sub == lane, 1.0, 0.0).astype(jnp.float32)
-
-    def step(k, carry):
-        row_a = a_ref[pl.ds(k, 1), :]
-        row_b = b_ref[pl.ds(k, 1), :]
-        a = a_ref[...]
-        pivot = jnp.sum(jnp.where(lane[:1] == k, row_a, 0.0), axis=1, keepdims=True)
-        col = jnp.sum(jnp.where(lane == k, a, 0.0), axis=1, keepdims=True)
-        factor = jnp.where(sub[:, :1] > k, col, 0.0) / pivot
-        a_ref[...] = a - factor * row_a
-        b_ref[...] = b_ref[...] - factor * row_b
-        return carry
-
-    lax.fori_loop(0, n, step, 0)
+    tile = 128
+    tiles = shape[1] // tile
+
+    def segment(k0, k1, r0):
+        ta, tb = k0 // tile, (k1 - 1) // tile + 1
+        rows = shape[0] - r0
+
+        def step(k, carry):
+            row_a = a_ref[pl.ds(k, 1), :][:, ta * tile :]
+            row_b = b_ref[pl.ds(k, 1), :][:, : tb * tile]
+            a = a_ref[r0:, ta * tile :]
+            lane_a = lax.broadcasted_iota(jnp.int32, a.shape, 1) + ta * tile
+            pivot = jnp.sum(jnp.where(lane_a[:1] == k, row_a, 0.0), axis=1, keepdims=True)
+            col = jnp.sum(jnp.where(lane_a == k, a, 0.0), axis=1, keepdims=True)
+            below = lax.broadcasted_iota(jnp.int32, (rows, 1), 0) + r0 > k
+            factor = jnp.where(below, col, 0.0) / pivot
+            a_ref[r0:, ta * tile :] = a - factor * row_a
+            b_ref[r0:, : tb * tile] = b_ref[r0:, : tb * tile] - factor * row_b
+            return carry
+
+        lax.fori_loop(k0, k1, step, 0)
+
+    bounds = sorted({0, n} | {t * tile for t in range(1, tiles) if t * tile < n})
+    for k0, k1 in zip(bounds[:-1], bounds[1:]):
+        segment(k0, k1, (k0 // 8) * 8)
     a = a_ref[...]
     diag = jnp.sum(jnp.where(sub == lane, a, 0.0), axis=1, keepdims=True)
     o_ref[...] = (b_ref[...] / jnp.sqrt(diag))[:, :n]

time: 224 us -> 221 us (0.987)
  Pallas kernels: 35.2 us -> 32 us
    pallas_call x1, Pallas kernels: 26.9 us -> 23.7 us  [lower_inverse(): pl.pallas_call(inverse_kernel, out_shape=jax.ShapeDtypeStruct((n, n), jnp...]
  transfers between devices with their start and end apart: 32 -> 32, of which waited for: 22 -> 22; matrix products, arithmetic and copies ran while one was open for 17% -> 18% of each run, Pallas kernels for 0% -> 0%
where the time goes in v7:
time: 221 us; the launch traced here: 218 us
  waiting for transfers between devices  79.9 us (36%)
  starting transfers between devices  42.4 us (19%)
  local copies, waits for them, and re-layouts  40.3 us (18%)
  Pallas kernels  32 us (14%)
  other arithmetic  20.3 us (9%)
    ppermute x10, waiting for transfers between devices, group_sum(): received.append(lax.ppermute(x, axis, pairs))  32.3 us
    pallas_call x1, Pallas kernels, lower_inverse(): pl.pallas_call(inverse_kernel, out_shape=jax.ShapeDtypeStruct((n, n), jnp...  23.7 us
    all_to_all x1, waiting for transfers between devices, local(): spread = lax.all_to_all(chunked, 'band', 2, 2, tiled=True)  19.8 us
    ppermute x10, starting transfers between devices, extended(): after = lax.ppermute(initial, axis, down)  19.5 us
    ppermute x10, waiting for transfers between devices, extended(): before = lax.ppermute(last, axis, up)  14.5 us
    slice x72, local copies, waits for them, and re-layouts, hamiltonian(): near = near + jnp.roll(field, reach, 3) + jnp.roll(field, -reach, 3)  14.3 us
    sub x6, other arithmetic, local(): 2.0 / half * (apply(c) - center * c) - p  11.3 us
    all_to_all x1, waiting for transfers between devices, local(): lax.all_to_all(basis_cd, 'band', 1, 1, tiled=True).reshape(psi.shape)  11.2 us
  transfers between devices with their start and end apart: 32, of which 22 were waited for; matrix products, arithmetic and copies ran while one was open for 18% of the time, Pallas kernels for 0%

profile of v7, /device:TPU:0, one launch (start us, length us, event | category | flops | bytes accessed | tf_op | source)
XLA Modules:
  0.0 217.8 jit_solution(5315860562632111856)
XLA Ops:
  1.9 2.3 %collective-permute-start = (f32[6,4,32,128]{3,2,1,0:T(8,128)S(1)}, f32[6,4,32,128]{3,2,1,0:T(8,128)S(1)}, u32[]{:S(2)}, u32[]{:S(2)}) collective-permute-start(f32[6,4,32,128]{3,2,1,0:T(8,128)S(1)} %get-tuple-element.76), channel_id=1, source_target_pairs={{16,0},{32,16},{48,32},{64,48},{80,64},{96,80},{112,96},{0,112},{1... | collective-permute-start | bytes 1179656 | tf_op jit(solution)/shard_map/ppermute | solution.py:26
  4.2 3.0 %collective-permute-start.8 = (f32[6,4,32,128]{3,2,1,0:T(8,128)S(1)}, f32[6,4,32,128]{3,2,1,0:T(8,128)S(1)}, u32[]{:S(2)}, u32[]{:S(2)}) collective-permute-start(f32[6,4,32,128]{3,2,1,0:T(8,128)S(1)} %get-tuple-element.77), channel_id=1, source_target_pairs={{16,0},{32,16},{48,32},{64,48},{80,64},{96,80},{112,96},{0,112},{1... | collective-permute-start | bytes 1179656 | tf_op jit(solution)/shard_map/ppermute | solution.py:26
  10.7 1.9 collective-permute-done.1
  12.6 1.9 broadcast_multiply_fusion.1
  17.7 1.9 broadcast_multiply_fusion
  21.4 3.0 %collective-permute-start.10 = (f32[6,4,32,128]{3,2,1,0:T(8,128)S(1)}, f32[6,4,32,128]{3,2,1,0:T(8,128)S(1)}, u32[]{:S(2)}, u32[]{:S(2)}) collective-permute-start(f32[6,4,32,128]{3,2,1,0:T(8,128)S(1)} %get-tuple-element.8), channel_id=1, source_target_pairs={{16,0},{32,16},{48,32},{64,48},{80,64},{96,80},{112,96},{0,112},{1... | collective-permute-start | bytes 1179656 | tf_op jit(solution)/shard_map/ppermute | solution.py:26
  32.8 1.9 fusion.108
  46.4 2.0 fusion.83
  53.3 1.9 fusion.156
  56.7 1.9 collective-permute-start.16
  68.7 2.1 collective-permute-done.18
  70.8 3.1 %collective-permute-done.19 = f32[6,4,32,128]{3,2,1,0:T(8,128)S(1)} collective-permute-done((f32[6,4,32,128]{3,2,1,0:T(8,128)S(1)}, f32[6,4,32,128]{3,2,1,0:T(8,128)S(1)}, u32[]{:S(2)}, u32[]{:S(2)}) %collective-permute-start.19) | collective-permute-done | bytes 393248 | tf_op jit(solution)/shard_map/ppermute | solution.py:25
  77.2 8.5 %all-to-all-start = ((f32[2,12,16,8,128]{4,3,1,0,2:T(8,128)}), f32[2,12,16,8,128]{4,3,1,0,2:T(8,128)S(1)}, u32[]{:S(2)}, u32[]{:S(2)}) async-start(f32[2,12,16,8,128]{4,3,1,0,2:T(8,128)} %copy.18), calls=%async_computation | async-start | bytes 3145728 | tf_op jit(solution)/shard_map/all_to_all | solution.py:200
  85.7 19.8 %all-to-all-done = f32[2,12,16,8,128]{4,3,1,0,2:T(8,128)S(1)} async-done(((f32[2,12,16,8,128]{4,3,1,0,2:T(8,128)}), f32[2,12,16,8,128]{4,3,1,0,2:T(8,128)S(1)}, u32[]{:S(2)}, u32[]{:S(2)}) %all-to-all-start) | async-done | bytes 1572896 | tf_op jit(solution)/shard_map/all_to_all | solution.py:200
  107.5 4.8 %shard_map.41 = (f32[192,192]{1,0:T(8,128)}, f32[192,192]{1,0:T(8,128)}) custom-call(f32[1536,128]{1,0:T(8,128)} %bitcast.25, f32[1536,128]{1,0:T(8,128)} %bitcast.31), custom_call_target="tpu_custom_call" | custom-call | tf_op jit(solution)/shard_map/pallas_call | solution.py:159
  113.3 3.2 %gather_fusion = f32[192]{0:T(256)S(1)} fusion(f32[192,192]{1,0:T(8,128)} %get-tuple-element.5, s32[192]{0:T(256)S(1)} %bitcast.24), kind=kCustom, calls=%fused_computation | custom fusion | bytes 3072 | tf_op jit(solution)/shard_map/jit(diagonal)/cond/branch_0_fun/gather | solution.py:208
  119.0 2.4 %collective-permute-start.22 = (f32[200,192]{1,0:T(8,128)S(1)}, f32[200,192]{1,0:T(8,128)S(1)}, u32[]{:S(2)}, u32[]{:S(2)}) collective-permute-start(f32[200,192]{1,0:T(8,128)S(1)} %select_add_fusion), channel_id=1, source_target_pairs={{0,64},{16,80},{32,96},{48,112},{64,0},{80,16},{96,32},{112,48},{1... | collective-permute-start | bytes 460808 | tf_op jit(solution)/shard_map/ppermute | solution.py:64
  122.8 3.5 %collective-permute-done.21 = f32[200,192]{1,0:T(8,128)S(1)} collective-permute-done((f32[200,192]{1,0:T(8,128)S(1)}, f32[200,192]{1,0:T(8,128)S(1)}, u32[]{:S(2)}, u32[]{:S(2)}) %collective-permute-start.21) | collective-permute-done | bytes 153632 | tf_op jit(solution)/shard_map/ppermute | solution.py:64
  126.3 2.2 collective-permute-done.22
  128.5 3.5 %collective-permute-done.23 = f32[200,192]{1,0:T(8,128)S(1)} collective-permute-done((f32[200,192]{1,0:T(8,128)S(1)}, f32[200,192]{1,0:T(8,128)S(1)}, u32[]{:S(2)}, u32[]{:S(2)}) %collective-permute-start.23) | collective-permute-done | bytes 153632 | tf_op jit(solution)/shard_map/ppermute | solution.py:64
  132.2 2.0 collective-permute-start.25
  134.2 5.9 %collective-permute-done.24 = f32[200,192]{1,0:T(8,128)S(1)} collective-permute-done((f32[200,192]{1,0:T(8,128)S(1)}, f32[200,192]{1,0:T(8,128)S(1)}, u32[]{:S(2)}, u32[]{:S(2)}) %collective-permute-start.24) | collective-permute-done | bytes 153632 | tf_op jit(solution)/shard_map/ppermute | solution.py:64
  141.8 3.4 %collective-permute-done.26 = f32[200,192]{1,0:T(8,128)S(1)} collective-permute-done((f32[200,192]{1,0:T(8,128)S(1)}, f32[200,192]{1,0:T(8,128)S(1)}, u32[]{:S(2)}, u32[]{:S(2)}) %collective-permute-start.26) | collective-permute-done | bytes 153632 | tf_op jit(solution)/shard_map/ppermute | solution.py:64
  148.7 4.6 %collective-permute-done.27 = f32[200,192]{1,0:T(8,128)S(1)} collective-permute-done((f32[200,192]{1,0:T(8,128)S(1)}, f32[200,192]{1,0:T(8,128)S(1)}, u32[]{:S(2)}, u32[]{:S(2)}) %collective-permute-start.27) | collective-permute-done | bytes 153632 | tf_op jit(solution)/shard_map/ppermute | solution.py:64
  153.3 3.1 %collective-permute-done.28 = f32[200,192]{1,0:T(8,128)S(1)} collective-permute-done((f32[200,192]{1,0:T(8,128)S(1)}, f32[200,192]{1,0:T(8,128)S(1)}, u32[]{:S(2)}, u32[]{:S(2)}) %collective-permute-start.28) | collective-permute-done | bytes 153632 | tf_op jit(solution)/shard_map/ppermute | solution.py:64
  156.4 3.1 %collective-permute-done.29 = f32[200,192]{1,0:T(8,128)S(1)} collective-permute-done((f32[200,192]{1,0:T(8,128)S(1)}, f32[200,192]{1,0:T(8,128)S(1)}, u32[]{:S(2)}, u32[]{:S(2)}) %collective-permute-start.29) | collective-permute-done | bytes 153632 | tf_op jit(solution)/shard_map/ppermute | solution.py:64
  162.9 23.7 %shard_map.42 = f32[192,192]{1,0:T(8,128)} custom-call(f32[192,192]{1,0:T(8,128)} %reshape.35.c_ref), custom_call_target="tpu_custom_call" | custom-call | tf_op jit(solution)/shard_map/pallas_call | solution.py:143
  190.8 3.5 %shard_map.43 = f32[1536,128]{1,0:T(8,128)} custom-call(f32[192,192]{1,0:T(8,128)} %reshape.37.refs_0_, f32[1536,128]{1,0:T(8,128)} %bitcast.26), custom_call_target="tpu_custom_call" | custom-call | tf_op jit(solution)/shard_map/pallas_call | solution.py:168
  194.3 2.1 copy.24
  196.4 4.3 %all-to-all-start.1 = ((f32[12,16,8,128]{3,2,0,1:T(8,128)}), f32[12,16,8,128]{3,2,0,1:T(8,128)}, u32[]{:S(2)}, u32[]{:S(2)}) async-start(f32[12,16,8,128]{3,2,0,1:T(8,128)} %copy.24), calls=%async_computation.1 | async-start | bytes 1572864 | tf_op jit(solution)/shard_map/all_to_all | solution.py:225
  204.4 11.2 %all-to-all-done.1 = f32[12,16,8,128]{3,2,0,1:T(8,128)} async-done(((f32[12,16,8,128]{3,2,0,1:T(8,128)}), f32[12,16,8,128]{3,2,0,1:T(8,128)}, u32[]{:S(2)}, u32[]{:S(2)}) %all-to-all-start.1) | async-done | bytes 786464 | tf_op jit(solution)/shard_map/all_to_all | solution.py:225
  215.5 2.1 copy.25
  (231 shorter events, 72.4 us)
Async XLA Ops:
  1.9 8.8 %collective-permute-start = (f32[6,4,32,128]{3,2,1,0:T(8,128)S(1)}, f32[6,4,32,128]{3,2,1,0:T(8,128)S(1)}, u32[]{:S(2)}, u32[]{:S(2)}) collective-permute-start(f32[6,4,32,128]{3,2,1,0:T(8,128)S(1)} %get-tuple-element.76), channel_id=1, source_target_pairs={{16,0},{32,16},{48,32},{64,48},{80,64},{96,80},{112,96},{0,112},{1... | collective-permute-start | bytes 1179656 | tf_op jit(solution)/shard_map/ppermute | solution.py:26
  4.2 8.4 %collective-permute-start.1 = (f32[6,4,32,128]{3,2,1,0:T(8,128)S(1)}, f32[6,4,32,128]{3,2,1,0:T(8,128)S(1)}, u32[]{:S(2)}, u32[]{:S(2)}) collective-permute-start(f32[6,4,32,128]{3,2,1,0:T(8,128)S(1)} %get-tuple-element.76), channel_id=1, source_target_pairs={{0,16},{16,32},{32,48},{48,64},{64,80},{80,96},{96,112},{112,0},{1... | collective-permute-start | bytes 1179656 | tf_op jit(solution)/shard_map/ppermute | solution.py:25
  4.2 13.4 %collective-permute-start.8 = (f32[6,4,32,128]{3,2,1,0:T(8,128)S(1)}, f32[6,4,32,128]{3,2,1,0:T(8,128)S(1)}, u32[]{:S(2)}, u32[]{:S(2)}) collective-permute-start(f32[6,4,32,128]{3,2,1,0:T(8,128)S(1)} %get-tuple-element.77), channel_id=1, source_target_pairs={{16,0},{32,16},{48,32},{64,48},{80,64},{96,80},{112,96},{0,112},{1... | collective-permute-start | bytes 1179656 | tf_op jit(solution)/shard_map/ppermute | solution.py:26
  7.2 10.5 %collective-permute-start.9 = (f32[6,4,32,128]{3,2,1,0:T(8,128)S(1)}, f32[6,4,32,128]{3,2,1,0:T(8,128)S(1)}, u32[]{:S(2)}, u32[]{:S(2)}) collective-permute-start(f32[6,4,32,128]{3,2,1,0:T(8,128)S(1)} %get-tuple-element.77), channel_id=1, source_target_pairs={{0,16},{16,32},{32,48},{48,64},{64,80},{80,96},{96,112},{112,0},{1... | collective-permute-start | bytes 1179656 | tf_op jit(solution)/shard_map/ppermute | solution.py:25
  16.4 8.0 %collective-permute-start.2 = (f32[6,4,32,128]{3,2,1,0:T(8,128)S(1)}, f32[6,4,32,128]{3,2,1,0:T(8,128)S(1)}, u32[]{:S(2)}, u32[]{:S(2)}) collective-permute-start(f32[6,4,32,128]{3,2,1,0:T(8,128)S(1)} %get-tuple-element.6), channel_id=1, source_target_pairs={{16,0},{32,16},{48,32},{64,48},{80,64},{96,80},{112,96},{0,112},{1... | collective-permute-start | bytes 1179656 | tf_op jit(solution)/shard_map/ppermute | solution.py:26
  17.6 8.4 %collective-permute-start.3 = (f32[6,4,32,128]{3,2,1,0:T(8,128)S(1)}, f32[6,4,32,128]{3,2,1,0:T(8,128)S(1)}, u32[]{:S(2)}, u32[]{:S(2)}) collective-permute-start(f32[6,4,32,128]{3,2,1,0:T(8,128)S(1)} %get-tuple-element.6), channel_id=1, source_target_pairs={{0,16},{16,32},{32,48},{48,64},{64,80},{80,96},{96,112},{112,0},{1... | collective-permute-start | bytes 1179656 | tf_op jit(solution)/shard_map/ppermute | solution.py:25
  21.4 9.9 %collective-permute-start.10 = (f32[6,4,32,128]{3,2,1,0:T(8,128)S(1)}, f32[6,4,32,128]{3,2,1,0:T(8,128)S(1)}, u32[]{:S(2)}, u32[]{:S(2)}) collective-permute-start(f32[6,4,32,128]{3,2,1,0:T(8,128)S(1)} %get-tuple-element.8), channel_id=1, source_target_pairs={{16,0},{32,16},{48,32},{64,48},{80,64},{96,80},{112,96},{0,112},{1... | collective-permute-start | bytes 1179656 | tf_op jit(solution)/shard_map/ppermute | solution.py:26
  24.4 8.4 %collective-permute-start.11 = (f32[6,4,32,128]{3,2,1,0:T(8,128)S(1)}, f32[6,4,32,128]{3,2,1,0:T(8,128)S(1)}, u32[]{:S(2)}, u32[]{:S(2)}) collective-permute-start(f32[6,4,32,128]{3,2,1,0:T(8,128)S(1)} %get-tuple-element.8), channel_id=1, source_target_pairs={{0,16},{16,32},{32,48},{48,64},{64,80},{80,96},{96,112},{112,0},{1... | collective-permute-start | bytes 1179656 | tf_op jit(solution)/shard_map/ppermute | solution.py:25
  29.6 8.6 %collective-permute-start.4 = (f32[6,4,32,128]{3,2,1,0:T(8,128)S(1)}, f32[6,4,32,128]{3,2,1,0:T(8,128)S(1)}, u32[]{:S(2)}, u32[]{:S(2)}) collective-permute-start(f32[6,4,32,128]{3,2,1,0:T(8,128)S(1)} %fusion.206), channel_id=1, source_target_pairs={{16,0},{32,16},{48,32},{64,48},{80,64},{96,80},{112,96},{0,112},{1... | collective-permute-start | bytes 1179656 | tf_op jit(solution)/shard_map/ppermute | solution.py:26
  31.1 8.4 %collective-permute-start.5 = (f32[6,4,32,128]{3,2,1,0:T(8,128)S(1)}, f32[6,4,32,128]{3,2,1,0:T(8,128)S(1)}, u32[]{:S(2)}, u32[]{:S(2)}) collective-permute-start(f32[6,4,32,128]{3,2,1,0:T(8,128)S(1)} %fusion.206), channel_id=1, source_target_pairs={{0,16},{16,32},{32,48},{48,64},{64,80},{80,96},{96,112},{112,0},{1... | collective-permute-start | bytes 1179656 | tf_op jit(solution)/shard_map/ppermute | solution.py:25
  36.4 8.7 %collective-permute-start.12 = (f32[6,4,32,128]{3,2,1,0:T(8,128)S(1)}, f32[6,4,32,128]{3,2,1,0:T(8,128)S(1)}, u32[]{:S(2)}, u32[]{:S(2)}) collective-permute-start(f32[6,4,32,128]{3,2,1,0:T(8,128)S(1)} %fusion.108), channel_id=1, source_target_pairs={{16,0},{32,16},{48,32},{64,48},{80,64},{96,80},{112,96},{0,112},{1... | collective-permute-start | bytes 1179656 | tf_op jit(solution)/shard_map/ppermute | solution.py:26
  38.0 8.4 %collective-permute-start.13 = (f32[6,4,32,128]{3,2,1,0:T(8,128)S(1)}, f32[6,4,32,128]{3,2,1,0:T(8,128)S(1)}, u32[]{:S(2)}, u32[]{:S(2)}) collective-permute-start(f32[6,4,32,128]{3,2,1,0:T(8,128)S(1)} %fusion.108), channel_id=1, source_target_pairs={{0,16},{16,32},{32,48},{48,64},{64,80},{80,96},{96,112},{112,0},{1... | collective-permute-start | bytes 1179656 | tf_op jit(solution)/shard_map/ppermute | solution.py:25
  43.1 8.9 %collective-permute-start.6 = (f32[6,4,32,128]{3,2,1,0:T(8,128)S(1)}, f32[6,4,32,128]{3,2,1,0:T(8,128)S(1)}, u32[]{:S(2)}, u32[]{:S(2)}) collective-permute-start(f32[6,4,32,128]{3,2,1,0:T(8,128)S(1)} %fusion.181), channel_id=1, source_target_pairs={{16,0},{32,16},{48,32},{64,48},{80,64},{96,80},{112,96},{0,112},{1... | collective-permute-start | bytes 1179656 | tf_op jit(solution)/shard_map/ppermute | solution.py:26
  44.8 8.4 %collective-permute-start.7 = (f32[6,4,32,128]{3,2,1,0:T(8,128)S(1)}, f32[6,4,32,128]{3,2,1,0:T(8,128)S(1)}, u32[]{:S(2)}, u32[]{:S(2)}) collective-permute-start(f32[6,4,32,128]{3,2,1,0:T(8,128)S(1)} %fusion.181), channel_id=1, source_target_pairs={{0,16},{16,32},{32,48},{48,64},{64,80},{80,96},{96,112},{112,0},{1... | collective-permute-start | bytes 1179656 | tf_op jit(solution)/shard_map/ppermute | solution.py:25
  50.2 8.7 %collective-permute-start.14 = (f32[6,4,32,128]{3,2,1,0:T(8,128)S(1)}, f32[6,4,32,128]{3,2,1,0:T(8,128)S(1)}, u32[]{:S(2)}, u32[]{:S(2)}) collective-permute-start(f32[6,4,32,128]{3,2,1,0:T(8,128)S(1)} %fusion.83), channel_id=1, source_target_pairs={{16,0},{32,16},{48,32},{64,48},{80,64},{96,80},{112,96},{0,112},{1... | collective-permute-start | bytes 1179656 | tf_op jit(solution)/shard_map/ppermute | solution.py:26
  51.9 8.4 %collective-permute-start.15 = (f32[6,4,32,128]{3,2,1,0:T(8,128)S(1)}, f32[6,4,32,128]{3,2,1,0:T(8,128)S(1)}, u32[]{:S(2)}, u32[]{:S(2)}) collective-permute-start(f32[6,4,32,128]{3,2,1,0:T(8,128)S(1)} %fusion.83), channel_id=1, source_target_pairs={{0,16},{16,32},{32,48},{48,64},{64,80},{80,96},{96,112},{112,0},{1... | collective-permute-start | bytes 1179656 | tf_op jit(solution)/shard_map/ppermute | solution.py:25
  56.7 9.1 %collective-permute-start.16 = (f32[6,4,32,128]{3,2,1,0:T(8,128)S(1)}, f32[6,4,32,128]{3,2,1,0:T(8,128)S(1)}, u32[]{:S(2)}, u32[]{:S(2)}) collective-permute-start(f32[6,4,32,128]{3,2,1,0:T(8,128)S(1)} %fusion.156), channel_id=1, source_target_pairs={{16,0},{32,16},{48,32},{64,48},{80,64},{96,80},{112,96},{0,112},{1... | collective-permute-start | bytes 1179656 | tf_op jit(solution)/shard_map/ppermute | solution.py:26
  58.6 8.4 %collective-permute-start.17 = (f32[6,4,32,128]{3,2,1,0:T(8,128)S(1)}, f32[6,4,32,128]{3,2,1,0:T(8,128)S(1)}, u32[]{:S(2)}, u32[]{:S(2)}) collective-permute-start(f32[6,4,32,128]{3,2,1,0:T(8,128)S(1)} %fusion.156), channel_id=1, source_target_pairs={{0,16},{16,32},{32,48},{48,64},{64,80},{80,96},{96,112},{112,0},{1... | collective-permute-start | bytes 1179656 | tf_op jit(solution)/shard_map/ppermute | solution.py:25
  63.9 7.0 %collective-permute-start.18 = (f32[6,4,32,128]{3,2,1,0:T(8,128)S(1)}, f32[6,4,32,128]{3,2,1,0:T(8,128)S(1)}, u32[]{:S(2)}, u32[]{:S(2)}) collective-permute-start(f32[6,4,32,128]{3,2,1,0:T(8,128)S(1)} %fusion.58), channel_id=1, source_target_pairs={{16,0},{32,16},{48,32},{64,48},{80,64},{96,80},{112,96},{0,112},{1... | collective-permute-start | bytes 1179656 | tf_op jit(solution)/shard_map/ppermute | solution.py:26
  65.6 8.4 %collective-permute-start.19 = (f32[6,4,32,128]{3,2,1,0:T(8,128)S(1)}, f32[6,4,32,128]{3,2,1,0:T(8,128)S(1)}, u32[]{:S(2)}, u32[]{:S(2)}) collective-permute-start(f32[6,4,32,128]{3,2,1,0:T(8,128)S(1)} %fusion.58), channel_id=1, source_target_pairs={{0,16},{16,32},{32,48},{48,64},{64,80},{80,96},{96,112},{112,0},{1... | collective-permute-start | bytes 1179656 | tf_op jit(solution)/shard_map/ppermute | solution.py:25
  77.2 28.3 %all-to-all-start = ((f32[2,12,16,8,128]{4,3,1,0,2:T(8,128)}), f32[2,12,16,8,128]{4,3,1,0,2:T(8,128)S(1)}, u32[]{:S(2)}, u32[]{:S(2)}) async-start(f32[2,12,16,8,128]{4,3,1,0,2:T(8,128)} %copy.18), calls=%async_computation | async-start | bytes 3145728 | tf_op jit(solution)/shard_map/all_to_all | solution.py:200
  116.7 1.5 collective-permute-start.20
  118.3 8.0 %collective-permute-start.21 = (f32[200,192]{1,0:T(8,128)S(1)}, f32[200,192]{1,0:T(8,128)S(1)}, u32[]{:S(2)}, u32[]{:S(2)}) collective-permute-start(f32[200,192]{1,0:T(8,128)S(1)} %select_add_fusion), channel_id=1, source_target_pairs={{0,96},{16,112},{32,0},{48,16},{64,32},{80,48},{96,64},{112,80},{1... | collective-permute-start | bytes 460808 | tf_op jit(solution)/shard_map/ppermute | solution.py:64
  119.0 9.5 %collective-permute-start.22 = (f32[200,192]{1,0:T(8,128)S(1)}, f32[200,192]{1,0:T(8,128)S(1)}, u32[]{:S(2)}, u32[]{:S(2)}) collective-permute-start(f32[200,192]{1,0:T(8,128)S(1)} %select_add_fusion), channel_id=1, source_target_pairs={{0,64},{16,80},{32,96},{48,112},{64,0},{80,16},{96,32},{112,48},{1... | collective-permute-start | bytes 460808 | tf_op jit(solution)/shard_map/ppermute | solution.py:64
  121.5 10.5 %collective-permute-start.23 = (f32[200,192]{1,0:T(8,128)S(1)}, f32[200,192]{1,0:T(8,128)S(1)}, u32[]{:S(2)}, u32[]{:S(2)}) collective-permute-start(f32[200,192]{1,0:T(8,128)S(1)} %select_add_fusion), channel_id=1, source_target_pairs={{0,32},{16,48},{32,64},{48,80},{64,96},{80,112},{96,0},{112,16},{1... | collective-permute-start | bytes 460808 | tf_op jit(solution)/shard_map/ppermute | solution.py:64
  132.1 8.0 %collective-permute-start.24 = (f32[200,192]{1,0:T(8,128)S(1)}, f32[200,192]{1,0:T(8,128)S(1)}, u32[]{:S(2)}, u32[]{:S(2)}) collective-permute-start(f32[200,192]{1,0:T(8,128)S(1)} %add_add_fusion.1), channel_id=1, source_target_pairs={{0,3},{1,0},{2,1},{3,2},{4,7},{5,4},{6,5},{7,6},{8,11},{9,8},{10,9... | collective-permute-start | bytes 460808 | tf_op jit(solution)/shard_map/ppermute | solution.py:64
  132.2 9.6 %collective-permute-start.25 = (f32[200,192]{1,0:T(8,128)S(1)}, f32[200,192]{1,0:T(8,128)S(1)}, u32[]{:S(2)}, u32[]{:S(2)}) collective-permute-start(f32[200,192]{1,0:T(8,128)S(1)} %add_add_fusion.1), channel_id=1, source_target_pairs={{0,2},{1,3},{2,0},{3,1},{4,6},{5,7},{6,4},{7,5},{8,10},{9,11},{10,... | collective-permute-start | bytes 460808 | tf_op jit(solution)/shard_map/ppermute | solution.py:64
  134.2 11.0 %collective-permute-start.26 = (f32[200,192]{1,0:T(8,128)S(1)}, f32[200,192]{1,0:T(8,128)S(1)}, u32[]{:S(2)}, u32[]{:S(2)}) collective-permute-start(f32[200,192]{1,0:T(8,128)S(1)} %add_add_fusion.1), channel_id=1, source_target_pairs={{0,1},{1,2},{2,3},{3,0},{4,5},{5,6},{6,7},{7,4},{8,9},{9,10},{10,1... | collective-permute-start | bytes 460808 | tf_op jit(solution)/shard_map/ppermute | solution.py:64
  145.3 8.0 %collective-permute-start.27 = (f32[200,192]{1,0:T(8,128)S(1)}, f32[200,192]{1,0:T(8,128)S(1)}, u32[]{:S(2)}, u32[]{:S(2)}) collective-permute-start(f32[200,192]{1,0:T(8,128)S(1)} %add_add_fusion), channel_id=1, source_target_pairs={{0,12},{1,13},{2,14},{3,15},{4,0},{5,1},{6,2},{7,3},{8,4},{9,5},{1... | collective-permute-start | bytes 460808 | tf_op jit(solution)/shard_map/ppermute | solution.py:64
  146.9 9.5 %collective-permute-start.28 = (f32[200,192]{1,0:T(8,128)S(1)}, f32[200,192]{1,0:T(8,128)S(1)}, u32[]{:S(2)}, u32[]{:S(2)}) collective-permute-start(f32[200,192]{1,0:T(8,128)S(1)} %add_add_fusion), channel_id=1, source_target_pairs={{0,8},{1,9},{2,10},{3,11},{4,12},{5,13},{6,14},{7,15},{8,0},{9,1},... | collective-permute-start | bytes 460808 | tf_op jit(solution)/shard_map/ppermute | solution.py:64
  147.9 11.6 %collective-permute-start.29 = (f32[200,192]{1,0:T(8,128)S(1)}, f32[200,192]{1,0:T(8,128)S(1)}, u32[]{:S(2)}, u32[]{:S(2)}) collective-permute-start(f32[200,192]{1,0:T(8,128)S(1)} %add_add_fusion), channel_id=1, source_target_pairs={{0,4},{1,5},{2,6},{3,7},{4,8},{5,9},{6,10},{7,11},{8,12},{9,13},{1... | collective-permute-start | bytes 460808 | tf_op jit(solution)/shard_map/ppermute | solution.py:64
  196.4 19.1 %all-to-all-start.1 = ((f32[12,16,8,128]{3,2,0,1:T(8,128)}), f32[12,16,8,128]{3,2,0,1:T(8,128)}, u32[]{:S(2)}, u32[]{:S(2)}) async-start(f32[12,16,8,128]{3,2,0,1:T(8,128)} %copy.24), calls=%async_computation.1 | async-start | bytes 1572864 | tf_op jit(solution)/shard_map/all_to_all | solution.py:225
  (3 other events, 8.3 us)

commit v8 on v7

--- a/solution.py
+++ b/solution.py
@@ -191,15 +191,18 @@
     for order in range(1, DEGREE):
         following = [2.0 / half * (apply(c) - center * c) - p for c, p in zip(current, previous)]
         previous, current = (current, following)
+    filtered = jnp.concatenate(current)
     image = jnp.concatenate([apply(c) for c in current])
-    current = jnp.concatenate(current)
+    current = filtered
     groups = lax.axis_size("band")
     rows = depth * rows_y * rows_x // groups // rows_x
     lanes = rows_x
-    chunked = jnp.stack([current, image]).reshape(2, bdev, groups, rows, lanes)
-    spread = lax.all_to_all(chunked, "band", 2, 2, tiled=True)
-    flat_cd = spread[0].reshape(bdev * groups * rows, lanes)
-    image_cd = spread[1].reshape(bdev * groups * rows, lanes)
+    def spread(x):
+        y = lax.all_to_all(x.reshape(bdev, groups, rows, lanes), "band", 1, 1, tiled=True)
+        return y.reshape(bdev * groups * rows, lanes)
+
+    flat_cd = spread(current)
+    image_cd = spread(image)
     c_perm, g_perm = grams(rows, flat_cd, image_cd)
     below = lax.broadcasted_iota(jnp.int32, (nbands, nbands), 0) >= lax.broadcasted_iota(
         jnp.int32, (nbands, nbands), 1

time: 221 us -> 245 us (1.11)
  local copies, waits for them, and re-layouts: 40.3 us -> 63.6 us
  waiting for transfers between devices: 79.9 us -> 65.2 us
  starting transfers between devices: 42.4 us -> 51.4 us
  other arithmetic: 20.3 us -> 25.9 us
    slice x72, local copies, waits for them, and re-layouts: 14.3 us -> 25.9 us  [hamiltonian(): near = near + jnp.roll(field, reach, 3) + jnp.roll(field, -reach, 3)]
    slice x72, local copies, waits for them, and re-layouts: 3.54 us -> 13.8 us  [hamiltonian(): near = near + jnp.roll(field, reach, 2) + jnp.roll(field, -reach, 2)]
    all_to_all x1 -> x2, waiting for transfers between devices: 19.8 us -> 11.7 us  [spread(): lax.all_to_all(x.reshape(bdev, groups, rows, lanes), 'band', 1, 1, tiled=...]
    ppermute x10, waiting for transfers between devices: 14.5 us -> 8.42 us  [extended(): before = lax.ppermute(last, axis, up)]
    all_to_all x1 -> x2, starting transfers between devices: 8.46 us -> 14.5 us  [spread(): lax.all_to_all(x.reshape(bdev, groups, rows, lanes), 'band', 1, 1, tiled=...]
    sub x2, other arithmetic: 3.3 us -> 8.56 us  [hamiltonian(): return potential[None] * field - 0.5 * laplace]
  transfers between devices with their start and end apart: 32 -> 33, of which waited for: 22 -> 19; matrix products, arithmetic and copies ran while one was open for 18% -> 29% of each run, Pallas kernels for 0% -> 0%
where the time goes in v8:
time: 245 us; the launch traced here: 241 us
  waiting for transfers between devices  65.2 us (27%)
  local copies, waits for them, and re-layouts  63.6 us (26%)
  starting transfers between devices  51.4 us (21%)
  Pallas kernels  32 us (13%)
  other arithmetic  25.9 us (11%)
    ppermute x10, waiting for transfers between devices, group_sum(): received.append(lax.ppermute(x, axis, pairs))  34 us
    slice x72, local copies, waits for them, and re-layouts, hamiltonian(): near = near + jnp.roll(field, reach, 3) + jnp.roll(field, -reach, 3)  25.9 us
    pallas_call x1, Pallas kernels, lower_inverse(): pl.pallas_call(inverse_kernel, out_shape=jax.ShapeDtypeStruct((n, n), jnp...  23.7 us
    ppermute x10, starting transfers between devices, extended(): after = lax.ppermute(initial, axis, down)  21.2 us
    all_to_all x2, starting transfers between devices, spread(): lax.all_to_all(x.reshape(bdev, groups, rows, lanes), 'band', 1, 1, tiled=...  14.5 us
    slice x72, local copies, waits for them, and re-layouts, hamiltonian(): near = near + jnp.roll(field, reach, 2) + jnp.roll(field, -reach, 2)  13.8 us
    all_to_all x2, waiting for transfers between devices, spread(): lax.all_to_all(x.reshape(bdev, groups, rows, lanes), 'band', 1, 1, tiled=...  11.7 us
    sub x6, other arithmetic, local(): 2.0 / half * (apply(c) - center * c) - p  11.6 us
  transfers between devices with their start and end apart: 33, of which 19 were waited for; matrix products, arithmetic and copies ran while one was open for 29% of the time, Pallas kernels for 0%

profile of v8, /device:TPU:0, one launch (start us, length us, event | category | flops | bytes accessed | tf_op | source)
XLA Modules:
  0.0 241.3 jit_solution(2140338791699695429)
XLA Ops:
  1.9 2.3 collective-permute-start
  4.2 3.0 %collective-permute-start.8 = (f32[6,4,32,128]{3,2,1,0:T(8,128)S(1)}, f32[6,4,32,128]{3,2,1,0:T(8,128)S(1)}, u32[]{:S(2)}, u32[]{:S(2)}) collective-permute-start(f32[6,4,32,128]{3,2,1,0:T(8,128)S(1)} %get-tuple-element.75), channel_id=1, source_target_pairs={{16,0},{32,16},{48,32},{64,48},{80,64},{96,80},{112,96},{0,112},{1... | collective-permute-start | bytes 1179656 | tf_op jit(solution)/shard_map/ppermute | solution.py:26
  12.6 2.0 broadcast_multiply_fusion.1
  17.8 1.9 broadcast_multiply_fusion
  21.6 3.0 %collective-permute-start.10 = (f32[6,4,32,128]{3,2,1,0:T(8,128)S(1)}, f32[6,4,32,128]{3,2,1,0:T(8,128)S(1)}, u32[]{:S(2)}, u32[]{:S(2)}) collective-permute-start(f32[6,4,32,128]{3,2,1,0:T(8,128)S(1)} %get-tuple-element.8), channel_id=1, source_target_pairs={{16,0},{32,16},{48,32},{64,48},{80,64},{96,80},{112,96},{0,112},{1... | collective-permute-start | bytes 1179656 | tf_op jit(solution)/shard_map/ppermute | solution.py:26
  46.7 2.1 fusion.83
  64.7 2.0 collective-permute-start.16
  69.0 2.0 fusion.58
  82.0 3.0 %collective-permute-start.18 = (f32[6,4,32,128]{3,2,1,0:T(8,128)S(1)}, f32[6,4,32,128]{3,2,1,0:T(8,128)}, u32[]{:S(2)}, u32[]{:S(2)}) collective-permute-start(f32[6,4,32,128]{3,2,1,0:T(8,128)S(1)} %fusion.58), channel_id=1, source_target_pairs={{16,0},{32,16},{48,32},{64,48},{80,64},{96,80},{112,96},{0,112},{1... | collective-permute-start | bytes 1179656 | tf_op jit(solution)/shard_map/ppermute | solution.py:26
  88.9 8.0 %all-to-all-start = ((f32[12,16,8,128]{3,2,0,1:T(8,128)}), f32[12,16,8,128]{3,2,0,1:T(8,128)S(1)}, u32[]{:S(2)}, u32[]{:S(2)}) async-start(f32[12,16,8,128]{3,2,0,1:T(8,128)} %copy.18), calls=%async_computation | async-start | bytes 1572864 | tf_op jit(solution)/shard_map/all_to_all | solution.py:201
  97.2 5.3 %fusion.33 = f32[6,4,32,128]{3,2,1,0:T(8,128)S(1)} fusion(f32[6,4,32,128]{3,2,1,0:T(8,128)} %collective-permute-done.17, f32[6,4,32,128]{3,2,1,0:T(8,128)S(1)} %fusion.156, f32[6,4,32,128]{3,2,1,0:T(8,128)} %collective-permute-done.16, f32[6,4,31,128]{3,2,1,0:T(8,128)} %get-tuple-element.107, f32[6,4,1,128]{3,2,1,0:T(1,128)} %get-tuple-element.109, ...), kind=kLoop, calls=%fused_computation.116 | loop fusion | flops 5308416 | bytes 7929856 | tf_op jit(solution)/shard_map/sub | solution.py:52
  103.6 3.2 %fusion.11 = f32[6,4,32,128]{3,2,1,0:T(8,128)S(1)} fusion(f32[6,4,32,128]{3,2,1,0:T(8,128)} %collective-permute-done.19, f32[6,4,32,128]{3,2,1,0:T(8,128)S(1)} %fusion.58, f32[6,4,32,128]{3,2,1,0:T(8,128)} %collective-permute-done.18, f32[6,4,31,128]{3,2,1,0:T(8,128)S(1)} %copy-done.26, f32[6,4,1,128]{3,2,1,0:T(1,128)S(1)} %copy-done.31, ...), kind=kLoop, calls=%fused_computation.94 | loop fusion | flops 5308416 | bytes 7929856 | tf_op jit(solution)/shard_map/sub | solution.py:52
  109.1 6.5 %all-to-all-start.1 = ((f32[12,16,8,128]{3,2,0,1:T(8,128)}), f32[12,16,8,128]{3,2,0,1:T(8,128)S(1)}, u32[]{:S(2)}, u32[]{:S(2)}) async-start(f32[12,16,8,128]{3,2,0,1:T(8,128)} %copy.20), calls=%async_computation.1 | async-start | bytes 1572864 | tf_op jit(solution)/shard_map/all_to_all | solution.py:201
  116.6 10.5 %all-to-all-done.1 = f32[12,16,8,128]{3,2,0,1:T(8,128)S(1)} async-done(((f32[12,16,8,128]{3,2,0,1:T(8,128)}), f32[12,16,8,128]{3,2,0,1:T(8,128)S(1)}, u32[]{:S(2)}, u32[]{:S(2)}) %all-to-all-start.1) | async-done | bytes 786464 | tf_op jit(solution)/shard_map/all_to_all | solution.py:201
  128.1 4.7 %shard_map.41 = (f32[192,192]{1,0:T(8,128)}, f32[192,192]{1,0:T(8,128)}) custom-call(f32[1536,128]{1,0:T(8,128)} %bitcast.25, f32[1536,128]{1,0:T(8,128)} %bitcast.31), custom_call_target="tpu_custom_call" | custom-call | tf_op jit(solution)/shard_map/pallas_call | solution.py:159
  133.9 3.2 %gather_fusion = f32[192]{0:T(256)S(1)} fusion(f32[192,192]{1,0:T(8,128)} %get-tuple-element.5, s32[192]{0:T(256)S(1)} %bitcast.24), kind=kCustom, calls=%fused_computation | custom fusion | bytes 3072 | tf_op jit(solution)/shard_map/jit(diagonal)/cond/branch_0_fun/gather | solution.py:211
  138.9 4.4 %collective-permute-start.21 = (f32[200,192]{1,0:T(8,128)S(1)}, f32[200,192]{1,0:T(8,128)S(1)}, u32[]{:S(2)}, u32[]{:S(2)}) collective-permute-start(f32[200,192]{1,0:T(8,128)S(1)} %select_add_fusion), channel_id=1, source_target_pairs={{0,96},{16,112},{32,0},{48,16},{64,32},{80,48},{96,64},{112,80},{1... | collective-permute-start | bytes 460808 | tf_op jit(solution)/shard_map/ppermute | solution.py:64
  144.3 8.3 %collective-permute-done.21 = f32[200,192]{1,0:T(8,128)S(1)} collective-permute-done((f32[200,192]{1,0:T(8,128)S(1)}, f32[200,192]{1,0:T(8,128)S(1)}, u32[]{:S(2)}, u32[]{:S(2)}) %collective-permute-start.21) | collective-permute-done | bytes 153632 | tf_op jit(solution)/shard_map/ppermute | solution.py:64
  152.8 3.2 %collective-permute-done.23 = f32[200,192]{1,0:T(8,128)S(1)} collective-permute-done((f32[200,192]{1,0:T(8,128)S(1)}, f32[200,192]{1,0:T(8,128)S(1)}, u32[]{:S(2)}, u32[]{:S(2)}) %collective-permute-start.23) | collective-permute-done | bytes 153632 | tf_op jit(solution)/shard_map/ppermute | solution.py:64
  156.7 2.2 collective-permute-start.25
  158.9 5.3 %collective-permute-done.24 = f32[200,192]{1,0:T(8,128)S(1)} collective-permute-done((f32[200,192]{1,0:T(8,128)S(1)}, f32[200,192]{1,0:T(8,128)S(1)}, u32[]{:S(2)}, u32[]{:S(2)}) %collective-permute-start.24) | collective-permute-done | bytes 153632 | tf_op jit(solution)/shard_map/ppermute | solution.py:64
  164.1 2.0 collective-permute-done.25
  166.1 2.9 %collective-permute-done.26 = f32[200,192]{1,0:T(8,128)S(1)} collective-permute-done((f32[200,192]{1,0:T(8,128)S(1)}, f32[200,192]{1,0:T(8,128)S(1)}, u32[]{:S(2)}, u32[]{:S(2)}) %collective-permute-start.26) | collective-permute-done | bytes 153632 | tf_op jit(solution)/shard_map/ppermute | solution.py:64
  172.3 4.8 %collective-permute-done.27 = f32[200,192]{1,0:T(8,128)S(1)} collective-permute-done((f32[200,192]{1,0:T(8,128)S(1)}, f32[200,192]{1,0:T(8,128)S(1)}, u32[]{:S(2)}, u32[]{:S(2)}) %collective-permute-start.27) | collective-permute-done | bytes 153632 | tf_op jit(solution)/shard_map/ppermute | solution.py:64
  177.1 2.8 %collective-permute-done.28 = f32[200,192]{1,0:T(8,128)S(1)} collective-permute-done((f32[200,192]{1,0:T(8,128)S(1)}, f32[200,192]{1,0:T(8,128)S(1)}, u32[]{:S(2)}, u32[]{:S(2)}) %collective-permute-start.28) | collective-permute-done | bytes 153632 | tf_op jit(solution)/shard_map/ppermute | solution.py:64
  179.9 3.1 %collective-permute-done.29 = f32[200,192]{1,0:T(8,128)S(1)} collective-permute-done((f32[200,192]{1,0:T(8,128)S(1)}, f32[200,192]{1,0:T(8,128)S(1)}, u32[]{:S(2)}, u32[]{:S(2)}) %collective-permute-start.29) | collective-permute-done | bytes 153632 | tf_op jit(solution)/shard_map/ppermute | solution.py:64
  186.4 23.7 %shard_map.42 = f32[192,192]{1,0:T(8,128)} custom-call(f32[192,192]{1,0:T(8,128)} %reshape.46.c_ref), custom_call_target="tpu_custom_call" | custom-call | tf_op jit(solution)/shard_map/pallas_call | solution.py:143
  214.3 3.5 %shard_map.43 = f32[1536,128]{1,0:T(8,128)} custom-call(f32[192,192]{1,0:T(8,128)} %reshape.48.refs_0_, f32[1536,128]{1,0:T(8,128)} %bitcast.26), custom_call_target="tpu_custom_call" | custom-call | tf_op jit(solution)/shard_map/pallas_call | solution.py:168
  217.9 2.1 copy.25
  219.9 4.3 %all-to-all-start.2 = ((f32[12,16,8,128]{3,2,0,1:T(8,128)}), f32[12,16,8,128]{3,2,0,1:T(8,128)}, u32[]{:S(2)}, u32[]{:S(2)}) async-start(f32[12,16,8,128]{3,2,0,1:T(8,128)} %copy.25), calls=%async_computation.2 | async-start | bytes 1572864 | tf_op jit(solution)/shard_map/all_to_all | solution.py:228
  227.9 11.1 %all-to-all-done.2 = f32[12,16,8,128]{3,2,0,1:T(8,128)} async-done(((f32[12,16,8,128]{3,2,0,1:T(8,128)}), f32[12,16,8,128]{3,2,0,1:T(8,128)}, u32[]{:S(2)}, u32[]{:S(2)}) %all-to-all-start.2) | async-done | bytes 786464 | tf_op jit(solution)/shard_map/all_to_all | solution.py:228
  239.1 2.1 copy.26
  (290 shorter events, 90.7 us)
Async XLA Ops:
  1.9 8.9 %collective-permute-start = (f32[6,4,32,128]{3,2,1,0:T(8,128)S(1)}, f32[6,4,32,128]{3,2,1,0:T(8,128)S(1)}, u32[]{:S(2)}, u32[]{:S(2)}) collective-permute-start(f32[6,4,32,128]{3,2,1,0:T(8,128)S(1)} %get-tuple-element.74), channel_id=1, source_target_pairs={{16,0},{32,16},{48,32},{64,48},{80,64},{96,80},{112,96},{0,112},{1... | collective-permute-start | bytes 1179656 | tf_op jit(solution)/shard_map/ppermute | solution.py:26
  4.2 8.4 %collective-permute-start.1 = (f32[6,4,32,128]{3,2,1,0:T(8,128)S(1)}, f32[6,4,32,128]{3,2,1,0:T(8,128)S(1)}, u32[]{:S(2)}, u32[]{:S(2)}) collective-permute-start(f32[6,4,32,128]{3,2,1,0:T(8,128)S(1)} %get-tuple-element.74), channel_id=1, source_target_pairs={{0,16},{16,32},{32,48},{48,64},{64,80},{80,96},{96,112},{112,0},{1... | collective-permute-start | bytes 1179656 | tf_op jit(solution)/shard_map/ppermute | solution.py:25
  4.2 13.6 %collective-permute-start.8 = (f32[6,4,32,128]{3,2,1,0:T(8,128)S(1)}, f32[6,4,32,128]{3,2,1,0:T(8,128)S(1)}, u32[]{:S(2)}, u32[]{:S(2)}) collective-permute-start(f32[6,4,32,128]{3,2,1,0:T(8,128)S(1)} %get-tuple-element.75), channel_id=1, source_target_pairs={{16,0},{32,16},{48,32},{64,48},{80,64},{96,80},{112,96},{0,112},{1... | collective-permute-start | bytes 1179656 | tf_op jit(solution)/shard_map/ppermute | solution.py:26
  7.2 10.7 %collective-permute-start.9 = (f32[6,4,32,128]{3,2,1,0:T(8,128)S(1)}, f32[6,4,32,128]{3,2,1,0:T(8,128)S(1)}, u32[]{:S(2)}, u32[]{:S(2)}) collective-permute-start(f32[6,4,32,128]{3,2,1,0:T(8,128)S(1)} %get-tuple-element.75), channel_id=1, source_target_pairs={{0,16},{16,32},{32,48},{48,64},{64,80},{80,96},{96,112},{112,0},{1... | collective-permute-start | bytes 1179656 | tf_op jit(solution)/shard_map/ppermute | solution.py:25
  16.5 8.2 %collective-permute-start.2 = (f32[6,4,32,128]{3,2,1,0:T(8,128)S(1)}, f32[6,4,32,128]{3,2,1,0:T(8,128)S(1)}, u32[]{:S(2)}, u32[]{:S(2)}) collective-permute-start(f32[6,4,32,128]{3,2,1,0:T(8,128)S(1)} %get-tuple-element.6), channel_id=1, source_target_pairs={{16,0},{32,16},{48,32},{64,48},{80,64},{96,80},{112,96},{0,112},{1... | collective-permute-start | bytes 1179656 | tf_op jit(solution)/shard_map/ppermute | solution.py:26
  17.7 8.4 %collective-permute-start.3 = (f32[6,4,32,128]{3,2,1,0:T(8,128)S(1)}, f32[6,4,32,128]{3,2,1,0:T(8,128)S(1)}, u32[]{:S(2)}, u32[]{:S(2)}) collective-permute-start(f32[6,4,32,128]{3,2,1,0:T(8,128)S(1)} %get-tuple-element.6), channel_id=1, source_target_pairs={{0,16},{16,32},{32,48},{48,64},{64,80},{80,96},{96,112},{112,0},{1... | collective-permute-start | bytes 1179656 | tf_op jit(solution)/shard_map/ppermute | solution.py:25
  21.6 9.9 %collective-permute-start.10 = (f32[6,4,32,128]{3,2,1,0:T(8,128)S(1)}, f32[6,4,32,128]{3,2,1,0:T(8,128)S(1)}, u32[]{:S(2)}, u32[]{:S(2)}) collective-permute-start(f32[6,4,32,128]{3,2,1,0:T(8,128)S(1)} %get-tuple-element.8), channel_id=1, source_target_pairs={{16,0},{32,16},{48,32},{64,48},{80,64},{96,80},{112,96},{0,112},{1... | collective-permute-start | bytes 1179656 | tf_op jit(solution)/shard_map/ppermute | solution.py:26
  24.6 8.4 %collective-permute-start.11 = (f32[6,4,32,128]{3,2,1,0:T(8,128)S(1)}, f32[6,4,32,128]{3,2,1,0:T(8,128)S(1)}, u32[]{:S(2)}, u32[]{:S(2)}) collective-permute-start(f32[6,4,32,128]{3,2,1,0:T(8,128)S(1)} %get-tuple-element.8), channel_id=1, source_target_pairs={{0,16},{16,32},{32,48},{48,64},{64,80},{80,96},{96,112},{112,0},{1... | collective-permute-start | bytes 1179656 | tf_op jit(solution)/shard_map/ppermute | solution.py:25
  29.8 8.7 %collective-permute-start.4 = (f32[6,4,32,128]{3,2,1,0:T(8,128)S(1)}, f32[6,4,32,128]{3,2,1,0:T(8,128)S(1)}, u32[]{:S(2)}, u32[]{:S(2)}) collective-permute-start(f32[6,4,32,128]{3,2,1,0:T(8,128)S(1)} %fusion.206), channel_id=1, source_target_pairs={{16,0},{32,16},{48,32},{64,48},{80,64},{96,80},{112,96},{0,112},{1... | collective-permute-start | bytes 1179656 | tf_op jit(solution)/shard_map/ppermute | solution.py:26
  31.4 8.4 %collective-permute-start.5 = (f32[6,4,32,128]{3,2,1,0:T(8,128)S(1)}, f32[6,4,32,128]{3,2,1,0:T(8,128)S(1)}, u32[]{:S(2)}, u32[]{:S(2)}) collective-permute-start(f32[6,4,32,128]{3,2,1,0:T(8,128)S(1)} %fusion.206), channel_id=1, source_target_pairs={{0,16},{16,32},{32,48},{48,64},{64,80},{80,96},{96,112},{112,0},{1... | collective-permute-start | bytes 1179656 | tf_op jit(solution)/shard_map/ppermute | solution.py:25
  36.6 8.7 %collective-permute-start.12 = (f32[6,4,32,128]{3,2,1,0:T(8,128)S(1)}, f32[6,4,32,128]{3,2,1,0:T(8,128)S(1)}, u32[]{:S(2)}, u32[]{:S(2)}) collective-permute-start(f32[6,4,32,128]{3,2,1,0:T(8,128)S(1)} %fusion.108), channel_id=1, source_target_pairs={{16,0},{32,16},{48,32},{64,48},{80,64},{96,80},{112,96},{0,112},{1... | collective-permute-start | bytes 1179656 | tf_op jit(solution)/shard_map/ppermute | solution.py:26
  38.3 8.4 %collective-permute-start.13 = (f32[6,4,32,128]{3,2,1,0:T(8,128)S(1)}, f32[6,4,32,128]{3,2,1,0:T(8,128)S(1)}, u32[]{:S(2)}, u32[]{:S(2)}) collective-permute-start(f32[6,4,32,128]{3,2,1,0:T(8,128)S(1)} %fusion.108), channel_id=1, source_target_pairs={{0,16},{16,32},{32,48},{48,64},{64,80},{80,96},{96,112},{112,0},{1... | collective-permute-start | bytes 1179656 | tf_op jit(solution)/shard_map/ppermute | solution.py:25
  43.5 9.0 %collective-permute-start.6 = (f32[6,4,32,128]{3,2,1,0:T(8,128)S(1)}, f32[6,4,32,128]{3,2,1,0:T(8,128)S(1)}, u32[]{:S(2)}, u32[]{:S(2)}) collective-permute-start(f32[6,4,32,128]{3,2,1,0:T(8,128)S(1)} %fusion.181), channel_id=1, source_target_pairs={{16,0},{32,16},{48,32},{64,48},{80,64},{96,80},{112,96},{0,112},{1... | collective-permute-start | bytes 1179656 | tf_op jit(solution)/shard_map/ppermute | solution.py:26
  45.2 8.4 %collective-permute-start.7 = (f32[6,4,32,128]{3,2,1,0:T(8,128)S(1)}, f32[6,4,32,128]{3,2,1,0:T(8,128)S(1)}, u32[]{:S(2)}, u32[]{:S(2)}) collective-permute-start(f32[6,4,32,128]{3,2,1,0:T(8,128)S(1)} %fusion.181), channel_id=1, source_target_pairs={{0,16},{16,32},{32,48},{48,64},{64,80},{80,96},{96,112},{112,0},{1... | collective-permute-start | bytes 1179656 | tf_op jit(solution)/shard_map/ppermute | solution.py:25
  50.6 18.4 %collective-permute-start.14 = (f32[6,4,32,128]{3,2,1,0:T(8,128)S(1)}, f32[6,4,32,128]{3,2,1,0:T(8,128)S(1)}, u32[]{:S(2)}, u32[]{:S(2)}) collective-permute-start(f32[6,4,32,128]{3,2,1,0:T(8,128)S(1)} %fusion.83), channel_id=1, source_target_pairs={{16,0},{32,16},{48,32},{64,48},{80,64},{96,80},{112,96},{0,112},{1... | collective-permute-start | bytes 1179656 | tf_op jit(solution)/shard_map/ppermute | solution.py:26
  52.3 16.7 %collective-permute-start.15 = (f32[6,4,32,128]{3,2,1,0:T(8,128)S(1)}, f32[6,4,32,128]{3,2,1,0:T(8,128)S(1)}, u32[]{:S(2)}, u32[]{:S(2)}) collective-permute-start(f32[6,4,32,128]{3,2,1,0:T(8,128)S(1)} %fusion.83), channel_id=1, source_target_pairs={{0,16},{16,32},{32,48},{48,64},{64,80},{80,96},{96,112},{112,0},{1... | collective-permute-start | bytes 1179656 | tf_op jit(solution)/shard_map/ppermute | solution.py:25
  64.7 32.2 %collective-permute-start.16 = (f32[6,4,32,128]{3,2,1,0:T(8,128)S(1)}, f32[6,4,32,128]{3,2,1,0:T(8,128)}, u32[]{:S(2)}, u32[]{:S(2)}) collective-permute-start(f32[6,4,32,128]{3,2,1,0:T(8,128)S(1)} %fusion.156), channel_id=1, source_target_pairs={{16,0},{32,16},{48,32},{64,48},{80,64},{96,80},{112,96},{0,112},{1... | collective-permute-start | bytes 1179656 | tf_op jit(solution)/shard_map/ppermute | solution.py:26
  66.7 30.2 %collective-permute-start.17 = (f32[6,4,32,128]{3,2,1,0:T(8,128)S(1)}, f32[6,4,32,128]{3,2,1,0:T(8,128)}, u32[]{:S(2)}, u32[]{:S(2)}) collective-permute-start(f32[6,4,32,128]{3,2,1,0:T(8,128)S(1)} %fusion.156), channel_id=1, source_target_pairs={{0,16},{16,32},{32,48},{48,64},{64,80},{80,96},{96,112},{112,0},{1... | collective-permute-start | bytes 1179656 | tf_op jit(solution)/shard_map/ppermute | solution.py:25
  82.0 20.6 %collective-permute-start.18 = (f32[6,4,32,128]{3,2,1,0:T(8,128)S(1)}, f32[6,4,32,128]{3,2,1,0:T(8,128)}, u32[]{:S(2)}, u32[]{:S(2)}) collective-permute-start(f32[6,4,32,128]{3,2,1,0:T(8,128)S(1)} %fusion.58), channel_id=1, source_target_pairs={{16,0},{32,16},{48,32},{64,48},{80,64},{96,80},{112,96},{0,112},{1... | collective-permute-start | bytes 1179656 | tf_op jit(solution)/shard_map/ppermute | solution.py:26
  84.9 17.7 %collective-permute-start.19 = (f32[6,4,32,128]{3,2,1,0:T(8,128)S(1)}, f32[6,4,32,128]{3,2,1,0:T(8,128)}, u32[]{:S(2)}, u32[]{:S(2)}) collective-permute-start(f32[6,4,32,128]{3,2,1,0:T(8,128)S(1)} %fusion.58), channel_id=1, source_target_pairs={{0,16},{16,32},{32,48},{48,64},{64,80},{80,96},{96,112},{112,0},{1... | collective-permute-start | bytes 1179656 | tf_op jit(solution)/shard_map/ppermute | solution.py:25
  88.9 20.2 %all-to-all-start = ((f32[12,16,8,128]{3,2,0,1:T(8,128)}), f32[12,16,8,128]{3,2,0,1:T(8,128)S(1)}, u32[]{:S(2)}, u32[]{:S(2)}) async-start(f32[12,16,8,128]{3,2,0,1:T(8,128)} %copy.18), calls=%async_computation | async-start | bytes 1572864 | tf_op jit(solution)/shard_map/all_to_all | solution.py:201
  109.1 18.1 %all-to-all-start.1 = ((f32[12,16,8,128]{3,2,0,1:T(8,128)}), f32[12,16,8,128]{3,2,0,1:T(8,128)S(1)}, u32[]{:S(2)}, u32[]{:S(2)}) async-start(f32[12,16,8,128]{3,2,0,1:T(8,128)} %copy.20), calls=%async_computation.1 | async-start | bytes 1572864 | tf_op jit(solution)/shard_map/all_to_all | solution.py:201
  138.9 13.7 %collective-permute-start.21 = (f32[200,192]{1,0:T(8,128)S(1)}, f32[200,192]{1,0:T(8,128)S(1)}, u32[]{:S(2)}, u32[]{:S(2)}) collective-permute-start(f32[200,192]{1,0:T(8,128)S(1)} %select_add_fusion), channel_id=1, source_target_pairs={{0,96},{16,112},{32,0},{48,16},{64,32},{80,48},{96,64},{112,80},{1... | collective-permute-start | bytes 460808 | tf_op jit(solution)/shard_map/ppermute | solution.py:64
  143.3 9.5 %collective-permute-start.22 = (f32[200,192]{1,0:T(8,128)S(1)}, f32[200,192]{1,0:T(8,128)S(1)}, u32[]{:S(2)}, u32[]{:S(2)}) collective-permute-start(f32[200,192]{1,0:T(8,128)S(1)} %select_add_fusion), channel_id=1, source_target_pairs={{0,64},{16,80},{32,96},{48,112},{64,0},{80,16},{96,32},{112,48},{1... | collective-permute-start | bytes 460808 | tf_op jit(solution)/shard_map/ppermute | solution.py:64
  143.3 12.7 %collective-permute-start.23 = (f32[200,192]{1,0:T(8,128)S(1)}, f32[200,192]{1,0:T(8,128)S(1)}, u32[]{:S(2)}, u32[]{:S(2)}) collective-permute-start(f32[200,192]{1,0:T(8,128)S(1)} %select_add_fusion), channel_id=1, source_target_pairs={{0,32},{16,48},{32,64},{48,80},{64,96},{80,112},{96,0},{112,16},{1... | collective-permute-start | bytes 460808 | tf_op jit(solution)/shard_map/ppermute | solution.py:64
  156.1 8.0 %collective-permute-start.24 = (f32[200,192]{1,0:T(8,128)S(1)}, f32[200,192]{1,0:T(8,128)S(1)}, u32[]{:S(2)}, u32[]{:S(2)}) collective-permute-start(f32[200,192]{1,0:T(8,128)S(1)} %add_add_fusion.1), channel_id=1, source_target_pairs={{0,3},{1,0},{2,1},{3,2},{4,7},{5,4},{6,5},{7,6},{8,11},{9,8},{10,9... | collective-permute-start | bytes 460808 | tf_op jit(solution)/shard_map/ppermute | solution.py:64
  156.7 9.5 %collective-permute-start.25 = (f32[200,192]{1,0:T(8,128)S(1)}, f32[200,192]{1,0:T(8,128)S(1)}, u32[]{:S(2)}, u32[]{:S(2)}) collective-permute-start(f32[200,192]{1,0:T(8,128)S(1)} %add_add_fusion.1), channel_id=1, source_target_pairs={{0,2},{1,3},{2,0},{3,1},{4,6},{5,7},{6,4},{7,5},{8,10},{9,11},{10,... | collective-permute-start | bytes 460808 | tf_op jit(solution)/shard_map/ppermute | solution.py:64
  158.9 10.1 %collective-permute-start.26 = (f32[200,192]{1,0:T(8,128)S(1)}, f32[200,192]{1,0:T(8,128)S(1)}, u32[]{:S(2)}, u32[]{:S(2)}) collective-permute-start(f32[200,192]{1,0:T(8,128)S(1)} %add_add_fusion.1), channel_id=1, source_target_pairs={{0,1},{1,2},{2,3},{3,0},{4,5},{5,6},{6,7},{7,4},{8,9},{9,10},{10,1... | collective-permute-start | bytes 460808 | tf_op jit(solution)/shard_map/ppermute | solution.py:64
  169.1 8.0 %collective-permute-start.27 = (f32[200,192]{1,0:T(8,128)S(1)}, f32[200,192]{1,0:T(8,128)S(1)}, u32[]{:S(2)}, u32[]{:S(2)}) collective-permute-start(f32[200,192]{1,0:T(8,128)S(1)} %add_add_fusion), channel_id=1, source_target_pairs={{0,12},{1,13},{2,14},{3,15},{4,0},{5,1},{6,2},{7,3},{8,4},{9,5},{1... | collective-permute-start | bytes 460808 | tf_op jit(solution)/shard_map/ppermute | solution.py:64
  170.4 9.5 %collective-permute-start.28 = (f32[200,192]{1,0:T(8,128)S(1)}, f32[200,192]{1,0:T(8,128)S(1)}, u32[]{:S(2)}, u32[]{:S(2)}) collective-permute-start(f32[200,192]{1,0:T(8,128)S(1)} %add_add_fusion), channel_id=1, source_target_pairs={{0,8},{1,9},{2,10},{3,11},{4,12},{5,13},{6,14},{7,15},{8,0},{9,1},... | collective-permute-start | bytes 460808 | tf_op jit(solution)/shard_map/ppermute | solution.py:64
  172.3 10.7 %collective-permute-start.29 = (f32[200,192]{1,0:T(8,128)S(1)}, f32[200,192]{1,0:T(8,128)S(1)}, u32[]{:S(2)}, u32[]{:S(2)}) collective-permute-start(f32[200,192]{1,0:T(8,128)S(1)} %add_add_fusion), channel_id=1, source_target_pairs={{0,4},{1,5},{2,6},{3,7},{4,8},{5,9},{6,10},{7,11},{8,12},{9,13},{1... | collective-permute-start | bytes 460808 | tf_op jit(solution)/shard_map/ppermute | solution.py:64
  219.9 19.1 %all-to-all-start.2 = ((f32[12,16,8,128]{3,2,0,1:T(8,128)}), f32[12,16,8,128]{3,2,0,1:T(8,128)}, u32[]{:S(2)}, u32[]{:S(2)}) async-start(f32[12,16,8,128]{3,2,0,1:T(8,128)} %copy.25), calls=%async_computation.2 | async-start | bytes 1572864 | tf_op jit(solution)/shard_map/all_to_all | solution.py:228
  (33 other events, 180.7 us)

commit v9 on v7

--- a/solution.py
+++ b/solution.py
@@ -122,7 +122,7 @@
             pivot = jnp.sum(jnp.where(lane_a[:1] == k, row_a, 0.0), axis=1, keepdims=True)
             col = jnp.sum(jnp.where(lane_a == k, a, 0.0), axis=1, keepdims=True)
             below = lax.broadcasted_iota(jnp.int32, (rows, 1), 0) + r0 > k
-            factor = jnp.where(below, col, 0.0) / pivot
+            factor = jnp.where(below, col, 0.0) * (1.0 / pivot)
             a_ref[r0:, ta * tile :] = a - factor * row_a
             b_ref[r0:, : tb * tile] = b_ref[r0:, : tb * tile] - factor * row_b
             return carry
@@ -205,7 +205,7 @@
         jnp.int32, (nbands, nbands), 1
     )
     packed = jnp.concatenate(
-        [jnp.where(below, c_perm, g_perm), jnp.diagonal(g_perm)[None], jnp.zeros((7, nbands), jnp.float32)]
+        [jnp.where(below, c_perm, g_perm), jnp.sum(jnp.where(lax.broadcasted_iota(jnp.int32, (nbands, nbands), 0) == lax.broadcasted_iota(jnp.int32, (nbands, nbands), 1), g_perm, 0.0), axis=0, keepdims=True), jnp.zeros((7, nbands), jnp.float32)]
     )
     packed = mesh_sum(packed) / ncells
     tri, g_diag = packed[:nbands], packed[nbands]

time: 221 us -> 218 us (0.986)
  local copies, waits for them, and re-layouts: 40.3 us -> 37.1 us
    gather x1 -> x0, local copies, waits for them, and re-layouts: 3.23 us -> none  [local(): jnp.diagonal(g_perm)[None]]
where the time goes in v9:
time: 218 us; the launch traced here: 215 us
  waiting for transfers between devices  79.9 us (37%)
  starting transfers between devices  42.2 us (19%)
  local copies, waits for them, and re-layouts  37.1 us (17%)
  Pallas kernels  32.1 us (15%)
  other arithmetic  20.6 us (9%)
    ppermute x10, waiting for transfers between devices, group_sum(): received.append(lax.ppermute(x, axis, pairs))  32.3 us
    pallas_call x1, Pallas kernels, lower_inverse(): pl.pallas_call(inverse_kernel, out_shape=jax.ShapeDtypeStruct((n, n), jnp...  23.8 us
    all_to_all x1, waiting for transfers between devices, local(): spread = lax.all_to_all(chunked, 'band', 2, 2, tiled=True)  19.8 us
    ppermute x10, starting transfers between devices, extended(): after = lax.ppermute(initial, axis, down)  19.5 us
    ppermute x10, waiting for transfers between devices, extended(): before = lax.ppermute(last, axis, up)  14.6 us
    slice x72, local copies, waits for them, and re-layouts, hamiltonian(): near = near + jnp.roll(field, reach, 3) + jnp.roll(field, -reach, 3)  14.3 us
    sub x6, other arithmetic, local(): 2.0 / half * (apply(c) - center * c) - p  11.2 us
    all_to_all x1, waiting for transfers between devices, local(): lax.all_to_all(basis_cd, 'band', 1, 1, tiled=True).reshape(psi.shape)  11.1 us
  transfers between devices with their start and end apart: 32, of which 22 were waited for; matrix products, arithmetic and copies ran while one was open for 18% of the time, Pallas kernels for 0%

profile of v9, /device:TPU:0, one launch (start us, length us, event | category | flops | bytes accessed | tf_op | source)
XLA Modules:
  0.0 214.9 jit_solution(16015192987630131193)
XLA Ops:
  1.9 2.3 %collective-permute-start = (f32[6,4,32,128]{3,2,1,0:T(8,128)S(1)}, f32[6,4,32,128]{3,2,1,0:T(8,128)S(1)}, u32[]{:S(2)}, u32[]{:S(2)}) collective-permute-start(f32[6,4,32,128]{3,2,1,0:T(8,128)S(1)} %get-tuple-element.76), channel_id=1, source_target_pairs={{16,0},{32,16},{48,32},{64,48},{80,64},{96,80},{112,96},{0,112},{1... | collective-permute-start | bytes 1179656 | tf_op jit(solution)/shard_map/ppermute | solution.py:26
  4.2 3.0 %collective-permute-start.8 = (f32[6,4,32,128]{3,2,1,0:T(8,128)S(1)}, f32[6,4,32,128]{3,2,1,0:T(8,128)S(1)}, u32[]{:S(2)}, u32[]{:S(2)}) collective-permute-start(f32[6,4,32,128]{3,2,1,0:T(8,128)S(1)} %get-tuple-element.77), channel_id=1, source_target_pairs={{16,0},{32,16},{48,32},{64,48},{80,64},{96,80},{112,96},{0,112},{1... | collective-permute-start | bytes 1179656 | tf_op jit(solution)/shard_map/ppermute | solution.py:26
  10.7 1.9 collective-permute-done.1
  12.6 2.3 %broadcast_multiply_fusion.1 = (f32[6,4,32,128]{3,2,1,0:T(8,128)S(1)}, f32[6,4,32,128]{3,2,1,0:T(8,128)S(1)}) fusion(f32[6,4,32,128]{3,2,1,0:T(8,128)S(1)} %get-tuple-element.76, f32[6,4,32,4]{3,2,1,0:T(8,128)S(1)} %get-tuple-element.70, f32[6,4,32,124]{3,2,1,0:T(8,128)S(1)} %get-tuple-element.74, f32[6,4,32,124]{3,2,1,0:T(8,128)S(1)} %get-tuple-element.72, ...), kind=kLoop, calls=%fused_computation.464 | loop fusion | flops 5603328 | bytes 8323072 | tf_op jit(solution)/shard_map/div | solution.py:190
  18.0 1.9 broadcast_multiply_fusion
  21.7 3.0 %collective-permute-start.10 = (f32[6,4,32,128]{3,2,1,0:T(8,128)S(1)}, f32[6,4,32,128]{3,2,1,0:T(8,128)S(1)}, u32[]{:S(2)}, u32[]{:S(2)}) collective-permute-start(f32[6,4,32,128]{3,2,1,0:T(8,128)S(1)} %get-tuple-element.8), channel_id=1, source_target_pairs={{16,0},{32,16},{48,32},{64,48},{80,64},{96,80},{112,96},{0,112},{1... | collective-permute-start | bytes 1179656 | tf_op jit(solution)/shard_map/ppermute | solution.py:26
  26.3 1.8 fusion.206
  33.1 1.9 fusion.108
  46.8 2.0 fusion.83
  53.6 1.9 fusion.156
  57.1 1.9 collective-permute-start.16
  69.0 2.1 collective-permute-done.18
  71.2 3.1 %collective-permute-done.19 = f32[6,4,32,128]{3,2,1,0:T(8,128)S(1)} collective-permute-done((f32[6,4,32,128]{3,2,1,0:T(8,128)S(1)}, f32[6,4,32,128]{3,2,1,0:T(8,128)S(1)}, u32[]{:S(2)}, u32[]{:S(2)}) %collective-permute-start.19) | collective-permute-done | bytes 393248 | tf_op jit(solution)/shard_map/ppermute | solution.py:25
  77.5 8.3 %all-to-all-start = ((f32[2,12,16,8,128]{4,3,1,0,2:T(8,128)}), f32[2,12,16,8,128]{4,3,1,0,2:T(8,128)S(1)}, u32[]{:S(2)}, u32[]{:S(2)}) async-start(f32[2,12,16,8,128]{4,3,1,0,2:T(8,128)} %copy.18), calls=%async_computation | async-start | bytes 3145728 | tf_op jit(solution)/shard_map/all_to_all | solution.py:200
  85.8 19.8 %all-to-all-done = f32[2,12,16,8,128]{4,3,1,0,2:T(8,128)S(1)} async-done(((f32[2,12,16,8,128]{4,3,1,0,2:T(8,128)}), f32[2,12,16,8,128]{4,3,1,0,2:T(8,128)S(1)}, u32[]{:S(2)}, u32[]{:S(2)}) %all-to-all-start) | async-done | bytes 1572896 | tf_op jit(solution)/shard_map/all_to_all | solution.py:200
  107.7 4.8 %shard_map.41 = (f32[192,192]{1,0:T(8,128)}, f32[192,192]{1,0:T(8,128)}) custom-call(f32[1536,128]{1,0:T(8,128)} %bitcast.23, f32[1536,128]{1,0:T(8,128)} %bitcast.29), custom_call_target="tpu_custom_call" | custom-call | tf_op jit(solution)/shard_map/pallas_call | solution.py:159
  115.9 2.4 %collective-permute-start.22 = (f32[200,192]{1,0:T(8,128)S(1)}, f32[200,192]{1,0:T(8,128)S(1)}, u32[]{:S(2)}, u32[]{:S(2)}) collective-permute-start(f32[200,192]{1,0:T(8,128)S(1)} %select_add_fusion), channel_id=1, source_target_pairs={{0,64},{16,80},{32,96},{48,112},{64,0},{80,16},{96,32},{112,48},{1... | collective-permute-start | bytes 460808 | tf_op jit(solution)/shard_map/ppermute | solution.py:64
  119.7 3.5 %collective-permute-done.21 = f32[200,192]{1,0:T(8,128)S(1)} collective-permute-done((f32[200,192]{1,0:T(8,128)S(1)}, f32[200,192]{1,0:T(8,128)S(1)}, u32[]{:S(2)}, u32[]{:S(2)}) %collective-permute-start.21) | collective-permute-done | bytes 153632 | tf_op jit(solution)/shard_map/ppermute | solution.py:64
  123.2 2.2 %collective-permute-done.22 = f32[200,192]{1,0:T(8,128)S(1)} collective-permute-done((f32[200,192]{1,0:T(8,128)S(1)}, f32[200,192]{1,0:T(8,128)S(1)}, u32[]{:S(2)}, u32[]{:S(2)}) %collective-permute-start.22) | collective-permute-done | bytes 153632 | tf_op jit(solution)/shard_map/ppermute | solution.py:64
  125.4 3.5 %collective-permute-done.23 = f32[200,192]{1,0:T(8,128)S(1)} collective-permute-done((f32[200,192]{1,0:T(8,128)S(1)}, f32[200,192]{1,0:T(8,128)S(1)}, u32[]{:S(2)}, u32[]{:S(2)}) %collective-permute-start.23) | collective-permute-done | bytes 153632 | tf_op jit(solution)/shard_map/ppermute | solution.py:64
  129.1 2.0 collective-permute-start.25
  131.1 5.9 %collective-permute-done.24 = f32[200,192]{1,0:T(8,128)S(1)} collective-permute-done((f32[200,192]{1,0:T(8,128)S(1)}, f32[200,192]{1,0:T(8,128)S(1)}, u32[]{:S(2)}, u32[]{:S(2)}) %collective-permute-start.24) | collective-permute-done | bytes 153632 | tf_op jit(solution)/shard_map/ppermute | solution.py:64
  138.7 3.4 %collective-permute-done.26 = f32[200,192]{1,0:T(8,128)S(1)} collective-permute-done((f32[200,192]{1,0:T(8,128)S(1)}, f32[200,192]{1,0:T(8,128)S(1)}, u32[]{:S(2)}, u32[]{:S(2)}) %collective-permute-start.26) | collective-permute-done | bytes 153632 | tf_op jit(solution)/shard_map/ppermute | solution.py:64
  145.6 4.6 %collective-permute-done.27 = f32[200,192]{1,0:T(8,128)S(1)} collective-permute-done((f32[200,192]{1,0:T(8,128)S(1)}, f32[200,192]{1,0:T(8,128)S(1)}, u32[]{:S(2)}, u32[]{:S(2)}) %collective-permute-start.27) | collective-permute-done | bytes 153632 | tf_op jit(solution)/shard_map/ppermute | solution.py:64
  150.2 3.1 %collective-permute-done.28 = f32[200,192]{1,0:T(8,128)S(1)} collective-permute-done((f32[200,192]{1,0:T(8,128)S(1)}, f32[200,192]{1,0:T(8,128)S(1)}, u32[]{:S(2)}, u32[]{:S(2)}) %collective-permute-start.28) | collective-permute-done | bytes 153632 | tf_op jit(solution)/shard_map/ppermute | solution.py:64
  153.3 3.1 %collective-permute-done.29 = f32[200,192]{1,0:T(8,128)S(1)} collective-permute-done((f32[200,192]{1,0:T(8,128)S(1)}, f32[200,192]{1,0:T(8,128)S(1)}, u32[]{:S(2)}, u32[]{:S(2)}) %collective-permute-start.29) | collective-permute-done | bytes 153632 | tf_op jit(solution)/shard_map/ppermute | solution.py:64
  159.8 23.8 %shard_map.42 = f32[192,192]{1,0:T(8,128)} custom-call(f32[192,192]{1,0:T(8,128)} %reshape.35.c_ref), custom_call_target="tpu_custom_call" | custom-call | tf_op jit(solution)/shard_map/pallas_call | solution.py:143
  187.8 3.5 %shard_map.43 = f32[1536,128]{1,0:T(8,128)} custom-call(f32[192,192]{1,0:T(8,128)} %reshape.37.refs_0_, f32[1536,128]{1,0:T(8,128)} %bitcast.24), custom_call_target="tpu_custom_call" | custom-call | tf_op jit(solution)/shard_map/pallas_call | solution.py:168
  191.3 2.1 copy.24
  193.4 4.3 %all-to-all-start.1 = ((f32[12,16,8,128]{3,2,0,1:T(8,128)}), f32[12,16,8,128]{3,2,0,1:T(8,128)}, u32[]{:S(2)}, u32[]{:S(2)}) async-start(f32[12,16,8,128]{3,2,0,1:T(8,128)} %copy.24), calls=%async_computation.1 | async-start | bytes 1572864 | tf_op jit(solution)/shard_map/all_to_all | solution.py:225
  201.4 11.1 %all-to-all-done.1 = f32[12,16,8,128]{3,2,0,1:T(8,128)} async-done(((f32[12,16,8,128]{3,2,0,1:T(8,128)}), f32[12,16,8,128]{3,2,0,1:T(8,128)}, u32[]{:S(2)}, u32[]{:S(2)}) %all-to-all-start.1) | async-done | bytes 786464 | tf_op jit(solution)/shard_map/all_to_all | solution.py:225
  212.5 2.1 copy.25
  (229 shorter events, 70.6 us)
Async XLA Ops:
  1.9 8.8 %collective-permute-start = (f32[6,4,32,128]{3,2,1,0:T(8,128)S(1)}, f32[6,4,32,128]{3,2,1,0:T(8,128)S(1)}, u32[]{:S(2)}, u32[]{:S(2)}) collective-permute-start(f32[6,4,32,128]{3,2,1,0:T(8,128)S(1)} %get-tuple-element.76), channel_id=1, source_target_pairs={{16,0},{32,16},{48,32},{64,48},{80,64},{96,80},{112,96},{0,112},{1... | collective-permute-start | bytes 1179656 | tf_op jit(solution)/shard_map/ppermute | solution.py:26
  4.2 8.4 %collective-permute-start.1 = (f32[6,4,32,128]{3,2,1,0:T(8,128)S(1)}, f32[6,4,32,128]{3,2,1,0:T(8,128)S(1)}, u32[]{:S(2)}, u32[]{:S(2)}) collective-permute-start(f32[6,4,32,128]{3,2,1,0:T(8,128)S(1)} %get-tuple-element.76), channel_id=1, source_target_pairs={{0,16},{16,32},{32,48},{48,64},{64,80},{80,96},{96,112},{112,0},{1... | collective-permute-start | bytes 1179656 | tf_op jit(solution)/shard_map/ppermute | solution.py:25
  4.2 13.8 %collective-permute-start.8 = (f32[6,4,32,128]{3,2,1,0:T(8,128)S(1)}, f32[6,4,32,128]{3,2,1,0:T(8,128)S(1)}, u32[]{:S(2)}, u32[]{:S(2)}) collective-permute-start(f32[6,4,32,128]{3,2,1,0:T(8,128)S(1)} %get-tuple-element.77), channel_id=1, source_target_pairs={{16,0},{32,16},{48,32},{64,48},{80,64},{96,80},{112,96},{0,112},{1... | collective-permute-start | bytes 1179656 | tf_op jit(solution)/shard_map/ppermute | solution.py:26
  7.2 10.8 %collective-permute-start.9 = (f32[6,4,32,128]{3,2,1,0:T(8,128)S(1)}, f32[6,4,32,128]{3,2,1,0:T(8,128)S(1)}, u32[]{:S(2)}, u32[]{:S(2)}) collective-permute-start(f32[6,4,32,128]{3,2,1,0:T(8,128)S(1)} %get-tuple-element.77), channel_id=1, source_target_pairs={{0,16},{16,32},{32,48},{48,64},{64,80},{80,96},{96,112},{112,0},{1... | collective-permute-start | bytes 1179656 | tf_op jit(solution)/shard_map/ppermute | solution.py:25
  16.8 8.0 %collective-permute-start.2 = (f32[6,4,32,128]{3,2,1,0:T(8,128)S(1)}, f32[6,4,32,128]{3,2,1,0:T(8,128)S(1)}, u32[]{:S(2)}, u32[]{:S(2)}) collective-permute-start(f32[6,4,32,128]{3,2,1,0:T(8,128)S(1)} %get-tuple-element.6), channel_id=1, source_target_pairs={{16,0},{32,16},{48,32},{64,48},{80,64},{96,80},{112,96},{0,112},{1... | collective-permute-start | bytes 1179656 | tf_op jit(solution)/shard_map/ppermute | solution.py:26
  17.9 8.4 %collective-permute-start.3 = (f32[6,4,32,128]{3,2,1,0:T(8,128)S(1)}, f32[6,4,32,128]{3,2,1,0:T(8,128)S(1)}, u32[]{:S(2)}, u32[]{:S(2)}) collective-permute-start(f32[6,4,32,128]{3,2,1,0:T(8,128)S(1)} %get-tuple-element.6), channel_id=1, source_target_pairs={{0,16},{16,32},{32,48},{48,64},{64,80},{80,96},{96,112},{112,0},{1... | collective-permute-start | bytes 1179656 | tf_op jit(solution)/shard_map/ppermute | solution.py:25
  21.7 9.9 %collective-permute-start.10 = (f32[6,4,32,128]{3,2,1,0:T(8,128)S(1)}, f32[6,4,32,128]{3,2,1,0:T(8,128)S(1)}, u32[]{:S(2)}, u32[]{:S(2)}) collective-permute-start(f32[6,4,32,128]{3,2,1,0:T(8,128)S(1)} %get-tuple-element.8), channel_id=1, source_target_pairs={{16,0},{32,16},{48,32},{64,48},{80,64},{96,80},{112,96},{0,112},{1... | collective-permute-start | bytes 1179656 | tf_op jit(solution)/shard_map/ppermute | solution.py:26
  24.7 8.4 %collective-permute-start.11 = (f32[6,4,32,128]{3,2,1,0:T(8,128)S(1)}, f32[6,4,32,128]{3,2,1,0:T(8,128)S(1)}, u32[]{:S(2)}, u32[]{:S(2)}) collective-permute-start(f32[6,4,32,128]{3,2,1,0:T(8,128)S(1)} %get-tuple-element.8), channel_id=1, source_target_pairs={{0,16},{16,32},{32,48},{48,64},{64,80},{80,96},{96,112},{112,0},{1... | collective-permute-start | bytes 1179656 | tf_op jit(solution)/shard_map/ppermute | solution.py:25
  29.9 8.6 %collective-permute-start.4 = (f32[6,4,32,128]{3,2,1,0:T(8,128)S(1)}, f32[6,4,32,128]{3,2,1,0:T(8,128)S(1)}, u32[]{:S(2)}, u32[]{:S(2)}) collective-permute-start(f32[6,4,32,128]{3,2,1,0:T(8,128)S(1)} %fusion.206), channel_id=1, source_target_pairs={{16,0},{32,16},{48,32},{64,48},{80,64},{96,80},{112,96},{0,112},{1... | collective-permute-start | bytes 1179656 | tf_op jit(solution)/shard_map/ppermute | solution.py:26
  31.5 8.4 %collective-permute-start.5 = (f32[6,4,32,128]{3,2,1,0:T(8,128)S(1)}, f32[6,4,32,128]{3,2,1,0:T(8,128)S(1)}, u32[]{:S(2)}, u32[]{:S(2)}) collective-permute-start(f32[6,4,32,128]{3,2,1,0:T(8,128)S(1)} %fusion.206), channel_id=1, source_target_pairs={{0,16},{16,32},{32,48},{48,64},{64,80},{80,96},{96,112},{112,0},{1... | collective-permute-start | bytes 1179656 | tf_op jit(solution)/shard_map/ppermute | solution.py:25
  36.7 8.7 %collective-permute-start.12 = (f32[6,4,32,128]{3,2,1,0:T(8,128)S(1)}, f32[6,4,32,128]{3,2,1,0:T(8,128)S(1)}, u32[]{:S(2)}, u32[]{:S(2)}) collective-permute-start(f32[6,4,32,128]{3,2,1,0:T(8,128)S(1)} %fusion.108), channel_id=1, source_target_pairs={{16,0},{32,16},{48,32},{64,48},{80,64},{96,80},{112,96},{0,112},{1... | collective-permute-start | bytes 1179656 | tf_op jit(solution)/shard_map/ppermute | solution.py:26
  38.4 8.4 %collective-permute-start.13 = (f32[6,4,32,128]{3,2,1,0:T(8,128)S(1)}, f32[6,4,32,128]{3,2,1,0:T(8,128)S(1)}, u32[]{:S(2)}, u32[]{:S(2)}) collective-permute-start(f32[6,4,32,128]{3,2,1,0:T(8,128)S(1)} %fusion.108), channel_id=1, source_target_pairs={{0,16},{16,32},{32,48},{48,64},{64,80},{80,96},{96,112},{112,0},{1... | collective-permute-start | bytes 1179656 | tf_op jit(solution)/shard_map/ppermute | solution.py:25
  43.5 8.9 %collective-permute-start.6 = (f32[6,4,32,128]{3,2,1,0:T(8,128)S(1)}, f32[6,4,32,128]{3,2,1,0:T(8,128)S(1)}, u32[]{:S(2)}, u32[]{:S(2)}) collective-permute-start(f32[6,4,32,128]{3,2,1,0:T(8,128)S(1)} %fusion.181), channel_id=1, source_target_pairs={{16,0},{32,16},{48,32},{64,48},{80,64},{96,80},{112,96},{0,112},{1... | collective-permute-start | bytes 1179656 | tf_op jit(solution)/shard_map/ppermute | solution.py:26
  45.2 8.4 %collective-permute-start.7 = (f32[6,4,32,128]{3,2,1,0:T(8,128)S(1)}, f32[6,4,32,128]{3,2,1,0:T(8,128)S(1)}, u32[]{:S(2)}, u32[]{:S(2)}) collective-permute-start(f32[6,4,32,128]{3,2,1,0:T(8,128)S(1)} %fusion.181), channel_id=1, source_target_pairs={{0,16},{16,32},{32,48},{48,64},{64,80},{80,96},{96,112},{112,0},{1... | collective-permute-start | bytes 1179656 | tf_op jit(solution)/shard_map/ppermute | solution.py:25
  50.5 8.7 %collective-permute-start.14 = (f32[6,4,32,128]{3,2,1,0:T(8,128)S(1)}, f32[6,4,32,128]{3,2,1,0:T(8,128)S(1)}, u32[]{:S(2)}, u32[]{:S(2)}) collective-permute-start(f32[6,4,32,128]{3,2,1,0:T(8,128)S(1)} %fusion.83), channel_id=1, source_target_pairs={{16,0},{32,16},{48,32},{64,48},{80,64},{96,80},{112,96},{0,112},{1... | collective-permute-start | bytes 1179656 | tf_op jit(solution)/shard_map/ppermute | solution.py:26
  52.2 8.4 %collective-permute-start.15 = (f32[6,4,32,128]{3,2,1,0:T(8,128)S(1)}, f32[6,4,32,128]{3,2,1,0:T(8,128)S(1)}, u32[]{:S(2)}, u32[]{:S(2)}) collective-permute-start(f32[6,4,32,128]{3,2,1,0:T(8,128)S(1)} %fusion.83), channel_id=1, source_target_pairs={{0,16},{16,32},{32,48},{48,64},{64,80},{80,96},{96,112},{112,0},{1... | collective-permute-start | bytes 1179656 | tf_op jit(solution)/shard_map/ppermute | solution.py:25
  57.1 9.0 %collective-permute-start.16 = (f32[6,4,32,128]{3,2,1,0:T(8,128)S(1)}, f32[6,4,32,128]{3,2,1,0:T(8,128)S(1)}, u32[]{:S(2)}, u32[]{:S(2)}) collective-permute-start(f32[6,4,32,128]{3,2,1,0:T(8,128)S(1)} %fusion.156), channel_id=1, source_target_pairs={{16,0},{32,16},{48,32},{64,48},{80,64},{96,80},{112,96},{0,112},{1... | collective-permute-start | bytes 1179656 | tf_op jit(solution)/shard_map/ppermute | solution.py:26
  58.9 8.4 %collective-permute-start.17 = (f32[6,4,32,128]{3,2,1,0:T(8,128)S(1)}, f32[6,4,32,128]{3,2,1,0:T(8,128)S(1)}, u32[]{:S(2)}, u32[]{:S(2)}) collective-permute-start(f32[6,4,32,128]{3,2,1,0:T(8,128)S(1)} %fusion.156), channel_id=1, source_target_pairs={{0,16},{16,32},{32,48},{48,64},{64,80},{80,96},{96,112},{112,0},{1... | collective-permute-start | bytes 1179656 | tf_op jit(solution)/shard_map/ppermute | solution.py:25
  64.2 7.0 %collective-permute-start.18 = (f32[6,4,32,128]{3,2,1,0:T(8,128)S(1)}, f32[6,4,32,128]{3,2,1,0:T(8,128)S(1)}, u32[]{:S(2)}, u32[]{:S(2)}) collective-permute-start(f32[6,4,32,128]{3,2,1,0:T(8,128)S(1)} %fusion.58), channel_id=1, source_target_pairs={{16,0},{32,16},{48,32},{64,48},{80,64},{96,80},{112,96},{0,112},{1... | collective-permute-start | bytes 1179656 | tf_op jit(solution)/shard_map/ppermute | solution.py:26
  65.9 8.4 %collective-permute-start.19 = (f32[6,4,32,128]{3,2,1,0:T(8,128)S(1)}, f32[6,4,32,128]{3,2,1,0:T(8,128)S(1)}, u32[]{:S(2)}, u32[]{:S(2)}) collective-permute-start(f32[6,4,32,128]{3,2,1,0:T(8,128)S(1)} %fusion.58), channel_id=1, source_target_pairs={{0,16},{16,32},{32,48},{48,64},{64,80},{80,96},{96,112},{112,0},{1... | collective-permute-start | bytes 1179656 | tf_op jit(solution)/shard_map/ppermute | solution.py:25
  77.5 28.1 %all-to-all-start = ((f32[2,12,16,8,128]{4,3,1,0,2:T(8,128)}), f32[2,12,16,8,128]{4,3,1,0,2:T(8,128)S(1)}, u32[]{:S(2)}, u32[]{:S(2)}) async-start(f32[2,12,16,8,128]{4,3,1,0,2:T(8,128)} %copy.18), calls=%async_computation | async-start | bytes 3145728 | tf_op jit(solution)/shard_map/all_to_all | solution.py:200
  113.6 1.5 collective-permute-start.20
  115.2 8.0 %collective-permute-start.21 = (f32[200,192]{1,0:T(8,128)S(1)}, f32[200,192]{1,0:T(8,128)S(1)}, u32[]{:S(2)}, u32[]{:S(2)}) collective-permute-start(f32[200,192]{1,0:T(8,128)S(1)} %select_add_fusion), channel_id=1, source_target_pairs={{0,96},{16,112},{32,0},{48,16},{64,32},{80,48},{96,64},{112,80},{1... | collective-permute-start | bytes 460808 | tf_op jit(solution)/shard_map/ppermute | solution.py:64
  115.9 9.5 %collective-permute-start.22 = (f32[200,192]{1,0:T(8,128)S(1)}, f32[200,192]{1,0:T(8,128)S(1)}, u32[]{:S(2)}, u32[]{:S(2)}) collective-permute-start(f32[200,192]{1,0:T(8,128)S(1)} %select_add_fusion), channel_id=1, source_target_pairs={{0,64},{16,80},{32,96},{48,112},{64,0},{80,16},{96,32},{112,48},{1... | collective-permute-start | bytes 460808 | tf_op jit(solution)/shard_map/ppermute | solution.py:64
  118.4 10.5 %collective-permute-start.23 = (f32[200,192]{1,0:T(8,128)S(1)}, f32[200,192]{1,0:T(8,128)S(1)}, u32[]{:S(2)}, u32[]{:S(2)}) collective-permute-start(f32[200,192]{1,0:T(8,128)S(1)} %select_add_fusion), channel_id=1, source_target_pairs={{0,32},{16,48},{32,64},{48,80},{64,96},{80,112},{96,0},{112,16},{1... | collective-permute-start | bytes 460808 | tf_op jit(solution)/shard_map/ppermute | solution.py:64
  129.0 8.0 %collective-permute-start.24 = (f32[200,192]{1,0:T(8,128)S(1)}, f32[200,192]{1,0:T(8,128)S(1)}, u32[]{:S(2)}, u32[]{:S(2)}) collective-permute-start(f32[200,192]{1,0:T(8,128)S(1)} %add_add_fusion.1), channel_id=1, source_target_pairs={{0,3},{1,0},{2,1},{3,2},{4,7},{5,4},{6,5},{7,6},{8,11},{9,8},{10,9... | collective-permute-start | bytes 460808 | tf_op jit(solution)/shard_map/ppermute | solution.py:64
  129.1 9.6 %collective-permute-start.25 = (f32[200,192]{1,0:T(8,128)S(1)}, f32[200,192]{1,0:T(8,128)S(1)}, u32[]{:S(2)}, u32[]{:S(2)}) collective-permute-start(f32[200,192]{1,0:T(8,128)S(1)} %add_add_fusion.1), channel_id=1, source_target_pairs={{0,2},{1,3},{2,0},{3,1},{4,6},{5,7},{6,4},{7,5},{8,10},{9,11},{10,... | collective-permute-start | bytes 460808 | tf_op jit(solution)/shard_map/ppermute | solution.py:64
  131.1 11.0 %collective-permute-start.26 = (f32[200,192]{1,0:T(8,128)S(1)}, f32[200,192]{1,0:T(8,128)S(1)}, u32[]{:S(2)}, u32[]{:S(2)}) collective-permute-start(f32[200,192]{1,0:T(8,128)S(1)} %add_add_fusion.1), channel_id=1, source_target_pairs={{0,1},{1,2},{2,3},{3,0},{4,5},{5,6},{6,7},{7,4},{8,9},{9,10},{10,1... | collective-permute-start | bytes 460808 | tf_op jit(solution)/shard_map/ppermute | solution.py:64
  142.2 8.0 %collective-permute-start.27 = (f32[200,192]{1,0:T(8,128)S(1)}, f32[200,192]{1,0:T(8,128)S(1)}, u32[]{:S(2)}, u32[]{:S(2)}) collective-permute-start(f32[200,192]{1,0:T(8,128)S(1)} %add_add_fusion), channel_id=1, source_target_pairs={{0,12},{1,13},{2,14},{3,15},{4,0},{5,1},{6,2},{7,3},{8,4},{9,5},{1... | collective-permute-start | bytes 460808 | tf_op jit(solution)/shard_map/ppermute | solution.py:64
  143.8 9.5 %collective-permute-start.28 = (f32[200,192]{1,0:T(8,128)S(1)}, f32[200,192]{1,0:T(8,128)S(1)}, u32[]{:S(2)}, u32[]{:S(2)}) collective-permute-start(f32[200,192]{1,0:T(8,128)S(1)} %add_add_fusion), channel_id=1, source_target_pairs={{0,8},{1,9},{2,10},{3,11},{4,12},{5,13},{6,14},{7,15},{8,0},{9,1},... | collective-permute-start | bytes 460808 | tf_op jit(solution)/shard_map/ppermute | solution.py:64
  144.8 11.6 %collective-permute-start.29 = (f32[200,192]{1,0:T(8,128)S(1)}, f32[200,192]{1,0:T(8,128)S(1)}, u32[]{:S(2)}, u32[]{:S(2)}) collective-permute-start(f32[200,192]{1,0:T(8,128)S(1)} %add_add_fusion), channel_id=1, source_target_pairs={{0,4},{1,5},{2,6},{3,7},{4,8},{5,9},{6,10},{7,11},{8,12},{9,13},{1... | collective-permute-start | bytes 460808 | tf_op jit(solution)/shard_map/ppermute | solution.py:64
  193.4 19.1 %all-to-all-start.1 = ((f32[12,16,8,128]{3,2,0,1:T(8,128)}), f32[12,16,8,128]{3,2,0,1:T(8,128)}, u32[]{:S(2)}, u32[]{:S(2)}) async-start(f32[12,16,8,128]{3,2,0,1:T(8,128)} %copy.24), calls=%async_computation.1 | async-start | bytes 1572864 | tf_op jit(solution)/shard_map/all_to_all | solution.py:225
  (3 other events, 8.3 us)

commit v10 on v9

--- a/solution.py
+++ b/solution.py
@@ -74,8 +74,7 @@
 
 
 def mesh_sum(x):
-    x = group_sum(x, "dom", 1, 2)
-    x = group_sum(x, "dom", 2, lax.axis_size("dom") // 2)
+    x = group_sum(x, "dom", 1, lax.axis_size("dom"))
     x = group_sum(x, "band", 1, 4)
     return group_sum(x, "band", 4, lax.axis_size("band") // 4)
 

time: 218 us -> 228 us (1.046)
  the two profiles are of different devices: /device:TPU:0 before, /device:TPU:4 now
where the time goes in v10:
time: 228 us; the launch traced here: 224 us
  waiting for transfers between devices  89.2 us (39%)
  starting transfers between devices  41.5 us (18%)
  local copies, waits for them, and re-layouts  37.2 us (16%)
  Pallas kernels  32 us (14%)
  other arithmetic  21.6 us (9%)
    ppermute x13, waiting for transfers between devices, group_sum(): received.append(lax.ppermute(x, axis, pairs))  38.9 us
    all_to_all x1, waiting for transfers between devices, local(): spread = lax.all_to_all(chunked, 'band', 2, 2, tiled=True)  27.8 us
    pallas_call x1, Pallas kernels, lower_inverse(): pl.pallas_call(inverse_kernel, out_shape=jax.ShapeDtypeStruct((n, n), jnp...  23.7 us
    slice x72, local copies, waits for them, and re-layouts, hamiltonian(): near = near + jnp.roll(field, reach, 3) + jnp.roll(field, -reach, 3)  14.4 us
    ppermute x13, starting transfers between devices, group_sum(): received.append(lax.ppermute(x, axis, pairs))  12.1 us
    sub x6, other arithmetic, local(): 2.0 / half * (apply(c) - center * c) - p  11.4 us
    all_to_all x1, waiting for transfers between devices, local(): lax.all_to_all(basis_cd, 'band', 1, 1, tiled=True).reshape(psi.shape)  11.2 us
    ppermute x10, starting transfers between devices, extended(): after = lax.ppermute(initial, axis, down)  10.2 us
  transfers between devices with their start and end apart: 35, of which 21 were waited for; matrix products, arithmetic and copies ran while one was open for 17% of the time, Pallas kernels for 0%

profile of v10, /device:TPU:4, one launch (start us, length us, event | category | flops | bytes accessed | tf_op | source)
XLA Modules:
  0.0 224.4 jit_solution(2397063045305460884)
XLA Ops:
  7.3 1.8 collective-permute-done.1
  9.1 2.0 broadcast_multiply_fusion.1
  13.6 1.9 broadcast_multiply_fusion
  20.5 1.9 fusion.206
  26.1 1.9 fusion.108
  32.2 1.8 fusion.181
  38.2 2.1 fusion.83
  42.2 2.0 collective-permute-start.14
  45.5 1.9 fusion.156
  49.0 1.9 collective-permute-start.16
  52.5 1.8 fusion.58
  60.7 2.0 collective-permute-done.18
  62.8 3.3 %collective-permute-done.19 = f32[6,4,32,128]{3,2,1,0:T(8,128)S(1)} collective-permute-done((f32[6,4,32,128]{3,2,1,0:T(8,128)S(1)}, f32[6,4,32,128]{3,2,1,0:T(8,128)S(1)}, u32[]{:S(2)}, u32[]{:S(2)}) %collective-permute-start.19) | collective-permute-done | bytes 393248 | tf_op jit(solution)/shard_map/ppermute | solution.py:25
  69.3 8.5 %all-to-all-start = ((f32[2,12,16,8,128]{4,3,1,0,2:T(8,128)}), f32[2,12,16,8,128]{4,3,1,0,2:T(8,128)S(1)}, u32[]{:S(2)}, u32[]{:S(2)}) async-start(f32[2,12,16,8,128]{4,3,1,0,2:T(8,128)} %copy.18), calls=%async_computation | async-start | bytes 3145728 | tf_op jit(solution)/shard_map/all_to_all | solution.py:199
  77.9 27.8 %all-to-all-done = f32[2,12,16,8,128]{4,3,1,0,2:T(8,128)S(1)} async-done(((f32[2,12,16,8,128]{4,3,1,0,2:T(8,128)}), f32[2,12,16,8,128]{4,3,1,0,2:T(8,128)S(1)}, u32[]{:S(2)}, u32[]{:S(2)}) %all-to-all-start) | async-done | bytes 1572896 | tf_op jit(solution)/shard_map/all_to_all | solution.py:199
  107.7 4.7 %shard_map.41 = (f32[192,192]{1,0:T(8,128)}, f32[192,192]{1,0:T(8,128)}) custom-call(f32[1536,128]{1,0:T(8,128)} %bitcast.23, f32[1536,128]{1,0:T(8,128)} %bitcast.29), custom_call_target="tpu_custom_call" | custom-call | tf_op jit(solution)/shard_map/pallas_call | solution.py:158
  114.5 2.7 %collective-permute-start.23 = (f32[200,192]{1,0:T(8,128)S(1)}, f32[200,192]{1,0:T(8,128)S(1)}, u32[]{:S(2)}, u32[]{:S(2)}) collective-permute-start(f32[200,192]{1,0:T(8,128)S(1)} %maximum_maximum_fusion), channel_id=1, source_target_pairs={{0,64},{16,80},{32,96},{48,112},{64,0},{80,16},{96,32},{112,48},{1... | collective-permute-start | bytes 460808 | tf_op jit(solution)/shard_map/ppermute | solution.py:64
  117.2 2.0 collective-permute-start.24
  120.6 4.8 %collective-permute-done.21 = f32[200,192]{1,0:T(8,128)S(1)} collective-permute-done((f32[200,192]{1,0:T(8,128)S(1)}, f32[200,192]{1,0:T(8,128)S(1)}, u32[]{:S(2)}, u32[]{:S(2)}) %collective-permute-start.21) | collective-permute-done | bytes 153632 | tf_op jit(solution)/shard_map/ppermute | solution.py:64
  128.3 7.9 %collective-permute-done.25 = f32[200,192]{1,0:T(8,128)S(1)} collective-permute-done((f32[200,192]{1,0:T(8,128)S(1)}, f32[200,192]{1,0:T(8,128)S(1)}, u32[]{:S(2)}, u32[]{:S(2)}) %collective-permute-start.25) | collective-permute-done | bytes 153632 | tf_op jit(solution)/shard_map/ppermute | solution.py:64
  139.7 5.9 %collective-permute-done.27 = f32[200,192]{1,0:T(8,128)S(1)} collective-permute-done((f32[200,192]{1,0:T(8,128)S(1)}, f32[200,192]{1,0:T(8,128)S(1)}, u32[]{:S(2)}, u32[]{:S(2)}) %collective-permute-start.27) | collective-permute-done | bytes 153632 | tf_op jit(solution)/shard_map/ppermute | solution.py:64
  147.3 4.3 %collective-permute-done.29 = f32[200,192]{1,0:T(8,128)S(1)} collective-permute-done((f32[200,192]{1,0:T(8,128)S(1)}, f32[200,192]{1,0:T(8,128)S(1)}, u32[]{:S(2)}, u32[]{:S(2)}) %collective-permute-start.29) | collective-permute-done | bytes 153632 | tf_op jit(solution)/shard_map/ppermute | solution.py:64
  154.8 5.0 %collective-permute-done.30 = f32[200,192]{1,0:T(8,128)S(1)} collective-permute-done((f32[200,192]{1,0:T(8,128)S(1)}, f32[200,192]{1,0:T(8,128)S(1)}, u32[]{:S(2)}, u32[]{:S(2)}) %collective-permute-start.30) | collective-permute-done | bytes 153632 | tf_op jit(solution)/shard_map/ppermute | solution.py:64
  159.8 3.1 %collective-permute-done.31 = f32[200,192]{1,0:T(8,128)S(1)} collective-permute-done((f32[200,192]{1,0:T(8,128)S(1)}, f32[200,192]{1,0:T(8,128)S(1)}, u32[]{:S(2)}, u32[]{:S(2)}) %collective-permute-start.31) | collective-permute-done | bytes 153632 | tf_op jit(solution)/shard_map/ppermute | solution.py:64
  162.9 3.2 %collective-permute-done.32 = f32[200,192]{1,0:T(8,128)S(1)} collective-permute-done((f32[200,192]{1,0:T(8,128)S(1)}, f32[200,192]{1,0:T(8,128)S(1)}, u32[]{:S(2)}, u32[]{:S(2)}) %collective-permute-start.32) | collective-permute-done | bytes 153632 | tf_op jit(solution)/shard_map/ppermute | solution.py:64
  169.4 23.7 %shard_map.42 = f32[192,192]{1,0:T(8,128)} custom-call(f32[192,192]{1,0:T(8,128)} %reshape.35.c_ref), custom_call_target="tpu_custom_call" | custom-call | tf_op jit(solution)/shard_map/pallas_call | solution.py:142
  193.1 1.8 reshape.36
  197.4 3.5 %shard_map.43 = f32[1536,128]{1,0:T(8,128)} custom-call(f32[192,192]{1,0:T(8,128)} %reshape.37.refs_0_, f32[1536,128]{1,0:T(8,128)} %bitcast.24), custom_call_target="tpu_custom_call" | custom-call | tf_op jit(solution)/shard_map/pallas_call | solution.py:167
  200.9 2.1 copy.24
  203.0 4.3 %all-to-all-start.1 = ((f32[12,16,8,128]{3,2,0,1:T(8,128)}), f32[12,16,8,128]{3,2,0,1:T(8,128)}, u32[]{:S(2)}, u32[]{:S(2)}) async-start(f32[12,16,8,128]{3,2,0,1:T(8,128)} %copy.24), calls=%async_computation.1 | async-start | bytes 1572864 | tf_op jit(solution)/shard_map/all_to_all | solution.py:224
  211.0 11.2 %all-to-all-done.1 = f32[12,16,8,128]{3,2,0,1:T(8,128)} async-done(((f32[12,16,8,128]{3,2,0,1:T(8,128)}), f32[12,16,8,128]{3,2,0,1:T(8,128)}, u32[]{:S(2)}, u32[]{:S(2)}) %all-to-all-start.1) | async-done | bytes 786464 | tf_op jit(solution)/shard_map/all_to_all | solution.py:224
  222.1 2.1 copy.25
  (234 shorter events, 67.7 us)
Async XLA Ops:
  1.9 7.2 %collective-permute-start.1 = (f32[6,4,32,128]{3,2,1,0:T(8,128)S(1)}, f32[6,4,32,128]{3,2,1,0:T(8,128)S(1)}, u32[]{:S(2)}, u32[]{:S(2)}) collective-permute-start(f32[6,4,32,128]{3,2,1,0:T(8,128)S(1)} %get-tuple-element.76), channel_id=1, source_target_pairs={{0,16},{16,32},{32,48},{48,64},{64,80},{80,96},{96,112},{112,0},{1... | collective-permute-start | bytes 1179656 | tf_op jit(solution)/shard_map/ppermute | solution.py:25
  2.4 11.2 %collective-permute-start.8 = (f32[6,4,32,128]{3,2,1,0:T(8,128)S(1)}, f32[6,4,32,128]{3,2,1,0:T(8,128)S(1)}, u32[]{:S(2)}, u32[]{:S(2)}) collective-permute-start(f32[6,4,32,128]{3,2,1,0:T(8,128)S(1)} %get-tuple-element.77), channel_id=1, source_target_pairs={{16,0},{32,16},{48,32},{64,48},{80,64},{96,80},{112,96},{0,112},{1... | collective-permute-start | bytes 1179656 | tf_op jit(solution)/shard_map/ppermute | solution.py:26
  3.7 9.9 %collective-permute-start.9 = (f32[6,4,32,128]{3,2,1,0:T(8,128)S(1)}, f32[6,4,32,128]{3,2,1,0:T(8,128)S(1)}, u32[]{:S(2)}, u32[]{:S(2)}) collective-permute-start(f32[6,4,32,128]{3,2,1,0:T(8,128)S(1)} %get-tuple-element.77), channel_id=1, source_target_pairs={{0,16},{16,32},{32,48},{48,64},{64,80},{80,96},{96,112},{112,0},{1... | collective-permute-start | bytes 1179656 | tf_op jit(solution)/shard_map/ppermute | solution.py:25
  13.3 7.2 %collective-permute-start.3 = (f32[6,4,32,128]{3,2,1,0:T(8,128)S(1)}, f32[6,4,32,128]{3,2,1,0:T(8,128)S(1)}, u32[]{:S(2)}, u32[]{:S(2)}) collective-permute-start(f32[6,4,32,128]{3,2,1,0:T(8,128)S(1)} %get-tuple-element.6), channel_id=1, source_target_pairs={{0,16},{16,32},{32,48},{48,64},{64,80},{80,96},{96,112},{112,0},{1... | collective-permute-start | bytes 1179656 | tf_op jit(solution)/shard_map/ppermute | solution.py:25
  17.3 7.4 %collective-permute-start.10 = (f32[6,4,32,128]{3,2,1,0:T(8,128)S(1)}, f32[6,4,32,128]{3,2,1,0:T(8,128)S(1)}, u32[]{:S(2)}, u32[]{:S(2)}) collective-permute-start(f32[6,4,32,128]{3,2,1,0:T(8,128)S(1)} %get-tuple-element.8), channel_id=1, source_target_pairs={{16,0},{32,16},{48,32},{64,48},{80,64},{96,80},{112,96},{0,112},{1... | collective-permute-start | bytes 1179656 | tf_op jit(solution)/shard_map/ppermute | solution.py:26
  18.9 7.2 %collective-permute-start.11 = (f32[6,4,32,128]{3,2,1,0:T(8,128)S(1)}, f32[6,4,32,128]{3,2,1,0:T(8,128)S(1)}, u32[]{:S(2)}, u32[]{:S(2)}) collective-permute-start(f32[6,4,32,128]{3,2,1,0:T(8,128)S(1)} %get-tuple-element.8), channel_id=1, source_target_pairs={{0,16},{16,32},{32,48},{48,64},{64,80},{80,96},{96,112},{112,0},{1... | collective-permute-start | bytes 1179656 | tf_op jit(solution)/shard_map/ppermute | solution.py:25
  24.1 7.3 %collective-permute-start.4 = (f32[6,4,32,128]{3,2,1,0:T(8,128)S(1)}, f32[6,4,32,128]{3,2,1,0:T(8,128)S(1)}, u32[]{:S(2)}, u32[]{:S(2)}) collective-permute-start(f32[6,4,32,128]{3,2,1,0:T(8,128)S(1)} %fusion.206), channel_id=1, source_target_pairs={{16,0},{32,16},{48,32},{64,48},{80,64},{96,80},{112,96},{0,112},{1... | collective-permute-start | bytes 1179656 | tf_op jit(solution)/shard_map/ppermute | solution.py:26
  24.5 7.7 %collective-permute-start.5 = (f32[6,4,32,128]{3,2,1,0:T(8,128)S(1)}, f32[6,4,32,128]{3,2,1,0:T(8,128)S(1)}, u32[]{:S(2)}, u32[]{:S(2)}) collective-permute-start(f32[6,4,32,128]{3,2,1,0:T(8,128)S(1)} %fusion.206), channel_id=1, source_target_pairs={{0,16},{16,32},{32,48},{48,64},{64,80},{80,96},{96,112},{112,0},{1... | collective-permute-start | bytes 1179656 | tf_op jit(solution)/shard_map/ppermute | solution.py:25
  29.7 8.5 %collective-permute-start.12 = (f32[6,4,32,128]{3,2,1,0:T(8,128)S(1)}, f32[6,4,32,128]{3,2,1,0:T(8,128)S(1)}, u32[]{:S(2)}, u32[]{:S(2)}) collective-permute-start(f32[6,4,32,128]{3,2,1,0:T(8,128)S(1)} %fusion.108), channel_id=1, source_target_pairs={{16,0},{32,16},{48,32},{64,48},{80,64},{96,80},{112,96},{0,112},{1... | collective-permute-start | bytes 1179656 | tf_op jit(solution)/shard_map/ppermute | solution.py:26
  30.7 7.6 %collective-permute-start.13 = (f32[6,4,32,128]{3,2,1,0:T(8,128)S(1)}, f32[6,4,32,128]{3,2,1,0:T(8,128)S(1)}, u32[]{:S(2)}, u32[]{:S(2)}) collective-permute-start(f32[6,4,32,128]{3,2,1,0:T(8,128)S(1)} %fusion.108), channel_id=1, source_target_pairs={{0,16},{16,32},{32,48},{48,64},{64,80},{80,96},{96,112},{112,0},{1... | collective-permute-start | bytes 1179656 | tf_op jit(solution)/shard_map/ppermute | solution.py:25
  35.8 9.5 %collective-permute-start.6 = (f32[6,4,32,128]{3,2,1,0:T(8,128)S(1)}, f32[6,4,32,128]{3,2,1,0:T(8,128)S(1)}, u32[]{:S(2)}, u32[]{:S(2)}) collective-permute-start(f32[6,4,32,128]{3,2,1,0:T(8,128)S(1)} %fusion.181), channel_id=1, source_target_pairs={{16,0},{32,16},{48,32},{64,48},{80,64},{96,80},{112,96},{0,112},{1... | collective-permute-start | bytes 1179656 | tf_op jit(solution)/shard_map/ppermute | solution.py:26
  36.3 9.2 %collective-permute-start.7 = (f32[6,4,32,128]{3,2,1,0:T(8,128)S(1)}, f32[6,4,32,128]{3,2,1,0:T(8,128)S(1)}, u32[]{:S(2)}, u32[]{:S(2)}) collective-permute-start(f32[6,4,32,128]{3,2,1,0:T(8,128)S(1)} %fusion.181), channel_id=1, source_target_pairs={{0,16},{16,32},{32,48},{48,64},{64,80},{80,96},{96,112},{112,0},{1... | collective-permute-start | bytes 1179656 | tf_op jit(solution)/shard_map/ppermute | solution.py:25
  42.2 10.0 %collective-permute-start.14 = (f32[6,4,32,128]{3,2,1,0:T(8,128)S(1)}, f32[6,4,32,128]{3,2,1,0:T(8,128)S(1)}, u32[]{:S(2)}, u32[]{:S(2)}) collective-permute-start(f32[6,4,32,128]{3,2,1,0:T(8,128)S(1)} %fusion.83), channel_id=1, source_target_pairs={{16,0},{32,16},{48,32},{64,48},{80,64},{96,80},{112,96},{0,112},{1... | collective-permute-start | bytes 1179656 | tf_op jit(solution)/shard_map/ppermute | solution.py:26
  44.1 8.4 %collective-permute-start.15 = (f32[6,4,32,128]{3,2,1,0:T(8,128)S(1)}, f32[6,4,32,128]{3,2,1,0:T(8,128)S(1)}, u32[]{:S(2)}, u32[]{:S(2)}) collective-permute-start(f32[6,4,32,128]{3,2,1,0:T(8,128)S(1)} %fusion.83), channel_id=1, source_target_pairs={{0,16},{16,32},{32,48},{48,64},{64,80},{80,96},{96,112},{112,0},{1... | collective-permute-start | bytes 1179656 | tf_op jit(solution)/shard_map/ppermute | solution.py:25
  49.0 10.1 %collective-permute-start.16 = (f32[6,4,32,128]{3,2,1,0:T(8,128)S(1)}, f32[6,4,32,128]{3,2,1,0:T(8,128)S(1)}, u32[]{:S(2)}, u32[]{:S(2)}) collective-permute-start(f32[6,4,32,128]{3,2,1,0:T(8,128)S(1)} %fusion.156), channel_id=1, source_target_pairs={{16,0},{32,16},{48,32},{64,48},{80,64},{96,80},{112,96},{0,112},{1... | collective-permute-start | bytes 1179656 | tf_op jit(solution)/shard_map/ppermute | solution.py:26
  50.8 8.2 %collective-permute-start.17 = (f32[6,4,32,128]{3,2,1,0:T(8,128)S(1)}, f32[6,4,32,128]{3,2,1,0:T(8,128)S(1)}, u32[]{:S(2)}, u32[]{:S(2)}) collective-permute-start(f32[6,4,32,128]{3,2,1,0:T(8,128)S(1)} %fusion.156), channel_id=1, source_target_pairs={{0,16},{16,32},{32,48},{48,64},{64,80},{80,96},{96,112},{112,0},{1... | collective-permute-start | bytes 1179656 | tf_op jit(solution)/shard_map/ppermute | solution.py:25
  56.1 6.7 %collective-permute-start.18 = (f32[6,4,32,128]{3,2,1,0:T(8,128)S(1)}, f32[6,4,32,128]{3,2,1,0:T(8,128)S(1)}, u32[]{:S(2)}, u32[]{:S(2)}) collective-permute-start(f32[6,4,32,128]{3,2,1,0:T(8,128)S(1)} %fusion.58), channel_id=1, source_target_pairs={{16,0},{32,16},{48,32},{64,48},{80,64},{96,80},{112,96},{0,112},{1... | collective-permute-start | bytes 1179656 | tf_op jit(solution)/shard_map/ppermute | solution.py:26
  57.5 8.6 %collective-permute-start.19 = (f32[6,4,32,128]{3,2,1,0:T(8,128)S(1)}, f32[6,4,32,128]{3,2,1,0:T(8,128)S(1)}, u32[]{:S(2)}, u32[]{:S(2)}) collective-permute-start(f32[6,4,32,128]{3,2,1,0:T(8,128)S(1)} %fusion.58), channel_id=1, source_target_pairs={{0,16},{16,32},{32,48},{48,64},{64,80},{80,96},{96,112},{112,0},{1... | collective-permute-start | bytes 1179656 | tf_op jit(solution)/shard_map/ppermute | solution.py:25
  69.3 36.3 %all-to-all-start = ((f32[2,12,16,8,128]{4,3,1,0,2:T(8,128)}), f32[2,12,16,8,128]{4,3,1,0,2:T(8,128)S(1)}, u32[]{:S(2)}, u32[]{:S(2)}) async-start(f32[2,12,16,8,128]{4,3,1,0,2:T(8,128)} %copy.18), calls=%async_computation | async-start | bytes 3145728 | tf_op jit(solution)/shard_map/all_to_all | solution.py:199
  113.6 11.8 %collective-permute-start.21 = (f32[200,192]{1,0:T(8,128)S(1)}, f32[200,192]{1,0:T(8,128)S(1)}, u32[]{:S(2)}, u32[]{:S(2)}) collective-permute-start(f32[200,192]{1,0:T(8,128)S(1)} %maximum_maximum_fusion), channel_id=1, source_target_pairs={{0,96},{16,112},{32,0},{48,16},{64,32},{80,48},{96,64},{112,80},{1... | collective-permute-start | bytes 460808 | tf_op jit(solution)/shard_map/ppermute | solution.py:64
  113.7 11.8 %collective-permute-start.22 = (f32[200,192]{1,0:T(8,128)S(1)}, f32[200,192]{1,0:T(8,128)S(1)}, u32[]{:S(2)}, u32[]{:S(2)}) collective-permute-start(f32[200,192]{1,0:T(8,128)S(1)} %maximum_maximum_fusion), channel_id=1, source_target_pairs={{0,80},{16,96},{32,112},{48,0},{64,16},{80,32},{96,48},{112,64},{1... | collective-permute-start | bytes 460808 | tf_op jit(solution)/shard_map/ppermute | solution.py:64
  114.5 12.3 %collective-permute-start.23 = (f32[200,192]{1,0:T(8,128)S(1)}, f32[200,192]{1,0:T(8,128)S(1)}, u32[]{:S(2)}, u32[]{:S(2)}) collective-permute-start(f32[200,192]{1,0:T(8,128)S(1)} %maximum_maximum_fusion), channel_id=1, source_target_pairs={{0,64},{16,80},{32,96},{48,112},{64,0},{80,16},{96,32},{112,48},{1... | collective-permute-start | bytes 460808 | tf_op jit(solution)/shard_map/ppermute | solution.py:64
  117.2 11.1 %collective-permute-start.24 = (f32[200,192]{1,0:T(8,128)S(1)}, f32[200,192]{1,0:T(8,128)S(1)}, u32[]{:S(2)}, u32[]{:S(2)}) collective-permute-start(f32[200,192]{1,0:T(8,128)S(1)} %maximum_maximum_fusion), channel_id=1, source_target_pairs={{0,48},{16,64},{32,80},{48,96},{64,112},{80,0},{96,16},{112,32},{1... | collective-permute-start | bytes 460808 | tf_op jit(solution)/shard_map/ppermute | solution.py:64
  119.3 17.0 %collective-permute-start.25 = (f32[200,192]{1,0:T(8,128)S(1)}, f32[200,192]{1,0:T(8,128)S(1)}, u32[]{:S(2)}, u32[]{:S(2)}) collective-permute-start(f32[200,192]{1,0:T(8,128)S(1)} %maximum_maximum_fusion), channel_id=1, source_target_pairs={{0,32},{16,48},{32,64},{48,80},{64,96},{80,112},{96,0},{112,16},{1... | collective-permute-start | bytes 460808 | tf_op jit(solution)/shard_map/ppermute | solution.py:64
  125.4 10.9 %collective-permute-start.26 = (f32[200,192]{1,0:T(8,128)S(1)}, f32[200,192]{1,0:T(8,128)S(1)}, u32[]{:S(2)}, u32[]{:S(2)}) collective-permute-start(f32[200,192]{1,0:T(8,128)S(1)} %maximum_maximum_fusion), channel_id=1, source_target_pairs={{0,16},{16,32},{32,48},{48,64},{64,80},{80,96},{96,112},{112,0},{1... | collective-permute-start | bytes 460808 | tf_op jit(solution)/shard_map/ppermute | solution.py:64
  137.6 8.0 %collective-permute-start.27 = (f32[200,192]{1,0:T(8,128)S(1)}, f32[200,192]{1,0:T(8,128)S(1)}, u32[]{:S(2)}, u32[]{:S(2)}) collective-permute-start(f32[200,192]{1,0:T(8,128)S(1)} %add_add_fusion.1), channel_id=1, source_target_pairs={{0,3},{1,0},{2,1},{3,2},{4,7},{5,4},{6,5},{7,6},{8,11},{9,8},{10,9... | collective-permute-start | bytes 460808 | tf_op jit(solution)/shard_map/ppermute | solution.py:64
  137.7 9.6 %collective-permute-start.28 = (f32[200,192]{1,0:T(8,128)S(1)}, f32[200,192]{1,0:T(8,128)S(1)}, u32[]{:S(2)}, u32[]{:S(2)}) collective-permute-start(f32[200,192]{1,0:T(8,128)S(1)} %add_add_fusion.1), channel_id=1, source_target_pairs={{0,2},{1,3},{2,0},{3,1},{4,6},{5,7},{6,4},{7,5},{8,10},{9,11},{10,... | collective-permute-start | bytes 460808 | tf_op jit(solution)/shard_map/ppermute | solution.py:64
  138.0 13.7 %collective-permute-start.29 = (f32[200,192]{1,0:T(8,128)S(1)}, f32[200,192]{1,0:T(8,128)S(1)}, u32[]{:S(2)}, u32[]{:S(2)}) collective-permute-start(f32[200,192]{1,0:T(8,128)S(1)} %add_add_fusion.1), channel_id=1, source_target_pairs={{0,1},{1,2},{2,3},{3,0},{4,5},{5,6},{6,7},{7,4},{8,9},{9,10},{10,1... | collective-permute-start | bytes 460808 | tf_op jit(solution)/shard_map/ppermute | solution.py:64
  151.7 8.0 %collective-permute-start.30 = (f32[200,192]{1,0:T(8,128)S(1)}, f32[200,192]{1,0:T(8,128)S(1)}, u32[]{:S(2)}, u32[]{:S(2)}) collective-permute-start(f32[200,192]{1,0:T(8,128)S(1)} %add_add_fusion), channel_id=1, source_target_pairs={{0,12},{1,13},{2,14},{3,15},{4,0},{5,1},{6,2},{7,3},{8,4},{9,5},{1... | collective-permute-start | bytes 460808 | tf_op jit(solution)/shard_map/ppermute | solution.py:64
  153.4 9.5 %collective-permute-start.31 = (f32[200,192]{1,0:T(8,128)S(1)}, f32[200,192]{1,0:T(8,128)S(1)}, u32[]{:S(2)}, u32[]{:S(2)}) collective-permute-start(f32[200,192]{1,0:T(8,128)S(1)} %add_add_fusion), channel_id=1, source_target_pairs={{0,8},{1,9},{2,10},{3,11},{4,12},{5,13},{6,14},{7,15},{8,0},{9,1},... | collective-permute-start | bytes 460808 | tf_op jit(solution)/shard_map/ppermute | solution.py:64
  154.1 11.9 %collective-permute-start.32 = (f32[200,192]{1,0:T(8,128)S(1)}, f32[200,192]{1,0:T(8,128)S(1)}, u32[]{:S(2)}, u32[]{:S(2)}) collective-permute-start(f32[200,192]{1,0:T(8,128)S(1)} %add_add_fusion), channel_id=1, source_target_pairs={{0,4},{1,5},{2,6},{3,7},{4,8},{5,9},{6,10},{7,11},{8,12},{9,13},{1... | collective-permute-start | bytes 460808 | tf_op jit(solution)/shard_map/ppermute | solution.py:64
  203.0 19.1 %all-to-all-start.1 = ((f32[12,16,8,128]{3,2,0,1:T(8,128)}), f32[12,16,8,128]{3,2,0,1:T(8,128)}, u32[]{:S(2)}, u32[]{:S(2)}) async-start(f32[12,16,8,128]{3,2,0,1:T(8,128)} %copy.24), calls=%async_computation.1 | async-start | bytes 1572864 | tf_op jit(solution)/shard_map/all_to_all | solution.py:224
  (6 other events, 22.0 us)

commit v11 on v9

--- a/solution.py
+++ b/solution.py
@@ -127,7 +127,7 @@
             b_ref[r0:, : tb * tile] = b_ref[r0:, : tb * tile] - factor * row_b
             return carry
 
-        lax.fori_loop(k0, k1, step, 0)
+        lax.fori_loop(k0, k1, step, 0, unroll=4)
 
     bounds = sorted({0, n} | {t * tile for t in range(1, tiles) if t * tile < n})
     for k0, k1 in zip(bounds[:-1], bounds[1:]):

time: 218 us -> 219 us (level)
  no operation moved by 1% of the time
where the time goes in v11:
time: 219 us; the launch traced here: 216 us
  waiting for transfers between devices  79.9 us (36%)
  starting transfers between devices  42.2 us (19%)
  local copies, waits for them, and re-layouts  37.1 us (17%)
  Pallas kernels  32.9 us (15%)
  other arithmetic  20.6 us (9%)
    ppermute x10, waiting for transfers between devices, group_sum(): received.append(lax.ppermute(x, axis, pairs))  32.3 us
    pallas_call x1, Pallas kernels, lower_inverse(): pl.pallas_call(inverse_kernel, out_shape=jax.ShapeDtypeStruct((n, n), jnp...  24.6 us
    all_to_all x1, waiting for transfers between devices, local(): spread = lax.all_to_all(chunked, 'band', 2, 2, tiled=True)  19.8 us
    ppermute x10, starting transfers between devices, extended(): after = lax.ppermute(initial, axis, down)  19.5 us
    ppermute x10, waiting for transfers between devices, extended(): before = lax.ppermute(last, axis, up)  14.6 us
    slice x72, local copies, waits for them, and re-layouts, hamiltonian(): near = near + jnp.roll(field, reach, 3) + jnp.roll(field, -reach, 3)  14.3 us
    sub x6, other arithmetic, local(): 2.0 / half * (apply(c) - center * c) - p  11.2 us
    all_to_all x1, waiting for transfers between devices, local(): lax.all_to_all(basis_cd, 'band', 1, 1, tiled=True).reshape(psi.shape)  11.1 us
  transfers between devices with their start and end apart: 32, of which 22 were waited for; matrix products, arithmetic and copies ran while one was open for 18% of the time, Pallas kernels for 0%

profile of v11, /device:TPU:0, one launch (start us, length us, event | category | flops | bytes accessed | tf_op | source)
XLA Modules:
  0.0 215.7 jit_solution(6324171645405627184)
XLA Ops:
  1.9 2.3 %collective-permute-start = (f32[6,4,32,128]{3,2,1,0:T(8,128)S(1)}, f32[6,4,32,128]{3,2,1,0:T(8,128)S(1)}, u32[]{:S(2)}, u32[]{:S(2)}) collective-permute-start(f32[6,4,32,128]{3,2,1,0:T(8,128)S(1)} %get-tuple-element.76), channel_id=1, source_target_pairs={{16,0},{32,16},{48,32},{64,48},{80,64},{96,80},{112,96},{0,112},{1... | collective-permute-start | bytes 1179656 | tf_op jit(solution)/shard_map/ppermute | solution.py:26
  4.2 3.0 %collective-permute-start.8 = (f32[6,4,32,128]{3,2,1,0:T(8,128)S(1)}, f32[6,4,32,128]{3,2,1,0:T(8,128)S(1)}, u32[]{:S(2)}, u32[]{:S(2)}) collective-permute-start(f32[6,4,32,128]{3,2,1,0:T(8,128)S(1)} %get-tuple-element.77), channel_id=1, source_target_pairs={{16,0},{32,16},{48,32},{64,48},{80,64},{96,80},{112,96},{0,112},{1... | collective-permute-start | bytes 1179656 | tf_op jit(solution)/shard_map/ppermute | solution.py:26
  10.7 1.9 collective-permute-done.1
  12.6 2.3 %broadcast_multiply_fusion.1 = (f32[6,4,32,128]{3,2,1,0:T(8,128)S(1)}, f32[6,4,32,128]{3,2,1,0:T(8,128)S(1)}) fusion(f32[6,4,32,128]{3,2,1,0:T(8,128)S(1)} %get-tuple-element.76, f32[6,4,32,4]{3,2,1,0:T(8,128)S(1)} %get-tuple-element.70, f32[6,4,32,124]{3,2,1,0:T(8,128)S(1)} %get-tuple-element.74, f32[6,4,32,124]{3,2,1,0:T(8,128)S(1)} %get-tuple-element.72, ...), kind=kLoop, calls=%fused_computation.464 | loop fusion | flops 5603328 | bytes 8323072 | tf_op jit(solution)/shard_map/div | solution.py:190
  18.0 1.9 broadcast_multiply_fusion
  21.7 3.0 %collective-permute-start.10 = (f32[6,4,32,128]{3,2,1,0:T(8,128)S(1)}, f32[6,4,32,128]{3,2,1,0:T(8,128)S(1)}, u32[]{:S(2)}, u32[]{:S(2)}) collective-permute-start(f32[6,4,32,128]{3,2,1,0:T(8,128)S(1)} %get-tuple-element.8), channel_id=1, source_target_pairs={{16,0},{32,16},{48,32},{64,48},{80,64},{96,80},{112,96},{0,112},{1... | collective-permute-start | bytes 1179656 | tf_op jit(solution)/shard_map/ppermute | solution.py:26
  26.3 1.8 fusion.206
  33.1 1.9 fusion.108
  46.8 2.0 fusion.83
  53.6 1.9 fusion.156
  57.1 1.9 collective-permute-start.16
  69.0 2.1 collective-permute-done.18
  71.2 3.1 %collective-permute-done.19 = f32[6,4,32,128]{3,2,1,0:T(8,128)S(1)} collective-permute-done((f32[6,4,32,128]{3,2,1,0:T(8,128)S(1)}, f32[6,4,32,128]{3,2,1,0:T(8,128)S(1)}, u32[]{:S(2)}, u32[]{:S(2)}) %collective-permute-start.19) | collective-permute-done | bytes 393248 | tf_op jit(solution)/shard_map/ppermute | solution.py:25
  77.5 8.3 %all-to-all-start = ((f32[2,12,16,8,128]{4,3,1,0,2:T(8,128)}), f32[2,12,16,8,128]{4,3,1,0,2:T(8,128)S(1)}, u32[]{:S(2)}, u32[]{:S(2)}) async-start(f32[2,12,16,8,128]{4,3,1,0,2:T(8,128)} %copy.18), calls=%async_computation | async-start | bytes 3145728 | tf_op jit(solution)/shard_map/all_to_all | solution.py:200
  85.8 19.8 %all-to-all-done = f32[2,12,16,8,128]{4,3,1,0,2:T(8,128)S(1)} async-done(((f32[2,12,16,8,128]{4,3,1,0,2:T(8,128)}), f32[2,12,16,8,128]{4,3,1,0,2:T(8,128)S(1)}, u32[]{:S(2)}, u32[]{:S(2)}) %all-to-all-start) | async-done | bytes 1572896 | tf_op jit(solution)/shard_map/all_to_all | solution.py:200
  107.7 4.8 %shard_map.41 = (f32[192,192]{1,0:T(8,128)}, f32[192,192]{1,0:T(8,128)}) custom-call(f32[1536,128]{1,0:T(8,128)} %bitcast.23, f32[1536,128]{1,0:T(8,128)} %bitcast.29), custom_call_target="tpu_custom_call" | custom-call | tf_op jit(solution)/shard_map/pallas_call | solution.py:159
  115.9 2.4 %collective-permute-start.22 = (f32[200,192]{1,0:T(8,128)S(1)}, f32[200,192]{1,0:T(8,128)S(1)}, u32[]{:S(2)}, u32[]{:S(2)}) collective-permute-start(f32[200,192]{1,0:T(8,128)S(1)} %select_add_fusion), channel_id=1, source_target_pairs={{0,64},{16,80},{32,96},{48,112},{64,0},{80,16},{96,32},{112,48},{1... | collective-permute-start | bytes 460808 | tf_op jit(solution)/shard_map/ppermute | solution.py:64
  119.7 3.5 %collective-permute-done.21 = f32[200,192]{1,0:T(8,128)S(1)} collective-permute-done((f32[200,192]{1,0:T(8,128)S(1)}, f32[200,192]{1,0:T(8,128)S(1)}, u32[]{:S(2)}, u32[]{:S(2)}) %collective-permute-start.21) | collective-permute-done | bytes 153632 | tf_op jit(solution)/shard_map/ppermute | solution.py:64
  123.2 2.2 %collective-permute-done.22 = f32[200,192]{1,0:T(8,128)S(1)} collective-permute-done((f32[200,192]{1,0:T(8,128)S(1)}, f32[200,192]{1,0:T(8,128)S(1)}, u32[]{:S(2)}, u32[]{:S(2)}) %collective-permute-start.22) | collective-permute-done | bytes 153632 | tf_op jit(solution)/shard_map/ppermute | solution.py:64
  125.4 3.5 %collective-permute-done.23 = f32[200,192]{1,0:T(8,128)S(1)} collective-permute-done((f32[200,192]{1,0:T(8,128)S(1)}, f32[200,192]{1,0:T(8,128)S(1)}, u32[]{:S(2)}, u32[]{:S(2)}) %collective-permute-start.23) | collective-permute-done | bytes 153632 | tf_op jit(solution)/shard_map/ppermute | solution.py:64
  129.1 2.0 collective-permute-start.25
  131.1 5.9 %collective-permute-done.24 = f32[200,192]{1,0:T(8,128)S(1)} collective-permute-done((f32[200,192]{1,0:T(8,128)S(1)}, f32[200,192]{1,0:T(8,128)S(1)}, u32[]{:S(2)}, u32[]{:S(2)}) %collective-permute-start.24) | collective-permute-done | bytes 153632 | tf_op jit(solution)/shard_map/ppermute | solution.py:64
  138.7 3.4 %collective-permute-done.26 = f32[200,192]{1,0:T(8,128)S(1)} collective-permute-done((f32[200,192]{1,0:T(8,128)S(1)}, f32[200,192]{1,0:T(8,128)S(1)}, u32[]{:S(2)}, u32[]{:S(2)}) %collective-permute-start.26) | collective-permute-done | bytes 153632 | tf_op jit(solution)/shard_map/ppermute | solution.py:64
  145.6 4.6 %collective-permute-done.27 = f32[200,192]{1,0:T(8,128)S(1)} collective-permute-done((f32[200,192]{1,0:T(8,128)S(1)}, f32[200,192]{1,0:T(8,128)S(1)}, u32[]{:S(2)}, u32[]{:S(2)}) %collective-permute-start.27) | collective-permute-done | bytes 153632 | tf_op jit(solution)/shard_map/ppermute | solution.py:64
  150.2 3.1 %collective-permute-done.28 = f32[200,192]{1,0:T(8,128)S(1)} collective-permute-done((f32[200,192]{1,0:T(8,128)S(1)}, f32[200,192]{1,0:T(8,128)S(1)}, u32[]{:S(2)}, u32[]{:S(2)}) %collective-permute-start.28) | collective-permute-done | bytes 153632 | tf_op jit(solution)/shard_map/ppermute | solution.py:64
  153.3 3.1 %collective-permute-done.29 = f32[200,192]{1,0:T(8,128)S(1)} collective-permute-done((f32[200,192]{1,0:T(8,128)S(1)}, f32[200,192]{1,0:T(8,128)S(1)}, u32[]{:S(2)}, u32[]{:S(2)}) %collective-permute-start.29) | collective-permute-done | bytes 153632 | tf_op jit(solution)/shard_map/ppermute | solution.py:64
  159.8 24.6 %shard_map.42 = f32[192,192]{1,0:T(8,128)} custom-call(f32[192,192]{1,0:T(8,128)} %reshape.35.c_ref), custom_call_target="tpu_custom_call" | custom-call | tf_op jit(solution)/shard_map/pallas_call | solution.py:143
  188.6 3.5 %shard_map.43 = f32[1536,128]{1,0:T(8,128)} custom-call(f32[192,192]{1,0:T(8,128)} %reshape.37.refs_0_, f32[1536,128]{1,0:T(8,128)} %bitcast.24), custom_call_target="tpu_custom_call" | custom-call | tf_op jit(solution)/shard_map/pallas_call | solution.py:168
  192.1 2.1 copy.24
  194.2 4.3 %all-to-all-start.1 = ((f32[12,16,8,128]{3,2,0,1:T(8,128)}), f32[12,16,8,128]{3,2,0,1:T(8,128)}, u32[]{:S(2)}, u32[]{:S(2)}) async-start(f32[12,16,8,128]{3,2,0,1:T(8,128)} %copy.24), calls=%async_computation.1 | async-start | bytes 1572864 | tf_op jit(solution)/shard_map/all_to_all | solution.py:225
  202.2 11.1 %all-to-all-done.1 = f32[12,16,8,128]{3,2,0,1:T(8,128)} async-done(((f32[12,16,8,128]{3,2,0,1:T(8,128)}), f32[12,16,8,128]{3,2,0,1:T(8,128)}, u32[]{:S(2)}, u32[]{:S(2)}) %all-to-all-start.1) | async-done | bytes 786464 | tf_op jit(solution)/shard_map/all_to_all | solution.py:225
  213.3 2.1 copy.25
  (229 shorter events, 70.6 us)
Async XLA Ops:
  1.9 8.8 %collective-permute-start = (f32[6,4,32,128]{3,2,1,0:T(8,128)S(1)}, f32[6,4,32,128]{3,2,1,0:T(8,128)S(1)}, u32[]{:S(2)}, u32[]{:S(2)}) collective-permute-start(f32[6,4,32,128]{3,2,1,0:T(8,128)S(1)} %get-tuple-element.76), channel_id=1, source_target_pairs={{16,0},{32,16},{48,32},{64,48},{80,64},{96,80},{112,96},{0,112},{1... | collective-permute-start | bytes 1179656 | tf_op jit(solution)/shard_map/ppermute | solution.py:26
  4.2 8.4 %collective-permute-start.1 = (f32[6,4,32,128]{3,2,1,0:T(8,128)S(1)}, f32[6,4,32,128]{3,2,1,0:T(8,128)S(1)}, u32[]{:S(2)}, u32[]{:S(2)}) collective-permute-start(f32[6,4,32,128]{3,2,1,0:T(8,128)S(1)} %get-tuple-element.76), channel_id=1, source_target_pairs={{0,16},{16,32},{32,48},{48,64},{64,80},{80,96},{96,112},{112,0},{1... | collective-permute-start | bytes 1179656 | tf_op jit(solution)/shard_map/ppermute | solution.py:25
  4.2 13.8 %collective-permute-start.8 = (f32[6,4,32,128]{3,2,1,0:T(8,128)S(1)}, f32[6,4,32,128]{3,2,1,0:T(8,128)S(1)}, u32[]{:S(2)}, u32[]{:S(2)}) collective-permute-start(f32[6,4,32,128]{3,2,1,0:T(8,128)S(1)} %get-tuple-element.77), channel_id=1, source_target_pairs={{16,0},{32,16},{48,32},{64,48},{80,64},{96,80},{112,96},{0,112},{1... | collective-permute-start | bytes 1179656 | tf_op jit(solution)/shard_map/ppermute | solution.py:26
  7.2 10.8 %collective-permute-start.9 = (f32[6,4,32,128]{3,2,1,0:T(8,128)S(1)}, f32[6,4,32,128]{3,2,1,0:T(8,128)S(1)}, u32[]{:S(2)}, u32[]{:S(2)}) collective-permute-start(f32[6,4,32,128]{3,2,1,0:T(8,128)S(1)} %get-tuple-element.77), channel_id=1, source_target_pairs={{0,16},{16,32},{32,48},{48,64},{64,80},{80,96},{96,112},{112,0},{1... | collective-permute-start | bytes 1179656 | tf_op jit(solution)/shard_map/ppermute | solution.py:25
  16.8 8.0 %collective-permute-start.2 = (f32[6,4,32,128]{3,2,1,0:T(8,128)S(1)}, f32[6,4,32,128]{3,2,1,0:T(8,128)S(1)}, u32[]{:S(2)}, u32[]{:S(2)}) collective-permute-start(f32[6,4,32,128]{3,2,1,0:T(8,128)S(1)} %get-tuple-element.6), channel_id=1, source_target_pairs={{16,0},{32,16},{48,32},{64,48},{80,64},{96,80},{112,96},{0,112},{1... | collective-permute-start | bytes 1179656 | tf_op jit(solution)/shard_map/ppermute | solution.py:26
  17.9 8.4 %collective-permute-start.3 = (f32[6,4,32,128]{3,2,1,0:T(8,128)S(1)}, f32[6,4,32,128]{3,2,1,0:T(8,128)S(1)}, u32[]{:S(2)}, u32[]{:S(2)}) collective-permute-start(f32[6,4,32,128]{3,2,1,0:T(8,128)S(1)} %get-tuple-element.6), channel_id=1, source_target_pairs={{0,16},{16,32},{32,48},{48,64},{64,80},{80,96},{96,112},{112,0},{1... | collective-permute-start | bytes 1179656 | tf_op jit(solution)/shard_map/ppermute | solution.py:25
  21.7 9.9 %collective-permute-start.10 = (f32[6,4,32,128]{3,2,1,0:T(8,128)S(1)}, f32[6,4,32,128]{3,2,1,0:T(8,128)S(1)}, u32[]{:S(2)}, u32[]{:S(2)}) collective-permute-start(f32[6,4,32,128]{3,2,1,0:T(8,128)S(1)} %get-tuple-element.8), channel_id=1, source_target_pairs={{16,0},{32,16},{48,32},{64,48},{80,64},{96,80},{112,96},{0,112},{1... | collective-permute-start | bytes 1179656 | tf_op jit(solution)/shard_map/ppermute | solution.py:26
  24.7 8.4 %collective-permute-start.11 = (f32[6,4,32,128]{3,2,1,0:T(8,128)S(1)}, f32[6,4,32,128]{3,2,1,0:T(8,128)S(1)}, u32[]{:S(2)}, u32[]{:S(2)}) collective-permute-start(f32[6,4,32,128]{3,2,1,0:T(8,128)S(1)} %get-tuple-element.8), channel_id=1, source_target_pairs={{0,16},{16,32},{32,48},{48,64},{64,80},{80,96},{96,112},{112,0},{1... | collective-permute-start | bytes 1179656 | tf_op jit(solution)/shard_map/ppermute | solution.py:25
  29.9 8.6 %collective-permute-start.4 = (f32[6,4,32,128]{3,2,1,0:T(8,128)S(1)}, f32[6,4,32,128]{3,2,1,0:T(8,128)S(1)}, u32[]{:S(2)}, u32[]{:S(2)}) collective-permute-start(f32[6,4,32,128]{3,2,1,0:T(8,128)S(1)} %fusion.206), channel_id=1, source_target_pairs={{16,0},{32,16},{48,32},{64,48},{80,64},{96,80},{112,96},{0,112},{1... | collective-permute-start | bytes 1179656 | tf_op jit(solution)/shard_map/ppermute | solution.py:26
  31.5 8.4 %collective-permute-start.5 = (f32[6,4,32,128]{3,2,1,0:T(8,128)S(1)}, f32[6,4,32,128]{3,2,1,0:T(8,128)S(1)}, u32[]{:S(2)}, u32[]{:S(2)}) collective-permute-start(f32[6,4,32,128]{3,2,1,0:T(8,128)S(1)} %fusion.206), channel_id=1, source_target_pairs={{0,16},{16,32},{32,48},{48,64},{64,80},{80,96},{96,112},{112,0},{1... | collective-permute-start | bytes 1179656 | tf_op jit(solution)/shard_map/ppermute | solution.py:25
  36.7 8.7 %collective-permute-start.12 = (f32[6,4,32,128]{3,2,1,0:T(8,128)S(1)}, f32[6,4,32,128]{3,2,1,0:T(8,128)S(1)}, u32[]{:S(2)}, u32[]{:S(2)}) collective-permute-start(f32[6,4,32,128]{3,2,1,0:T(8,128)S(1)} %fusion.108), channel_id=1, source_target_pairs={{16,0},{32,16},{48,32},{64,48},{80,64},{96,80},{112,96},{0,112},{1... | collective-permute-start | bytes 1179656 | tf_op jit(solution)/shard_map/ppermute | solution.py:26
  38.4 8.4 %collective-permute-start.13 = (f32[6,4,32,128]{3,2,1,0:T(8,128)S(1)}, f32[6,4,32,128]{3,2,1,0:T(8,128)S(1)}, u32[]{:S(2)}, u32[]{:S(2)}) collective-permute-start(f32[6,4,32,128]{3,2,1,0:T(8,128)S(1)} %fusion.108), channel_id=1, source_target_pairs={{0,16},{16,32},{32,48},{48,64},{64,80},{80,96},{96,112},{112,0},{1... | collective-permute-start | bytes 1179656 | tf_op jit(solution)/shard_map/ppermute | solution.py:25
  43.5 8.9 %collective-permute-start.6 = (f32[6,4,32,128]{3,2,1,0:T(8,128)S(1)}, f32[6,4,32,128]{3,2,1,0:T(8,128)S(1)}, u32[]{:S(2)}, u32[]{:S(2)}) collective-permute-start(f32[6,4,32,128]{3,2,1,0:T(8,128)S(1)} %fusion.181), channel_id=1, source_target_pairs={{16,0},{32,16},{48,32},{64,48},{80,64},{96,80},{112,96},{0,112},{1... | collective-permute-start | bytes 1179656 | tf_op jit(solution)/shard_map/ppermute | solution.py:26
  45.2 8.4 %collective-permute-start.7 = (f32[6,4,32,128]{3,2,1,0:T(8,128)S(1)}, f32[6,4,32,128]{3,2,1,0:T(8,128)S(1)}, u32[]{:S(2)}, u32[]{:S(2)}) collective-permute-start(f32[6,4,32,128]{3,2,1,0:T(8,128)S(1)} %fusion.181), channel_id=1, source_target_pairs={{0,16},{16,32},{32,48},{48,64},{64,80},{80,96},{96,112},{112,0},{1... | collective-permute-start | bytes 1179656 | tf_op jit(solution)/shard_map/ppermute | solution.py:25
  50.5 8.7 %collective-permute-start.14 = (f32[6,4,32,128]{3,2,1,0:T(8,128)S(1)}, f32[6,4,32,128]{3,2,1,0:T(8,128)S(1)}, u32[]{:S(2)}, u32[]{:S(2)}) collective-permute-start(f32[6,4,32,128]{3,2,1,0:T(8,128)S(1)} %fusion.83), channel_id=1, source_target_pairs={{16,0},{32,16},{48,32},{64,48},{80,64},{96,80},{112,96},{0,112},{1... | collective-permute-start | bytes 1179656 | tf_op jit(solution)/shard_map/ppermute | solution.py:26
  52.2 8.4 %collective-permute-start.15 = (f32[6,4,32,128]{3,2,1,0:T(8,128)S(1)}, f32[6,4,32,128]{3,2,1,0:T(8,128)S(1)}, u32[]{:S(2)}, u32[]{:S(2)}) collective-permute-start(f32[6,4,32,128]{3,2,1,0:T(8,128)S(1)} %fusion.83), channel_id=1, source_target_pairs={{0,16},{16,32},{32,48},{48,64},{64,80},{80,96},{96,112},{112,0},{1... | collective-permute-start | bytes 1179656 | tf_op jit(solution)/shard_map/ppermute | solution.py:25
  57.1 9.0 %collective-permute-start.16 = (f32[6,4,32,128]{3,2,1,0:T(8,128)S(1)}, f32[6,4,32,128]{3,2,1,0:T(8,128)S(1)}, u32[]{:S(2)}, u32[]{:S(2)}) collective-permute-start(f32[6,4,32,128]{3,2,1,0:T(8,128)S(1)} %fusion.156), channel_id=1, source_target_pairs={{16,0},{32,16},{48,32},{64,48},{80,64},{96,80},{112,96},{0,112},{1... | collective-permute-start | bytes 1179656 | tf_op jit(solution)/shard_map/ppermute | solution.py:26
  58.9 8.4 %collective-permute-start.17 = (f32[6,4,32,128]{3,2,1,0:T(8,128)S(1)}, f32[6,4,32,128]{3,2,1,0:T(8,128)S(1)}, u32[]{:S(2)}, u32[]{:S(2)}) collective-permute-start(f32[6,4,32,128]{3,2,1,0:T(8,128)S(1)} %fusion.156), channel_id=1, source_target_pairs={{0,16},{16,32},{32,48},{48,64},{64,80},{80,96},{96,112},{112,0},{1... | collective-permute-start | bytes 1179656 | tf_op jit(solution)/shard_map/ppermute | solution.py:25
  64.2 7.0 %collective-permute-start.18 = (f32[6,4,32,128]{3,2,1,0:T(8,128)S(1)}, f32[6,4,32,128]{3,2,1,0:T(8,128)S(1)}, u32[]{:S(2)}, u32[]{:S(2)}) collective-permute-start(f32[6,4,32,128]{3,2,1,0:T(8,128)S(1)} %fusion.58), channel_id=1, source_target_pairs={{16,0},{32,16},{48,32},{64,48},{80,64},{96,80},{112,96},{0,112},{1... | collective-permute-start | bytes 1179656 | tf_op jit(solution)/shard_map/ppermute | solution.py:26
  65.9 8.4 %collective-permute-start.19 = (f32[6,4,32,128]{3,2,1,0:T(8,128)S(1)}, f32[6,4,32,128]{3,2,1,0:T(8,128)S(1)}, u32[]{:S(2)}, u32[]{:S(2)}) collective-permute-start(f32[6,4,32,128]{3,2,1,0:T(8,128)S(1)} %fusion.58), channel_id=1, source_target_pairs={{0,16},{16,32},{32,48},{48,64},{64,80},{80,96},{96,112},{112,0},{1... | collective-permute-start | bytes 1179656 | tf_op jit(solution)/shard_map/ppermute | solution.py:25
  77.5 28.1 %all-to-all-start = ((f32[2,12,16,8,128]{4,3,1,0,2:T(8,128)}), f32[2,12,16,8,128]{4,3,1,0,2:T(8,128)S(1)}, u32[]{:S(2)}, u32[]{:S(2)}) async-start(f32[2,12,16,8,128]{4,3,1,0,2:T(8,128)} %copy.18), calls=%async_computation | async-start | bytes 3145728 | tf_op jit(solution)/shard_map/all_to_all | solution.py:200
  113.6 1.5 collective-permute-start.20
  115.2 8.0 %collective-permute-start.21 = (f32[200,192]{1,0:T(8,128)S(1)}, f32[200,192]{1,0:T(8,128)S(1)}, u32[]{:S(2)}, u32[]{:S(2)}) collective-permute-start(f32[200,192]{1,0:T(8,128)S(1)} %select_add_fusion), channel_id=1, source_target_pairs={{0,96},{16,112},{32,0},{48,16},{64,32},{80,48},{96,64},{112,80},{1... | collective-permute-start | bytes 460808 | tf_op jit(solution)/shard_map/ppermute | solution.py:64
  115.9 9.5 %collective-permute-start.22 = (f32[200,192]{1,0:T(8,128)S(1)}, f32[200,192]{1,0:T(8,128)S(1)}, u32[]{:S(2)}, u32[]{:S(2)}) collective-permute-start(f32[200,192]{1,0:T(8,128)S(1)} %select_add_fusion), channel_id=1, source_target_pairs={{0,64},{16,80},{32,96},{48,112},{64,0},{80,16},{96,32},{112,48},{1... | collective-permute-start | bytes 460808 | tf_op jit(solution)/shard_map/ppermute | solution.py:64
  118.4 10.5 %collective-permute-start.23 = (f32[200,192]{1,0:T(8,128)S(1)}, f32[200,192]{1,0:T(8,128)S(1)}, u32[]{:S(2)}, u32[]{:S(2)}) collective-permute-start(f32[200,192]{1,0:T(8,128)S(1)} %select_add_fusion), channel_id=1, source_target_pairs={{0,32},{16,48},{32,64},{48,80},{64,96},{80,112},{96,0},{112,16},{1... | collective-permute-start | bytes 460808 | tf_op jit(solution)/shard_map/ppermute | solution.py:64
  129.0 8.0 %collective-permute-start.24 = (f32[200,192]{1,0:T(8,128)S(1)}, f32[200,192]{1,0:T(8,128)S(1)}, u32[]{:S(2)}, u32[]{:S(2)}) collective-permute-start(f32[200,192]{1,0:T(8,128)S(1)} %add_add_fusion.1), channel_id=1, source_target_pairs={{0,3},{1,0},{2,1},{3,2},{4,7},{5,4},{6,5},{7,6},{8,11},{9,8},{10,9... | collective-permute-start | bytes 460808 | tf_op jit(solution)/shard_map/ppermute | solution.py:64
  129.1 9.6 %collective-permute-start.25 = (f32[200,192]{1,0:T(8,128)S(1)}, f32[200,192]{1,0:T(8,128)S(1)}, u32[]{:S(2)}, u32[]{:S(2)}) collective-permute-start(f32[200,192]{1,0:T(8,128)S(1)} %add_add_fusion.1), channel_id=1, source_target_pairs={{0,2},{1,3},{2,0},{3,1},{4,6},{5,7},{6,4},{7,5},{8,10},{9,11},{10,... | collective-permute-start | bytes 460808 | tf_op jit(solution)/shard_map/ppermute | solution.py:64
  131.1 11.0 %collective-permute-start.26 = (f32[200,192]{1,0:T(8,128)S(1)}, f32[200,192]{1,0:T(8,128)S(1)}, u32[]{:S(2)}, u32[]{:S(2)}) collective-permute-start(f32[200,192]{1,0:T(8,128)S(1)} %add_add_fusion.1), channel_id=1, source_target_pairs={{0,1},{1,2},{2,3},{3,0},{4,5},{5,6},{6,7},{7,4},{8,9},{9,10},{10,1... | collective-permute-start | bytes 460808 | tf_op jit(solution)/shard_map/ppermute | solution.py:64
  142.2 8.0 %collective-permute-start.27 = (f32[200,192]{1,0:T(8,128)S(1)}, f32[200,192]{1,0:T(8,128)S(1)}, u32[]{:S(2)}, u32[]{:S(2)}) collective-permute-start(f32[200,192]{1,0:T(8,128)S(1)} %add_add_fusion), channel_id=1, source_target_pairs={{0,12},{1,13},{2,14},{3,15},{4,0},{5,1},{6,2},{7,3},{8,4},{9,5},{1... | collective-permute-start | bytes 460808 | tf_op jit(solution)/shard_map/ppermute | solution.py:64
  143.8 9.5 %collective-permute-start.28 = (f32[200,192]{1,0:T(8,128)S(1)}, f32[200,192]{1,0:T(8,128)S(1)}, u32[]{:S(2)}, u32[]{:S(2)}) collective-permute-start(f32[200,192]{1,0:T(8,128)S(1)} %add_add_fusion), channel_id=1, source_target_pairs={{0,8},{1,9},{2,10},{3,11},{4,12},{5,13},{6,14},{7,15},{8,0},{9,1},... | collective-permute-start | bytes 460808 | tf_op jit(solution)/shard_map/ppermute | solution.py:64
  144.8 11.6 %collective-permute-start.29 = (f32[200,192]{1,0:T(8,128)S(1)}, f32[200,192]{1,0:T(8,128)S(1)}, u32[]{:S(2)}, u32[]{:S(2)}) collective-permute-start(f32[200,192]{1,0:T(8,128)S(1)} %add_add_fusion), channel_id=1, source_target_pairs={{0,4},{1,5},{2,6},{3,7},{4,8},{5,9},{6,10},{7,11},{8,12},{9,13},{1... | collective-permute-start | bytes 460808 | tf_op jit(solution)/shard_map/ppermute | solution.py:64
  194.2 19.1 %all-to-all-start.1 = ((f32[12,16,8,128]{3,2,0,1:T(8,128)}), f32[12,16,8,128]{3,2,0,1:T(8,128)}, u32[]{:S(2)}, u32[]{:S(2)}) async-start(f32[12,16,8,128]{3,2,0,1:T(8,128)} %copy.24), calls=%async_computation.1 | async-start | bytes 1572864 | tf_op jit(solution)/shard_map/all_to_all | solution.py:225
  (3 other events, 8.3 us)

commit v12 on v10

--- a/solution.py
+++ b/solution.py
@@ -74,9 +74,10 @@
 
 
 def mesh_sum(x):
-    x = group_sum(x, "dom", 1, lax.axis_size("dom"))
     x = group_sum(x, "band", 1, 4)
-    return group_sum(x, "band", 4, lax.axis_size("band") // 4)
+    x = group_sum(x, "band", 4, lax.axis_size("band") // 4)
+    x = group_sum(x, "dom", 1, 2)
+    return group_sum(x, "dom", 2, lax.axis_size("dom") // 2)
 
 
 def gram_kernel(rows, f_ref, h_ref, c_ref, g_ref):

time: 228 us -> 217 us (0.952)
  the two profiles are of different devices: /device:TPU:4 before, /device:TPU:0 now
where the time goes in v12:
time: 217 us; the launch traced here: 214 us
  waiting for transfers between devices  72.8 us (34%)
  starting transfers between devices  48.5 us (22%)
  local copies, waits for them, and re-layouts  37.1 us (17%)
  Pallas kernels  32.1 us (15%)
  other arithmetic  20.6 us (9%)
    ppermute x10, waiting for transfers between devices, group_sum(): received.append(lax.ppermute(x, axis, pairs))  25.1 us
    pallas_call x1, Pallas kernels, lower_inverse(): pl.pallas_call(inverse_kernel, out_shape=jax.ShapeDtypeStruct((n, n), jnp...  23.8 us
    all_to_all x1, waiting for transfers between devices, local(): spread = lax.all_to_all(chunked, 'band', 2, 2, tiled=True)  19.8 us
    ppermute x10, starting transfers between devices, extended(): after = lax.ppermute(initial, axis, down)  19.5 us
    ppermute x10, starting transfers between devices, group_sum(): received.append(lax.ppermute(x, axis, pairs))  16.4 us
    ppermute x10, waiting for transfers between devices, extended(): before = lax.ppermute(last, axis, up)  14.6 us
    slice x72, local copies, waits for them, and re-layouts, hamiltonian(): near = near + jnp.roll(field, reach, 3) + jnp.roll(field, -reach, 3)  14.3 us
    sub x6, other arithmetic, local(): 2.0 / half * (apply(c) - center * c) - p  11.2 us
  transfers between devices with their start and end apart: 32, of which 22 were waited for; matrix products, arithmetic and copies ran while one was open for 18% of the time, Pallas kernels for 0%

profile of v12, /device:TPU:0, one launch (start us, length us, event | category | flops | bytes accessed | tf_op | source)
XLA Modules:
  0.0 214.0 jit_solution(2002157662450950924)
XLA Ops:
  1.9 2.3 %collective-permute-start = (f32[6,4,32,128]{3,2,1,0:T(8,128)S(1)}, f32[6,4,32,128]{3,2,1,0:T(8,128)S(1)}, u32[]{:S(2)}, u32[]{:S(2)}) collective-permute-start(f32[6,4,32,128]{3,2,1,0:T(8,128)S(1)} %get-tuple-element.76), channel_id=1, source_target_pairs={{16,0},{32,16},{48,32},{64,48},{80,64},{96,80},{112,96},{0,112},{1... | collective-permute-start | bytes 1179656 | tf_op jit(solution)/shard_map/ppermute | solution.py:26
  4.2 3.0 %collective-permute-start.8 = (f32[6,4,32,128]{3,2,1,0:T(8,128)S(1)}, f32[6,4,32,128]{3,2,1,0:T(8,128)S(1)}, u32[]{:S(2)}, u32[]{:S(2)}) collective-permute-start(f32[6,4,32,128]{3,2,1,0:T(8,128)S(1)} %get-tuple-element.77), channel_id=1, source_target_pairs={{16,0},{32,16},{48,32},{64,48},{80,64},{96,80},{112,96},{0,112},{1... | collective-permute-start | bytes 1179656 | tf_op jit(solution)/shard_map/ppermute | solution.py:26
  10.7 1.9 collective-permute-done.1
  12.6 2.3 %broadcast_multiply_fusion.1 = (f32[6,4,32,128]{3,2,1,0:T(8,128)S(1)}, f32[6,4,32,128]{3,2,1,0:T(8,128)S(1)}) fusion(f32[6,4,32,128]{3,2,1,0:T(8,128)S(1)} %get-tuple-element.76, f32[6,4,32,4]{3,2,1,0:T(8,128)S(1)} %get-tuple-element.70, f32[6,4,32,124]{3,2,1,0:T(8,128)S(1)} %get-tuple-element.74, f32[6,4,32,124]{3,2,1,0:T(8,128)S(1)} %get-tuple-element.72, ...), kind=kLoop, calls=%fused_computation.464 | loop fusion | flops 5603328 | bytes 8323072 | tf_op jit(solution)/shard_map/div | solution.py:190
  18.0 1.9 broadcast_multiply_fusion
  21.7 3.0 %collective-permute-start.10 = (f32[6,4,32,128]{3,2,1,0:T(8,128)S(1)}, f32[6,4,32,128]{3,2,1,0:T(8,128)S(1)}, u32[]{:S(2)}, u32[]{:S(2)}) collective-permute-start(f32[6,4,32,128]{3,2,1,0:T(8,128)S(1)} %get-tuple-element.8), channel_id=1, source_target_pairs={{16,0},{32,16},{48,32},{64,48},{80,64},{96,80},{112,96},{0,112},{1... | collective-permute-start | bytes 1179656 | tf_op jit(solution)/shard_map/ppermute | solution.py:26
  26.3 1.8 fusion.206
  33.1 1.9 fusion.108
  39.9 1.8 fusion.181
  46.8 2.0 fusion.83
  53.6 1.9 fusion.156
  57.1 1.9 collective-permute-start.16
  69.0 2.1 collective-permute-done.18
  71.2 3.1 %collective-permute-done.19 = f32[6,4,32,128]{3,2,1,0:T(8,128)S(1)} collective-permute-done((f32[6,4,32,128]{3,2,1,0:T(8,128)S(1)}, f32[6,4,32,128]{3,2,1,0:T(8,128)S(1)}, u32[]{:S(2)}, u32[]{:S(2)}) %collective-permute-start.19) | collective-permute-done | bytes 393248 | tf_op jit(solution)/shard_map/ppermute | solution.py:25
  77.5 8.3 %all-to-all-start = ((f32[2,12,16,8,128]{4,3,1,0,2:T(8,128)}), f32[2,12,16,8,128]{4,3,1,0,2:T(8,128)S(1)}, u32[]{:S(2)}, u32[]{:S(2)}) async-start(f32[2,12,16,8,128]{4,3,1,0,2:T(8,128)} %copy.18), calls=%async_computation | async-start | bytes 3145728 | tf_op jit(solution)/shard_map/all_to_all | solution.py:200
  85.8 19.8 %all-to-all-done = f32[2,12,16,8,128]{4,3,1,0,2:T(8,128)S(1)} async-done(((f32[2,12,16,8,128]{4,3,1,0,2:T(8,128)}), f32[2,12,16,8,128]{4,3,1,0,2:T(8,128)S(1)}, u32[]{:S(2)}, u32[]{:S(2)}) %all-to-all-start) | async-done | bytes 1572896 | tf_op jit(solution)/shard_map/all_to_all | solution.py:200
  107.7 4.8 %shard_map.41 = (f32[192,192]{1,0:T(8,128)}, f32[192,192]{1,0:T(8,128)}) custom-call(f32[1536,128]{1,0:T(8,128)} %bitcast.23, f32[1536,128]{1,0:T(8,128)} %bitcast.29), custom_call_target="tpu_custom_call" | custom-call | tf_op jit(solution)/shard_map/pallas_call | solution.py:159
  115.7 3.7 %collective-permute-done.20 = f32[200,192]{1,0:T(8,128)S(1)} collective-permute-done((f32[200,192]{1,0:T(8,128)S(1)}, f32[200,192]{1,0:T(8,128)S(1)}, u32[]{:S(2)}, u32[]{:S(2)}) %collective-permute-start.20) | collective-permute-done | bytes 153632 | tf_op jit(solution)/shard_map/ppermute | solution.py:64
  121.1 2.1 collective-permute-done.22
  126.6 2.7 %collective-permute-done.23 = f32[200,192]{1,0:T(8,128)S(1)} collective-permute-done((f32[200,192]{1,0:T(8,128)S(1)}, f32[200,192]{1,0:T(8,128)S(1)}, u32[]{:S(2)}, u32[]{:S(2)}) %collective-permute-start.23) | collective-permute-done | bytes 153632 | tf_op jit(solution)/shard_map/ppermute | solution.py:64
  129.2 3.0 %collective-permute-done.24 = f32[200,192]{1,0:T(8,128)S(1)} collective-permute-done((f32[200,192]{1,0:T(8,128)S(1)}, f32[200,192]{1,0:T(8,128)S(1)}, u32[]{:S(2)}, u32[]{:S(2)}) %collective-permute-start.24) | collective-permute-done | bytes 153632 | tf_op jit(solution)/shard_map/ppermute | solution.py:64
  132.2 2.1 collective-permute-done.25
  136.0 6.5 %collective-permute-start.27 = (f32[200,192]{1,0:T(8,128)S(1)}, f32[200,192]{1,0:T(8,128)S(1)}, u32[]{:S(2)}, u32[]{:S(2)}) collective-permute-start(f32[200,192]{1,0:T(8,128)S(1)} %select_add_fusion), channel_id=1, source_target_pairs={{0,96},{16,112},{32,0},{48,16},{64,32},{80,48},{96,64},{112,80},{1... | collective-permute-start | bytes 460808 | tf_op jit(solution)/shard_map/ppermute | solution.py:64
  142.6 3.2 %collective-permute-start.28 = (f32[200,192]{1,0:T(8,128)S(1)}, f32[200,192]{1,0:T(8,128)S(1)}, u32[]{:S(2)}, u32[]{:S(2)}) collective-permute-start(f32[200,192]{1,0:T(8,128)S(1)} %select_add_fusion), channel_id=1, source_target_pairs={{0,64},{16,80},{32,96},{48,112},{64,0},{80,16},{96,32},{112,48},{1... | collective-permute-start | bytes 460808 | tf_op jit(solution)/shard_map/ppermute | solution.py:64
  147.1 4.5 %collective-permute-done.27 = f32[200,192]{1,0:T(8,128)S(1)} collective-permute-done((f32[200,192]{1,0:T(8,128)S(1)}, f32[200,192]{1,0:T(8,128)S(1)}, u32[]{:S(2)}, u32[]{:S(2)}) %collective-permute-start.27) | collective-permute-done | bytes 153632 | tf_op jit(solution)/shard_map/ppermute | solution.py:64
  152.0 3.5 %collective-permute-done.29 = f32[200,192]{1,0:T(8,128)S(1)} collective-permute-done((f32[200,192]{1,0:T(8,128)S(1)}, f32[200,192]{1,0:T(8,128)S(1)}, u32[]{:S(2)}, u32[]{:S(2)}) %collective-permute-start.29) | collective-permute-done | bytes 153632 | tf_op jit(solution)/shard_map/ppermute | solution.py:64
  158.9 23.8 %shard_map.42 = f32[192,192]{1,0:T(8,128)} custom-call(f32[192,192]{1,0:T(8,128)} %reshape.35.c_ref), custom_call_target="tpu_custom_call" | custom-call | tf_op jit(solution)/shard_map/pallas_call | solution.py:143
  187.0 3.5 %shard_map.43 = f32[1536,128]{1,0:T(8,128)} custom-call(f32[192,192]{1,0:T(8,128)} %reshape.37.refs_0_, f32[1536,128]{1,0:T(8,128)} %bitcast.24), custom_call_target="tpu_custom_call" | custom-call | tf_op jit(solution)/shard_map/pallas_call | solution.py:168
  190.5 2.1 copy.24
  192.6 4.3 %all-to-all-start.1 = ((f32[12,16,8,128]{3,2,0,1:T(8,128)}), f32[12,16,8,128]{3,2,0,1:T(8,128)}, u32[]{:S(2)}, u32[]{:S(2)}) async-start(f32[12,16,8,128]{3,2,0,1:T(8,128)} %copy.24), calls=%async_computation.1 | async-start | bytes 1572864 | tf_op jit(solution)/shard_map/all_to_all | solution.py:225
  200.6 11.1 %all-to-all-done.1 = f32[12,16,8,128]{3,2,0,1:T(8,128)} async-done(((f32[12,16,8,128]{3,2,0,1:T(8,128)}), f32[12,16,8,128]{3,2,0,1:T(8,128)}, u32[]{:S(2)}, u32[]{:S(2)}) %all-to-all-start.1) | async-done | bytes 786464 | tf_op jit(solution)/shard_map/all_to_all | solution.py:225
  211.7 2.1 copy.25
  (229 shorter events, 70.2 us)
Async XLA Ops:
  1.9 8.8 %collective-permute-start = (f32[6,4,32,128]{3,2,1,0:T(8,128)S(1)}, f32[6,4,32,128]{3,2,1,0:T(8,128)S(1)}, u32[]{:S(2)}, u32[]{:S(2)}) collective-permute-start(f32[6,4,32,128]{3,2,1,0:T(8,128)S(1)} %get-tuple-element.76), channel_id=1, source_target_pairs={{16,0},{32,16},{48,32},{64,48},{80,64},{96,80},{112,96},{0,112},{1... | collective-permute-start | bytes 1179656 | tf_op jit(solution)/shard_map/ppermute | solution.py:26
  4.2 8.4 %collective-permute-start.1 = (f32[6,4,32,128]{3,2,1,0:T(8,128)S(1)}, f32[6,4,32,128]{3,2,1,0:T(8,128)S(1)}, u32[]{:S(2)}, u32[]{:S(2)}) collective-permute-start(f32[6,4,32,128]{3,2,1,0:T(8,128)S(1)} %get-tuple-element.76), channel_id=1, source_target_pairs={{0,16},{16,32},{32,48},{48,64},{64,80},{80,96},{96,112},{112,0},{1... | collective-permute-start | bytes 1179656 | tf_op jit(solution)/shard_map/ppermute | solution.py:25
  4.2 13.8 %collective-permute-start.8 = (f32[6,4,32,128]{3,2,1,0:T(8,128)S(1)}, f32[6,4,32,128]{3,2,1,0:T(8,128)S(1)}, u32[]{:S(2)}, u32[]{:S(2)}) collective-permute-start(f32[6,4,32,128]{3,2,1,0:T(8,128)S(1)} %get-tuple-element.77), channel_id=1, source_target_pairs={{16,0},{32,16},{48,32},{64,48},{80,64},{96,80},{112,96},{0,112},{1... | collective-permute-start | bytes 1179656 | tf_op jit(solution)/shard_map/ppermute | solution.py:26
  7.2 10.8 %collective-permute-start.9 = (f32[6,4,32,128]{3,2,1,0:T(8,128)S(1)}, f32[6,4,32,128]{3,2,1,0:T(8,128)S(1)}, u32[]{:S(2)}, u32[]{:S(2)}) collective-permute-start(f32[6,4,32,128]{3,2,1,0:T(8,128)S(1)} %get-tuple-element.77), channel_id=1, source_target_pairs={{0,16},{16,32},{32,48},{48,64},{64,80},{80,96},{96,112},{112,0},{1... | collective-permute-start | bytes 1179656 | tf_op jit(solution)/shard_map/ppermute | solution.py:25
  16.8 8.0 %collective-permute-start.2 = (f32[6,4,32,128]{3,2,1,0:T(8,128)S(1)}, f32[6,4,32,128]{3,2,1,0:T(8,128)S(1)}, u32[]{:S(2)}, u32[]{:S(2)}) collective-permute-start(f32[6,4,32,128]{3,2,1,0:T(8,128)S(1)} %get-tuple-element.6), channel_id=1, source_target_pairs={{16,0},{32,16},{48,32},{64,48},{80,64},{96,80},{112,96},{0,112},{1... | collective-permute-start | bytes 1179656 | tf_op jit(solution)/shard_map/ppermute | solution.py:26
  17.9 8.4 %collective-permute-start.3 = (f32[6,4,32,128]{3,2,1,0:T(8,128)S(1)}, f32[6,4,32,128]{3,2,1,0:T(8,128)S(1)}, u32[]{:S(2)}, u32[]{:S(2)}) collective-permute-start(f32[6,4,32,128]{3,2,1,0:T(8,128)S(1)} %get-tuple-element.6), channel_id=1, source_target_pairs={{0,16},{16,32},{32,48},{48,64},{64,80},{80,96},{96,112},{112,0},{1... | collective-permute-start | bytes 1179656 | tf_op jit(solution)/shard_map/ppermute | solution.py:25
  21.7 9.9 %collective-permute-start.10 = (f32[6,4,32,128]{3,2,1,0:T(8,128)S(1)}, f32[6,4,32,128]{3,2,1,0:T(8,128)S(1)}, u32[]{:S(2)}, u32[]{:S(2)}) collective-permute-start(f32[6,4,32,128]{3,2,1,0:T(8,128)S(1)} %get-tuple-element.8), channel_id=1, source_target_pairs={{16,0},{32,16},{48,32},{64,48},{80,64},{96,80},{112,96},{0,112},{1... | collective-permute-start | bytes 1179656 | tf_op jit(solution)/shard_map/ppermute | solution.py:26
  24.7 8.4 %collective-permute-start.11 = (f32[6,4,32,128]{3,2,1,0:T(8,128)S(1)}, f32[6,4,32,128]{3,2,1,0:T(8,128)S(1)}, u32[]{:S(2)}, u32[]{:S(2)}) collective-permute-start(f32[6,4,32,128]{3,2,1,0:T(8,128)S(1)} %get-tuple-element.8), channel_id=1, source_target_pairs={{0,16},{16,32},{32,48},{48,64},{64,80},{80,96},{96,112},{112,0},{1... | collective-permute-start | bytes 1179656 | tf_op jit(solution)/shard_map/ppermute | solution.py:25
  29.9 8.6 %collective-permute-start.4 = (f32[6,4,32,128]{3,2,1,0:T(8,128)S(1)}, f32[6,4,32,128]{3,2,1,0:T(8,128)S(1)}, u32[]{:S(2)}, u32[]{:S(2)}) collective-permute-start(f32[6,4,32,128]{3,2,1,0:T(8,128)S(1)} %fusion.206), channel_id=1, source_target_pairs={{16,0},{32,16},{48,32},{64,48},{80,64},{96,80},{112,96},{0,112},{1... | collective-permute-start | bytes 1179656 | tf_op jit(solution)/shard_map/ppermute | solution.py:26
  31.5 8.4 %collective-permute-start.5 = (f32[6,4,32,128]{3,2,1,0:T(8,128)S(1)}, f32[6,4,32,128]{3,2,1,0:T(8,128)S(1)}, u32[]{:S(2)}, u32[]{:S(2)}) collective-permute-start(f32[6,4,32,128]{3,2,1,0:T(8,128)S(1)} %fusion.206), channel_id=1, source_target_pairs={{0,16},{16,32},{32,48},{48,64},{64,80},{80,96},{96,112},{112,0},{1... | collective-permute-start | bytes 1179656 | tf_op jit(solution)/shard_map/ppermute | solution.py:25
  36.7 8.7 %collective-permute-start.12 = (f32[6,4,32,128]{3,2,1,0:T(8,128)S(1)}, f32[6,4,32,128]{3,2,1,0:T(8,128)S(1)}, u32[]{:S(2)}, u32[]{:S(2)}) collective-permute-start(f32[6,4,32,128]{3,2,1,0:T(8,128)S(1)} %fusion.108), channel_id=1, source_target_pairs={{16,0},{32,16},{48,32},{64,48},{80,64},{96,80},{112,96},{0,112},{1... | collective-permute-start | bytes 1179656 | tf_op jit(solution)/shard_map/ppermute | solution.py:26
  38.4 8.4 %collective-permute-start.13 = (f32[6,4,32,128]{3,2,1,0:T(8,128)S(1)}, f32[6,4,32,128]{3,2,1,0:T(8,128)S(1)}, u32[]{:S(2)}, u32[]{:S(2)}) collective-permute-start(f32[6,4,32,128]{3,2,1,0:T(8,128)S(1)} %fusion.108), channel_id=1, source_target_pairs={{0,16},{16,32},{32,48},{48,64},{64,80},{80,96},{96,112},{112,0},{1... | collective-permute-start | bytes 1179656 | tf_op jit(solution)/shard_map/ppermute | solution.py:25
  43.5 8.9 %collective-permute-start.6 = (f32[6,4,32,128]{3,2,1,0:T(8,128)S(1)}, f32[6,4,32,128]{3,2,1,0:T(8,128)S(1)}, u32[]{:S(2)}, u32[]{:S(2)}) collective-permute-start(f32[6,4,32,128]{3,2,1,0:T(8,128)S(1)} %fusion.181), channel_id=1, source_target_pairs={{16,0},{32,16},{48,32},{64,48},{80,64},{96,80},{112,96},{0,112},{1... | collective-permute-start | bytes 1179656 | tf_op jit(solution)/shard_map/ppermute | solution.py:26
  45.2 8.4 %collective-permute-start.7 = (f32[6,4,32,128]{3,2,1,0:T(8,128)S(1)}, f32[6,4,32,128]{3,2,1,0:T(8,128)S(1)}, u32[]{:S(2)}, u32[]{:S(2)}) collective-permute-start(f32[6,4,32,128]{3,2,1,0:T(8,128)S(1)} %fusion.181), channel_id=1, source_target_pairs={{0,16},{16,32},{32,48},{48,64},{64,80},{80,96},{96,112},{112,0},{1... | collective-permute-start | bytes 1179656 | tf_op jit(solution)/shard_map/ppermute | solution.py:25
  50.5 8.7 %collective-permute-start.14 = (f32[6,4,32,128]{3,2,1,0:T(8,128)S(1)}, f32[6,4,32,128]{3,2,1,0:T(8,128)S(1)}, u32[]{:S(2)}, u32[]{:S(2)}) collective-permute-start(f32[6,4,32,128]{3,2,1,0:T(8,128)S(1)} %fusion.83), channel_id=1, source_target_pairs={{16,0},{32,16},{48,32},{64,48},{80,64},{96,80},{112,96},{0,112},{1... | collective-permute-start | bytes 1179656 | tf_op jit(solution)/shard_map/ppermute | solution.py:26
  52.2 8.4 %collective-permute-start.15 = (f32[6,4,32,128]{3,2,1,0:T(8,128)S(1)}, f32[6,4,32,128]{3,2,1,0:T(8,128)S(1)}, u32[]{:S(2)}, u32[]{:S(2)}) collective-permute-start(f32[6,4,32,128]{3,2,1,0:T(8,128)S(1)} %fusion.83), channel_id=1, source_target_pairs={{0,16},{16,32},{32,48},{48,64},{64,80},{80,96},{96,112},{112,0},{1... | collective-permute-start | bytes 1179656 | tf_op jit(solution)/shard_map/ppermute | solution.py:25
  57.1 9.0 %collective-permute-start.16 = (f32[6,4,32,128]{3,2,1,0:T(8,128)S(1)}, f32[6,4,32,128]{3,2,1,0:T(8,128)S(1)}, u32[]{:S(2)}, u32[]{:S(2)}) collective-permute-start(f32[6,4,32,128]{3,2,1,0:T(8,128)S(1)} %fusion.156), channel_id=1, source_target_pairs={{16,0},{32,16},{48,32},{64,48},{80,64},{96,80},{112,96},{0,112},{1... | collective-permute-start | bytes 1179656 | tf_op jit(solution)/shard_map/ppermute | solution.py:26
  58.9 8.4 %collective-permute-start.17 = (f32[6,4,32,128]{3,2,1,0:T(8,128)S(1)}, f32[6,4,32,128]{3,2,1,0:T(8,128)S(1)}, u32[]{:S(2)}, u32[]{:S(2)}) collective-permute-start(f32[6,4,32,128]{3,2,1,0:T(8,128)S(1)} %fusion.156), channel_id=1, source_target_pairs={{0,16},{16,32},{32,48},{48,64},{64,80},{80,96},{96,112},{112,0},{1... | collective-permute-start | bytes 1179656 | tf_op jit(solution)/shard_map/ppermute | solution.py:25
  64.2 7.0 %collective-permute-start.18 = (f32[6,4,32,128]{3,2,1,0:T(8,128)S(1)}, f32[6,4,32,128]{3,2,1,0:T(8,128)S(1)}, u32[]{:S(2)}, u32[]{:S(2)}) collective-permute-start(f32[6,4,32,128]{3,2,1,0:T(8,128)S(1)} %fusion.58), channel_id=1, source_target_pairs={{16,0},{32,16},{48,32},{64,48},{80,64},{96,80},{112,96},{0,112},{1... | collective-permute-start | bytes 1179656 | tf_op jit(solution)/shard_map/ppermute | solution.py:26
  65.9 8.4 %collective-permute-start.19 = (f32[6,4,32,128]{3,2,1,0:T(8,128)S(1)}, f32[6,4,32,128]{3,2,1,0:T(8,128)S(1)}, u32[]{:S(2)}, u32[]{:S(2)}) collective-permute-start(f32[6,4,32,128]{3,2,1,0:T(8,128)S(1)} %fusion.58), channel_id=1, source_target_pairs={{0,16},{16,32},{32,48},{48,64},{64,80},{80,96},{96,112},{112,0},{1... | collective-permute-start | bytes 1179656 | tf_op jit(solution)/shard_map/ppermute | solution.py:25
  77.5 28.1 %all-to-all-start = ((f32[2,12,16,8,128]{4,3,1,0,2:T(8,128)}), f32[2,12,16,8,128]{4,3,1,0,2:T(8,128)S(1)}, u32[]{:S(2)}, u32[]{:S(2)}) async-start(f32[2,12,16,8,128]{4,3,1,0,2:T(8,128)} %copy.18), calls=%async_computation | async-start | bytes 3145728 | tf_op jit(solution)/shard_map/all_to_all | solution.py:200
  113.6 5.8 %collective-permute-start.20 = (f32[200,192]{1,0:T(8,128)S(1)}, f32[200,192]{1,0:T(8,128)S(1)}, u32[]{:S(2)}, u32[]{:S(2)}) collective-permute-start(f32[200,192]{1,0:T(8,128)S(1)} %maximum_maximum_fusion), channel_id=1, source_target_pairs={{0,3},{1,0},{2,1},{3,2},{4,7},{5,4},{6,5},{7,6},{8,11},{9,8},{10,9... | collective-permute-start | bytes 460808 | tf_op jit(solution)/shard_map/ppermute | solution.py:64
  113.7 7.4 %collective-permute-start.21 = (f32[200,192]{1,0:T(8,128)S(1)}, f32[200,192]{1,0:T(8,128)S(1)}, u32[]{:S(2)}, u32[]{:S(2)}) collective-permute-start(f32[200,192]{1,0:T(8,128)S(1)} %maximum_maximum_fusion), channel_id=1, source_target_pairs={{0,2},{1,3},{2,0},{3,1},{4,6},{5,7},{6,4},{7,5},{8,10},{9,11},{10,... | collective-permute-start | bytes 460808 | tf_op jit(solution)/shard_map/ppermute | solution.py:64
  115.3 7.9 %collective-permute-start.22 = (f32[200,192]{1,0:T(8,128)S(1)}, f32[200,192]{1,0:T(8,128)S(1)}, u32[]{:S(2)}, u32[]{:S(2)}) collective-permute-start(f32[200,192]{1,0:T(8,128)S(1)} %maximum_maximum_fusion), channel_id=1, source_target_pairs={{0,1},{1,2},{2,3},{3,0},{4,5},{5,6},{6,7},{7,4},{8,9},{9,10},{10,1... | collective-permute-start | bytes 460808 | tf_op jit(solution)/shard_map/ppermute | solution.py:64
  123.4 5.8 %collective-permute-start.23 = (f32[200,192]{1,0:T(8,128)S(1)}, f32[200,192]{1,0:T(8,128)S(1)}, u32[]{:S(2)}, u32[]{:S(2)}) collective-permute-start(f32[200,192]{1,0:T(8,128)S(1)} %add_add_fusion.1), channel_id=1, source_target_pairs={{0,12},{1,13},{2,14},{3,15},{4,0},{5,1},{6,2},{7,3},{8,4},{9,5},{1... | collective-permute-start | bytes 460808 | tf_op jit(solution)/shard_map/ppermute | solution.py:64
  124.9 7.3 %collective-permute-start.24 = (f32[200,192]{1,0:T(8,128)S(1)}, f32[200,192]{1,0:T(8,128)S(1)}, u32[]{:S(2)}, u32[]{:S(2)}) collective-permute-start(f32[200,192]{1,0:T(8,128)S(1)} %add_add_fusion.1), channel_id=1, source_target_pairs={{0,8},{1,9},{2,10},{3,11},{4,12},{5,13},{6,14},{7,15},{8,0},{9,1},... | collective-permute-start | bytes 460808 | tf_op jit(solution)/shard_map/ppermute | solution.py:64
  126.5 7.8 %collective-permute-start.25 = (f32[200,192]{1,0:T(8,128)S(1)}, f32[200,192]{1,0:T(8,128)S(1)}, u32[]{:S(2)}, u32[]{:S(2)}) collective-permute-start(f32[200,192]{1,0:T(8,128)S(1)} %add_add_fusion.1), channel_id=1, source_target_pairs={{0,4},{1,5},{2,6},{3,7},{4,8},{5,9},{6,10},{7,11},{8,12},{9,13},{1... | collective-permute-start | bytes 460808 | tf_op jit(solution)/shard_map/ppermute | solution.py:64
  134.5 1.5 collective-permute-start.26
  136.0 15.6 %collective-permute-start.27 = (f32[200,192]{1,0:T(8,128)S(1)}, f32[200,192]{1,0:T(8,128)S(1)}, u32[]{:S(2)}, u32[]{:S(2)}) collective-permute-start(f32[200,192]{1,0:T(8,128)S(1)} %select_add_fusion), channel_id=1, source_target_pairs={{0,96},{16,112},{32,0},{48,16},{64,32},{80,48},{96,64},{112,80},{1... | collective-permute-start | bytes 460808 | tf_op jit(solution)/shard_map/ppermute | solution.py:64
  142.6 9.5 %collective-permute-start.28 = (f32[200,192]{1,0:T(8,128)S(1)}, f32[200,192]{1,0:T(8,128)S(1)}, u32[]{:S(2)}, u32[]{:S(2)}) collective-permute-start(f32[200,192]{1,0:T(8,128)S(1)} %select_add_fusion), channel_id=1, source_target_pairs={{0,64},{16,80},{32,96},{48,112},{64,0},{80,16},{96,32},{112,48},{1... | collective-permute-start | bytes 460808 | tf_op jit(solution)/shard_map/ppermute | solution.py:64
  145.8 9.8 %collective-permute-start.29 = (f32[200,192]{1,0:T(8,128)S(1)}, f32[200,192]{1,0:T(8,128)S(1)}, u32[]{:S(2)}, u32[]{:S(2)}) collective-permute-start(f32[200,192]{1,0:T(8,128)S(1)} %select_add_fusion), channel_id=1, source_target_pairs={{0,32},{16,48},{32,64},{48,80},{64,96},{80,112},{96,0},{112,16},{1... | collective-permute-start | bytes 460808 | tf_op jit(solution)/shard_map/ppermute | solution.py:64
  192.6 19.1 %all-to-all-start.1 = ((f32[12,16,8,128]{3,2,0,1:T(8,128)}), f32[12,16,8,128]{3,2,0,1:T(8,128)}, u32[]{:S(2)}, u32[]{:S(2)}) async-start(f32[12,16,8,128]{3,2,0,1:T(8,128)} %copy.24), calls=%async_computation.1 | async-start | bytes 1572864 | tf_op jit(solution)/shard_map/all_to_all | solution.py:225
  (3 other events, 8.3 us)

commit v13 on v12

--- a/solution.py
+++ b/solution.py
@@ -221,8 +221,10 @@
 
     correlation, gram = to_true(c_sum), to_true(g_sum)
     inverse = lower_inverse(correlation)
-    basis_cd = rotate(rows, to_perm(inverse), flat_cd).reshape(bdev, groups, rows, lanes)
-    basis = lax.all_to_all(basis_cd, "band", 1, 1, tiled=True).reshape(psi.shape)
+    mixed = inverse.reshape(nbands, groups, bdev).transpose(0, 2, 1).reshape(nbands, nbands)
+    basis_cd = rotate(rows, mixed, flat_cd).reshape(groups, bdev, rows, lanes)
+    basis = lax.all_to_all(basis_cd, "band", 0, 0, tiled=True)
+    basis = basis.transpose(1, 0, 2, 3).reshape(psi.shape)
     own_rows = lax.dynamic_slice_in_dim(inverse, own_start, bdev, 0)
     projected = hp_dot(hp_dot(own_rows, gram, ((1,), (0,))), inverse, ((1,), (1,)))
     return (basis, projected)

time: 217 us -> 213 us (0.982)
  local copies, waits for them, and re-layouts: 37.1 us -> 32.7 us
    reshape x3 -> x2, local copies, waits for them, and re-layouts: 5.09 us -> 0.8 us  [local(): inverse.reshape(nbands, groups, bdev).transpose(0, 2, 1)]
where the time goes in v13:
time: 213 us; the launch traced here: 209 us
  waiting for transfers between devices  72.7 us (34%)
  starting transfers between devices  48.6 us (23%)
  local copies, waits for them, and re-layouts  32.7 us (15%)
  Pallas kernels  31.9 us (15%)
  other arithmetic  20.3 us (10%)
    ppermute x10, waiting for transfers between devices, group_sum(): received.append(lax.ppermute(x, axis, pairs))  25.1 us
    pallas_call x1, Pallas kernels, lower_inverse(): pl.pallas_call(inverse_kernel, out_shape=jax.ShapeDtypeStruct((n, n), jnp...  23.6 us
    all_to_all x1, waiting for transfers between devices, local(): spread = lax.all_to_all(chunked, 'band', 2, 2, tiled=True)  19.8 us
    ppermute x10, starting transfers between devices, extended(): after = lax.ppermute(initial, axis, down)  19.5 us
    ppermute x10, starting transfers between devices, group_sum(): received.append(lax.ppermute(x, axis, pairs))  16.5 us
    ppermute x10, waiting for transfers between devices, extended(): before = lax.ppermute(last, axis, up)  14.5 us
    slice x72, local copies, waits for them, and re-layouts, hamiltonian(): near = near + jnp.roll(field, reach, 3) + jnp.roll(field, -reach, 3)  14.3 us
    sub x6, other arithmetic, local(): 2.0 / half * (apply(c) - center * c) - p  11.3 us
  transfers between devices with their start and end apart: 32, of which 22 were waited for; matrix products, arithmetic and copies ran while one was open for 18% of the time, Pallas kernels for 0%

profile of v13, /device:TPU:0, one launch (start us, length us, event | category | flops | bytes accessed | tf_op | source)
XLA Modules:
  0.0 209.3 jit_solution(15250147267545084956)
XLA Ops:
  1.9 2.3 %collective-permute-start = (f32[6,4,32,128]{3,2,1,0:T(8,128)S(1)}, f32[6,4,32,128]{3,2,1,0:T(8,128)S(1)}, u32[]{:S(2)}, u32[]{:S(2)}) collective-permute-start(f32[6,4,32,128]{3,2,1,0:T(8,128)S(1)} %get-tuple-element.76), channel_id=1, source_target_pairs={{16,0},{32,16},{48,32},{64,48},{80,64},{96,80},{112,96},{0,112},{1... | collective-permute-start | bytes 1179656 | tf_op jit(solution)/shard_map/ppermute | solution.py:26
  4.2 3.0 %collective-permute-start.8 = (f32[6,4,32,128]{3,2,1,0:T(8,128)S(1)}, f32[6,4,32,128]{3,2,1,0:T(8,128)S(1)}, u32[]{:S(2)}, u32[]{:S(2)}) collective-permute-start(f32[6,4,32,128]{3,2,1,0:T(8,128)S(1)} %get-tuple-element.77), channel_id=1, source_target_pairs={{16,0},{32,16},{48,32},{64,48},{80,64},{96,80},{112,96},{0,112},{1... | collective-permute-start | bytes 1179656 | tf_op jit(solution)/shard_map/ppermute | solution.py:26
  10.7 1.9 collective-permute-done.1
  12.6 1.9 broadcast_multiply_fusion.1
  17.7 1.9 broadcast_multiply_fusion
  21.4 3.0 %collective-permute-start.10 = (f32[6,4,32,128]{3,2,1,0:T(8,128)S(1)}, f32[6,4,32,128]{3,2,1,0:T(8,128)S(1)}, u32[]{:S(2)}, u32[]{:S(2)}) collective-permute-start(f32[6,4,32,128]{3,2,1,0:T(8,128)S(1)} %get-tuple-element.8), channel_id=1, source_target_pairs={{16,0},{32,16},{48,32},{64,48},{80,64},{96,80},{112,96},{0,112},{1... | collective-permute-start | bytes 1179656 | tf_op jit(solution)/shard_map/ppermute | solution.py:26
  26.0 1.8 fusion.206
  32.8 1.9 fusion.108
  39.5 1.8 fusion.181
  46.4 2.0 fusion.83
  53.3 1.9 fusion.156
  56.7 1.9 collective-permute-start.16
  60.3 1.8 fusion.58
  68.7 2.1 %collective-permute-done.18 = f32[6,4,32,128]{3,2,1,0:T(8,128)S(1)} collective-permute-done((f32[6,4,32,128]{3,2,1,0:T(8,128)S(1)}, f32[6,4,32,128]{3,2,1,0:T(8,128)S(1)}, u32[]{:S(2)}, u32[]{:S(2)}) %collective-permute-start.18) | collective-permute-done | bytes 393248 | tf_op jit(solution)/shard_map/ppermute | solution.py:26
  70.8 3.1 %collective-permute-done.19 = f32[6,4,32,128]{3,2,1,0:T(8,128)S(1)} collective-permute-done((f32[6,4,32,128]{3,2,1,0:T(8,128)S(1)}, f32[6,4,32,128]{3,2,1,0:T(8,128)S(1)}, u32[]{:S(2)}, u32[]{:S(2)}) %collective-permute-start.19) | collective-permute-done | bytes 393248 | tf_op jit(solution)/shard_map/ppermute | solution.py:25
  77.2 8.3 %all-to-all-start = ((f32[2,12,16,8,128]{4,3,1,0,2:T(8,128)}), f32[2,12,16,8,128]{4,3,1,0,2:T(8,128)S(1)}, u32[]{:S(2)}, u32[]{:S(2)}) async-start(f32[2,12,16,8,128]{4,3,1,0,2:T(8,128)} %copy.24), calls=%async_computation | async-start | bytes 3145728 | tf_op jit(solution)/shard_map/all_to_all | solution.py:200
  85.6 19.8 %all-to-all-done = f32[2,12,16,8,128]{4,3,1,0,2:T(8,128)S(1)} async-done(((f32[2,12,16,8,128]{4,3,1,0,2:T(8,128)}), f32[2,12,16,8,128]{4,3,1,0,2:T(8,128)S(1)}, u32[]{:S(2)}, u32[]{:S(2)}) %all-to-all-start) | async-done | bytes 1572896 | tf_op jit(solution)/shard_map/all_to_all | solution.py:200
  107.4 4.8 %shard_map.41 = (f32[192,192]{1,0:T(8,128)}, f32[192,192]{1,0:T(8,128)}) custom-call(f32[1536,128]{1,0:T(8,128)} %bitcast.27, f32[1536,128]{1,0:T(8,128)} %bitcast.32), custom_call_target="tpu_custom_call" | custom-call | tf_op jit(solution)/shard_map/pallas_call | solution.py:159
  115.4 3.7 %collective-permute-done.20 = f32[200,192]{1,0:T(8,128)S(1)} collective-permute-done((f32[200,192]{1,0:T(8,128)S(1)}, f32[200,192]{1,0:T(8,128)S(1)}, u32[]{:S(2)}, u32[]{:S(2)}) %collective-permute-start.20) | collective-permute-done | bytes 153632 | tf_op jit(solution)/shard_map/ppermute | solution.py:64
  120.8 2.1 %collective-permute-done.22 = f32[200,192]{1,0:T(8,128)S(1)} collective-permute-done((f32[200,192]{1,0:T(8,128)S(1)}, f32[200,192]{1,0:T(8,128)S(1)}, u32[]{:S(2)}, u32[]{:S(2)}) %collective-permute-start.22) | collective-permute-done | bytes 153632 | tf_op jit(solution)/shard_map/ppermute | solution.py:64
  126.3 2.7 %collective-permute-done.23 = f32[200,192]{1,0:T(8,128)S(1)} collective-permute-done((f32[200,192]{1,0:T(8,128)S(1)}, f32[200,192]{1,0:T(8,128)S(1)}, u32[]{:S(2)}, u32[]{:S(2)}) %collective-permute-start.23) | collective-permute-done | bytes 153632 | tf_op jit(solution)/shard_map/ppermute | solution.py:64
  128.9 3.0 %collective-permute-done.24 = f32[200,192]{1,0:T(8,128)S(1)} collective-permute-done((f32[200,192]{1,0:T(8,128)S(1)}, f32[200,192]{1,0:T(8,128)S(1)}, u32[]{:S(2)}, u32[]{:S(2)}) %collective-permute-start.24) | collective-permute-done | bytes 153632 | tf_op jit(solution)/shard_map/ppermute | solution.py:64
  132.0 2.1 %collective-permute-done.25 = f32[200,192]{1,0:T(8,128)S(1)} collective-permute-done((f32[200,192]{1,0:T(8,128)S(1)}, f32[200,192]{1,0:T(8,128)S(1)}, u32[]{:S(2)}, u32[]{:S(2)}) %collective-permute-start.25) | collective-permute-done | bytes 153632 | tf_op jit(solution)/shard_map/ppermute | solution.py:64
  135.7 6.6 %collective-permute-start.27 = (f32[200,192]{1,0:T(8,128)S(1)}, f32[200,192]{1,0:T(8,128)S(1)}, u32[]{:S(2)}, u32[]{:S(2)}) collective-permute-start(f32[200,192]{1,0:T(8,128)S(1)} %select_add_fusion), channel_id=1, source_target_pairs={{0,96},{16,112},{32,0},{48,16},{64,32},{80,48},{96,64},{112,80},{1... | collective-permute-start | bytes 460808 | tf_op jit(solution)/shard_map/ppermute | solution.py:64
  142.3 3.2 %collective-permute-start.28 = (f32[200,192]{1,0:T(8,128)S(1)}, f32[200,192]{1,0:T(8,128)S(1)}, u32[]{:S(2)}, u32[]{:S(2)}) collective-permute-start(f32[200,192]{1,0:T(8,128)S(1)} %select_add_fusion), channel_id=1, source_target_pairs={{0,64},{16,80},{32,96},{48,112},{64,0},{80,16},{96,32},{112,48},{1... | collective-permute-start | bytes 460808 | tf_op jit(solution)/shard_map/ppermute | solution.py:64
  146.8 4.5 %collective-permute-done.27 = f32[200,192]{1,0:T(8,128)S(1)} collective-permute-done((f32[200,192]{1,0:T(8,128)S(1)}, f32[200,192]{1,0:T(8,128)S(1)}, u32[]{:S(2)}, u32[]{:S(2)}) %collective-permute-start.27) | collective-permute-done | bytes 153632 | tf_op jit(solution)/shard_map/ppermute | solution.py:64
  151.7 3.5 %collective-permute-done.29 = f32[200,192]{1,0:T(8,128)S(1)} collective-permute-done((f32[200,192]{1,0:T(8,128)S(1)}, f32[200,192]{1,0:T(8,128)S(1)}, u32[]{:S(2)}, u32[]{:S(2)}) %collective-permute-start.29) | collective-permute-done | bytes 153632 | tf_op jit(solution)/shard_map/ppermute | solution.py:64
  158.7 23.6 %shard_map.42 = f32[192,192]{1,0:T(8,128)} custom-call(f32[192,192]{1,0:T(8,128)} %reshape.35.c_ref), custom_call_target="tpu_custom_call" | custom-call | tf_op jit(solution)/shard_map/pallas_call | solution.py:143
  184.2 3.5 %shard_map.43 = f32[1536,128]{1,0:T(8,128)} custom-call(f32[192,192]{1,0:T(8,128)} %copy.31.refs_0_, f32[1536,128]{1,0:T(8,128)} %bitcast.28), custom_call_target="tpu_custom_call" | custom-call | tf_op jit(solution)/shard_map/pallas_call | solution.py:168
  187.7 4.3 %all-to-all-start.1 = ((f32[16,12,8,128]{3,2,1,0:T(8,128)}), f32[16,12,8,128]{3,2,1,0:T(8,128)}, u32[]{:S(2)}, u32[]{:S(2)}) async-start(f32[16,12,8,128]{3,2,1,0:T(8,128)} %bitcast.31), calls=%async_computation.1 | async-start | bytes 1572864 | tf_op jit(solution)/shard_map/all_to_all | solution.py:226
  195.7 11.1 %all-to-all-done.1 = f32[16,12,8,128]{3,2,1,0:T(8,128)} async-done(((f32[16,12,8,128]{3,2,1,0:T(8,128)}), f32[16,12,8,128]{3,2,1,0:T(8,128)}, u32[]{:S(2)}, u32[]{:S(2)}) %all-to-all-start.1) | async-done | bytes 786464 | tf_op jit(solution)/shard_map/all_to_all | solution.py:226
  206.8 2.1 copy.32
  (229 shorter events, 66.1 us)
Async XLA Ops:
  1.9 8.8 %collective-permute-start = (f32[6,4,32,128]{3,2,1,0:T(8,128)S(1)}, f32[6,4,32,128]{3,2,1,0:T(8,128)S(1)}, u32[]{:S(2)}, u32[]{:S(2)}) collective-permute-start(f32[6,4,32,128]{3,2,1,0:T(8,128)S(1)} %get-tuple-element.76), channel_id=1, source_target_pairs={{16,0},{32,16},{48,32},{64,48},{80,64},{96,80},{112,96},{0,112},{1... | collective-permute-start | bytes 1179656 | tf_op jit(solution)/shard_map/ppermute | solution.py:26
  4.2 8.4 %collective-permute-start.1 = (f32[6,4,32,128]{3,2,1,0:T(8,128)S(1)}, f32[6,4,32,128]{3,2,1,0:T(8,128)S(1)}, u32[]{:S(2)}, u32[]{:S(2)}) collective-permute-start(f32[6,4,32,128]{3,2,1,0:T(8,128)S(1)} %get-tuple-element.76), channel_id=1, source_target_pairs={{0,16},{16,32},{32,48},{48,64},{64,80},{80,96},{96,112},{112,0},{1... | collective-permute-start | bytes 1179656 | tf_op jit(solution)/shard_map/ppermute | solution.py:25
  4.2 13.4 %collective-permute-start.8 = (f32[6,4,32,128]{3,2,1,0:T(8,128)S(1)}, f32[6,4,32,128]{3,2,1,0:T(8,128)S(1)}, u32[]{:S(2)}, u32[]{:S(2)}) collective-permute-start(f32[6,4,32,128]{3,2,1,0:T(8,128)S(1)} %get-tuple-element.77), channel_id=1, source_target_pairs={{16,0},{32,16},{48,32},{64,48},{80,64},{96,80},{112,96},{0,112},{1... | collective-permute-start | bytes 1179656 | tf_op jit(solution)/shard_map/ppermute | solution.py:26
  7.2 10.5 %collective-permute-start.9 = (f32[6,4,32,128]{3,2,1,0:T(8,128)S(1)}, f32[6,4,32,128]{3,2,1,0:T(8,128)S(1)}, u32[]{:S(2)}, u32[]{:S(2)}) collective-permute-start(f32[6,4,32,128]{3,2,1,0:T(8,128)S(1)} %get-tuple-element.77), channel_id=1, source_target_pairs={{0,16},{16,32},{32,48},{48,64},{64,80},{80,96},{96,112},{112,0},{1... | collective-permute-start | bytes 1179656 | tf_op jit(solution)/shard_map/ppermute | solution.py:25
  16.4 8.0 %collective-permute-start.2 = (f32[6,4,32,128]{3,2,1,0:T(8,128)S(1)}, f32[6,4,32,128]{3,2,1,0:T(8,128)S(1)}, u32[]{:S(2)}, u32[]{:S(2)}) collective-permute-start(f32[6,4,32,128]{3,2,1,0:T(8,128)S(1)} %get-tuple-element.6), channel_id=1, source_target_pairs={{16,0},{32,16},{48,32},{64,48},{80,64},{96,80},{112,96},{0,112},{1... | collective-permute-start | bytes 1179656 | tf_op jit(solution)/shard_map/ppermute | solution.py:26
  17.6 8.4 %collective-permute-start.3 = (f32[6,4,32,128]{3,2,1,0:T(8,128)S(1)}, f32[6,4,32,128]{3,2,1,0:T(8,128)S(1)}, u32[]{:S(2)}, u32[]{:S(2)}) collective-permute-start(f32[6,4,32,128]{3,2,1,0:T(8,128)S(1)} %get-tuple-element.6), channel_id=1, source_target_pairs={{0,16},{16,32},{32,48},{48,64},{64,80},{80,96},{96,112},{112,0},{1... | collective-permute-start | bytes 1179656 | tf_op jit(solution)/shard_map/ppermute | solution.py:25
  21.4 9.9 %collective-permute-start.10 = (f32[6,4,32,128]{3,2,1,0:T(8,128)S(1)}, f32[6,4,32,128]{3,2,1,0:T(8,128)S(1)}, u32[]{:S(2)}, u32[]{:S(2)}) collective-permute-start(f32[6,4,32,128]{3,2,1,0:T(8,128)S(1)} %get-tuple-element.8), channel_id=1, source_target_pairs={{16,0},{32,16},{48,32},{64,48},{80,64},{96,80},{112,96},{0,112},{1... | collective-permute-start | bytes 1179656 | tf_op jit(solution)/shard_map/ppermute | solution.py:26
  24.4 8.4 %collective-permute-start.11 = (f32[6,4,32,128]{3,2,1,0:T(8,128)S(1)}, f32[6,4,32,128]{3,2,1,0:T(8,128)S(1)}, u32[]{:S(2)}, u32[]{:S(2)}) collective-permute-start(f32[6,4,32,128]{3,2,1,0:T(8,128)S(1)} %get-tuple-element.8), channel_id=1, source_target_pairs={{0,16},{16,32},{32,48},{48,64},{64,80},{80,96},{96,112},{112,0},{1... | collective-permute-start | bytes 1179656 | tf_op jit(solution)/shard_map/ppermute | solution.py:25
  29.6 8.6 %collective-permute-start.4 = (f32[6,4,32,128]{3,2,1,0:T(8,128)S(1)}, f32[6,4,32,128]{3,2,1,0:T(8,128)S(1)}, u32[]{:S(2)}, u32[]{:S(2)}) collective-permute-start(f32[6,4,32,128]{3,2,1,0:T(8,128)S(1)} %fusion.206), channel_id=1, source_target_pairs={{16,0},{32,16},{48,32},{64,48},{80,64},{96,80},{112,96},{0,112},{1... | collective-permute-start | bytes 1179656 | tf_op jit(solution)/shard_map/ppermute | solution.py:26
  31.1 8.4 %collective-permute-start.5 = (f32[6,4,32,128]{3,2,1,0:T(8,128)S(1)}, f32[6,4,32,128]{3,2,1,0:T(8,128)S(1)}, u32[]{:S(2)}, u32[]{:S(2)}) collective-permute-start(f32[6,4,32,128]{3,2,1,0:T(8,128)S(1)} %fusion.206), channel_id=1, source_target_pairs={{0,16},{16,32},{32,48},{48,64},{64,80},{80,96},{96,112},{112,0},{1... | collective-permute-start | bytes 1179656 | tf_op jit(solution)/shard_map/ppermute | solution.py:25
  36.4 8.7 %collective-permute-start.12 = (f32[6,4,32,128]{3,2,1,0:T(8,128)S(1)}, f32[6,4,32,128]{3,2,1,0:T(8,128)S(1)}, u32[]{:S(2)}, u32[]{:S(2)}) collective-permute-start(f32[6,4,32,128]{3,2,1,0:T(8,128)S(1)} %fusion.108), channel_id=1, source_target_pairs={{16,0},{32,16},{48,32},{64,48},{80,64},{96,80},{112,96},{0,112},{1... | collective-permute-start | bytes 1179656 | tf_op jit(solution)/shard_map/ppermute | solution.py:26
  38.0 8.4 %collective-permute-start.13 = (f32[6,4,32,128]{3,2,1,0:T(8,128)S(1)}, f32[6,4,32,128]{3,2,1,0:T(8,128)S(1)}, u32[]{:S(2)}, u32[]{:S(2)}) collective-permute-start(f32[6,4,32,128]{3,2,1,0:T(8,128)S(1)} %fusion.108), channel_id=1, source_target_pairs={{0,16},{16,32},{32,48},{48,64},{64,80},{80,96},{96,112},{112,0},{1... | collective-permute-start | bytes 1179656 | tf_op jit(solution)/shard_map/ppermute | solution.py:25
  43.1 8.9 %collective-permute-start.6 = (f32[6,4,32,128]{3,2,1,0:T(8,128)S(1)}, f32[6,4,32,128]{3,2,1,0:T(8,128)S(1)}, u32[]{:S(2)}, u32[]{:S(2)}) collective-permute-start(f32[6,4,32,128]{3,2,1,0:T(8,128)S(1)} %fusion.181), channel_id=1, source_target_pairs={{16,0},{32,16},{48,32},{64,48},{80,64},{96,80},{112,96},{0,112},{1... | collective-permute-start | bytes 1179656 | tf_op jit(solution)/shard_map/ppermute | solution.py:26
  44.8 8.4 %collective-permute-start.7 = (f32[6,4,32,128]{3,2,1,0:T(8,128)S(1)}, f32[6,4,32,128]{3,2,1,0:T(8,128)S(1)}, u32[]{:S(2)}, u32[]{:S(2)}) collective-permute-start(f32[6,4,32,128]{3,2,1,0:T(8,128)S(1)} %fusion.181), channel_id=1, source_target_pairs={{0,16},{16,32},{32,48},{48,64},{64,80},{80,96},{96,112},{112,0},{1... | collective-permute-start | bytes 1179656 | tf_op jit(solution)/shard_map/ppermute | solution.py:25
  50.2 8.7 %collective-permute-start.14 = (f32[6,4,32,128]{3,2,1,0:T(8,128)S(1)}, f32[6,4,32,128]{3,2,1,0:T(8,128)S(1)}, u32[]{:S(2)}, u32[]{:S(2)}) collective-permute-start(f32[6,4,32,128]{3,2,1,0:T(8,128)S(1)} %fusion.83), channel_id=1, source_target_pairs={{16,0},{32,16},{48,32},{64,48},{80,64},{96,80},{112,96},{0,112},{1... | collective-permute-start | bytes 1179656 | tf_op jit(solution)/shard_map/ppermute | solution.py:26
  51.9 8.4 %collective-permute-start.15 = (f32[6,4,32,128]{3,2,1,0:T(8,128)S(1)}, f32[6,4,32,128]{3,2,1,0:T(8,128)S(1)}, u32[]{:S(2)}, u32[]{:S(2)}) collective-permute-start(f32[6,4,32,128]{3,2,1,0:T(8,128)S(1)} %fusion.83), channel_id=1, source_target_pairs={{0,16},{16,32},{32,48},{48,64},{64,80},{80,96},{96,112},{112,0},{1... | collective-permute-start | bytes 1179656 | tf_op jit(solution)/shard_map/ppermute | solution.py:25
  56.7 9.1 %collective-permute-start.16 = (f32[6,4,32,128]{3,2,1,0:T(8,128)S(1)}, f32[6,4,32,128]{3,2,1,0:T(8,128)S(1)}, u32[]{:S(2)}, u32[]{:S(2)}) collective-permute-start(f32[6,4,32,128]{3,2,1,0:T(8,128)S(1)} %fusion.156), channel_id=1, source_target_pairs={{16,0},{32,16},{48,32},{64,48},{80,64},{96,80},{112,96},{0,112},{1... | collective-permute-start | bytes 1179656 | tf_op jit(solution)/shard_map/ppermute | solution.py:26
  58.6 8.4 %collective-permute-start.17 = (f32[6,4,32,128]{3,2,1,0:T(8,128)S(1)}, f32[6,4,32,128]{3,2,1,0:T(8,128)S(1)}, u32[]{:S(2)}, u32[]{:S(2)}) collective-permute-start(f32[6,4,32,128]{3,2,1,0:T(8,128)S(1)} %fusion.156), channel_id=1, source_target_pairs={{0,16},{16,32},{32,48},{48,64},{64,80},{80,96},{96,112},{112,0},{1... | collective-permute-start | bytes 1179656 | tf_op jit(solution)/shard_map/ppermute | solution.py:25
  63.9 7.0 %collective-permute-start.18 = (f32[6,4,32,128]{3,2,1,0:T(8,128)S(1)}, f32[6,4,32,128]{3,2,1,0:T(8,128)S(1)}, u32[]{:S(2)}, u32[]{:S(2)}) collective-permute-start(f32[6,4,32,128]{3,2,1,0:T(8,128)S(1)} %fusion.58), channel_id=1, source_target_pairs={{16,0},{32,16},{48,32},{64,48},{80,64},{96,80},{112,96},{0,112},{1... | collective-permute-start | bytes 1179656 | tf_op jit(solution)/shard_map/ppermute | solution.py:26
  65.6 8.4 %collective-permute-start.19 = (f32[6,4,32,128]{3,2,1,0:T(8,128)S(1)}, f32[6,4,32,128]{3,2,1,0:T(8,128)S(1)}, u32[]{:S(2)}, u32[]{:S(2)}) collective-permute-start(f32[6,4,32,128]{3,2,1,0:T(8,128)S(1)} %fusion.58), channel_id=1, source_target_pairs={{0,16},{16,32},{32,48},{48,64},{64,80},{80,96},{96,112},{112,0},{1... | collective-permute-start | bytes 1179656 | tf_op jit(solution)/shard_map/ppermute | solution.py:25
  77.2 28.2 %all-to-all-start = ((f32[2,12,16,8,128]{4,3,1,0,2:T(8,128)}), f32[2,12,16,8,128]{4,3,1,0,2:T(8,128)S(1)}, u32[]{:S(2)}, u32[]{:S(2)}) async-start(f32[2,12,16,8,128]{4,3,1,0,2:T(8,128)} %copy.24), calls=%async_computation | async-start | bytes 3145728 | tf_op jit(solution)/shard_map/all_to_all | solution.py:200
  113.3 5.8 %collective-permute-start.20 = (f32[200,192]{1,0:T(8,128)S(1)}, f32[200,192]{1,0:T(8,128)S(1)}, u32[]{:S(2)}, u32[]{:S(2)}) collective-permute-start(f32[200,192]{1,0:T(8,128)S(1)} %maximum_maximum_fusion), channel_id=1, source_target_pairs={{0,3},{1,0},{2,1},{3,2},{4,7},{5,4},{6,5},{7,6},{8,11},{9,8},{10,9... | collective-permute-start | bytes 460808 | tf_op jit(solution)/shard_map/ppermute | solution.py:64
  113.4 7.4 %collective-permute-start.21 = (f32[200,192]{1,0:T(8,128)S(1)}, f32[200,192]{1,0:T(8,128)S(1)}, u32[]{:S(2)}, u32[]{:S(2)}) collective-permute-start(f32[200,192]{1,0:T(8,128)S(1)} %maximum_maximum_fusion), channel_id=1, source_target_pairs={{0,2},{1,3},{2,0},{3,1},{4,6},{5,7},{6,4},{7,5},{8,10},{9,11},{10,... | collective-permute-start | bytes 460808 | tf_op jit(solution)/shard_map/ppermute | solution.py:64
  115.0 7.9 %collective-permute-start.22 = (f32[200,192]{1,0:T(8,128)S(1)}, f32[200,192]{1,0:T(8,128)S(1)}, u32[]{:S(2)}, u32[]{:S(2)}) collective-permute-start(f32[200,192]{1,0:T(8,128)S(1)} %maximum_maximum_fusion), channel_id=1, source_target_pairs={{0,1},{1,2},{2,3},{3,0},{4,5},{5,6},{6,7},{7,4},{8,9},{9,10},{10,1... | collective-permute-start | bytes 460808 | tf_op jit(solution)/shard_map/ppermute | solution.py:64
  123.1 5.8 %collective-permute-start.23 = (f32[200,192]{1,0:T(8,128)S(1)}, f32[200,192]{1,0:T(8,128)S(1)}, u32[]{:S(2)}, u32[]{:S(2)}) collective-permute-start(f32[200,192]{1,0:T(8,128)S(1)} %add_add_fusion.1), channel_id=1, source_target_pairs={{0,12},{1,13},{2,14},{3,15},{4,0},{5,1},{6,2},{7,3},{8,4},{9,5},{1... | collective-permute-start | bytes 460808 | tf_op jit(solution)/shard_map/ppermute | solution.py:64
  124.6 7.3 %collective-permute-start.24 = (f32[200,192]{1,0:T(8,128)S(1)}, f32[200,192]{1,0:T(8,128)S(1)}, u32[]{:S(2)}, u32[]{:S(2)}) collective-permute-start(f32[200,192]{1,0:T(8,128)S(1)} %add_add_fusion.1), channel_id=1, source_target_pairs={{0,8},{1,9},{2,10},{3,11},{4,12},{5,13},{6,14},{7,15},{8,0},{9,1},... | collective-permute-start | bytes 460808 | tf_op jit(solution)/shard_map/ppermute | solution.py:64
  126.3 7.8 %collective-permute-start.25 = (f32[200,192]{1,0:T(8,128)S(1)}, f32[200,192]{1,0:T(8,128)S(1)}, u32[]{:S(2)}, u32[]{:S(2)}) collective-permute-start(f32[200,192]{1,0:T(8,128)S(1)} %add_add_fusion.1), channel_id=1, source_target_pairs={{0,4},{1,5},{2,6},{3,7},{4,8},{5,9},{6,10},{7,11},{8,12},{9,13},{1... | collective-permute-start | bytes 460808 | tf_op jit(solution)/shard_map/ppermute | solution.py:64
  134.2 1.5 collective-permute-start.26
  135.7 15.6 %collective-permute-start.27 = (f32[200,192]{1,0:T(8,128)S(1)}, f32[200,192]{1,0:T(8,128)S(1)}, u32[]{:S(2)}, u32[]{:S(2)}) collective-permute-start(f32[200,192]{1,0:T(8,128)S(1)} %select_add_fusion), channel_id=1, source_target_pairs={{0,96},{16,112},{32,0},{48,16},{64,32},{80,48},{96,64},{112,80},{1... | collective-permute-start | bytes 460808 | tf_op jit(solution)/shard_map/ppermute | solution.py:64
  142.3 9.5 %collective-permute-start.28 = (f32[200,192]{1,0:T(8,128)S(1)}, f32[200,192]{1,0:T(8,128)S(1)}, u32[]{:S(2)}, u32[]{:S(2)}) collective-permute-start(f32[200,192]{1,0:T(8,128)S(1)} %select_add_fusion), channel_id=1, source_target_pairs={{0,64},{16,80},{32,96},{48,112},{64,0},{80,16},{96,32},{112,48},{1... | collective-permute-start | bytes 460808 | tf_op jit(solution)/shard_map/ppermute | solution.py:64
  145.5 9.8 %collective-permute-start.29 = (f32[200,192]{1,0:T(8,128)S(1)}, f32[200,192]{1,0:T(8,128)S(1)}, u32[]{:S(2)}, u32[]{:S(2)}) collective-permute-start(f32[200,192]{1,0:T(8,128)S(1)} %select_add_fusion), channel_id=1, source_target_pairs={{0,32},{16,48},{32,64},{48,80},{64,96},{80,112},{96,0},{112,16},{1... | collective-permute-start | bytes 460808 | tf_op jit(solution)/shard_map/ppermute | solution.py:64
  187.7 19.1 %all-to-all-start.1 = ((f32[16,12,8,128]{3,2,1,0:T(8,128)}), f32[16,12,8,128]{3,2,1,0:T(8,128)}, u32[]{:S(2)}, u32[]{:S(2)}) async-start(f32[16,12,8,128]{3,2,1,0:T(8,128)} %bitcast.31), calls=%async_computation.1 | async-start | bytes 1572864 | tf_op jit(solution)/shard_map/all_to_all | solution.py:226
  (3 other events, 8.3 us)

commit v14 on v13

--- a/solution.py
+++ b/solution.py
@@ -196,10 +196,10 @@
     groups = lax.axis_size("band")
     rows = depth * rows_y * rows_x // groups // rows_x
     lanes = rows_x
-    chunked = jnp.stack([current, image]).reshape(2, bdev, groups, rows, lanes)
-    spread = lax.all_to_all(chunked, "band", 2, 2, tiled=True)
-    flat_cd = spread[0].reshape(bdev * groups * rows, lanes)
-    image_cd = spread[1].reshape(bdev * groups * rows, lanes)
+    chunked = jnp.stack([current, image]).reshape(2, bdev, groups, rows, lanes).transpose(2, 0, 1, 3, 4)
+    spread = lax.all_to_all(chunked, "band", 0, 0, tiled=True)
+    flat_cd = spread[:, 0].reshape(bdev * groups * rows, lanes)
+    image_cd = spread[:, 1].reshape(bdev * groups * rows, lanes)
     c_perm, g_perm = grams(rows, flat_cd, image_cd)
     below = lax.broadcasted_iota(jnp.int32, (nbands, nbands), 0) >= lax.broadcasted_iota(
         jnp.int32, (nbands, nbands), 1
@@ -219,9 +219,9 @@
     def to_perm(m):
         return m.reshape(groups, bdev, groups, bdev).transpose(1, 0, 3, 2).reshape(nbands, nbands)
 
-    correlation, gram = to_true(c_sum), to_true(g_sum)
+    correlation, gram = c_sum, g_sum
     inverse = lower_inverse(correlation)
-    mixed = inverse.reshape(nbands, groups, bdev).transpose(0, 2, 1).reshape(nbands, nbands)
+    mixed = inverse
     basis_cd = rotate(rows, mixed, flat_cd).reshape(groups, bdev, rows, lanes)
     basis = lax.all_to_all(basis_cd, "band", 0, 0, tiled=True)
     basis = basis.transpose(1, 0, 2, 3).reshape(psi.shape)

time: 213 us -> 203 us (0.953); the launches traced: 209 us -> 202 us
  local copies, waits for them, and re-layouts: 32.7 us -> 23.3 us
    reshape x6 -> x0, local copies, waits for them, and re-layouts: 3.86 us -> none  [the longest x4 3.06 us: to_true(): m.reshape(bdev, groups, bdev, groups).transpose(1, 0, 3, 2)]
    all_to_all x1, waiting for transfers between devices: 11.1 us -> 13.5 us  [local(): basis = lax.all_to_all(basis_cd, 'band', 0, 0, tiled=True)]
where the time goes in v14:
time: 203 us; the launch traced here: 202 us
  waiting for transfers between devices  74.7 us (37%)
  starting transfers between devices  48.9 us (24%)
  Pallas kernels  31.8 us (16%)
  local copies, waits for them, and re-layouts  23.3 us (11%)
  other arithmetic  20.8 us (10%)
    ppermute x10, waiting for transfers between devices, group_sum(): received.append(lax.ppermute(x, axis, pairs))  25.1 us
    pallas_call x1, Pallas kernels, lower_inverse(): pl.pallas_call(inverse_kernel, out_shape=jax.ShapeDtypeStruct((n, n), jnp...  23.5 us
    ppermute x10, starting transfers between devices, extended(): after = lax.ppermute(initial, axis, down)  20.2 us
    all_to_all x1, waiting for transfers between devices, local(): spread = lax.all_to_all(chunked, 'band', 0, 0, tiled=True)  19.8 us
    ppermute x10, starting transfers between devices, group_sum(): received.append(lax.ppermute(x, axis, pairs))  16.8 us
    slice x72, local copies, waits for them, and re-layouts, hamiltonian(): near = near + jnp.roll(field, reach, 3) + jnp.roll(field, -reach, 3)  14.4 us
    ppermute x10, waiting for transfers between devices, extended(): before = lax.ppermute(last, axis, up)  14.3 us
    all_to_all x1, waiting for transfers between devices, local(): basis = lax.all_to_all(basis_cd, 'band', 0, 0, tiled=True)  13.5 us
  transfers between devices with their start and end apart: 32, of which 22 were waited for; matrix products, arithmetic and copies ran while one was open for 18% of the time, Pallas kernels for 0%

profile of v14, /device:TPU:0, one launch (start us, length us, event | category | flops | bytes accessed | tf_op | source)
XLA Modules:
  0.0 202.3 jit_solution(6220958992760671860)
XLA Ops:
  1.9 2.3 %collective-permute-start = (f32[6,4,32,128]{3,2,1,0:T(8,128)S(1)}, f32[6,4,32,128]{3,2,1,0:T(8,128)S(1)}, u32[]{:S(2)}, u32[]{:S(2)}) collective-permute-start(f32[6,4,32,128]{3,2,1,0:T(8,128)S(1)} %get-tuple-element.76), channel_id=1, source_target_pairs={{16,0},{32,16},{48,32},{64,48},{80,64},{96,80},{112,96},{0,112},{1... | collective-permute-start | bytes 1179656 | tf_op jit(solution)/shard_map/ppermute | solution.py:26
  4.2 3.0 %collective-permute-start.8 = (f32[6,4,32,128]{3,2,1,0:T(8,128)S(1)}, f32[6,4,32,128]{3,2,1,0:T(8,128)S(1)}, u32[]{:S(2)}, u32[]{:S(2)}) collective-permute-start(f32[6,4,32,128]{3,2,1,0:T(8,128)S(1)} %get-tuple-element.77), channel_id=1, source_target_pairs={{16,0},{32,16},{48,32},{64,48},{80,64},{96,80},{112,96},{0,112},{1... | collective-permute-start | bytes 1179656 | tf_op jit(solution)/shard_map/ppermute | solution.py:26
  10.8 1.8 collective-permute-done.1
  12.6 1.8 broadcast_multiply_fusion.1
  17.8 1.9 broadcast_multiply_fusion
  21.6 3.0 %collective-permute-start.10 = (f32[6,4,32,128]{3,2,1,0:T(8,128)S(1)}, f32[6,4,32,128]{3,2,1,0:T(8,128)S(1)}, u32[]{:S(2)}, u32[]{:S(2)}) collective-permute-start(f32[6,4,32,128]{3,2,1,0:T(8,128)S(1)} %get-tuple-element.8), channel_id=1, source_target_pairs={{16,0},{32,16},{48,32},{64,48},{80,64},{96,80},{112,96},{0,112},{1... | collective-permute-start | bytes 1179656 | tf_op jit(solution)/shard_map/ppermute | solution.py:26
  26.1 1.9 fusion.206
  33.0 1.9 fusion.108
  39.8 1.9 fusion.181
  46.7 1.9 fusion.83
  50.3 2.0 collective-permute-start.14
  53.6 1.8 fusion.156
  57.1 1.9 collective-permute-start.16
  60.7 1.8 fusion.58
  69.2 2.0 collective-permute-done.18
  71.2 3.1 %collective-permute-done.19 = f32[6,4,32,128]{3,2,1,0:T(8,128)S(1)} collective-permute-done((f32[6,4,32,128]{3,2,1,0:T(8,128)S(1)}, f32[6,4,32,128]{3,2,1,0:T(8,128)S(1)}, u32[]{:S(2)}, u32[]{:S(2)}) %collective-permute-start.19) | collective-permute-done | bytes 393248 | tf_op jit(solution)/shard_map/ppermute | solution.py:25
  77.5 8.1 %all-to-all-start = ((f32[16,2,12,8,128]{4,3,2,1,0:T(8,128)}), f32[16,2,12,8,128]{4,3,2,1,0:T(8,128)S(1)}, u32[]{:S(2)}, u32[]{:S(2)}) async-start(f32[16,2,12,8,128]{4,3,2,1,0:T(8,128)} %copy.10), calls=%async_computation | async-start | bytes 3145728 | tf_op jit(solution)/shard_map/all_to_all | solution.py:200
  85.6 19.8 %all-to-all-done = f32[16,2,12,8,128]{4,3,2,1,0:T(8,128)S(1)} async-done(((f32[16,2,12,8,128]{4,3,2,1,0:T(8,128)}), f32[16,2,12,8,128]{4,3,2,1,0:T(8,128)S(1)}, u32[]{:S(2)}, u32[]{:S(2)}) %all-to-all-start) | async-done | bytes 1572896 | tf_op jit(solution)/shard_map/all_to_all | solution.py:200
  106.7 4.8 %shard_map.41 = (f32[192,192]{1,0:T(8,128)}, f32[192,192]{1,0:T(8,128)}) custom-call(f32[1536,128]{1,0:T(8,128)} %bitcast.19, f32[1536,128]{1,0:T(8,128)} %bitcast.24), custom_call_target="tpu_custom_call" | custom-call | tf_op jit(solution)/shard_map/pallas_call | solution.py:159
  114.7 3.7 %collective-permute-done.20 = f32[200,192]{1,0:T(8,128)S(1)} collective-permute-done((f32[200,192]{1,0:T(8,128)S(1)}, f32[200,192]{1,0:T(8,128)S(1)}, u32[]{:S(2)}, u32[]{:S(2)}) %collective-permute-start.20) | collective-permute-done | bytes 153632 | tf_op jit(solution)/shard_map/ppermute | solution.py:64
  120.1 2.1 %collective-permute-done.22 = f32[200,192]{1,0:T(8,128)S(1)} collective-permute-done((f32[200,192]{1,0:T(8,128)S(1)}, f32[200,192]{1,0:T(8,128)S(1)}, u32[]{:S(2)}, u32[]{:S(2)}) %collective-permute-start.22) | collective-permute-done | bytes 153632 | tf_op jit(solution)/shard_map/ppermute | solution.py:64
  125.6 2.6 %collective-permute-done.23 = f32[200,192]{1,0:T(8,128)S(1)} collective-permute-done((f32[200,192]{1,0:T(8,128)S(1)}, f32[200,192]{1,0:T(8,128)S(1)}, u32[]{:S(2)}, u32[]{:S(2)}) %collective-permute-start.23) | collective-permute-done | bytes 153632 | tf_op jit(solution)/shard_map/ppermute | solution.py:64
  128.2 3.0 %collective-permute-done.24 = f32[200,192]{1,0:T(8,128)S(1)} collective-permute-done((f32[200,192]{1,0:T(8,128)S(1)}, f32[200,192]{1,0:T(8,128)S(1)}, u32[]{:S(2)}, u32[]{:S(2)}) %collective-permute-start.24) | collective-permute-done | bytes 153632 | tf_op jit(solution)/shard_map/ppermute | solution.py:64
  131.2 2.1 %collective-permute-done.25 = f32[200,192]{1,0:T(8,128)S(1)} collective-permute-done((f32[200,192]{1,0:T(8,128)S(1)}, f32[200,192]{1,0:T(8,128)S(1)}, u32[]{:S(2)}, u32[]{:S(2)}) %collective-permute-start.25) | collective-permute-done | bytes 153632 | tf_op jit(solution)/shard_map/ppermute | solution.py:64
  135.0 6.6 %collective-permute-start.27 = (f32[200,192]{1,0:T(8,128)S(1)}, f32[200,192]{1,0:T(8,128)S(1)}, u32[]{:S(2)}, u32[]{:S(2)}) collective-permute-start(f32[200,192]{1,0:T(8,128)S(1)} %select_add_fusion), channel_id=1, source_target_pairs={{0,96},{16,112},{32,0},{48,16},{64,32},{80,48},{96,64},{112,80},{1... | collective-permute-start | bytes 460808 | tf_op jit(solution)/shard_map/ppermute | solution.py:64
  141.7 3.5 %collective-permute-start.28 = (f32[200,192]{1,0:T(8,128)S(1)}, f32[200,192]{1,0:T(8,128)S(1)}, u32[]{:S(2)}, u32[]{:S(2)}) collective-permute-start(f32[200,192]{1,0:T(8,128)S(1)} %select_add_fusion), channel_id=1, source_target_pairs={{0,64},{16,80},{32,96},{48,112},{64,0},{80,16},{96,32},{112,48},{1... | collective-permute-start | bytes 460808 | tf_op jit(solution)/shard_map/ppermute | solution.py:64
  146.4 4.3 %collective-permute-done.27 = f32[200,192]{1,0:T(8,128)S(1)} collective-permute-done((f32[200,192]{1,0:T(8,128)S(1)}, f32[200,192]{1,0:T(8,128)S(1)}, u32[]{:S(2)}, u32[]{:S(2)}) %collective-permute-start.27) | collective-permute-done | bytes 153632 | tf_op jit(solution)/shard_map/ppermute | solution.py:64
  151.1 3.8 %collective-permute-done.29 = f32[200,192]{1,0:T(8,128)S(1)} collective-permute-done((f32[200,192]{1,0:T(8,128)S(1)}, f32[200,192]{1,0:T(8,128)S(1)}, u32[]{:S(2)}, u32[]{:S(2)}) %collective-permute-start.29) | collective-permute-done | bytes 153632 | tf_op jit(solution)/shard_map/ppermute | solution.py:64
  155.9 23.5 %shard_map.42.refs_0_ = f32[192,192]{1,0:T(8,128)} custom-call(f32[192,192]{1,0:T(8,128)} %bitcast_select_fusion.1.c_ref), custom_call_target="tpu_custom_call" | custom-call | tf_op jit(solution)/shard_map/pallas_call | solution.py:143
  179.4 3.5 %shard_map.43 = f32[1536,128]{1,0:T(8,128)} custom-call(f32[192,192]{1,0:T(8,128)} %shard_map.42.refs_0_, f32[1536,128]{1,0:T(8,128)} %bitcast.20), custom_call_target="tpu_custom_call" | custom-call | tf_op jit(solution)/shard_map/pallas_call | solution.py:168
  182.9 3.8 %all-to-all-start.1 = ((f32[16,12,8,128]{3,2,1,0:T(8,128)}), f32[16,12,8,128]{3,2,1,0:T(8,128)S(1)}, u32[]{:S(2)}, u32[]{:S(2)}) async-start(f32[16,12,8,128]{3,2,1,0:T(8,128)} %bitcast.21), calls=%async_computation.1 | async-start | bytes 1572864 | tf_op jit(solution)/shard_map/all_to_all | solution.py:226
  187.9 13.5 %all-to-all-done.1 = f32[16,12,8,128]{3,2,1,0:T(8,128)S(1)} async-done(((f32[16,12,8,128]{3,2,1,0:T(8,128)}), f32[16,12,8,128]{3,2,1,0:T(8,128)S(1)}, u32[]{:S(2)}, u32[]{:S(2)}) %all-to-all-start.1) | async-done | bytes 786464 | tf_op jit(solution)/shard_map/all_to_all | solution.py:226
  (217 shorter events, 58.0 us)
Async XLA Ops:
  1.9 8.9 %collective-permute-start = (f32[6,4,32,128]{3,2,1,0:T(8,128)S(1)}, f32[6,4,32,128]{3,2,1,0:T(8,128)S(1)}, u32[]{:S(2)}, u32[]{:S(2)}) collective-permute-start(f32[6,4,32,128]{3,2,1,0:T(8,128)S(1)} %get-tuple-element.76), channel_id=1, source_target_pairs={{16,0},{32,16},{48,32},{64,48},{80,64},{96,80},{112,96},{0,112},{1... | collective-permute-start | bytes 1179656 | tf_op jit(solution)/shard_map/ppermute | solution.py:26
  4.2 8.4 %collective-permute-start.1 = (f32[6,4,32,128]{3,2,1,0:T(8,128)S(1)}, f32[6,4,32,128]{3,2,1,0:T(8,128)S(1)}, u32[]{:S(2)}, u32[]{:S(2)}) collective-permute-start(f32[6,4,32,128]{3,2,1,0:T(8,128)S(1)} %get-tuple-element.76), channel_id=1, source_target_pairs={{0,16},{16,32},{32,48},{48,64},{64,80},{80,96},{96,112},{112,0},{1... | collective-permute-start | bytes 1179656 | tf_op jit(solution)/shard_map/ppermute | solution.py:25
  4.2 13.6 %collective-permute-start.8 = (f32[6,4,32,128]{3,2,1,0:T(8,128)S(1)}, f32[6,4,32,128]{3,2,1,0:T(8,128)S(1)}, u32[]{:S(2)}, u32[]{:S(2)}) collective-permute-start(f32[6,4,32,128]{3,2,1,0:T(8,128)S(1)} %get-tuple-element.77), channel_id=1, source_target_pairs={{16,0},{32,16},{48,32},{64,48},{80,64},{96,80},{112,96},{0,112},{1... | collective-permute-start | bytes 1179656 | tf_op jit(solution)/shard_map/ppermute | solution.py:26
  7.2 10.6 %collective-permute-start.9 = (f32[6,4,32,128]{3,2,1,0:T(8,128)S(1)}, f32[6,4,32,128]{3,2,1,0:T(8,128)S(1)}, u32[]{:S(2)}, u32[]{:S(2)}) collective-permute-start(f32[6,4,32,128]{3,2,1,0:T(8,128)S(1)} %get-tuple-element.77), channel_id=1, source_target_pairs={{0,16},{16,32},{32,48},{48,64},{64,80},{80,96},{96,112},{112,0},{1... | collective-permute-start | bytes 1179656 | tf_op jit(solution)/shard_map/ppermute | solution.py:25
  16.3 8.4 %collective-permute-start.2 = (f32[6,4,32,128]{3,2,1,0:T(8,128)S(1)}, f32[6,4,32,128]{3,2,1,0:T(8,128)S(1)}, u32[]{:S(2)}, u32[]{:S(2)}) collective-permute-start(f32[6,4,32,128]{3,2,1,0:T(8,128)S(1)} %get-tuple-element.6), channel_id=1, source_target_pairs={{16,0},{32,16},{48,32},{64,48},{80,64},{96,80},{112,96},{0,112},{1... | collective-permute-start | bytes 1179656 | tf_op jit(solution)/shard_map/ppermute | solution.py:26
  17.7 8.4 %collective-permute-start.3 = (f32[6,4,32,128]{3,2,1,0:T(8,128)S(1)}, f32[6,4,32,128]{3,2,1,0:T(8,128)S(1)}, u32[]{:S(2)}, u32[]{:S(2)}) collective-permute-start(f32[6,4,32,128]{3,2,1,0:T(8,128)S(1)} %get-tuple-element.6), channel_id=1, source_target_pairs={{0,16},{16,32},{32,48},{48,64},{64,80},{80,96},{96,112},{112,0},{1... | collective-permute-start | bytes 1179656 | tf_op jit(solution)/shard_map/ppermute | solution.py:25
  21.6 9.9 %collective-permute-start.10 = (f32[6,4,32,128]{3,2,1,0:T(8,128)S(1)}, f32[6,4,32,128]{3,2,1,0:T(8,128)S(1)}, u32[]{:S(2)}, u32[]{:S(2)}) collective-permute-start(f32[6,4,32,128]{3,2,1,0:T(8,128)S(1)} %get-tuple-element.8), channel_id=1, source_target_pairs={{16,0},{32,16},{48,32},{64,48},{80,64},{96,80},{112,96},{0,112},{1... | collective-permute-start | bytes 1179656 | tf_op jit(solution)/shard_map/ppermute | solution.py:26
  24.6 8.4 %collective-permute-start.11 = (f32[6,4,32,128]{3,2,1,0:T(8,128)S(1)}, f32[6,4,32,128]{3,2,1,0:T(8,128)S(1)}, u32[]{:S(2)}, u32[]{:S(2)}) collective-permute-start(f32[6,4,32,128]{3,2,1,0:T(8,128)S(1)} %get-tuple-element.8), channel_id=1, source_target_pairs={{0,16},{16,32},{32,48},{48,64},{64,80},{80,96},{96,112},{112,0},{1... | collective-permute-start | bytes 1179656 | tf_op jit(solution)/shard_map/ppermute | solution.py:25
  29.7 8.7 %collective-permute-start.4 = (f32[6,4,32,128]{3,2,1,0:T(8,128)S(1)}, f32[6,4,32,128]{3,2,1,0:T(8,128)S(1)}, u32[]{:S(2)}, u32[]{:S(2)}) collective-permute-start(f32[6,4,32,128]{3,2,1,0:T(8,128)S(1)} %fusion.206), channel_id=1, source_target_pairs={{16,0},{32,16},{48,32},{64,48},{80,64},{96,80},{112,96},{0,112},{1... | collective-permute-start | bytes 1179656 | tf_op jit(solution)/shard_map/ppermute | solution.py:26
  31.4 8.4 %collective-permute-start.5 = (f32[6,4,32,128]{3,2,1,0:T(8,128)S(1)}, f32[6,4,32,128]{3,2,1,0:T(8,128)S(1)}, u32[]{:S(2)}, u32[]{:S(2)}) collective-permute-start(f32[6,4,32,128]{3,2,1,0:T(8,128)S(1)} %fusion.206), channel_id=1, source_target_pairs={{0,16},{16,32},{32,48},{48,64},{64,80},{80,96},{96,112},{112,0},{1... | collective-permute-start | bytes 1179656 | tf_op jit(solution)/shard_map/ppermute | solution.py:25
  36.6 8.7 %collective-permute-start.12 = (f32[6,4,32,128]{3,2,1,0:T(8,128)S(1)}, f32[6,4,32,128]{3,2,1,0:T(8,128)S(1)}, u32[]{:S(2)}, u32[]{:S(2)}) collective-permute-start(f32[6,4,32,128]{3,2,1,0:T(8,128)S(1)} %fusion.108), channel_id=1, source_target_pairs={{16,0},{32,16},{48,32},{64,48},{80,64},{96,80},{112,96},{0,112},{1... | collective-permute-start | bytes 1179656 | tf_op jit(solution)/shard_map/ppermute | solution.py:26
  38.2 8.4 %collective-permute-start.13 = (f32[6,4,32,128]{3,2,1,0:T(8,128)S(1)}, f32[6,4,32,128]{3,2,1,0:T(8,128)S(1)}, u32[]{:S(2)}, u32[]{:S(2)}) collective-permute-start(f32[6,4,32,128]{3,2,1,0:T(8,128)S(1)} %fusion.108), channel_id=1, source_target_pairs={{0,16},{16,32},{32,48},{48,64},{64,80},{80,96},{96,112},{112,0},{1... | collective-permute-start | bytes 1179656 | tf_op jit(solution)/shard_map/ppermute | solution.py:25
  43.4 9.0 %collective-permute-start.6 = (f32[6,4,32,128]{3,2,1,0:T(8,128)S(1)}, f32[6,4,32,128]{3,2,1,0:T(8,128)S(1)}, u32[]{:S(2)}, u32[]{:S(2)}) collective-permute-start(f32[6,4,32,128]{3,2,1,0:T(8,128)S(1)} %fusion.181), channel_id=1, source_target_pairs={{16,0},{32,16},{48,32},{64,48},{80,64},{96,80},{112,96},{0,112},{1... | collective-permute-start | bytes 1179656 | tf_op jit(solution)/shard_map/ppermute | solution.py:26
  45.1 8.4 %collective-permute-start.7 = (f32[6,4,32,128]{3,2,1,0:T(8,128)S(1)}, f32[6,4,32,128]{3,2,1,0:T(8,128)S(1)}, u32[]{:S(2)}, u32[]{:S(2)}) collective-permute-start(f32[6,4,32,128]{3,2,1,0:T(8,128)S(1)} %fusion.181), channel_id=1, source_target_pairs={{0,16},{16,32},{32,48},{48,64},{64,80},{80,96},{96,112},{112,0},{1... | collective-permute-start | bytes 1179656 | tf_op jit(solution)/shard_map/ppermute | solution.py:25
  50.3 9.0 %collective-permute-start.14 = (f32[6,4,32,128]{3,2,1,0:T(8,128)S(1)}, f32[6,4,32,128]{3,2,1,0:T(8,128)S(1)}, u32[]{:S(2)}, u32[]{:S(2)}) collective-permute-start(f32[6,4,32,128]{3,2,1,0:T(8,128)S(1)} %fusion.83), channel_id=1, source_target_pairs={{16,0},{32,16},{48,32},{64,48},{80,64},{96,80},{112,96},{0,112},{1... | collective-permute-start | bytes 1179656 | tf_op jit(solution)/shard_map/ppermute | solution.py:26
  52.2 8.4 %collective-permute-start.15 = (f32[6,4,32,128]{3,2,1,0:T(8,128)S(1)}, f32[6,4,32,128]{3,2,1,0:T(8,128)S(1)}, u32[]{:S(2)}, u32[]{:S(2)}) collective-permute-start(f32[6,4,32,128]{3,2,1,0:T(8,128)S(1)} %fusion.83), channel_id=1, source_target_pairs={{0,16},{16,32},{32,48},{48,64},{64,80},{80,96},{96,112},{112,0},{1... | collective-permute-start | bytes 1179656 | tf_op jit(solution)/shard_map/ppermute | solution.py:25
  57.1 9.0 %collective-permute-start.16 = (f32[6,4,32,128]{3,2,1,0:T(8,128)S(1)}, f32[6,4,32,128]{3,2,1,0:T(8,128)S(1)}, u32[]{:S(2)}, u32[]{:S(2)}) collective-permute-start(f32[6,4,32,128]{3,2,1,0:T(8,128)S(1)} %fusion.156), channel_id=1, source_target_pairs={{16,0},{32,16},{48,32},{64,48},{80,64},{96,80},{112,96},{0,112},{1... | collective-permute-start | bytes 1179656 | tf_op jit(solution)/shard_map/ppermute | solution.py:26
  59.1 8.4 %collective-permute-start.17 = (f32[6,4,32,128]{3,2,1,0:T(8,128)S(1)}, f32[6,4,32,128]{3,2,1,0:T(8,128)S(1)}, u32[]{:S(2)}, u32[]{:S(2)}) collective-permute-start(f32[6,4,32,128]{3,2,1,0:T(8,128)S(1)} %fusion.156), channel_id=1, source_target_pairs={{0,16},{16,32},{32,48},{48,64},{64,80},{80,96},{96,112},{112,0},{1... | collective-permute-start | bytes 1179656 | tf_op jit(solution)/shard_map/ppermute | solution.py:25
  64.2 7.0 %collective-permute-start.18 = (f32[6,4,32,128]{3,2,1,0:T(8,128)S(1)}, f32[6,4,32,128]{3,2,1,0:T(8,128)S(1)}, u32[]{:S(2)}, u32[]{:S(2)}) collective-permute-start(f32[6,4,32,128]{3,2,1,0:T(8,128)S(1)} %fusion.58), channel_id=1, source_target_pairs={{16,0},{32,16},{48,32},{64,48},{80,64},{96,80},{112,96},{0,112},{1... | collective-permute-start | bytes 1179656 | tf_op jit(solution)/shard_map/ppermute | solution.py:26
  65.9 8.4 %collective-permute-start.19 = (f32[6,4,32,128]{3,2,1,0:T(8,128)S(1)}, f32[6,4,32,128]{3,2,1,0:T(8,128)S(1)}, u32[]{:S(2)}, u32[]{:S(2)}) collective-permute-start(f32[6,4,32,128]{3,2,1,0:T(8,128)S(1)} %fusion.58), channel_id=1, source_target_pairs={{0,16},{16,32},{32,48},{48,64},{64,80},{80,96},{96,112},{112,0},{1... | collective-permute-start | bytes 1179656 | tf_op jit(solution)/shard_map/ppermute | solution.py:25
  77.5 27.9 %all-to-all-start = ((f32[16,2,12,8,128]{4,3,2,1,0:T(8,128)}), f32[16,2,12,8,128]{4,3,2,1,0:T(8,128)S(1)}, u32[]{:S(2)}, u32[]{:S(2)}) async-start(f32[16,2,12,8,128]{4,3,2,1,0:T(8,128)} %copy.10), calls=%async_computation | async-start | bytes 3145728 | tf_op jit(solution)/shard_map/all_to_all | solution.py:200
  112.6 5.8 %collective-permute-start.20 = (f32[200,192]{1,0:T(8,128)S(1)}, f32[200,192]{1,0:T(8,128)S(1)}, u32[]{:S(2)}, u32[]{:S(2)}) collective-permute-start(f32[200,192]{1,0:T(8,128)S(1)} %maximum_maximum_fusion), channel_id=1, source_target_pairs={{0,3},{1,0},{2,1},{3,2},{4,7},{5,4},{6,5},{7,6},{8,11},{9,8},{10,9... | collective-permute-start | bytes 460808 | tf_op jit(solution)/shard_map/ppermute | solution.py:64
  112.7 7.4 %collective-permute-start.21 = (f32[200,192]{1,0:T(8,128)S(1)}, f32[200,192]{1,0:T(8,128)S(1)}, u32[]{:S(2)}, u32[]{:S(2)}) collective-permute-start(f32[200,192]{1,0:T(8,128)S(1)} %maximum_maximum_fusion), channel_id=1, source_target_pairs={{0,2},{1,3},{2,0},{3,1},{4,6},{5,7},{6,4},{7,5},{8,10},{9,11},{10,... | collective-permute-start | bytes 460808 | tf_op jit(solution)/shard_map/ppermute | solution.py:64
  114.4 7.8 %collective-permute-start.22 = (f32[200,192]{1,0:T(8,128)S(1)}, f32[200,192]{1,0:T(8,128)S(1)}, u32[]{:S(2)}, u32[]{:S(2)}) collective-permute-start(f32[200,192]{1,0:T(8,128)S(1)} %maximum_maximum_fusion), channel_id=1, source_target_pairs={{0,1},{1,2},{2,3},{3,0},{4,5},{5,6},{6,7},{7,4},{8,9},{9,10},{10,1... | collective-permute-start | bytes 460808 | tf_op jit(solution)/shard_map/ppermute | solution.py:64
  122.4 5.8 %collective-permute-start.23 = (f32[200,192]{1,0:T(8,128)S(1)}, f32[200,192]{1,0:T(8,128)S(1)}, u32[]{:S(2)}, u32[]{:S(2)}) collective-permute-start(f32[200,192]{1,0:T(8,128)S(1)} %add_add_fusion.1), channel_id=1, source_target_pairs={{0,12},{1,13},{2,14},{3,15},{4,0},{5,1},{6,2},{7,3},{8,4},{9,5},{1... | collective-permute-start | bytes 460808 | tf_op jit(solution)/shard_map/ppermute | solution.py:64
  123.9 7.3 %collective-permute-start.24 = (f32[200,192]{1,0:T(8,128)S(1)}, f32[200,192]{1,0:T(8,128)S(1)}, u32[]{:S(2)}, u32[]{:S(2)}) collective-permute-start(f32[200,192]{1,0:T(8,128)S(1)} %add_add_fusion.1), channel_id=1, source_target_pairs={{0,8},{1,9},{2,10},{3,11},{4,12},{5,13},{6,14},{7,15},{8,0},{9,1},... | collective-permute-start | bytes 460808 | tf_op jit(solution)/shard_map/ppermute | solution.py:64
  125.6 7.7 %collective-permute-start.25 = (f32[200,192]{1,0:T(8,128)S(1)}, f32[200,192]{1,0:T(8,128)S(1)}, u32[]{:S(2)}, u32[]{:S(2)}) collective-permute-start(f32[200,192]{1,0:T(8,128)S(1)} %add_add_fusion.1), channel_id=1, source_target_pairs={{0,4},{1,5},{2,6},{3,7},{4,8},{5,9},{6,10},{7,11},{8,12},{9,13},{1... | collective-permute-start | bytes 460808 | tf_op jit(solution)/shard_map/ppermute | solution.py:64
  133.4 1.5 collective-permute-start.26
  135.0 15.7 %collective-permute-start.27 = (f32[200,192]{1,0:T(8,128)S(1)}, f32[200,192]{1,0:T(8,128)S(1)}, u32[]{:S(2)}, u32[]{:S(2)}) collective-permute-start(f32[200,192]{1,0:T(8,128)S(1)} %select_add_fusion), channel_id=1, source_target_pairs={{0,96},{16,112},{32,0},{48,16},{64,32},{80,48},{96,64},{112,80},{1... | collective-permute-start | bytes 460808 | tf_op jit(solution)/shard_map/ppermute | solution.py:64
  141.7 9.5 %collective-permute-start.28 = (f32[200,192]{1,0:T(8,128)S(1)}, f32[200,192]{1,0:T(8,128)S(1)}, u32[]{:S(2)}, u32[]{:S(2)}) collective-permute-start(f32[200,192]{1,0:T(8,128)S(1)} %select_add_fusion), channel_id=1, source_target_pairs={{0,64},{16,80},{32,96},{48,112},{64,0},{80,16},{96,32},{112,48},{1... | collective-permute-start | bytes 460808 | tf_op jit(solution)/shard_map/ppermute | solution.py:64
  145.1 9.8 %collective-permute-start.29 = (f32[200,192]{1,0:T(8,128)S(1)}, f32[200,192]{1,0:T(8,128)S(1)}, u32[]{:S(2)}, u32[]{:S(2)}) collective-permute-start(f32[200,192]{1,0:T(8,128)S(1)} %select_add_fusion), channel_id=1, source_target_pairs={{0,32},{16,48},{32,64},{48,80},{64,96},{80,112},{96,0},{112,16},{1... | collective-permute-start | bytes 460808 | tf_op jit(solution)/shard_map/ppermute | solution.py:64
  182.9 18.4 %all-to-all-start.1 = ((f32[16,12,8,128]{3,2,1,0:T(8,128)}), f32[16,12,8,128]{3,2,1,0:T(8,128)S(1)}, u32[]{:S(2)}, u32[]{:S(2)}) async-start(f32[16,12,8,128]{3,2,1,0:T(8,128)} %bitcast.21), calls=%async_computation.1 | async-start | bytes 1572864 | tf_op jit(solution)/shard_map/all_to_all | solution.py:226
  (3 other events, 14.8 us)
